TPU v7x, 256 devices: a whole 4x4x8 slice. The times are simulated.
256 devices in a mesh: tm: 64 (over y, z, core), freq: 4 (over x).
Axes of the slice: x: 4, y: 4, z: 8, core: 2. Of those that a mesh axis runs over, the one named last changes fastest.
Arguments:
- visibility: float32 [64, 2, 4096, 1024], P('freq', None, 'tm'), may hold values from -6 to 6
- codebook: bfloat16 [16, 8, 64, 128], replicated, may hold values from -0.1875 to 0.1875
- block_index: int32 [64, 64, 16, 16], P('tm', 'freq'), may hold values from -1 to 7, as said below
- block_scale: float32 [64, 64, 16, 16], P('tm', 'freq'), may hold values from 0.5 to 2
- fg_basis: float32 [16, 64, 64], replicated, may hold values from -0.75 to 0.75
- fg_count: int32 [64], P('tm'), may hold values from 1 to 32
Outputs:
- filtered: float32 [64, 64, 16, 128], P('tm', 'freq')
Inputs may be any that keep to these rules, and one draw needn't show every extreme that they name: `block_index`: -1 marks an absent block; block (k, f, j, l) is absent whenever 64 * l + 63 < 15 * k; other entries name a pattern.
All inputs are finite; a program needn't handle non-finite values.
Results may differ from a plain program's by a relative error of at most 0.014.
Values may be sent and summed in bfloat16 or wider, within the bound.
No kernel may reach another device: no remote copies, remote signals or barrier semaphores. Data moves between devices by JAX's collectives and lax.ppermute only.
A program may use at most 128 MiB of HBM per device.

v0:
```python
import math

import jax
import jax.numpy as jnp
import numpy as np
from jax import lax
from jax.sharding import Mesh
from jax.sharding import PartitionSpec as P

ELLS = 1024
TM_AXES = ("ty", "tz", "tc")


def realify(codebook):
    half = codebook.shape[-1] // 2
    real_part = codebook[..., :half]
    imag_part = codebook[..., half:]
    upper = jnp.concatenate([real_part, -imag_part], axis=-1)
    lower = jnp.concatenate([imag_part, real_part], axis=-1)
    return jnp.concatenate([upper, lower], axis=-2)


def phases(mode_values, time_index, sidereal_period):
    product = mode_values[:, None] * time_index[None, :] % sidereal_period
    angle = product.astype(jnp.float32) * jnp.float32(2.0 * math.pi / sidereal_period)
    return (jnp.cos(angle), jnp.sin(angle))


def ring_reduce_scatter(x, axis, n):
    i = lax.axis_index(axis)
    fwd = [(j, (j + 1) % n) for j in range(n)]

    def take(a, k):
        return lax.dynamic_index_in_dim(a, k % n, 0, keepdims=False)

    s = take(x, i - 1)
    for k in range(n - 1):
        s = lax.ppermute(s, axis, fwd) + take(x, i - k - 2)
    return s


def dft_table(mode_values, time_index, sidereal_period, norm_factor):
    cosine, sine = phases(mode_values, time_index, sidereal_period)
    cosine = cosine * jnp.float32(norm_factor)
    sine = sine * jnp.float32(norm_factor)
    return jnp.stack([jnp.stack([cosine, sine], 1), jnp.stack([-sine, cosine], 1)], 1)


def spectra_of(visibility, time_index, sidereal_period, norm_factor, mode_step, ny, nz):
    c = lax.axis_index("tc")
    h = visibility.shape[0] // 2
    jy = jnp.arange(ny, dtype=jnp.int32)
    jz = jnp.arange(nz, dtype=jnp.int32)
    halves = []
    for part, z_major in ((visibility[:h], True), (visibility[h:], False)):
        if z_major:
            pair = (jy[None, :] * nz + jz[:, None]).reshape(-1)
        else:
            pair = (jy[:, None] * nz + jz[None, :]).reshape(-1)
        rows = jnp.concatenate([pair * 2 + (1 - c), pair * 2 + c])
        table = dft_table(mode_step * rows, time_index, sidereal_period, norm_factor)
        out = jnp.einsum("rdct,fctb->rdfb", table, part, precision=lax.Precision.HIGH)
        half_rows = ny * nz
        y = out[half_rows:] + lax.ppermute(out[:half_rows], "tc", [(0, 1), (1, 0)])
        if z_major:
            y = y.reshape(nz, ny, *y.shape[1:])
            y = ring_reduce_scatter(ring_reduce_scatter(y, "tz", nz), "ty", ny)
        else:
            y = y.reshape(ny, nz, *y.shape[1:])
            y = ring_reduce_scatter(ring_reduce_scatter(y, "ty", ny), "tz", nz)
        halves.append(y)
    return jnp.concatenate(halves, axis=1)


def local(visibility, codebook, block_index, block_scale, fg_basis, fg_count, ny, nz):
    tm_count = ny * nz * 2
    fr_count = lax.axis_size("freq")
    chans_dev = visibility.shape[0]
    time_dev = visibility.shape[2]
    base_all = visibility.shape[3]
    modes_dev = block_index.shape[0]
    modes_all = modes_dev * tm_count
    mode_step = 2 * (ELLS // (2 * modes_all)) - 1
    code_count = codebook.shape[1]
    block_len = codebook.shape[2]
    bblocks = base_all // block_len
    sidereal_period = time_dev * tm_count
    norm_factor = float(sidereal_period) ** (-0.5)
    tm_pos = (lax.axis_index("ty") * nz + lax.axis_index("tz")) * 2 + lax.axis_index("tc")
    time_index = tm_pos * time_dev + jnp.arange(time_dev, dtype=jnp.int32)
    spectra = spectra_of(visibility, time_index, sidereal_period, norm_factor, mode_step, ny, nz)
    spectra = spectra.astype(jnp.bfloat16)
    vectors = spectra.reshape(modes_dev, 2, chans_dev, bblocks, block_len)
    vectors = jnp.transpose(vectors, (0, 2, 3, 1, 4)).reshape(
        modes_dev, chans_dev, bblocks, 2 * block_len
    )
    vectors = vectors.astype(jnp.float32)
    code_matrix = realify(codebook).astype(jnp.float32)
    block_selector = jnp.where(
        block_index[..., None] == jnp.arange(code_count, dtype=jnp.int32),
        block_scale[..., None],
        jnp.float32(0.0),
    )
    combined = jnp.einsum(
        "mfblp,mfbi->mflpi", block_selector, vectors, precision=lax.Precision.HIGHEST
    )
    weights = jnp.einsum("mflpi,lpij->mflj", combined, code_matrix, precision=lax.Precision.HIGHEST)
    weights_bf = weights.astype(jnp.bfloat16)
    fr_pos = lax.axis_index("freq")
    basis_cols = lax.dynamic_slice_in_dim(fg_basis, fr_pos * chans_dev, chans_dev, 2)
    basis_cols = basis_cols.reshape(fg_basis.shape[0], fr_count, chans_dev, chans_dev)
    summed = None
    for s in range(fr_count):
        if s == 0:
            got = weights_bf
        else:
            got = lax.ppermute(weights_bf, "freq", [(j, (j + s) % fr_count) for j in range(fr_count)])
        rows = lax.dynamic_index_in_dim(basis_cols, (fr_pos - s) % fr_count, 1, keepdims=False)
        term = jnp.einsum(
            "lfk,mflj->mklj", rows, got.astype(jnp.float32), precision=lax.Precision.HIGHEST
        )
        summed = term if summed is None else summed + term
    mode_index = fr_pos * chans_dev + jnp.arange(chans_dev, dtype=jnp.int32)
    retained = mode_index[None, :] >= fg_count[:, None]
    return jnp.where(retained[:, :, None, None], summed, jnp.float32(0.0))


def solution(mesh):
    tm_count = mesh.shape["tm"]
    nz = 8 if tm_count % 16 == 0 else 1
    ny = tm_count // (2 * nz)
    devices = np.asarray(mesh.devices).reshape(ny, nz, 2, mesh.shape["freq"])
    split_mesh = Mesh(devices, TM_AXES + ("freq",))
    placed = (
        P("freq", None, TM_AXES, None),
        P(),
        P(TM_AXES, "freq", None, None),
        P(TM_AXES, "freq", None, None),
        P(),
        P(TM_AXES),
    )

    def body(*args):
        return local(*args, ny=ny, nz=nz)

    return jax.shard_map(
        body, mesh=split_mesh, in_specs=placed, out_specs=P(TM_AXES, "freq", None, None), check_vma=False
    )
```

profile of v0, /device:TPU:6, one launch (start us, length us, event | category | flops | bytes accessed | tf_op | source)
XLA Modules:
  0.0 132.6 jit_solution(7283065176801828773)
XLA Ops:
  0.5 0.4 sine_multiply_fusion.1
  0.9 4.4 %fusion.14 = f32[64,2,8,1024]{3,0,2,1:T(8,128)S(1)} fusion(f32[16,2,64,1024]{3,2,1,0:T(8,128)} %param.6, f32[64,1,2,64]{3,0,2,1:T(8,128)S(1)} %get-tuple-element.13, f32[64,1,2,64]{3,0,2,1:T(8,128)S(1)} %get-tuple-element.12), kind=kOutput, calls=%fused_computation.14 | convolution fusion | flops 805322752 | bytes 8454144 | tf_op jit(solution)/shard_map/rdct,fctb->rdfb/dot_general | solution.py:62
  5.3 1.6 %slice.33 = f32[32,2,8,1024]{3,0,2,1:T(8,128)} slice(f32[64,2,8,1024]{3,0,2,1:T(8,128)S(1)} %fusion.14), slice={[0:32], [0:2], [0:8], [0:1024]} | slice | bytes 4194304 | tf_op jit(solution)/shard_map/slice | solution.py:64
  6.8 1.1 copy-done.1
  8.0 2.1 %fusion.17 = f32[64,2,8,1024]{3,0,2,1:T(8,128)S(1)} fusion(f32[16,2,64,1024]{3,2,1,0:T(8,128)S(1)} %copy-done.4, f32[64,1,2,64]{3,0,2,1:T(8,128)S(1)} %get-tuple-element.15, f32[64,1,2,64]{3,0,2,1:T(8,128)S(1)} %get-tuple-element.14), kind=kOutput, calls=%fused_computation.15 | convolution fusion | flops 805322752 | bytes 8519680 | tf_op jit(solution)/shard_map/rdct,fctb->rdfb/dot_general | solution.py:62
  10.1 2.0 %copy-done.2 = f32[64,2,8,1024]{3,0,2,1:T(8,128)} copy-done((f32[64,2,8,1024]{3,0,2,1:T(8,128)}, f32[64,2,8,1024]{3,0,2,1:T(8,128)S(1)}, u32[]{:S(2)}) %copy-start.2) | copy-done | bytes 4194328
  12.1 1.5 %slice.35 = f32[32,2,8,1024]{3,0,2,1:T(8,128)} slice(f32[64,2,8,1024]{3,0,2,1:T(8,128)S(1)} %fusion.17), slice={[0:32], [0:2], [0:8], [0:1024]} | slice | bytes 4194304 | tf_op jit(solution)/shard_map/slice | solution.py:64
  13.6 2.0 %slice_add_fusion.1 = f32[32,2,8,1024]{3,0,2,1:T(8,128)S(1)} fusion(f32[32,2,8,1024]{3,0,2,1:T(8,128)S(1)} %collective-permute-done, f32[64,2,8,1024]{3,0,2,1:T(8,128)} %copy-done.1), kind=kLoop, calls=%fused_computation.18 | loop fusion | flops 524288 | bytes 6291456 | tf_op jit(solution)/shard_map/add | solution.py:64
  15.6 1.2 copy.41
  16.9 2.0 %collective-permute-start.1 = (f32[4,2,8,1024]{3,2,1,0:T(8,128)S(1)}, f32[4,2,8,1024]{3,2,1,0:T(8,128)S(1)}, u32[]{:S(2)}, u32[]{:S(2)}) collective-permute-start(f32[4,2,8,1024]{3,2,1,0:T(8,128)S(1)} %dynamic-slice_bitcast_fusion), channel_id=1, source_target_pairs={{0,8},{8,16},{16,24},{24,32},{32,40},{40,48},{48,56},{56,0},{1,9},... | collective-permute-start | bytes 786440 | tf_op jit(solution)/shard_map/ppermute | solution.py:38
  18.9 2.0 %fusion.20 = f32[4,8,2,8,1024]{4,1,0,3,2:T(8,128)S(1)} fusion(f32[32,2,8,1024]{3,0,2,1:T(8,128)} %collective-permute-done.11, f32[64,2,8,1024]{3,0,2,1:T(8,128)S(1)} %copy-done.3), kind=kLoop, calls=%fused_computation.17 | loop fusion | flops 524288 | bytes 6291456 | tf_op jit(solution)/shard_map/reshape | solution.py:69
  20.9 1.2 constant_dynamic-slice_fusion.1
  22.0 1.1 copy.62
  23.1 1.6 %collective-permute-start.12 = (f32[8,2,8,1024]{3,2,1,0:T(8,128)}, f32[8,2,8,1024]{3,2,1,0:T(8,128)}, u32[]{:S(2)}, u32[]{:S(2)}) collective-permute-start(f32[8,2,8,1024]{3,2,1,0:T(8,128)} %bitcast.149), channel_id=1, source_target_pairs={{0,64},{64,128},{128,192},{192,0},{1,65},{65,129},{129,193},{193,1... | collective-permute-start | bytes 1572872 | tf_op jit(solution)/shard_map/ppermute | solution.py:38
  24.7 5.1 %collective-permute-done.1 = f32[4,2,8,1024]{3,2,1,0:T(8,128)S(1)} collective-permute-done((f32[4,2,8,1024]{3,2,1,0:T(8,128)S(1)}, f32[4,2,8,1024]{3,2,1,0:T(8,128)S(1)}, u32[]{:S(2)}, u32[]{:S(2)}) %collective-permute-start.1) | collective-permute-done | bytes 262176 | tf_op jit(solution)/shard_map/ppermute | solution.py:38
  30.0 9.5 %collective-permute-done.2 = f32[4,2,8,1024]{3,2,1,0:T(8,128)} collective-permute-done((f32[4,2,8,1024]{3,2,1,0:T(8,128)S(1)}, f32[4,2,8,1024]{3,2,1,0:T(8,128)}, u32[]{:S(2)}, u32[]{:S(2)}) %collective-permute-start.2) | collective-permute-done | bytes 262176 | tf_op jit(solution)/shard_map/ppermute | solution.py:38
  39.5 1.0 bitcast_add_fusion.5
  40.5 0.3 collective-permute-start.3
  40.7 2.3 %fusion.36 = f32[8,2,8,1024]{3,2,1,0:T(8,128)} fusion(f32[8,2,8,1024]{3,2,1,0:T(8,128)} %collective-permute-done.12, f32[1,8,2,8,1024]{4,1,0,3,2:T(8,128)} %get-tuple-element.7), kind=kLoop, calls=%fused_computation.36 | loop fusion | flops 131072 | bytes 1572864 | tf_op jit(solution)/shard_map/add | solution.py:38
  43.1 1.5 %collective-permute-start.13 = (f32[8,2,8,1024]{3,2,1,0:T(8,128)}, f32[8,2,8,1024]{3,2,1,0:T(8,128)}, u32[]{:S(2)}, u32[]{:S(2)}) collective-permute-start(f32[8,2,8,1024]{3,2,1,0:T(8,128)} %fusion.36), channel_id=1, source_target_pairs={{0,64},{64,128},{128,192},{192,0},{1,65},{65,129},{129,193},{193,1... | collective-permute-start | bytes 1572872 | tf_op jit(solution)/shard_map/ppermute | solution.py:38
  44.5 4.8 %collective-permute-done.3 = f32[4,2,8,1024]{3,2,1,0:T(8,128)S(1)} collective-permute-done((f32[4,2,8,1024]{3,2,1,0:T(8,128)S(1)}, f32[4,2,8,1024]{3,2,1,0:T(8,128)S(1)}, u32[]{:S(2)}, u32[]{:S(2)}) %collective-permute-start.3) | collective-permute-done | bytes 262176 | tf_op jit(solution)/shard_map/ppermute | solution.py:38
  49.5 7.8 %collective-permute-done.4 = f32[4,2,8,1024]{3,2,1,0:T(8,128)} collective-permute-done((f32[4,2,8,1024]{3,2,1,0:T(8,128)S(1)}, f32[4,2,8,1024]{3,2,1,0:T(8,128)}, u32[]{:S(2)}, u32[]{:S(2)}) %collective-permute-start.4) | collective-permute-done | bytes 262176 | tf_op jit(solution)/shard_map/ppermute | solution.py:38
  57.3 1.0 bitcast_add_fusion.3
  58.4 1.4 %fusion.35 = f32[8,2,8,1024]{3,2,1,0:T(8,128)S(1)} fusion(f32[8,2,8,1024]{3,2,1,0:T(8,128)} %collective-permute-done.13, f32[1,8,2,8,1024]{4,1,0,3,2:T(8,128)S(1)} %get-tuple-element.6), kind=kLoop, calls=%fused_computation.34 | loop fusion | flops 131072 | bytes 1572864 | tf_op jit(solution)/shard_map/add | solution.py:38
  59.8 1.3 %collective-permute-start.14 = (f32[8,2,8,1024]{3,2,1,0:T(8,128)S(1)}, f32[8,2,8,1024]{3,2,1,0:T(8,128)S(1)}, u32[]{:S(2)}, u32[]{:S(2)}) collective-permute-start(f32[8,2,8,1024]{3,2,1,0:T(8,128)S(1)} %fusion.35), channel_id=1, source_target_pairs={{0,64},{64,128},{128,192},{192,0},{1,65},{65,129},{129,193},{193,1... | collective-permute-start | bytes 1572872 | tf_op jit(solution)/shard_map/ppermute | solution.py:38
  61.1 3.5 %slice_negate_fusion = (bf16[16,8,64,64]{3,2,1,0:T(8,128)(2,1)}, bf16[16,8,64,64]{3,2,1,0:T(8,128)(2,1)}, bf16[16,8,64,64]{3,2,1,0:T(8,128)(2,1)}) fusion(bf16[16,8,64,128]{3,2,1,0:T(8,128)(2,1)S(1)} %copy-done.5), kind=kLoop, calls=%fused_computation.135 | loop fusion | flops 524288 | bytes 5242880 | tf_op jit(solution)/shard_map/neg | solution.py:18
  64.6 1.3 %collective-permute-done.5 = f32[4,2,8,1024]{3,2,1,0:T(8,128)S(1)} collective-permute-done((f32[4,2,8,1024]{3,2,1,0:T(8,128)S(1)}, f32[4,2,8,1024]{3,2,1,0:T(8,128)S(1)}, u32[]{:S(2)}, u32[]{:S(2)}) %collective-permute-start.5) | collective-permute-done | bytes 262176 | tf_op jit(solution)/shard_map/ppermute | solution.py:38
  66.1 6.4 %collective-permute-done.14 = f32[8,2,8,1024]{3,2,1,0:T(8,128)S(1)} collective-permute-done((f32[8,2,8,1024]{3,2,1,0:T(8,128)S(1)}, f32[8,2,8,1024]{3,2,1,0:T(8,128)S(1)}, u32[]{:S(2)}, u32[]{:S(2)}) %collective-permute-start.14) | collective-permute-done | bytes 524320 | tf_op jit(solution)/shard_map/ppermute | solution.py:38
  72.4 0.3 fusion.34
  72.8 0.6 dynamic-slice_bitcast_fusion.1
  73.4 0.4 collective-permute-start.15
  73.8 1.0 constant_dynamic-slice_fusion
  75.5 3.8 %collective-permute-done.15 = f32[2,8,1024]{2,1,0:T(8,128)} collective-permute-done((f32[2,8,1024]{2,1,0:T(8,128)}, f32[2,8,1024]{2,1,0:T(8,128)}, u32[]{:S(2)}, u32[]{:S(2)}) %collective-permute-start.15) | collective-permute-done | bytes 65568 | tf_op jit(solution)/shard_map/ppermute | solution.py:38
  79.3 0.8 bitcast_add_fusion.13
  80.2 1.7 %bitcast_add_fusion.1 = f32[4,2,8,1024]{3,2,1,0:T(8,128)} fusion(f32[4,2,8,1024]{3,2,1,0:T(8,128)} %collective-permute-done.6, f32[8,4,2,8,1024]{4,3,2,1,0:T(8,128)S(1)} %bitcast.157, s32[]{:T(128)S(6)} %select_n.228), kind=kLoop, calls=%fused_computation.42 | loop fusion | flops 65536 | bytes 786436 | tf_op jit(solution)/shard_map/add | solution.py:38
  81.9 1.3 collective-permute-start.7
  83.2 3.1 %collective-permute-done.16 = f32[2,8,1024]{2,1,0:T(8,128)S(1)} collective-permute-done((f32[2,8,1024]{2,1,0:T(8,128)S(1)}, f32[2,8,1024]{2,1,0:T(8,128)S(1)}, u32[]{:S(2)}, u32[]{:S(2)}) %collective-permute-start.16) | collective-permute-done | bytes 65568 | tf_op jit(solution)/shard_map/ppermute | solution.py:38
  86.2 0.6 bitcast_add_fusion.12
  87.1 1.0 copy.17
  88.1 4.6 %collective-permute-done.17 = f32[2,8,1024]{2,1,0:T(8,128)} collective-permute-done((f32[2,8,1024]{2,1,0:T(8,128)}, f32[2,8,1024]{2,1,0:T(8,128)}, u32[]{:S(2)}, u32[]{:S(2)}) %collective-permute-start.17) | collective-permute-done | bytes 65568 | tf_op jit(solution)/shard_map/ppermute | solution.py:38
  92.7 0.8 bitcast_add_fusion.11
  93.6 1.0 bitcast_add_fusion
  94.7 4.3 %collective-permute-done.18 = f32[2,8,1024]{2,1,0:T(8,128)S(1)} collective-permute-done((f32[2,8,1024]{2,1,0:T(8,128)S(1)}, f32[2,8,1024]{2,1,0:T(8,128)S(1)}, u32[]{:S(2)}, u32[]{:S(2)}) %collective-permute-start.18) | collective-permute-done | bytes 65568 | tf_op jit(solution)/shard_map/ppermute | solution.py:38
  99.2 1.0 collective-permute-done.8
  100.2 0.3 collective-permute-start.9
  100.5 4.4 %collective-permute-done.19 = f32[2,8,1024]{2,1,0:T(8,128)S(1)} collective-permute-done((f32[2,8,1024]{2,1,0:T(8,128)S(1)}, f32[2,8,1024]{2,1,0:T(8,128)S(1)}, u32[]{:S(2)}, u32[]{:S(2)}) %collective-permute-start.19) | collective-permute-done | bytes 65568 | tf_op jit(solution)/shard_map/ppermute | solution.py:38
  105.0 0.9 collective-permute-done.9
  106.1 4.4 %collective-permute-done.20 = f32[2,8,1024]{2,1,0:T(8,128)S(1)} collective-permute-done((f32[2,8,1024]{2,1,0:T(8,128)S(1)}, f32[2,8,1024]{2,1,0:T(8,128)S(1)}, u32[]{:S(2)}, u32[]{:S(2)}) %collective-permute-start.20) | collective-permute-done | bytes 65568 | tf_op jit(solution)/shard_map/ppermute | solution.py:38
  110.6 0.9 collective-permute-done.10
  111.7 4.4 %collective-permute-done.21 = f32[2,8,1024]{2,1,0:T(8,128)S(1)} collective-permute-done((f32[2,8,1024]{2,1,0:T(8,128)S(1)}, f32[2,8,1024]{2,1,0:T(8,128)S(1)}, u32[]{:S(2)}, u32[]{:S(2)}) %collective-permute-start.21) | collective-permute-done | bytes 65568 | tf_op jit(solution)/shard_map/ppermute | solution.py:38
  116.2 0.1 copy.30
  116.5 0.7 fusion.32
  117.2 6.5 %fusion.26 = bf16[16,128,16]{1,2,0:T(8,128)(2,1)S(1)} fusion(bf16[16,8,64,64]{3,2,1,0:T(8,128)(2,1)} %get-tuple-element.11, bf16[16,8,64,64]{3,2,1,0:T(8,128)(2,1)} %get-tuple-element.10, bf16[16,8,64,64]{3,2,1,0:T(8,128)(2,1)} %get-tuple-element.9, f32[16,16,8,128]{3,2,1,0:T(8,128)S(1)} %fusion.32), kind=kOutput, calls=%fused_computation.24 | convolution fusion | flops 419463168 | bytes 4259840 | tf_op jit(solution)/shard_map/mflpi,lpij->mflj/dot_general | solution.py:107
  123.7 0.6 collective-permute-start.22
  124.3 1.5 %collective-permute-start.24 = (bf16[1,16,16,128]{3,1,2,0:T(8,128)(2,1)S(1)}, bf16[1,16,16,128]{3,1,2,0:T(8,128)(2,1)S(1)}, u32[]{:S(2)}, u32[]{:S(2)}) collective-permute-start(bf16[1,16,16,128]{3,1,2,0:T(8,128)(2,1)S(1)} %bitcast.166), channel_id=1, source_target_pairs={{0,3},{1,0},{2,1},{3,2},{4,7},{5,4},{6,5},{7,6},{8,11},{9,8},{10,9... | collective-permute-start | bytes 196616 | tf_op jit(solution)/shard_map/ppermute | solution.py:117
  125.8 1.4 %collective-permute-start.23 = (bf16[1,16,16,128]{3,1,2,0:T(8,128)(2,1)S(1)}, bf16[1,16,16,128]{3,1,2,0:T(8,128)(2,1)S(1)}, u32[]{:S(2)}, u32[]{:S(2)}) collective-permute-start(bf16[1,16,16,128]{3,1,2,0:T(8,128)(2,1)S(1)} %bitcast.167), channel_id=1, source_target_pairs={{0,2},{1,3},{2,0},{3,1},{4,6},{5,7},{6,4},{7,5},{8,10},{9,11},{10,... | collective-permute-start | bytes 196616 | tf_op jit(solution)/shard_map/ppermute | solution.py:117
  127.2 0.3 fusion.48
  127.5 0.6 collective-permute-done.22
  128.1 0.3 convolution_add_fusion.1
  128.4 1.4 %collective-permute-done.24 = bf16[1,16,16,128]{3,1,2,0:T(8,128)(2,1)S(1)} collective-permute-done((bf16[1,16,16,128]{3,1,2,0:T(8,128)(2,1)S(1)}, bf16[1,16,16,128]{3,1,2,0:T(8,128)(2,1)S(1)}, u32[]{:S(2)}, u32[]{:S(2)}) %collective-permute-start.24) | collective-permute-done | bytes 65568 | tf_op jit(solution)/shard_map/ppermute | solution.py:117
  129.8 0.3 fusion.44
  130.0 1.5 %collective-permute-done.23 = bf16[1,16,16,128]{3,1,2,0:T(8,128)(2,1)S(1)} collective-permute-done((bf16[1,16,16,128]{3,1,2,0:T(8,128)(2,1)S(1)}, bf16[1,16,16,128]{3,1,2,0:T(8,128)(2,1)S(1)}, u32[]{:S(2)}, u32[]{:S(2)}) %collective-permute-start.23) | collective-permute-done | bytes 65568 | tf_op jit(solution)/shard_map/ppermute | solution.py:117
  131.6 0.3 fusion.30
  131.9 0.7 copy.33
  (65 shorter events, 2.2 us)
Async XLA Ops:
  0.0 73.8 %copy-start = (f32[16,64,64]{2,1,0:T(8,128)S(1)}, f32[16,64,64]{2,1,0:T(8,128)}, u32[]{:S(2)}) copy-start(f32[16,64,64]{2,1,0:T(8,128)} %param.10) | copy-start | bytes 786436
  0.9 7.1 %copy-start.4 = (f32[16,2,64,1024]{3,2,1,0:T(8,128)S(1)}, f32[16,2,64,1024]{3,2,1,0:T(8,128)}, u32[]{:S(2)}) copy-start(f32[16,2,64,1024]{3,2,1,0:T(8,128)} %param.6) | copy-start | bytes 25165828
  5.3 2.7 %copy-start.1 = (f32[64,2,8,1024]{3,0,2,1:T(8,128)}, f32[64,2,8,1024]{3,0,2,1:T(8,128)S(1)}, u32[]{:S(2)}) copy-start(f32[64,2,8,1024]{3,0,2,1:T(8,128)S(1)} %fusion.14) | copy-start | bytes 12582916
  6.8 6.8 %collective-permute-start = (f32[32,2,8,1024]{3,0,2,1:T(8,128)}, f32[32,2,8,1024]{3,0,2,1:T(8,128)S(1)}, u32[]{:S(2)}, u32[]{:S(2)}) collective-permute-start(f32[32,2,8,1024]{3,0,2,1:T(8,128)} %slice.33), channel_id=1, source_target_pairs={{0,4},{4,0},{1,5},{5,1},{2,6},{6,2},{3,7},{7,3},{8,12},{12,8},{9,1... | collective-permute-start | bytes 6291464 | tf_op jit(solution)/shard_map/ppermute | solution.py:64
  10.1 2.0 %copy-start.2 = (f32[64,2,8,1024]{3,0,2,1:T(8,128)}, f32[64,2,8,1024]{3,0,2,1:T(8,128)S(1)}, u32[]{:S(2)}) copy-start(f32[64,2,8,1024]{3,0,2,1:T(8,128)S(1)} %fusion.17) | copy-start | bytes 12582916
  13.6 5.3 %collective-permute-start.11 = (f32[32,2,8,1024]{3,0,2,1:T(8,128)}, f32[32,2,8,1024]{3,0,2,1:T(8,128)}, u32[]{:S(2)}, u32[]{:S(2)}) collective-permute-start(f32[32,2,8,1024]{3,0,2,1:T(8,128)} %slice.35), channel_id=1, source_target_pairs={{0,4},{4,0},{1,5},{5,1},{2,6},{6,2},{3,7},{7,3},{8,12},{12,8},{9,1... | collective-permute-start | bytes 6291464 | tf_op jit(solution)/shard_map/ppermute | solution.py:64
  15.6 3.3 %copy-start.3 = (f32[64,2,8,1024]{3,0,2,1:T(8,128)S(1)}, f32[64,2,8,1024]{3,0,2,1:T(8,128)}, u32[]{:S(2)}) copy-start(f32[64,2,8,1024]{3,0,2,1:T(8,128)} %copy-done.2) | copy-start | bytes 12582916
  16.9 12.9 %collective-permute-start.1 = (f32[4,2,8,1024]{3,2,1,0:T(8,128)S(1)}, f32[4,2,8,1024]{3,2,1,0:T(8,128)S(1)}, u32[]{:S(2)}, u32[]{:S(2)}) collective-permute-start(f32[4,2,8,1024]{3,2,1,0:T(8,128)S(1)} %dynamic-slice_bitcast_fusion), channel_id=1, source_target_pairs={{0,8},{8,16},{16,24},{24,32},{32,40},{40,48},{48,56},{56,0},{1,9},... | collective-permute-start | bytes 786440 | tf_op jit(solution)/shard_map/ppermute | solution.py:38
  23.1 17.6 %collective-permute-start.12 = (f32[8,2,8,1024]{3,2,1,0:T(8,128)}, f32[8,2,8,1024]{3,2,1,0:T(8,128)}, u32[]{:S(2)}, u32[]{:S(2)}) collective-permute-start(f32[8,2,8,1024]{3,2,1,0:T(8,128)} %bitcast.149), channel_id=1, source_target_pairs={{0,64},{64,128},{128,192},{192,0},{1,65},{65,129},{129,193},{193,1... | collective-permute-start | bytes 1572872 | tf_op jit(solution)/shard_map/ppermute | solution.py:38
  29.8 9.6 %collective-permute-start.2 = (f32[4,2,8,1024]{3,2,1,0:T(8,128)S(1)}, f32[4,2,8,1024]{3,2,1,0:T(8,128)}, u32[]{:S(2)}, u32[]{:S(2)}) collective-permute-start(f32[4,2,8,1024]{3,2,1,0:T(8,128)S(1)} %bitcast_add_fusion.6), channel_id=1, source_target_pairs={{0,8},{8,16},{16,24},{24,32},{32,40},{40,48},{48,56},{56,0},{1,9},... | collective-permute-start | bytes 786440 | tf_op jit(solution)/shard_map/ppermute | solution.py:38
  40.5 8.9 %collective-permute-start.3 = (f32[4,2,8,1024]{3,2,1,0:T(8,128)S(1)}, f32[4,2,8,1024]{3,2,1,0:T(8,128)S(1)}, u32[]{:S(2)}, u32[]{:S(2)}) collective-permute-start(f32[4,2,8,1024]{3,2,1,0:T(8,128)S(1)} %bitcast_add_fusion.5), channel_id=1, source_target_pairs={{0,8},{8,16},{16,24},{24,32},{32,40},{40,48},{48,56},{56,0},{1,9},... | collective-permute-start | bytes 786440 | tf_op jit(solution)/shard_map/ppermute | solution.py:38
  43.1 15.3 %collective-permute-start.13 = (f32[8,2,8,1024]{3,2,1,0:T(8,128)}, f32[8,2,8,1024]{3,2,1,0:T(8,128)}, u32[]{:S(2)}, u32[]{:S(2)}) collective-permute-start(f32[8,2,8,1024]{3,2,1,0:T(8,128)} %fusion.36), channel_id=1, source_target_pairs={{0,64},{64,128},{128,192},{192,0},{1,65},{65,129},{129,193},{193,1... | collective-permute-start | bytes 1572872 | tf_op jit(solution)/shard_map/ppermute | solution.py:38
  49.4 7.9 %collective-permute-start.4 = (f32[4,2,8,1024]{3,2,1,0:T(8,128)S(1)}, f32[4,2,8,1024]{3,2,1,0:T(8,128)}, u32[]{:S(2)}, u32[]{:S(2)}) collective-permute-start(f32[4,2,8,1024]{3,2,1,0:T(8,128)S(1)} %bitcast_add_fusion.4), channel_id=1, source_target_pairs={{0,8},{8,16},{16,24},{24,32},{32,40},{40,48},{48,56},{56,0},{1,9},... | collective-permute-start | bytes 786440 | tf_op jit(solution)/shard_map/ppermute | solution.py:38
  49.5 11.6 %copy-start.5 = (bf16[16,8,64,128]{3,2,1,0:T(8,128)(2,1)S(1)}, bf16[16,8,64,128]{3,2,1,0:T(8,128)(2,1)}, u32[]{:S(2)}) copy-start(bf16[16,8,64,128]{3,2,1,0:T(8,128)(2,1)} %param.7) | copy-start | bytes 6291460
  58.3 7.7 %collective-permute-start.5 = (f32[4,2,8,1024]{3,2,1,0:T(8,128)S(1)}, f32[4,2,8,1024]{3,2,1,0:T(8,128)S(1)}, u32[]{:S(2)}, u32[]{:S(2)}) collective-permute-start(f32[4,2,8,1024]{3,2,1,0:T(8,128)S(1)} %bitcast_add_fusion.3), channel_id=1, source_target_pairs={{0,8},{8,16},{16,24},{24,32},{32,40},{40,48},{48,56},{56,0},{1,9},... | collective-permute-start | bytes 786440 | tf_op jit(solution)/shard_map/ppermute | solution.py:38
  59.7 12.7 %copy-start.7 = (f32[1,8,2,8,1024]{4,1,0,3,2:T(8,128)S(1)}, f32[1,8,2,8,1024]{4,1,0,3,2:T(8,128)}, u32[]{:S(2)}) copy-start(f32[1,8,2,8,1024]{4,1,0,3,2:T(8,128)} %get-tuple-element.5) | copy-start | bytes 1572868
  59.8 12.7 %collective-permute-start.14 = (f32[8,2,8,1024]{3,2,1,0:T(8,128)S(1)}, f32[8,2,8,1024]{3,2,1,0:T(8,128)S(1)}, u32[]{:S(2)}, u32[]{:S(2)}) collective-permute-start(f32[8,2,8,1024]{3,2,1,0:T(8,128)S(1)} %fusion.35), channel_id=1, source_target_pairs={{0,64},{64,128},{128,192},{192,0},{1,65},{65,129},{129,193},{193,1... | collective-permute-start | bytes 1572872 | tf_op jit(solution)/shard_map/ppermute | solution.py:38
  66.0 21.0 %copy-start.8 = (s32[1,16,16,16]{3,2,1,0:T(8,128)S(1)}, s32[1,16,16,16]{3,2,1,0:T(8,128)}, u32[]{:S(2)}) copy-start(s32[1,16,16,16]{3,2,1,0:T(8,128)} %param.8) | copy-start | bytes 49156
  66.0 14.2 %collective-permute-start.6 = (f32[4,2,8,1024]{3,2,1,0:T(8,128)S(1)}, f32[4,2,8,1024]{3,2,1,0:T(8,128)}, u32[]{:S(2)}, u32[]{:S(2)}) collective-permute-start(f32[4,2,8,1024]{3,2,1,0:T(8,128)S(1)} %bitcast_add_fusion.2), channel_id=1, source_target_pairs={{0,8},{8,16},{16,24},{24,32},{32,40},{40,48},{48,56},{56,0},{1,9},... | collective-permute-start | bytes 786440 | tf_op jit(solution)/shard_map/ppermute | solution.py:38
  73.4 5.9 %collective-permute-start.15 = (f32[2,8,1024]{2,1,0:T(8,128)}, f32[2,8,1024]{2,1,0:T(8,128)}, u32[]{:S(2)}, u32[]{:S(2)}) collective-permute-start(f32[2,8,1024]{2,1,0:T(8,128)} %dynamic-slice_bitcast_fusion.1), channel_id=1, source_target_pairs={{0,8},{8,16},{16,24},{24,32},{32,40},{40,48},{48,56},{56,0},{1,9},... | collective-permute-start | bytes 196616 | tf_op jit(solution)/shard_map/ppermute | solution.py:38
  80.1 6.1 %collective-permute-start.16 = (f32[2,8,1024]{2,1,0:T(8,128)S(1)}, f32[2,8,1024]{2,1,0:T(8,128)S(1)}, u32[]{:S(2)}, u32[]{:S(2)}) collective-permute-start(f32[2,8,1024]{2,1,0:T(8,128)S(1)} %bitcast_add_fusion.13), channel_id=1, source_target_pairs={{0,8},{8,16},{16,24},{24,32},{32,40},{40,48},{48,56},{56,0},{1,9},... | collective-permute-start | bytes 196616 | tf_op jit(solution)/shard_map/ppermute | solution.py:38
  81.9 11.7 %collective-permute-start.7 = (f32[4,2,8,1024]{3,2,1,0:T(8,128)}, f32[4,2,8,1024]{3,2,1,0:T(8,128)}, u32[]{:S(2)}, u32[]{:S(2)}) collective-permute-start(f32[4,2,8,1024]{3,2,1,0:T(8,128)} %bitcast_add_fusion.1), channel_id=1, source_target_pairs={{0,8},{8,16},{16,24},{24,32},{32,40},{40,48},{48,56},{56,0},{1,9},... | collective-permute-start | bytes 786440 | tf_op jit(solution)/shard_map/ppermute | solution.py:38
  86.9 5.8 %collective-permute-start.17 = (f32[2,8,1024]{2,1,0:T(8,128)}, f32[2,8,1024]{2,1,0:T(8,128)}, u32[]{:S(2)}, u32[]{:S(2)}) collective-permute-start(f32[2,8,1024]{2,1,0:T(8,128)} %bitcast_add_fusion.12), channel_id=1, source_target_pairs={{0,8},{8,16},{16,24},{24,32},{32,40},{40,48},{48,56},{56,0},{1,9},... | collective-permute-start | bytes 196616 | tf_op jit(solution)/shard_map/ppermute | solution.py:38
  93.5 5.5 %collective-permute-start.18 = (f32[2,8,1024]{2,1,0:T(8,128)S(1)}, f32[2,8,1024]{2,1,0:T(8,128)S(1)}, u32[]{:S(2)}, u32[]{:S(2)}) collective-permute-start(f32[2,8,1024]{2,1,0:T(8,128)S(1)} %bitcast_add_fusion.11), channel_id=1, source_target_pairs={{0,8},{8,16},{16,24},{24,32},{32,40},{40,48},{48,56},{56,0},{1,9},... | collective-permute-start | bytes 196616 | tf_op jit(solution)/shard_map/ppermute | solution.py:38
  94.6 5.6 %collective-permute-start.8 = (f32[2,8,1024]{2,1,0:T(8,128)S(1)}, f32[2,8,1024]{2,1,0:T(8,128)S(1)}, u32[]{:S(2)}, u32[]{:S(2)}) collective-permute-start(f32[2,8,1024]{2,1,0:T(8,128)S(1)} %dynamic-slice_bitcast_fusion.2), channel_id=1, source_target_pairs={{0,64},{64,128},{128,192},{192,0},{1,65},{65,129},{129,193},{193,1... | collective-permute-start | bytes 196616 | tf_op jit(solution)/shard_map/ppermute | solution.py:38
  99.1 5.9 %collective-permute-start.19 = (f32[2,8,1024]{2,1,0:T(8,128)S(1)}, f32[2,8,1024]{2,1,0:T(8,128)S(1)}, u32[]{:S(2)}, u32[]{:S(2)}) collective-permute-start(f32[2,8,1024]{2,1,0:T(8,128)S(1)} %bitcast_add_fusion.10), channel_id=1, source_target_pairs={{0,8},{8,16},{16,24},{24,32},{32,40},{40,48},{48,56},{56,0},{1,9},... | collective-permute-start | bytes 196616 | tf_op jit(solution)/shard_map/ppermute | solution.py:38
  100.2 5.8 %collective-permute-start.9 = (f32[2,8,1024]{2,1,0:T(8,128)S(1)}, f32[2,8,1024]{2,1,0:T(8,128)S(1)}, u32[]{:S(2)}, u32[]{:S(2)}) collective-permute-start(f32[2,8,1024]{2,1,0:T(8,128)S(1)} %bitcast_add_fusion.16), channel_id=1, source_target_pairs={{0,64},{64,128},{128,192},{192,0},{1,65},{65,129},{129,193},{193,1... | collective-permute-start | bytes 196616 | tf_op jit(solution)/shard_map/ppermute | solution.py:38
  105.0 5.6 %collective-permute-start.20 = (f32[2,8,1024]{2,1,0:T(8,128)S(1)}, f32[2,8,1024]{2,1,0:T(8,128)S(1)}, u32[]{:S(2)}, u32[]{:S(2)}) collective-permute-start(f32[2,8,1024]{2,1,0:T(8,128)S(1)} %bitcast_add_fusion.9), channel_id=1, source_target_pairs={{0,8},{8,16},{16,24},{24,32},{32,40},{40,48},{48,56},{56,0},{1,9},... | collective-permute-start | bytes 196616 | tf_op jit(solution)/shard_map/ppermute | solution.py:38
  106.0 5.6 %collective-permute-start.10 = (f32[2,8,1024]{2,1,0:T(8,128)S(1)}, f32[2,8,1024]{2,1,0:T(8,128)S(1)}, u32[]{:S(2)}, u32[]{:S(2)}) collective-permute-start(f32[2,8,1024]{2,1,0:T(8,128)S(1)} %bitcast_add_fusion.15), channel_id=1, source_target_pairs={{0,64},{64,128},{128,192},{192,0},{1,65},{65,129},{129,193},{193,1... | collective-permute-start | bytes 196616 | tf_op jit(solution)/shard_map/ppermute | solution.py:38
  110.5 5.6 %collective-permute-start.21 = (f32[2,8,1024]{2,1,0:T(8,128)S(1)}, f32[2,8,1024]{2,1,0:T(8,128)S(1)}, u32[]{:S(2)}, u32[]{:S(2)}) collective-permute-start(f32[2,8,1024]{2,1,0:T(8,128)S(1)} %bitcast_add_fusion.8), channel_id=1, source_target_pairs={{0,8},{8,16},{16,24},{24,32},{32,40},{40,48},{48,56},{56,0},{1,9},... | collective-permute-start | bytes 196616 | tf_op jit(solution)/shard_map/ppermute | solution.py:38
  117.2 10.0 %copy-start.6 = (f32[16,64,16]{2,1,0:T(8,128)S(1)}, f32[16,64,16]{2,1,0:T(8,128)}, u32[]{:S(2)}) copy-start(f32[16,64,16]{2,1,0:T(8,128)} %constant_dynamic-slice_fusion) | copy-start | bytes 196612
  123.7 4.3 %collective-permute-start.22 = (bf16[1,16,16,128]{3,1,2,0:T(8,128)(2,1)S(1)}, bf16[1,16,16,128]{3,1,2,0:T(8,128)(2,1)S(1)}, u32[]{:S(2)}, u32[]{:S(2)}) collective-permute-start(bf16[1,16,16,128]{3,1,2,0:T(8,128)(2,1)S(1)} %bitcast.165), channel_id=1, source_target_pairs={{0,1},{1,2},{2,3},{3,0},{4,5},{5,6},{6,7},{7,4},{8,9},{9,10},{10,1... | collective-permute-start | bytes 196616 | tf_op jit(solution)/shard_map/ppermute | solution.py:117
  124.3 5.5 %collective-permute-start.24 = (bf16[1,16,16,128]{3,1,2,0:T(8,128)(2,1)S(1)}, bf16[1,16,16,128]{3,1,2,0:T(8,128)(2,1)S(1)}, u32[]{:S(2)}, u32[]{:S(2)}) collective-permute-start(bf16[1,16,16,128]{3,1,2,0:T(8,128)(2,1)S(1)} %bitcast.166), channel_id=1, source_target_pairs={{0,3},{1,0},{2,1},{3,2},{4,7},{5,4},{6,5},{7,6},{8,11},{9,8},{10,9... | collective-permute-start | bytes 196616 | tf_op jit(solution)/shard_map/ppermute | solution.py:117
  125.8 5.8 %collective-permute-start.23 = (bf16[1,16,16,128]{3,1,2,0:T(8,128)(2,1)S(1)}, bf16[1,16,16,128]{3,1,2,0:T(8,128)(2,1)S(1)}, u32[]{:S(2)}, u32[]{:S(2)}) collective-permute-start(bf16[1,16,16,128]{3,1,2,0:T(8,128)(2,1)S(1)} %bitcast.167), channel_id=1, source_target_pairs={{0,2},{1,3},{2,0},{3,1},{4,6},{5,7},{6,4},{7,5},{8,10},{9,11},{10,... | collective-permute-start | bytes 196616 | tf_op jit(solution)/shard_map/ppermute | solution.py:117
where the time goes:
time: 133 us
  waiting for transfers between devices  70.2 us (53%)
  other arithmetic  19.2 us (14%)
  matrix products  14.9 us (11%)
  local copies, waits for them, and re-layouts  13.9 us (10%)
  starting transfers between devices  13.1 us (10%)
    ppermute x20, waiting for transfers between devices, ring_reduce_scatter(): s = lax.ppermute(s, axis, fwd) + take(x, i - k - 2)  66.7 us
    add x18, other arithmetic, ring_reduce_scatter(): s = lax.ppermute(s, axis, fwd) + take(x, i - k - 2)  11.2 us
    ppermute x20, starting transfers between devices, ring_reduce_scatter(): s = lax.ppermute(s, axis, fwd) + take(x, i - k - 2)  9.6 us
    dot_general x2, matrix products, spectra_of(): jnp.einsum('rdct,fctb->rdfb', table, part, precision=lax.Precision.HIGH)  6.52 us
    dot_general x1, matrix products, local(): jnp.einsum('mflpi,lpij->mflj', combined, code_matrix, precision=lax.Preci...  6.51 us
    unnamed x19, local copies, waits for them, and re-layouts  4.19 us
    ppermute x3, waiting for transfers between devices, local(): lax.ppermute(weights_bf, 'freq', [(j, (j + s) % fr_count) for j in range(...  3.52 us
    neg x1, other arithmetic, realify(): upper = jnp.concatenate([real_part, -imag_part], axis=-1)  3.49 us
  transfers between devices with their start and end apart: 25, of which 19 were waited for; matrix products, arithmetic and copies ran while one was open for 22% of the time, Pallas kernels for 0%

commit v1 on v0

--- a/solution.py
+++ b/solution.py
@@ -35,7 +35,8 @@
 
     s = take(x, i - 1)
     for k in range(n - 1):
-        s = lax.ppermute(s, axis, fwd) + take(x, i - k - 2)
+        got = lax.ppermute(s.astype(jnp.bfloat16), axis, fwd)
+        s = got.astype(jnp.float32) + take(x, i - k - 2)
     return s
 
 

time: 133 us -> 123 us (0.925)
  waiting for transfers between devices: 70.2 us -> 58.6 us
  starting transfers between devices: 13.1 us -> 17.9 us
  local copies, waits for them, and re-layouts: 13.9 us -> 11 us
  other arithmetic: 19.2 us -> 17.7 us
    ppermute x20, waiting for transfers between devices: 66.7 us -> 55.1 us  [ring_reduce_scatter(): got = lax.ppermute(s.astype(jnp.bfloat16), axis, fwd)]
    add x18 -> x2, other arithmetic: 11.2 us -> 0.48 us  [ring_reduce_scatter(): s = got.astype(jnp.float32) + take(x, i - k - 2)]
    ppermute x20, starting transfers between devices: 9.6 us -> 14.4 us  [ring_reduce_scatter(): got = lax.ppermute(s.astype(jnp.bfloat16), axis, fwd)]
    convert_element_type x0 -> x16, other arithmetic: none -> 4.68 us  [ring_reduce_scatter(): got = lax.ppermute(s.astype(jnp.bfloat16), axis, fwd)]
    select_n x0 -> x1, other arithmetic: none -> 2.67 us  [local(): jnp.where(block_index[..., None] == jnp.arange(code_count, dtype=jnp.int3...]
    unnamed x19 -> x26, local copies, waits for them, and re-layouts: 4.19 us -> 3.28 us
  transfers between devices with their start and end apart: 25 -> 25, of which waited for: 19 -> 20; matrix products, arithmetic and copies ran while one was open for 22% -> 17% of each run, Pallas kernels for 0% -> 0%
where the time goes in v1:
time: 123 us; the launch traced here: 122 us
  waiting for transfers between devices  58.6 us (48%)
  starting transfers between devices  17.9 us (15%)
  other arithmetic  17.7 us (14%)
  matrix products  15.9 us (13%)
  local copies, waits for them, and re-layouts  11 us (9%)
  between operations  1.34 us (1%)
    ppermute x20, waiting for transfers between devices, ring_reduce_scatter(): got = lax.ppermute(s.astype(jnp.bfloat16), axis, fwd)  55.1 us
    ppermute x20, starting transfers between devices, ring_reduce_scatter(): got = lax.ppermute(s.astype(jnp.bfloat16), axis, fwd)  14.4 us
    dot_general x2, matrix products, spectra_of(): jnp.einsum('rdct,fctb->rdfb', table, part, precision=lax.Precision.HIGH)  6.54 us
    dot_general x1, matrix products, local(): jnp.einsum('mflpi,lpij->mflj', combined, code_matrix, precision=lax.Preci...  6.21 us
    convert_element_type x16, other arithmetic, ring_reduce_scatter(): got = lax.ppermute(s.astype(jnp.bfloat16), axis, fwd)  4.68 us
    neg x1, other arithmetic, realify(): upper = jnp.concatenate([real_part, -imag_part], axis=-1)  3.54 us
    ppermute x3, waiting for transfers between devices, local(): lax.ppermute(weights_bf, 'freq', [(j, (j + s) % fr_count) for j in range(...  3.53 us
    ppermute x3, starting transfers between devices, local(): lax.ppermute(weights_bf, 'freq', [(j, (j + s) % fr_count) for j in range(...  3.47 us
  transfers between devices with their start and end apart: 25, of which 20 were waited for; matrix products, arithmetic and copies ran while one was open for 17% of the time, Pallas kernels for 0%

profile of v1, /device:TPU:6, one launch (start us, length us, event | category | flops | bytes accessed | tf_op | source)
XLA Modules:
  0.0 122.5 jit_solution(8025257362547559029)
XLA Ops:
  0.5 0.4 sine_multiply_fusion.1
  0.9 4.4 %fusion.14 = f32[64,2,8,1024]{3,0,2,1:T(8,128)S(1)} fusion(f32[16,2,64,1024]{3,2,1,0:T(8,128)} %param.6, f32[64,1,2,64]{3,0,2,1:T(8,128)S(1)} %get-tuple-element.19, f32[64,1,2,64]{3,0,2,1:T(8,128)S(1)} %get-tuple-element.18), kind=kOutput, calls=%fused_computation.14 | convolution fusion | flops 805322752 | bytes 8454144 | tf_op jit(solution)/shard_map/rdct,fctb->rdfb/dot_general | solution.py:63
  5.3 1.6 %slice.33 = f32[32,2,8,1024]{3,0,2,1:T(8,128)} slice(f32[64,2,8,1024]{3,0,2,1:T(8,128)S(1)} %fusion.14), slice={[0:32], [0:2], [0:8], [0:1024]} | slice | bytes 4194304 | tf_op jit(solution)/shard_map/slice | solution.py:65
  6.9 1.1 copy-done.1
  8.0 2.2 %fusion.17 = f32[64,2,8,1024]{3,0,2,1:T(8,128)S(1)} fusion(f32[16,2,64,1024]{3,2,1,0:T(8,128)S(1)} %copy-done.4, f32[64,1,2,64]{3,0,2,1:T(8,128)S(1)} %get-tuple-element.21, f32[64,1,2,64]{3,0,2,1:T(8,128)S(1)} %get-tuple-element.20), kind=kOutput, calls=%fused_computation.15 | convolution fusion | flops 805322752 | bytes 8519680 | tf_op jit(solution)/shard_map/rdct,fctb->rdfb/dot_general | solution.py:63
  10.2 2.0 %copy-done.3 = f32[64,2,8,1024]{3,0,2,1:T(8,128)} copy-done((f32[64,2,8,1024]{3,0,2,1:T(8,128)}, f32[64,2,8,1024]{3,0,2,1:T(8,128)S(1)}, u32[]{:S(2)}) %copy-start.3) | copy-done | bytes 4194328
  12.2 1.5 %slice.35 = f32[32,2,8,1024]{3,0,2,1:T(8,128)} slice(f32[64,2,8,1024]{3,0,2,1:T(8,128)S(1)} %fusion.17), slice={[0:32], [0:2], [0:8], [0:1024]} | slice | bytes 4194304 | tf_op jit(solution)/shard_map/slice | solution.py:65
  14.5 0.2 constant_dynamic-slice_fusion
  14.7 2.7 %fusion.23 = f32[16,16,16,8]{3,2,1,0:T(8,128)} fusion(f32[16,16,16]{2,1,0:T(8,128)S(1)} %bitcast.186, s32[16,16,16]{2,1,0:T(8,128)S(1)} %bitcast.187), kind=kLoop, calls=%fused_computation.22 | loop fusion | flops 65536 | bytes 163840 | tf_op jit(solution)/shard_map/jit(_where)/select_n | solution.py:100
  17.4 3.5 %slice_negate_fusion = (bf16[16,8,64,64]{3,2,1,0:T(8,128)(2,1)}, bf16[16,8,64,64]{3,2,1,0:T(8,128)(2,1)}, bf16[16,8,64,64]{3,2,1,0:T(8,128)(2,1)}) fusion(bf16[16,8,64,128]{3,2,1,0:T(8,128)(2,1)S(1)} %copy-done.5), kind=kLoop, calls=%fused_computation.157 | loop fusion | flops 524288 | bytes 5242880 | tf_op jit(solution)/shard_map/neg | solution.py:18
  20.9 2.0 %slice_add_fusion.1 = f32[32,2,8,1024]{3,0,2,1:T(8,128)S(1)} fusion(f32[32,2,8,1024]{3,0,2,1:T(8,128)} %collective-permute-done, f32[64,2,8,1024]{3,0,2,1:T(8,128)S(1)} %copy-done.2), kind=kLoop, calls=%fused_computation.18 | loop fusion | flops 524288 | bytes 6291456 | tf_op jit(solution)/shard_map/add | solution.py:65
  22.9 1.7 %reshape.498 = f32[8,4,2,8,1024]{4,1,0,3,2:T(4,128)} reshape(f32[32,2,8,1024]{3,0,2,1:T(8,128)S(1)} %slice_add_fusion.1) | data formatting | bytes 4194304 | tf_op jit(solution)/shard_map/reshape | solution.py:67
  24.6 2.8 %fusion.20 = f32[4,8,2,8,1024]{4,1,0,3,2:T(8,128)S(1)} fusion(f32[32,2,8,1024]{3,0,2,1:T(8,128)} %collective-permute-done.11, f32[64,2,8,1024]{3,0,2,1:T(8,128)} %copy-done.3), kind=kLoop, calls=%fused_computation.17 | loop fusion | flops 524288 | bytes 6291456 | tf_op jit(solution)/shard_map/reshape | solution.py:70
  27.6 1.7 %collective-permute-start.12 = (bf16[8,2,8,1024]{3,2,1,0:T(8,128)(2,1)S(1)}, bf16[8,2,8,1024]{3,2,1,0:T(8,128)(2,1)S(1)}, u32[]{:S(2)}, u32[]{:S(2)}) collective-permute-start(bf16[8,2,8,1024]{3,2,1,0:T(8,128)(2,1)S(1)} %bitcast.185), channel_id=1, source_target_pairs={{0,64},{64,128},{128,192},{192,0},{1,65},{65,129},{129,193},{193,1... | collective-permute-start | bytes 786440 | tf_op jit(solution)/shard_map/ppermute | solution.py:38
  29.4 2.0 %collective-permute-start.1 = (bf16[4,2,8,1024]{3,2,1,0:T(8,128)(2,1)S(1)}, bf16[4,2,8,1024]{3,2,1,0:T(8,128)(2,1)S(1)}, u32[]{:S(2)}, u32[]{:S(2)}) collective-permute-start(bf16[4,2,8,1024]{3,2,1,0:T(8,128)(2,1)S(1)} %bitcast.188), channel_id=1, source_target_pairs={{0,8},{8,16},{16,24},{24,32},{32,40},{40,48},{48,56},{56,0},{1,9},... | collective-permute-start | bytes 393224 | tf_op jit(solution)/shard_map/ppermute | solution.py:38
  31.5 6.1 %collective-permute-done.12 = bf16[8,2,8,1024]{3,2,1,0:T(8,128)(2,1)S(1)} collective-permute-done((bf16[8,2,8,1024]{3,2,1,0:T(8,128)(2,1)S(1)}, bf16[8,2,8,1024]{3,2,1,0:T(8,128)(2,1)S(1)}, u32[]{:S(2)}, u32[]{:S(2)}) %collective-permute-start.12) | collective-permute-done | bytes 262176 | tf_op jit(solution)/shard_map/ppermute | solution.py:38
  37.5 0.3 fusion.36
  37.8 0.6 collective-permute-start.13
  38.4 0.9 constant_dynamic-slice_fusion.11
  39.3 0.2 fusion.43
  39.5 2.0 %collective-permute-start.2 = (bf16[4,2,8,1024]{3,2,1,0:T(8,128)(2,1)S(1)}, bf16[4,2,8,1024]{3,2,1,0:T(8,128)(2,1)S(1)}, u32[]{:S(2)}, u32[]{:S(2)}) collective-permute-start(bf16[4,2,8,1024]{3,2,1,0:T(8,128)(2,1)S(1)} %fusion.43), channel_id=1, source_target_pairs={{0,8},{8,16},{16,24},{24,32},{32,40},{40,48},{48,56},{56,0},{1,9},... | collective-permute-start | bytes 393224 | tf_op jit(solution)/shard_map/ppermute | solution.py:38
  41.5 5.6 %collective-permute-done.13 = bf16[8,2,8,1024]{3,2,1,0:T(8,128)(2,1)S(1)} collective-permute-done((bf16[8,2,8,1024]{3,2,1,0:T(8,128)(2,1)S(1)}, bf16[8,2,8,1024]{3,2,1,0:T(8,128)(2,1)S(1)}, u32[]{:S(2)}, u32[]{:S(2)}) %collective-permute-start.13) | collective-permute-done | bytes 262176 | tf_op jit(solution)/shard_map/ppermute | solution.py:38
  47.1 0.3 fusion.35
  47.6 0.8 collective-permute-done.2
  48.4 0.2 fusion.42
  48.6 1.2 collective-permute-start.3
  49.8 5.8 %collective-permute-done.14 = bf16[8,2,8,1024]{3,2,1,0:T(8,128)(2,1)S(1)} collective-permute-done((bf16[8,2,8,1024]{3,2,1,0:T(8,128)(2,1)S(1)}, bf16[8,2,8,1024]{3,2,1,0:T(8,128)(2,1)S(1)}, u32[]{:S(2)}, u32[]{:S(2)}) %collective-permute-start.14) | collective-permute-done | bytes 262176 | tf_op jit(solution)/shard_map/ppermute | solution.py:38
  55.6 0.3 bitcast_add_fusion
  55.9 2.0 %collective-permute-start.15 = (bf16[2,8,1024]{2,1,0:T(8,128)(2,1)S(1)}, bf16[2,8,1024]{2,1,0:T(8,128)(2,1)S(1)}, u32[]{:S(2)}, u32[]{:S(2)}) collective-permute-start(bf16[2,8,1024]{2,1,0:T(8,128)(2,1)S(1)} %fusion.81), channel_id=1, source_target_pairs={{0,8},{8,16},{16,24},{24,32},{32,40},{40,48},{48,56},{56,0},{1,9},... | collective-permute-start | bytes 98312 | tf_op jit(solution)/shard_map/ppermute | solution.py:38
  58.1 2.0 %collective-permute-start.4 = (bf16[4,2,8,1024]{3,2,1,0:T(8,128)(2,1)S(1)}, bf16[4,2,8,1024]{3,2,1,0:T(8,128)(2,1)S(1)}, u32[]{:S(2)}, u32[]{:S(2)}) collective-permute-start(bf16[4,2,8,1024]{3,2,1,0:T(8,128)(2,1)S(1)} %fusion.41), channel_id=1, source_target_pairs={{0,8},{8,16},{16,24},{24,32},{32,40},{40,48},{48,56},{56,0},{1,9},... | collective-permute-start | bytes 393224 | tf_op jit(solution)/shard_map/ppermute | solution.py:38
  60.1 3.7 %collective-permute-done.15 = bf16[2,8,1024]{2,1,0:T(8,128)(2,1)S(1)} collective-permute-done((bf16[2,8,1024]{2,1,0:T(8,128)(2,1)S(1)}, bf16[2,8,1024]{2,1,0:T(8,128)(2,1)S(1)}, u32[]{:S(2)}, u32[]{:S(2)}) %collective-permute-start.15) | collective-permute-done | bytes 32800 | tf_op jit(solution)/shard_map/ppermute | solution.py:38
  63.9 1.7 %collective-permute-done.4 = bf16[4,2,8,1024]{3,2,1,0:T(8,128)(2,1)S(1)} collective-permute-done((bf16[4,2,8,1024]{3,2,1,0:T(8,128)(2,1)S(1)}, bf16[4,2,8,1024]{3,2,1,0:T(8,128)(2,1)S(1)}, u32[]{:S(2)}, u32[]{:S(2)}) %collective-permute-start.4) | collective-permute-done | bytes 131104 | tf_op jit(solution)/shard_map/ppermute | solution.py:38
  65.5 1.3 %fusion.40 = bf16[4,2,8,1024]{3,2,1,0:T(8,128)(2,1)S(1)} fusion(f32[1,4,2,8,1024]{4,1,0,3,2:T(4,128)} %get-tuple-element.9, bf16[4,2,8,1024]{3,2,1,0:T(8,128)(2,1)S(1)} %collective-permute-done.4), kind=kLoop, calls=%fused_computation.46 | loop fusion | flops 196608 | bytes 524288 | tf_op jit(solution)/shard_map/convert_element_type | solution.py:38
  66.9 2.2 %collective-permute-done.16 = bf16[2,8,1024]{2,1,0:T(8,128)(2,1)S(1)} collective-permute-done((bf16[2,8,1024]{2,1,0:T(8,128)(2,1)S(1)}, bf16[2,8,1024]{2,1,0:T(8,128)(2,1)S(1)}, u32[]{:S(2)}, u32[]{:S(2)}) %collective-permute-start.16) | collective-permute-done | bytes 32800 | tf_op jit(solution)/shard_map/ppermute | solution.py:38
  69.2 3.9 %collective-permute-done.5 = bf16[4,2,8,1024]{3,2,1,0:T(8,128)(2,1)S(1)} collective-permute-done((bf16[4,2,8,1024]{3,2,1,0:T(8,128)(2,1)S(1)}, bf16[4,2,8,1024]{3,2,1,0:T(8,128)(2,1)S(1)}, u32[]{:S(2)}, u32[]{:S(2)}) %collective-permute-start.5) | collective-permute-done | bytes 131104 | tf_op jit(solution)/shard_map/ppermute | solution.py:38
  73.1 1.1 fusion.39
  74.3 0.4 collective-permute-done.17
  74.7 1.1 collective-permute-start.18
  75.7 4.7 %collective-permute-done.6 = bf16[4,2,8,1024]{3,2,1,0:T(8,128)(2,1)S(1)} collective-permute-done((bf16[4,2,8,1024]{3,2,1,0:T(8,128)(2,1)S(1)}, bf16[4,2,8,1024]{3,2,1,0:T(8,128)(2,1)S(1)}, u32[]{:S(2)}, u32[]{:S(2)}) %collective-permute-start.6) | collective-permute-done | bytes 131104 | tf_op jit(solution)/shard_map/ppermute | solution.py:38
  80.4 1.1 fusion.38
  81.7 0.9 collective-permute-start.19
  82.5 5.6 %collective-permute-done.7 = bf16[4,2,8,1024]{3,2,1,0:T(8,128)(2,1)S(1)} collective-permute-done((bf16[4,2,8,1024]{3,2,1,0:T(8,128)(2,1)S(1)}, bf16[4,2,8,1024]{3,2,1,0:T(8,128)(2,1)S(1)}, u32[]{:S(2)}, u32[]{:S(2)}) %collective-permute-start.7) | collective-permute-done | bytes 131104 | tf_op jit(solution)/shard_map/ppermute | solution.py:38
  88.1 0.2 bitcast_add_fusion.3
  88.5 0.3 collective-permute-start.20
  88.8 4.7 %collective-permute-done.8 = bf16[2,8,1024]{2,1,0:T(8,128)(2,1)S(1)} collective-permute-done((bf16[2,8,1024]{2,1,0:T(8,128)(2,1)S(1)}, bf16[2,8,1024]{2,1,0:T(8,128)(2,1)S(1)}, u32[]{:S(2)}, u32[]{:S(2)}) %collective-permute-start.8) | collective-permute-done | bytes 32800 | tf_op jit(solution)/shard_map/ppermute | solution.py:38
  93.7 0.3 collective-permute-done.20
  94.0 4.7 %collective-permute-done.9 = bf16[2,8,1024]{2,1,0:T(8,128)(2,1)S(1)} collective-permute-done((bf16[2,8,1024]{2,1,0:T(8,128)(2,1)S(1)}, bf16[2,8,1024]{2,1,0:T(8,128)(2,1)S(1)}, u32[]{:S(2)}, u32[]{:S(2)}) %collective-permute-start.9) | collective-permute-done | bytes 32800 | tf_op jit(solution)/shard_map/ppermute | solution.py:38
  98.9 0.3 collective-permute-done.21
  99.4 4.6 %collective-permute-done.10 = bf16[2,8,1024]{2,1,0:T(8,128)(2,1)S(1)} collective-permute-done((bf16[2,8,1024]{2,1,0:T(8,128)(2,1)S(1)}, bf16[2,8,1024]{2,1,0:T(8,128)(2,1)S(1)}, u32[]{:S(2)}, u32[]{:S(2)}) %collective-permute-start.10) | collective-permute-done | bytes 32800 | tf_op jit(solution)/shard_map/ppermute | solution.py:38
  104.0 0.8 fusion.71
  105.0 0.2 maximum_bitcast_fusion.4
  105.4 2.0 %fusion.21 = f32[16,16,8,128]{3,2,1,0:T(8,128)S(1)} fusion(f32[16,16,16,8]{3,2,1,0:T(8,128)S(1)} %copy-done.6, bf16[16,16,128,1]{2,1,0,3:T(8,128)(2,1)S(1)} %reshape.512), kind=kOutput, calls=%fused_computation.19 | convolution fusion | flops 50331648 | bytes 1245184 | tf_op jit(solution)/shard_map/mfblp,mfbi->mflpi/dot_general | solution.py:105
  107.4 6.2 %fusion.29 = bf16[16,128,16]{1,2,0:T(8,128)(2,1)S(1)} fusion(bf16[16,8,64,64]{3,2,1,0:T(8,128)(2,1)} %get-tuple-element.17, bf16[16,8,64,64]{3,2,1,0:T(8,128)(2,1)} %get-tuple-element.16, bf16[16,8,64,64]{3,2,1,0:T(8,128)(2,1)S(1)} %copy-done.8, f32[16,16,8,128]{3,2,1,0:T(8,128)S(1)} %fusion.21), kind=kOutput, calls=%fused_computation.28 | convolution fusion | flops 419463168 | bytes 4259840 | tf_op jit(solution)/shard_map/mflpi,lpij->mflj/dot_general | solution.py:108
  113.6 0.6 collective-permute-start.22
  114.1 1.6 %collective-permute-start.24 = (bf16[1,16,16,128]{3,1,2,0:T(8,128)(2,1)S(1)}, bf16[1,16,16,128]{3,1,2,0:T(8,128)(2,1)S(1)}, u32[]{:S(2)}, u32[]{:S(2)}) collective-permute-start(bf16[1,16,16,128]{3,1,2,0:T(8,128)(2,1)S(1)} %bitcast.190), channel_id=1, source_target_pairs={{0,3},{1,0},{2,1},{3,2},{4,7},{5,4},{6,5},{7,6},{8,11},{9,8},{10,9... | collective-permute-start | bytes 196616 | tf_op jit(solution)/shard_map/ppermute | solution.py:118
  115.7 1.4 %collective-permute-start.23 = (bf16[1,16,16,128]{3,1,2,0:T(8,128)(2,1)S(1)}, bf16[1,16,16,128]{3,1,2,0:T(8,128)(2,1)S(1)}, u32[]{:S(2)}, u32[]{:S(2)}) collective-permute-start(bf16[1,16,16,128]{3,1,2,0:T(8,128)(2,1)S(1)} %bitcast.191), channel_id=1, source_target_pairs={{0,2},{1,3},{2,0},{3,1},{4,6},{5,7},{6,4},{7,5},{8,10},{9,11},{10,... | collective-permute-start | bytes 196616 | tf_op jit(solution)/shard_map/ppermute | solution.py:118
  117.1 0.3 fusion.53
  117.3 0.6 collective-permute-done.22
  117.9 0.3 convolution_add_fusion.1
  118.2 1.4 %collective-permute-done.24 = bf16[1,16,16,128]{3,1,2,0:T(8,128)(2,1)S(1)} collective-permute-done((bf16[1,16,16,128]{3,1,2,0:T(8,128)(2,1)S(1)}, bf16[1,16,16,128]{3,1,2,0:T(8,128)(2,1)S(1)}, u32[]{:S(2)}, u32[]{:S(2)}) %collective-permute-start.24) | collective-permute-done | bytes 65568 | tf_op jit(solution)/shard_map/ppermute | solution.py:118
  119.6 0.3 fusion.49
  119.9 1.6 %collective-permute-done.23 = bf16[1,16,16,128]{3,1,2,0:T(8,128)(2,1)S(1)} collective-permute-done((bf16[1,16,16,128]{3,1,2,0:T(8,128)(2,1)S(1)}, bf16[1,16,16,128]{3,1,2,0:T(8,128)(2,1)S(1)}, u32[]{:S(2)}, u32[]{:S(2)}) %collective-permute-start.23) | collective-permute-done | bytes 65568 | tf_op jit(solution)/shard_map/ppermute | solution.py:118
  121.5 0.3 fusion.33
  121.8 0.7 copy.23
  (74 shorter events, 2.6 us)
Async XLA Ops:
  0.0 14.5 %copy-start = (f32[16,64,64]{2,1,0:T(8,128)S(1)}, f32[16,64,64]{2,1,0:T(8,128)}, u32[]{:S(2)}) copy-start(f32[16,64,64]{2,1,0:T(8,128)} %param.10) | copy-start | bytes 786436
  0.9 7.2 %copy-start.4 = (f32[16,2,64,1024]{3,2,1,0:T(8,128)S(1)}, f32[16,2,64,1024]{3,2,1,0:T(8,128)}, u32[]{:S(2)}) copy-start(f32[16,2,64,1024]{3,2,1,0:T(8,128)} %param.6) | copy-start | bytes 25165828
  5.3 2.7 %copy-start.1 = (f32[64,2,8,1024]{3,0,2,1:T(8,128)}, f32[64,2,8,1024]{3,0,2,1:T(8,128)S(1)}, u32[]{:S(2)}) copy-start(f32[64,2,8,1024]{3,0,2,1:T(8,128)S(1)} %fusion.14) | copy-start | bytes 12582916
  6.9 14.0 %collective-permute-start = (f32[32,2,8,1024]{3,0,2,1:T(8,128)}, f32[32,2,8,1024]{3,0,2,1:T(8,128)}, u32[]{:S(2)}, u32[]{:S(2)}) collective-permute-start(f32[32,2,8,1024]{3,0,2,1:T(8,128)} %slice.33), channel_id=1, source_target_pairs={{0,4},{4,0},{1,5},{5,1},{2,6},{6,2},{3,7},{7,3},{8,12},{12,8},{9,1... | collective-permute-start | bytes 6291464 | tf_op jit(solution)/shard_map/ppermute | solution.py:65
  10.2 2.0 %copy-start.3 = (f32[64,2,8,1024]{3,0,2,1:T(8,128)}, f32[64,2,8,1024]{3,0,2,1:T(8,128)S(1)}, u32[]{:S(2)}) copy-start(f32[64,2,8,1024]{3,0,2,1:T(8,128)S(1)} %fusion.17) | copy-start | bytes 12582916
  12.2 2.5 %copy-start.10 = (f32[1,16,16,16]{3,2,1,0:T(8,128)S(1)}, f32[1,16,16,16]{3,2,1,0:T(8,128)}, u32[]{:S(2)}) copy-start(f32[1,16,16,16]{3,2,1,0:T(8,128)} %param.9) | copy-start | bytes 49156
  12.2 2.5 %copy-start.11 = (s32[1,16,16,16]{3,2,1,0:T(8,128)S(1)}, s32[1,16,16,16]{3,2,1,0:T(8,128)}, u32[]{:S(2)}) copy-start(s32[1,16,16,16]{3,2,1,0:T(8,128)} %param.8) | copy-start | bytes 49156
  13.6 3.7 %copy-start.5 = (bf16[16,8,64,128]{3,2,1,0:T(8,128)(2,1)S(1)}, bf16[16,8,64,128]{3,2,1,0:T(8,128)(2,1)}, u32[]{:S(2)}) copy-start(bf16[16,8,64,128]{3,2,1,0:T(8,128)(2,1)} %param.7) | copy-start | bytes 6291460
  13.6 11.0 %collective-permute-start.11 = (f32[32,2,8,1024]{3,0,2,1:T(8,128)}, f32[32,2,8,1024]{3,0,2,1:T(8,128)}, u32[]{:S(2)}, u32[]{:S(2)}) collective-permute-start(f32[32,2,8,1024]{3,0,2,1:T(8,128)} %slice.35), channel_id=1, source_target_pairs={{0,4},{4,0},{1,5},{5,1},{2,6},{6,2},{3,7},{7,3},{8,12},{12,8},{9,1... | collective-permute-start | bytes 6291464 | tf_op jit(solution)/shard_map/ppermute | solution.py:65
  17.4 3.5 %copy-start.2 = (f32[64,2,8,1024]{3,0,2,1:T(8,128)S(1)}, f32[64,2,8,1024]{3,0,2,1:T(8,128)}, u32[]{:S(2)}) copy-start(f32[64,2,8,1024]{3,0,2,1:T(8,128)} %copy-done.1) | copy-start | bytes 12582916
  24.6 4.6 %copy-start.7 = (f32[8,4,2,8,1024]{4,1,0,3,2:T(4,128)S(1)}, f32[8,4,2,8,1024]{4,1,0,3,2:T(4,128)}, u32[]{:S(2)}) copy-start(f32[8,4,2,8,1024]{4,1,0,3,2:T(4,128)} %reshape.498) | copy-start | bytes 6291460
  27.6 9.9 %collective-permute-start.12 = (bf16[8,2,8,1024]{3,2,1,0:T(8,128)(2,1)S(1)}, bf16[8,2,8,1024]{3,2,1,0:T(8,128)(2,1)S(1)}, u32[]{:S(2)}, u32[]{:S(2)}) collective-permute-start(bf16[8,2,8,1024]{3,2,1,0:T(8,128)(2,1)S(1)} %bitcast.185), channel_id=1, source_target_pairs={{0,64},{64,128},{128,192},{192,0},{1,65},{65,129},{129,193},{193,1... | collective-permute-start | bytes 786440 | tf_op jit(solution)/shard_map/ppermute | solution.py:38
  29.4 10.0 %collective-permute-start.1 = (bf16[4,2,8,1024]{3,2,1,0:T(8,128)(2,1)S(1)}, bf16[4,2,8,1024]{3,2,1,0:T(8,128)(2,1)S(1)}, u32[]{:S(2)}, u32[]{:S(2)}) collective-permute-start(bf16[4,2,8,1024]{3,2,1,0:T(8,128)(2,1)S(1)} %bitcast.188), channel_id=1, source_target_pairs={{0,8},{8,16},{16,24},{24,32},{32,40},{40,48},{48,56},{56,0},{1,9},... | collective-permute-start | bytes 393224 | tf_op jit(solution)/shard_map/ppermute | solution.py:38
  37.8 9.2 %collective-permute-start.13 = (bf16[8,2,8,1024]{3,2,1,0:T(8,128)(2,1)S(1)}, bf16[8,2,8,1024]{3,2,1,0:T(8,128)(2,1)S(1)}, u32[]{:S(2)}, u32[]{:S(2)}) collective-permute-start(bf16[8,2,8,1024]{3,2,1,0:T(8,128)(2,1)S(1)} %fusion.36), channel_id=1, source_target_pairs={{0,64},{64,128},{128,192},{192,0},{1,65},{65,129},{129,193},{193,1... | collective-permute-start | bytes 786440 | tf_op jit(solution)/shard_map/ppermute | solution.py:38
  39.5 8.9 %collective-permute-start.2 = (bf16[4,2,8,1024]{3,2,1,0:T(8,128)(2,1)S(1)}, bf16[4,2,8,1024]{3,2,1,0:T(8,128)(2,1)S(1)}, u32[]{:S(2)}, u32[]{:S(2)}) collective-permute-start(bf16[4,2,8,1024]{3,2,1,0:T(8,128)(2,1)S(1)} %fusion.43), channel_id=1, source_target_pairs={{0,8},{8,16},{16,24},{24,32},{32,40},{40,48},{48,56},{56,0},{1,9},... | collective-permute-start | bytes 393224 | tf_op jit(solution)/shard_map/ppermute | solution.py:38
  47.4 8.2 %collective-permute-start.14 = (bf16[8,2,8,1024]{3,2,1,0:T(8,128)(2,1)S(1)}, bf16[8,2,8,1024]{3,2,1,0:T(8,128)(2,1)S(1)}, u32[]{:S(2)}, u32[]{:S(2)}) collective-permute-start(bf16[8,2,8,1024]{3,2,1,0:T(8,128)(2,1)S(1)} %fusion.35), channel_id=1, source_target_pairs={{0,64},{64,128},{128,192},{192,0},{1,65},{65,129},{129,193},{193,1... | collective-permute-start | bytes 786440 | tf_op jit(solution)/shard_map/ppermute | solution.py:38
  48.6 9.4 %collective-permute-start.3 = (bf16[4,2,8,1024]{3,2,1,0:T(8,128)(2,1)S(1)}, bf16[4,2,8,1024]{3,2,1,0:T(8,128)(2,1)S(1)}, u32[]{:S(2)}, u32[]{:S(2)}) collective-permute-start(bf16[4,2,8,1024]{3,2,1,0:T(8,128)(2,1)S(1)} %fusion.42), channel_id=1, source_target_pairs={{0,8},{8,16},{16,24},{24,32},{32,40},{40,48},{48,56},{56,0},{1,9},... | collective-permute-start | bytes 393224 | tf_op jit(solution)/shard_map/ppermute | solution.py:38
  55.9 7.8 %collective-permute-start.15 = (bf16[2,8,1024]{2,1,0:T(8,128)(2,1)S(1)}, bf16[2,8,1024]{2,1,0:T(8,128)(2,1)S(1)}, u32[]{:S(2)}, u32[]{:S(2)}) collective-permute-start(bf16[2,8,1024]{2,1,0:T(8,128)(2,1)S(1)} %fusion.81), channel_id=1, source_target_pairs={{0,8},{8,16},{16,24},{24,32},{32,40},{40,48},{48,56},{56,0},{1,9},... | collective-permute-start | bytes 98312 | tf_op jit(solution)/shard_map/ppermute | solution.py:38
  58.1 7.4 %collective-permute-start.4 = (bf16[4,2,8,1024]{3,2,1,0:T(8,128)(2,1)S(1)}, bf16[4,2,8,1024]{3,2,1,0:T(8,128)(2,1)S(1)}, u32[]{:S(2)}, u32[]{:S(2)}) collective-permute-start(bf16[4,2,8,1024]{3,2,1,0:T(8,128)(2,1)S(1)} %fusion.41), channel_id=1, source_target_pairs={{0,8},{8,16},{16,24},{24,32},{32,40},{40,48},{48,56},{56,0},{1,9},... | collective-permute-start | bytes 393224 | tf_op jit(solution)/shard_map/ppermute | solution.py:38
  63.8 5.3 %collective-permute-start.16 = (bf16[2,8,1024]{2,1,0:T(8,128)(2,1)S(1)}, bf16[2,8,1024]{2,1,0:T(8,128)(2,1)S(1)}, u32[]{:S(2)}, u32[]{:S(2)}) collective-permute-start(bf16[2,8,1024]{2,1,0:T(8,128)(2,1)S(1)} %fusion.70), channel_id=1, source_target_pairs={{0,8},{8,16},{16,24},{24,32},{32,40},{40,48},{48,56},{56,0},{1,9},... | collective-permute-start | bytes 98312 | tf_op jit(solution)/shard_map/ppermute | solution.py:38
  65.5 39.8 %copy-start.6 = (f32[16,16,16,8]{3,2,1,0:T(8,128)S(1)}, f32[16,16,16,8]{3,2,1,0:T(8,128)}, u32[]{:S(2)}) copy-start(f32[16,16,16,8]{3,2,1,0:T(8,128)} %fusion.23) | copy-start | bytes 393220
  66.8 6.3 %collective-permute-start.5 = (bf16[4,2,8,1024]{3,2,1,0:T(8,128)(2,1)S(1)}, bf16[4,2,8,1024]{3,2,1,0:T(8,128)(2,1)S(1)}, u32[]{:S(2)}, u32[]{:S(2)}) collective-permute-start(bf16[4,2,8,1024]{3,2,1,0:T(8,128)(2,1)S(1)} %fusion.40), channel_id=1, source_target_pairs={{0,8},{8,16},{16,24},{24,32},{32,40},{40,48},{48,56},{56,0},{1,9},... | collective-permute-start | bytes 393224 | tf_op jit(solution)/shard_map/ppermute | solution.py:38
  69.1 5.6 %collective-permute-start.17 = (bf16[2,8,1024]{2,1,0:T(8,128)(2,1)S(1)}, bf16[2,8,1024]{2,1,0:T(8,128)(2,1)S(1)}, u32[]{:S(2)}, u32[]{:S(2)}) collective-permute-start(bf16[2,8,1024]{2,1,0:T(8,128)(2,1)S(1)} %fusion.69), channel_id=1, source_target_pairs={{0,8},{8,16},{16,24},{24,32},{32,40},{40,48},{48,56},{56,0},{1,9},... | collective-permute-start | bytes 98312 | tf_op jit(solution)/shard_map/ppermute | solution.py:38
  74.2 6.3 %collective-permute-start.6 = (bf16[4,2,8,1024]{3,2,1,0:T(8,128)(2,1)S(1)}, bf16[4,2,8,1024]{3,2,1,0:T(8,128)(2,1)S(1)}, u32[]{:S(2)}, u32[]{:S(2)}) collective-permute-start(bf16[4,2,8,1024]{3,2,1,0:T(8,128)(2,1)S(1)} %fusion.39), channel_id=1, source_target_pairs={{0,8},{8,16},{16,24},{24,32},{32,40},{40,48},{48,56},{56,0},{1,9},... | collective-permute-start | bytes 393224 | tf_op jit(solution)/shard_map/ppermute | solution.py:38
  74.7 7.0 %collective-permute-start.18 = (bf16[2,8,1024]{2,1,0:T(8,128)(2,1)S(1)}, bf16[2,8,1024]{2,1,0:T(8,128)(2,1)S(1)}, u32[]{:S(2)}, u32[]{:S(2)}) collective-permute-start(bf16[2,8,1024]{2,1,0:T(8,128)(2,1)S(1)} %fusion.68), channel_id=1, source_target_pairs={{0,8},{8,16},{16,24},{24,32},{32,40},{40,48},{48,56},{56,0},{1,9},... | collective-permute-start | bytes 98312 | tf_op jit(solution)/shard_map/ppermute | solution.py:38
  81.5 6.6 %collective-permute-start.7 = (bf16[4,2,8,1024]{3,2,1,0:T(8,128)(2,1)S(1)}, bf16[4,2,8,1024]{3,2,1,0:T(8,128)(2,1)S(1)}, u32[]{:S(2)}, u32[]{:S(2)}) collective-permute-start(bf16[4,2,8,1024]{3,2,1,0:T(8,128)(2,1)S(1)} %fusion.38), channel_id=1, source_target_pairs={{0,8},{8,16},{16,24},{24,32},{32,40},{40,48},{48,56},{56,0},{1,9},... | collective-permute-start | bytes 393224 | tf_op jit(solution)/shard_map/ppermute | solution.py:38
  81.7 6.8 %collective-permute-start.19 = (bf16[2,8,1024]{2,1,0:T(8,128)(2,1)S(1)}, bf16[2,8,1024]{2,1,0:T(8,128)(2,1)S(1)}, u32[]{:S(2)}, u32[]{:S(2)}) collective-permute-start(bf16[2,8,1024]{2,1,0:T(8,128)(2,1)S(1)} %fusion.67), channel_id=1, source_target_pairs={{0,8},{8,16},{16,24},{24,32},{32,40},{40,48},{48,56},{56,0},{1,9},... | collective-permute-start | bytes 98312 | tf_op jit(solution)/shard_map/ppermute | solution.py:38
  88.3 10.5 %copy-start.9 = (f32[4,2,8,1024]{3,2,1,0:T(8,128)}, f32[4,2,8,1024]{3,2,1,0:T(8,128)S(1)}, u32[]{:S(2)}) copy-start(f32[4,2,8,1024]{3,2,1,0:T(8,128)S(1)} %bitcast_add_fusion.3) | copy-start | bytes 786436
  88.3 5.2 %collective-permute-start.8 = (bf16[2,8,1024]{2,1,0:T(8,128)(2,1)S(1)}, bf16[2,8,1024]{2,1,0:T(8,128)(2,1)S(1)}, u32[]{:S(2)}, u32[]{:S(2)}) collective-permute-start(bf16[2,8,1024]{2,1,0:T(8,128)(2,1)S(1)} %fusion.80), channel_id=1, source_target_pairs={{0,64},{64,128},{128,192},{192,0},{1,65},{65,129},{129,193},{193,1... | collective-permute-start | bytes 98312 | tf_op jit(solution)/shard_map/ppermute | solution.py:38
  88.5 5.4 %collective-permute-start.20 = (bf16[2,8,1024]{2,1,0:T(8,128)(2,1)S(1)}, bf16[2,8,1024]{2,1,0:T(8,128)(2,1)S(1)}, u32[]{:S(2)}, u32[]{:S(2)}) collective-permute-start(bf16[2,8,1024]{2,1,0:T(8,128)(2,1)S(1)} %fusion.66), channel_id=1, source_target_pairs={{0,8},{8,16},{16,24},{24,32},{32,40},{40,48},{48,56},{56,0},{1,9},... | collective-permute-start | bytes 98312 | tf_op jit(solution)/shard_map/ppermute | solution.py:38
  93.6 5.2 %collective-permute-start.9 = (bf16[2,8,1024]{2,1,0:T(8,128)(2,1)S(1)}, bf16[2,8,1024]{2,1,0:T(8,128)(2,1)S(1)}, u32[]{:S(2)}, u32[]{:S(2)}) collective-permute-start(bf16[2,8,1024]{2,1,0:T(8,128)(2,1)S(1)} %fusion.73), channel_id=1, source_target_pairs={{0,64},{64,128},{128,192},{192,0},{1,65},{65,129},{129,193},{193,1... | collective-permute-start | bytes 98312 | tf_op jit(solution)/shard_map/ppermute | solution.py:38
  93.9 5.2 %collective-permute-start.21 = (bf16[2,8,1024]{2,1,0:T(8,128)(2,1)S(1)}, bf16[2,8,1024]{2,1,0:T(8,128)(2,1)S(1)}, u32[]{:S(2)}, u32[]{:S(2)}) collective-permute-start(bf16[2,8,1024]{2,1,0:T(8,128)(2,1)S(1)} %fusion.65), channel_id=1, source_target_pairs={{0,8},{8,16},{16,24},{24,32},{32,40},{40,48},{48,56},{56,0},{1,9},... | collective-permute-start | bytes 98312 | tf_op jit(solution)/shard_map/ppermute | solution.py:38
  98.8 5.2 %collective-permute-start.10 = (bf16[2,8,1024]{2,1,0:T(8,128)(2,1)S(1)}, bf16[2,8,1024]{2,1,0:T(8,128)(2,1)S(1)}, u32[]{:S(2)}, u32[]{:S(2)}) collective-permute-start(bf16[2,8,1024]{2,1,0:T(8,128)(2,1)S(1)} %fusion.72), channel_id=1, source_target_pairs={{0,64},{64,128},{128,192},{192,0},{1,65},{65,129},{129,193},{193,1... | collective-permute-start | bytes 98312 | tf_op jit(solution)/shard_map/ppermute | solution.py:38
  105.4 2.0 %copy-start.8 = (bf16[16,8,64,64]{3,2,1,0:T(8,128)(2,1)S(1)}, bf16[16,8,64,64]{3,2,1,0:T(8,128)(2,1)}, u32[]{:S(2)}) copy-start(bf16[16,8,64,64]{3,2,1,0:T(8,128)(2,1)} %get-tuple-element.15) | copy-start | bytes 3145732
  113.6 4.3 %collective-permute-start.22 = (bf16[1,16,16,128]{3,1,2,0:T(8,128)(2,1)S(1)}, bf16[1,16,16,128]{3,1,2,0:T(8,128)(2,1)S(1)}, u32[]{:S(2)}, u32[]{:S(2)}) collective-permute-start(bf16[1,16,16,128]{3,1,2,0:T(8,128)(2,1)S(1)} %bitcast.189), channel_id=1, source_target_pairs={{0,1},{1,2},{2,3},{3,0},{4,5},{5,6},{6,7},{7,4},{8,9},{9,10},{10,1... | collective-permute-start | bytes 196616 | tf_op jit(solution)/shard_map/ppermute | solution.py:118
  114.1 5.5 %collective-permute-start.24 = (bf16[1,16,16,128]{3,1,2,0:T(8,128)(2,1)S(1)}, bf16[1,16,16,128]{3,1,2,0:T(8,128)(2,1)S(1)}, u32[]{:S(2)}, u32[]{:S(2)}) collective-permute-start(bf16[1,16,16,128]{3,1,2,0:T(8,128)(2,1)S(1)} %bitcast.190), channel_id=1, source_target_pairs={{0,3},{1,0},{2,1},{3,2},{4,7},{5,4},{6,5},{7,6},{8,11},{9,8},{10,9... | collective-permute-start | bytes 196616 | tf_op jit(solution)/shard_map/ppermute | solution.py:118
  115.7 5.8 %collective-permute-start.23 = (bf16[1,16,16,128]{3,1,2,0:T(8,128)(2,1)S(1)}, bf16[1,16,16,128]{3,1,2,0:T(8,128)(2,1)S(1)}, u32[]{:S(2)}, u32[]{:S(2)}) collective-permute-start(bf16[1,16,16,128]{3,1,2,0:T(8,128)(2,1)S(1)} %bitcast.191), channel_id=1, source_target_pairs={{0,2},{1,3},{2,0},{3,1},{4,6},{5,7},{6,4},{7,5},{8,10},{9,11},{10,... | collective-permute-start | bytes 196616 | tf_op jit(solution)/shard_map/ppermute | solution.py:118

commit v2 on v1

--- a/solution.py
+++ b/solution.py
@@ -62,7 +62,8 @@
         table = dft_table(mode_step * rows, time_index, sidereal_period, norm_factor)
         out = jnp.einsum("rdct,fctb->rdfb", table, part, precision=lax.Precision.HIGH)
         half_rows = ny * nz
-        y = out[half_rows:] + lax.ppermute(out[:half_rows], "tc", [(0, 1), (1, 0)])
+        got = lax.ppermute(out[:half_rows].astype(jnp.bfloat16), "tc", [(0, 1), (1, 0)])
+        y = out[half_rows:] + got.astype(jnp.float32)
         if z_major:
             y = y.reshape(nz, ny, *y.shape[1:])
             y = ring_reduce_scatter(ring_reduce_scatter(y, "tz", nz), "ty", ny)
@@ -103,9 +104,9 @@
         jnp.float32(0.0),
     )
     combined = jnp.einsum(
-        "mfblp,mfbi->mflpi", block_selector, vectors, precision=lax.Precision.HIGHEST
+        "mfblp,mfbi->mflpi", block_selector, vectors, precision=lax.Precision.HIGH
     )
-    weights = jnp.einsum("mflpi,lpij->mflj", combined, code_matrix, precision=lax.Precision.HIGHEST)
+    weights = jnp.einsum("mflpi,lpij->mflj", combined, code_matrix, precision=lax.Precision.HIGH)
     weights_bf = weights.astype(jnp.bfloat16)
     fr_pos = lax.axis_index("freq")
     basis_cols = lax.dynamic_slice_in_dim(fg_basis, fr_pos * chans_dev, chans_dev, 2)

time: 123 us -> 112 us (0.911)
  waiting for transfers between devices: 58.6 us -> 45.4 us
  starting transfers between devices: 17.9 us -> 24.1 us
  other arithmetic: 17.7 us -> 15.6 us
  local copies, waits for them, and re-layouts: 11 us -> 9.64 us
    ppermute x20, waiting for transfers between devices: 55.1 us -> 42 us  [ring_reduce_scatter(): got = lax.ppermute(s.astype(jnp.bfloat16), axis, fwd)]
    ppermute x20, starting transfers between devices: 14.4 us -> 20.1 us  [ring_reduce_scatter(): got = lax.ppermute(s.astype(jnp.bfloat16), axis, fwd)]
    unnamed x26, local copies, waits for them, and re-layouts: 3.28 us -> 1.69 us
  transfers between devices with their start and end apart: 25 -> 25, of which waited for: 20 -> 17; matrix products, arithmetic and copies ran while one was open for 17% -> 20% of each run, Pallas kernels for 0% -> 0%
where the time goes in v2:
time: 112 us; the launch traced here: 111 us
  waiting for transfers between devices  45.4 us (41%)
  starting transfers between devices  24.1 us (22%)
  other arithmetic  15.6 us (14%)
  matrix products  14.7 us (13%)
  local copies, waits for them, and re-layouts  9.64 us (9%)
  between operations  1.17 us (1%)
    ppermute x20, waiting for transfers between devices, ring_reduce_scatter(): got = lax.ppermute(s.astype(jnp.bfloat16), axis, fwd)  42 us
    ppermute x20, starting transfers between devices, ring_reduce_scatter(): got = lax.ppermute(s.astype(jnp.bfloat16), axis, fwd)  20.1 us
    dot_general x2, matrix products, spectra_of(): jnp.einsum('rdct,fctb->rdfb', table, part, precision=lax.Precision.HIGH)  6.54 us
    dot_general x1, matrix products, local(): jnp.einsum('mflpi,lpij->mflj', combined, code_matrix, precision=lax.Preci...  5.59 us
    convert_element_type x16, other arithmetic, ring_reduce_scatter(): got = lax.ppermute(s.astype(jnp.bfloat16), axis, fwd)  3.58 us
    neg x1, other arithmetic, realify(): upper = jnp.concatenate([real_part, -imag_part], axis=-1)  3.54 us
    ppermute x3, starting transfers between devices, local(): lax.ppermute(weights_bf, 'freq', [(j, (j + s) % fr_count) for j in range(...  3.52 us
    ppermute x3, waiting for transfers between devices, local(): lax.ppermute(weights_bf, 'freq', [(j, (j + s) % fr_count) for j in range(...  3.48 us
  transfers between devices with their start and end apart: 25, of which 17 were waited for; matrix products, arithmetic and copies ran while one was open for 20% of the time, Pallas kernels for 0%

profile of v2, /device:TPU:6, one launch (start us, length us, event | category | flops | bytes accessed | tf_op | source)
XLA Modules:
  0.0 110.7 jit_solution(1274233792012873128)
XLA Ops:
  0.5 0.4 sine_multiply_fusion.1
  0.9 4.4 %fusion.14 = f32[64,2,8,1024]{3,0,2,1:T(8,128)S(1)} fusion(f32[16,2,64,1024]{3,2,1,0:T(8,128)} %param.6, f32[64,1,2,64]{3,0,2,1:T(8,128)S(1)} %get-tuple-element.19, f32[64,1,2,64]{3,0,2,1:T(8,128)S(1)} %get-tuple-element.18), kind=kOutput, calls=%fused_computation.14 | convolution fusion | flops 805322752 | bytes 8454144 | tf_op jit(solution)/shard_map/rdct,fctb->rdfb/dot_general | solution.py:63
  5.3 1.3 %slice.58 = bf16[32,2,8,1024]{3,0,2,1:T(8,128)(2,1)} slice(f32[64,2,8,1024]{3,0,2,1:T(8,128)S(1)} %fusion.14), slice={[0:32], [0:2], [0:8], [0:1024]} | slice | bytes 2097152 | tf_op jit(solution)/shard_map/slice | solution.py:65
  6.6 2.2 %fusion.17 = f32[64,2,8,1024]{3,0,2,1:T(8,128)S(1)} fusion(f32[16,2,64,1024]{3,2,1,0:T(8,128)S(1)} %copy-done.4, f32[64,1,2,64]{3,0,2,1:T(8,128)S(1)} %get-tuple-element.21, f32[64,1,2,64]{3,0,2,1:T(8,128)S(1)} %get-tuple-element.20), kind=kOutput, calls=%fused_computation.15 | convolution fusion | flops 805322752 | bytes 8519680 | tf_op jit(solution)/shard_map/rdct,fctb->rdfb/dot_general | solution.py:63
  8.8 1.1 %slice.57 = bf16[32,2,8,1024]{3,0,2,1:T(8,128)(2,1)} slice(f32[64,2,8,1024]{3,0,2,1:T(8,128)S(1)} %fusion.17), slice={[0:32], [0:2], [0:8], [0:1024]} | slice | bytes 2097152 | tf_op jit(solution)/shard_map/slice | solution.py:65
  9.9 1.3 %copy-done.3 = f32[64,2,8,1024]{3,0,2,1:T(8,128)} copy-done((f32[64,2,8,1024]{3,0,2,1:T(8,128)}, f32[64,2,8,1024]{3,0,2,1:T(8,128)S(1)}, u32[]{:S(2)}) %copy-start.3) | copy-done | bytes 4194328
  11.3 0.5 collective-permute-start.11
  11.8 2.6 %fusion.23 = f32[16,16,16,8]{3,2,1,0:T(8,128)} fusion(f32[16,16,16]{2,1,0:T(8,128)S(1)} %bitcast.186, s32[16,16,16]{2,1,0:T(8,128)S(1)} %bitcast.187), kind=kLoop, calls=%fused_computation.24 | loop fusion | flops 65536 | bytes 163840 | tf_op jit(solution)/shard_map/jit(_where)/select_n | solution.py:101
  14.4 3.5 %slice_negate_fusion = (bf16[16,8,64,64]{3,2,1,0:T(8,128)(2,1)}, bf16[16,8,64,64]{3,2,1,0:T(8,128)(2,1)}, bf16[16,8,64,64]{3,2,1,0:T(8,128)(2,1)}) fusion(bf16[16,8,64,128]{3,2,1,0:T(8,128)(2,1)S(1)} %copy-done.5), kind=kLoop, calls=%fused_computation.159 | loop fusion | flops 524288 | bytes 5242880 | tf_op jit(solution)/shard_map/neg | solution.py:18
  18.0 1.6 %slice_add_fusion.1 = f32[32,2,8,1024]{3,0,2,1:T(8,128)S(1)} fusion(f32[64,2,8,1024]{3,0,2,1:T(8,128)S(1)} %copy-done.2, bf16[32,2,8,1024]{3,0,2,1:T(8,128)(2,1)} %collective-permute-done), kind=kLoop, calls=%fused_computation.20 | loop fusion | flops 1048576 | bytes 5242880 | tf_op jit(solution)/shard_map/add | solution.py:66
  19.5 1.7 %reshape.498 = f32[8,4,2,8,1024]{4,1,0,3,2:T(4,128)} reshape(f32[32,2,8,1024]{3,0,2,1:T(8,128)S(1)} %slice_add_fusion.1) | data formatting | bytes 4194304 | tf_op jit(solution)/shard_map/reshape | solution.py:68
  21.3 1.0 constant_dynamic-slice_fusion.12
  22.3 2.0 %collective-permute-start.1 = (bf16[4,2,8,1024]{3,2,1,0:T(8,128)(2,1)S(1)}, bf16[4,2,8,1024]{3,2,1,0:T(8,128)(2,1)S(1)}, u32[]{:S(2)}, u32[]{:S(2)}) collective-permute-start(bf16[4,2,8,1024]{3,2,1,0:T(8,128)(2,1)S(1)} %bitcast.188), channel_id=1, source_target_pairs={{0,8},{8,16},{16,24},{24,32},{32,40},{40,48},{48,56},{56,0},{1,9},... | collective-permute-start | bytes 393224 | tf_op jit(solution)/shard_map/ppermute | solution.py:38
  24.3 2.2 %fusion.20 = f32[4,8,2,8,1024]{4,1,0,3,2:T(8,128)S(1)} fusion(f32[64,2,8,1024]{3,0,2,1:T(8,128)} %copy-done.3, bf16[32,2,8,1024]{3,0,2,1:T(8,128)(2,1)} %collective-permute-done.11), kind=kLoop, calls=%fused_computation.18 | loop fusion | flops 1048576 | bytes 5242880 | tf_op jit(solution)/shard_map/reshape | solution.py:71
  26.7 1.7 %collective-permute-start.12 = (bf16[8,2,8,1024]{3,2,1,0:T(8,128)(2,1)S(1)}, bf16[8,2,8,1024]{3,2,1,0:T(8,128)(2,1)S(1)}, u32[]{:S(2)}, u32[]{:S(2)}) collective-permute-start(bf16[8,2,8,1024]{3,2,1,0:T(8,128)(2,1)S(1)} %bitcast.185), channel_id=1, source_target_pairs={{0,64},{64,128},{128,192},{192,0},{1,65},{65,129},{129,193},{193,1... | collective-permute-start | bytes 786440 | tf_op jit(solution)/shard_map/ppermute | solution.py:38
  28.3 1.0 constant_dynamic-slice_fusion.11
  29.4 2.5 %collective-permute-done.1 = bf16[4,2,8,1024]{3,2,1,0:T(8,128)(2,1)S(1)} collective-permute-done((bf16[4,2,8,1024]{3,2,1,0:T(8,128)(2,1)S(1)}, bf16[4,2,8,1024]{3,2,1,0:T(8,128)(2,1)S(1)}, u32[]{:S(2)}, u32[]{:S(2)}) %collective-permute-start.1) | collective-permute-done | bytes 131104 | tf_op jit(solution)/shard_map/ppermute | solution.py:38
  32.2 3.8 %collective-permute-done.12 = bf16[8,2,8,1024]{3,2,1,0:T(8,128)(2,1)S(1)} collective-permute-done((bf16[8,2,8,1024]{3,2,1,0:T(8,128)(2,1)S(1)}, bf16[8,2,8,1024]{3,2,1,0:T(8,128)(2,1)S(1)}, u32[]{:S(2)}, u32[]{:S(2)}) %collective-permute-start.12) | collective-permute-done | bytes 262176 | tf_op jit(solution)/shard_map/ppermute | solution.py:38
  36.0 0.3 fusion.36
  36.3 0.6 collective-permute-start.13
  36.9 0.2 constant_dynamic-slice_fusion
  37.7 0.6 collective-permute-done.2
  38.5 1.4 %collective-permute-start.3 = (bf16[4,2,8,1024]{3,2,1,0:T(8,128)(2,1)S(1)}, bf16[4,2,8,1024]{3,2,1,0:T(8,128)(2,1)S(1)}, u32[]{:S(2)}, u32[]{:S(2)}) collective-permute-start(bf16[4,2,8,1024]{3,2,1,0:T(8,128)(2,1)S(1)} %fusion.42), channel_id=1, source_target_pairs={{0,8},{8,16},{16,24},{24,32},{32,40},{40,48},{48,56},{56,0},{1,9},... | collective-permute-start | bytes 393224 | tf_op jit(solution)/shard_map/ppermute | solution.py:38
  39.9 5.0 %collective-permute-done.13 = bf16[8,2,8,1024]{3,2,1,0:T(8,128)(2,1)S(1)} collective-permute-done((bf16[8,2,8,1024]{3,2,1,0:T(8,128)(2,1)S(1)}, bf16[8,2,8,1024]{3,2,1,0:T(8,128)(2,1)S(1)}, u32[]{:S(2)}, u32[]{:S(2)}) %collective-permute-start.13) | collective-permute-done | bytes 262176 | tf_op jit(solution)/shard_map/ppermute | solution.py:38
  44.9 0.3 fusion.35
  45.4 0.2 fusion.41
  45.6 2.0 %collective-permute-start.4 = (bf16[4,2,8,1024]{3,2,1,0:T(8,128)(2,1)S(1)}, bf16[4,2,8,1024]{3,2,1,0:T(8,128)(2,1)S(1)}, u32[]{:S(2)}, u32[]{:S(2)}) collective-permute-start(bf16[4,2,8,1024]{3,2,1,0:T(8,128)(2,1)S(1)} %fusion.41), channel_id=1, source_target_pairs={{0,8},{8,16},{16,24},{24,32},{32,40},{40,48},{48,56},{56,0},{1,9},... | collective-permute-start | bytes 393224 | tf_op jit(solution)/shard_map/ppermute | solution.py:38
  47.6 5.3 %collective-permute-done.14 = bf16[8,2,8,1024]{3,2,1,0:T(8,128)(2,1)S(1)} collective-permute-done((bf16[8,2,8,1024]{3,2,1,0:T(8,128)(2,1)S(1)}, bf16[8,2,8,1024]{3,2,1,0:T(8,128)(2,1)S(1)}, u32[]{:S(2)}, u32[]{:S(2)}) %collective-permute-start.14) | collective-permute-done | bytes 262176 | tf_op jit(solution)/shard_map/ppermute | solution.py:38
  52.9 0.3 bitcast_add_fusion
  53.2 2.0 %collective-permute-start.15 = (bf16[2,8,1024]{2,1,0:T(8,128)(2,1)S(1)}, bf16[2,8,1024]{2,1,0:T(8,128)(2,1)S(1)}, u32[]{:S(2)}, u32[]{:S(2)}) collective-permute-start(bf16[2,8,1024]{2,1,0:T(8,128)(2,1)S(1)} %fusion.81), channel_id=1, source_target_pairs={{0,8},{8,16},{16,24},{24,32},{32,40},{40,48},{48,56},{56,0},{1,9},... | collective-permute-start | bytes 98312 | tf_op jit(solution)/shard_map/ppermute | solution.py:38
  55.4 2.0 %collective-permute-start.5 = (bf16[4,2,8,1024]{3,2,1,0:T(8,128)(2,1)S(1)}, bf16[4,2,8,1024]{3,2,1,0:T(8,128)(2,1)S(1)}, u32[]{:S(2)}, u32[]{:S(2)}) collective-permute-start(bf16[4,2,8,1024]{3,2,1,0:T(8,128)(2,1)S(1)} %fusion.40), channel_id=1, source_target_pairs={{0,8},{8,16},{16,24},{24,32},{32,40},{40,48},{48,56},{56,0},{1,9},... | collective-permute-start | bytes 393224 | tf_op jit(solution)/shard_map/ppermute | solution.py:38
  57.4 2.7 %collective-permute-done.15 = bf16[2,8,1024]{2,1,0:T(8,128)(2,1)S(1)} collective-permute-done((bf16[2,8,1024]{2,1,0:T(8,128)(2,1)S(1)}, bf16[2,8,1024]{2,1,0:T(8,128)(2,1)S(1)}, u32[]{:S(2)}, u32[]{:S(2)}) %collective-permute-start.15) | collective-permute-done | bytes 32800 | tf_op jit(solution)/shard_map/ppermute | solution.py:38
  60.1 0.5 collective-permute-start.16
  60.6 1.4 %collective-permute-done.5 = bf16[4,2,8,1024]{3,2,1,0:T(8,128)(2,1)S(1)} collective-permute-done((bf16[4,2,8,1024]{3,2,1,0:T(8,128)(2,1)S(1)}, bf16[4,2,8,1024]{3,2,1,0:T(8,128)(2,1)S(1)}, u32[]{:S(2)}, u32[]{:S(2)}) %collective-permute-start.5) | collective-permute-done | bytes 131104 | tf_op jit(solution)/shard_map/ppermute | solution.py:38
  62.0 1.1 %fusion.39 = bf16[4,2,8,1024]{3,2,1,0:T(8,128)(2,1)S(1)} fusion(f32[1,4,2,8,1024]{4,1,0,3,2:T(4,128)} %get-tuple-element.8, bf16[4,2,8,1024]{3,2,1,0:T(8,128)(2,1)S(1)} %collective-permute-done.5), kind=kLoop, calls=%fused_computation.46 | loop fusion | flops 196608 | bytes 524288 | tf_op jit(solution)/shard_map/convert_element_type | solution.py:38
  63.1 1.2 %collective-permute-start.6 = (bf16[4,2,8,1024]{3,2,1,0:T(8,128)(2,1)S(1)}, bf16[4,2,8,1024]{3,2,1,0:T(8,128)(2,1)S(1)}, u32[]{:S(2)}, u32[]{:S(2)}) collective-permute-start(bf16[4,2,8,1024]{3,2,1,0:T(8,128)(2,1)S(1)} %fusion.39), channel_id=1, source_target_pairs={{0,8},{8,16},{16,24},{24,32},{32,40},{40,48},{48,56},{56,0},{1,9},... | collective-permute-start | bytes 393224 | tf_op jit(solution)/shard_map/ppermute | solution.py:38
  64.4 0.9 collective-permute-done.16
  65.3 1.6 %collective-permute-start.17 = (bf16[2,8,1024]{2,1,0:T(8,128)(2,1)S(1)}, bf16[2,8,1024]{2,1,0:T(8,128)(2,1)S(1)}, u32[]{:S(2)}, u32[]{:S(2)}) collective-permute-start(bf16[2,8,1024]{2,1,0:T(8,128)(2,1)S(1)} %fusion.69), channel_id=1, source_target_pairs={{0,8},{8,16},{16,24},{24,32},{32,40},{40,48},{48,56},{56,0},{1,9},... | collective-permute-start | bytes 98312 | tf_op jit(solution)/shard_map/ppermute | solution.py:38
  67.0 2.5 %collective-permute-done.6 = bf16[4,2,8,1024]{3,2,1,0:T(8,128)(2,1)S(1)} collective-permute-done((bf16[4,2,8,1024]{3,2,1,0:T(8,128)(2,1)S(1)}, bf16[4,2,8,1024]{3,2,1,0:T(8,128)(2,1)S(1)}, u32[]{:S(2)}, u32[]{:S(2)}) %collective-permute-start.6) | collective-permute-done | bytes 131104 | tf_op jit(solution)/shard_map/ppermute | solution.py:38
  69.4 1.1 %fusion.38 = bf16[4,2,8,1024]{3,2,1,0:T(8,128)(2,1)S(1)} fusion(f32[1,4,2,8,1024]{4,1,0,3,2:T(4,128)} %get-tuple-element.7, bf16[4,2,8,1024]{3,2,1,0:T(8,128)(2,1)S(1)} %collective-permute-done.6), kind=kLoop, calls=%fused_computation.44 | loop fusion | flops 196608 | bytes 524288 | tf_op jit(solution)/shard_map/convert_element_type | solution.py:38
  70.5 1.0 collective-permute-start.7
  71.5 2.6 %collective-permute-start.18 = (bf16[2,8,1024]{2,1,0:T(8,128)(2,1)S(1)}, bf16[2,8,1024]{2,1,0:T(8,128)(2,1)S(1)}, u32[]{:S(2)}, u32[]{:S(2)}) collective-permute-start(bf16[2,8,1024]{2,1,0:T(8,128)(2,1)S(1)} %fusion.68), channel_id=1, source_target_pairs={{0,8},{8,16},{16,24},{24,32},{32,40},{40,48},{48,56},{56,0},{1,9},... | collective-permute-start | bytes 98312 | tf_op jit(solution)/shard_map/ppermute | solution.py:38
  74.1 2.9 %collective-permute-done.7 = bf16[4,2,8,1024]{3,2,1,0:T(8,128)(2,1)S(1)} collective-permute-done((bf16[4,2,8,1024]{3,2,1,0:T(8,128)(2,1)S(1)}, bf16[4,2,8,1024]{3,2,1,0:T(8,128)(2,1)S(1)}, u32[]{:S(2)}, u32[]{:S(2)}) %collective-permute-start.7) | collective-permute-done | bytes 131104 | tf_op jit(solution)/shard_map/ppermute | solution.py:38
  77.0 0.2 bitcast_add_fusion.3
  77.3 0.7 collective-permute-start.19
  78.1 4.3 %collective-permute-done.8 = bf16[2,8,1024]{2,1,0:T(8,128)(2,1)S(1)} collective-permute-done((bf16[2,8,1024]{2,1,0:T(8,128)(2,1)S(1)}, bf16[2,8,1024]{2,1,0:T(8,128)(2,1)S(1)}, u32[]{:S(2)}, u32[]{:S(2)}) %collective-permute-start.8) | collective-permute-done | bytes 32800 | tf_op jit(solution)/shard_map/ppermute | solution.py:38
  82.4 0.3 collective-permute-start.9
  82.8 5.0 %collective-permute-done.9 = bf16[2,8,1024]{2,1,0:T(8,128)(2,1)S(1)} collective-permute-done((bf16[2,8,1024]{2,1,0:T(8,128)(2,1)S(1)}, bf16[2,8,1024]{2,1,0:T(8,128)(2,1)S(1)}, u32[]{:S(2)}, u32[]{:S(2)}) %collective-permute-start.9) | collective-permute-done | bytes 32800 | tf_op jit(solution)/shard_map/ppermute | solution.py:38
  88.0 5.0 %collective-permute-done.10 = bf16[2,8,1024]{2,1,0:T(8,128)(2,1)S(1)} collective-permute-done((bf16[2,8,1024]{2,1,0:T(8,128)(2,1)S(1)}, bf16[2,8,1024]{2,1,0:T(8,128)(2,1)S(1)}, u32[]{:S(2)}, u32[]{:S(2)}) %collective-permute-start.10) | collective-permute-done | bytes 32800 | tf_op jit(solution)/shard_map/ppermute | solution.py:38
  93.2 0.9 fusion.64
  94.3 0.2 maximum_bitcast_fusion.4
  94.6 1.5 %fusion.21 = f32[16,16,8,128]{3,2,1,0:T(8,128)S(1)} fusion(f32[16,16,16,8]{3,2,1,0:T(8,128)S(1)} %copy-done.6, bf16[16,16,128,1]{2,1,0,3:T(8,128)(2,1)S(1)} %reshape.512), kind=kOutput, calls=%fused_computation.21 | convolution fusion | flops 25165824 | bytes 1245184 | tf_op jit(solution)/shard_map/mfblp,mfbi->mflpi/dot_general | solution.py:106
  96.2 5.6 %fusion.29 = bf16[16,128,16]{1,2,0:T(8,128)(2,1)S(1)} fusion(bf16[16,8,64,64]{3,2,1,0:T(8,128)(2,1)} %get-tuple-element.17, bf16[16,8,64,64]{3,2,1,0:T(8,128)(2,1)} %get-tuple-element.16, bf16[16,8,64,64]{3,2,1,0:T(8,128)(2,1)S(1)} %copy-done.8, f32[16,16,8,128]{3,2,1,0:T(8,128)S(1)} %fusion.21), kind=kOutput, calls=%fused_computation.30 | convolution fusion | flops 218136576 | bytes 4259840 | tf_op jit(solution)/shard_map/mflpi,lpij->mflj/dot_general | solution.py:109
  101.8 0.6 collective-permute-start.22
  102.4 1.6 %collective-permute-start.24 = (bf16[1,16,16,128]{3,1,2,0:T(8,128)(2,1)S(1)}, bf16[1,16,16,128]{3,1,2,0:T(8,128)(2,1)S(1)}, u32[]{:S(2)}, u32[]{:S(2)}) collective-permute-start(bf16[1,16,16,128]{3,1,2,0:T(8,128)(2,1)S(1)} %bitcast.190), channel_id=1, source_target_pairs={{0,3},{1,0},{2,1},{3,2},{4,7},{5,4},{6,5},{7,6},{8,11},{9,8},{10,9... | collective-permute-start | bytes 196616 | tf_op jit(solution)/shard_map/ppermute | solution.py:119
  103.9 1.4 %collective-permute-start.23 = (bf16[1,16,16,128]{3,1,2,0:T(8,128)(2,1)S(1)}, bf16[1,16,16,128]{3,1,2,0:T(8,128)(2,1)S(1)}, u32[]{:S(2)}, u32[]{:S(2)}) collective-permute-start(bf16[1,16,16,128]{3,1,2,0:T(8,128)(2,1)S(1)} %bitcast.191), channel_id=1, source_target_pairs={{0,2},{1,3},{2,0},{3,1},{4,6},{5,7},{6,4},{7,5},{8,10},{9,11},{10,... | collective-permute-start | bytes 196616 | tf_op jit(solution)/shard_map/ppermute | solution.py:119
  105.3 0.3 fusion.53
  105.6 0.5 collective-permute-done.22
  106.2 0.3 convolution_add_fusion.1
  106.5 1.4 %collective-permute-done.24 = bf16[1,16,16,128]{3,1,2,0:T(8,128)(2,1)S(1)} collective-permute-done((bf16[1,16,16,128]{3,1,2,0:T(8,128)(2,1)S(1)}, bf16[1,16,16,128]{3,1,2,0:T(8,128)(2,1)S(1)}, u32[]{:S(2)}, u32[]{:S(2)}) %collective-permute-start.24) | collective-permute-done | bytes 65568 | tf_op jit(solution)/shard_map/ppermute | solution.py:119
  107.9 0.3 fusion.49
  108.1 1.6 %collective-permute-done.23 = bf16[1,16,16,128]{3,1,2,0:T(8,128)(2,1)S(1)} collective-permute-done((bf16[1,16,16,128]{3,1,2,0:T(8,128)(2,1)S(1)}, bf16[1,16,16,128]{3,1,2,0:T(8,128)(2,1)S(1)}, u32[]{:S(2)}, u32[]{:S(2)}) %collective-permute-start.23) | collective-permute-done | bytes 65568 | tf_op jit(solution)/shard_map/ppermute | solution.py:119
  109.7 0.3 fusion.33
  110.0 0.7 copy.23
  (74 shorter events, 2.7 us)
Async XLA Ops:
  0.0 36.9 %copy-start = (f32[16,64,64]{2,1,0:T(8,128)S(1)}, f32[16,64,64]{2,1,0:T(8,128)}, u32[]{:S(2)}) copy-start(f32[16,64,64]{2,1,0:T(8,128)} %param.10) | copy-start | bytes 786436
  0.9 5.7 %copy-start.4 = (f32[16,2,64,1024]{3,2,1,0:T(8,128)S(1)}, f32[16,2,64,1024]{3,2,1,0:T(8,128)}, u32[]{:S(2)}) copy-start(f32[16,2,64,1024]{3,2,1,0:T(8,128)} %param.6) | copy-start | bytes 25165828
  5.3 3.5 %copy-start.1 = (f32[64,2,8,1024]{3,0,2,1:T(8,128)}, f32[64,2,8,1024]{3,0,2,1:T(8,128)S(1)}, u32[]{:S(2)}) copy-start(f32[64,2,8,1024]{3,0,2,1:T(8,128)S(1)} %fusion.14) | copy-start | bytes 12582916
  6.6 11.4 %collective-permute-start = (bf16[32,2,8,1024]{3,0,2,1:T(8,128)(2,1)}, bf16[32,2,8,1024]{3,0,2,1:T(8,128)(2,1)}, u32[]{:S(2)}, u32[]{:S(2)}) collective-permute-start(bf16[32,2,8,1024]{3,0,2,1:T(8,128)(2,1)} %slice.58), channel_id=1, source_target_pairs={{0,4},{4,0},{1,5},{5,1},{2,6},{6,2},{3,7},{7,3},{8,12},{12,8},{9,1... | collective-permute-start | bytes 3145736 | tf_op jit(solution)/shard_map/ppermute | solution.py:65
  6.6 5.2 %copy-start.10 = (f32[1,16,16,16]{3,2,1,0:T(8,128)S(1)}, f32[1,16,16,16]{3,2,1,0:T(8,128)}, u32[]{:S(2)}) copy-start(f32[1,16,16,16]{3,2,1,0:T(8,128)} %param.9) | copy-start | bytes 49156
  6.6 5.2 %copy-start.11 = (s32[1,16,16,16]{3,2,1,0:T(8,128)S(1)}, s32[1,16,16,16]{3,2,1,0:T(8,128)}, u32[]{:S(2)}) copy-start(s32[1,16,16,16]{3,2,1,0:T(8,128)} %param.8) | copy-start | bytes 49156
  8.8 2.5 %copy-start.3 = (f32[64,2,8,1024]{3,0,2,1:T(8,128)}, f32[64,2,8,1024]{3,0,2,1:T(8,128)S(1)}, u32[]{:S(2)}) copy-start(f32[64,2,8,1024]{3,0,2,1:T(8,128)S(1)} %fusion.17) | copy-start | bytes 12582916
  8.8 5.6 %copy-start.5 = (bf16[16,8,64,128]{3,2,1,0:T(8,128)(2,1)S(1)}, bf16[16,8,64,128]{3,2,1,0:T(8,128)(2,1)}, u32[]{:S(2)}) copy-start(bf16[16,8,64,128]{3,2,1,0:T(8,128)(2,1)} %param.7) | copy-start | bytes 6291460
  11.3 13.0 %collective-permute-start.11 = (bf16[32,2,8,1024]{3,0,2,1:T(8,128)(2,1)}, bf16[32,2,8,1024]{3,0,2,1:T(8,128)(2,1)}, u32[]{:S(2)}, u32[]{:S(2)}) collective-permute-start(bf16[32,2,8,1024]{3,0,2,1:T(8,128)(2,1)} %slice.57), channel_id=1, source_target_pairs={{0,4},{4,0},{1,5},{5,1},{2,6},{6,2},{3,7},{7,3},{8,12},{12,8},{9,1... | collective-permute-start | bytes 3145736 | tf_op jit(solution)/shard_map/ppermute | solution.py:65
  14.4 3.5 %copy-start.2 = (f32[64,2,8,1024]{3,0,2,1:T(8,128)S(1)}, f32[64,2,8,1024]{3,0,2,1:T(8,128)}, u32[]{:S(2)}) copy-start(f32[64,2,8,1024]{3,0,2,1:T(8,128)} %copy-done.1) | copy-start | bytes 12582916
  22.3 6.0 %copy-start.7 = (f32[8,4,2,8,1024]{4,1,0,3,2:T(4,128)S(1)}, f32[8,4,2,8,1024]{4,1,0,3,2:T(4,128)}, u32[]{:S(2)}) copy-start(f32[8,4,2,8,1024]{4,1,0,3,2:T(4,128)} %reshape.498) | copy-start | bytes 6291460
  22.3 9.6 %collective-permute-start.1 = (bf16[4,2,8,1024]{3,2,1,0:T(8,128)(2,1)S(1)}, bf16[4,2,8,1024]{3,2,1,0:T(8,128)(2,1)S(1)}, u32[]{:S(2)}, u32[]{:S(2)}) collective-permute-start(bf16[4,2,8,1024]{3,2,1,0:T(8,128)(2,1)S(1)} %bitcast.188), channel_id=1, source_target_pairs={{0,8},{8,16},{16,24},{24,32},{32,40},{40,48},{48,56},{56,0},{1,9},... | collective-permute-start | bytes 393224 | tf_op jit(solution)/shard_map/ppermute | solution.py:38
  26.7 9.3 %collective-permute-start.12 = (bf16[8,2,8,1024]{3,2,1,0:T(8,128)(2,1)S(1)}, bf16[8,2,8,1024]{3,2,1,0:T(8,128)(2,1)S(1)}, u32[]{:S(2)}, u32[]{:S(2)}) collective-permute-start(bf16[8,2,8,1024]{3,2,1,0:T(8,128)(2,1)S(1)} %bitcast.185), channel_id=1, source_target_pairs={{0,64},{64,128},{128,192},{192,0},{1,65},{65,129},{129,193},{193,1... | collective-permute-start | bytes 786440 | tf_op jit(solution)/shard_map/ppermute | solution.py:38
  32.1 6.3 %collective-permute-start.2 = (bf16[4,2,8,1024]{3,2,1,0:T(8,128)(2,1)S(1)}, bf16[4,2,8,1024]{3,2,1,0:T(8,128)(2,1)S(1)}, u32[]{:S(2)}, u32[]{:S(2)}) collective-permute-start(bf16[4,2,8,1024]{3,2,1,0:T(8,128)(2,1)S(1)} %fusion.43), channel_id=1, source_target_pairs={{0,8},{8,16},{16,24},{24,32},{32,40},{40,48},{48,56},{56,0},{1,9},... | collective-permute-start | bytes 393224 | tf_op jit(solution)/shard_map/ppermute | solution.py:38
  36.3 8.6 %collective-permute-start.13 = (bf16[8,2,8,1024]{3,2,1,0:T(8,128)(2,1)S(1)}, bf16[8,2,8,1024]{3,2,1,0:T(8,128)(2,1)S(1)}, u32[]{:S(2)}, u32[]{:S(2)}) collective-permute-start(bf16[8,2,8,1024]{3,2,1,0:T(8,128)(2,1)S(1)} %fusion.36), channel_id=1, source_target_pairs={{0,64},{64,128},{128,192},{192,0},{1,65},{65,129},{129,193},{193,1... | collective-permute-start | bytes 786440 | tf_op jit(solution)/shard_map/ppermute | solution.py:38
  38.5 6.9 %collective-permute-start.3 = (bf16[4,2,8,1024]{3,2,1,0:T(8,128)(2,1)S(1)}, bf16[4,2,8,1024]{3,2,1,0:T(8,128)(2,1)S(1)}, u32[]{:S(2)}, u32[]{:S(2)}) collective-permute-start(bf16[4,2,8,1024]{3,2,1,0:T(8,128)(2,1)S(1)} %fusion.42), channel_id=1, source_target_pairs={{0,8},{8,16},{16,24},{24,32},{32,40},{40,48},{48,56},{56,0},{1,9},... | collective-permute-start | bytes 393224 | tf_op jit(solution)/shard_map/ppermute | solution.py:38
  45.2 7.7 %collective-permute-start.14 = (bf16[8,2,8,1024]{3,2,1,0:T(8,128)(2,1)S(1)}, bf16[8,2,8,1024]{3,2,1,0:T(8,128)(2,1)S(1)}, u32[]{:S(2)}, u32[]{:S(2)}) collective-permute-start(bf16[8,2,8,1024]{3,2,1,0:T(8,128)(2,1)S(1)} %fusion.35), channel_id=1, source_target_pairs={{0,64},{64,128},{128,192},{192,0},{1,65},{65,129},{129,193},{193,1... | collective-permute-start | bytes 786440 | tf_op jit(solution)/shard_map/ppermute | solution.py:38
  45.6 9.6 %collective-permute-start.4 = (bf16[4,2,8,1024]{3,2,1,0:T(8,128)(2,1)S(1)}, bf16[4,2,8,1024]{3,2,1,0:T(8,128)(2,1)S(1)}, u32[]{:S(2)}, u32[]{:S(2)}) collective-permute-start(bf16[4,2,8,1024]{3,2,1,0:T(8,128)(2,1)S(1)} %fusion.41), channel_id=1, source_target_pairs={{0,8},{8,16},{16,24},{24,32},{32,40},{40,48},{48,56},{56,0},{1,9},... | collective-permute-start | bytes 393224 | tf_op jit(solution)/shard_map/ppermute | solution.py:38
  53.2 34.7 %copy-start.9 = (f32[8,2,8,1024]{3,2,1,0:T(8,128)}, f32[8,2,8,1024]{3,2,1,0:T(8,128)S(1)}, u32[]{:S(2)}) copy-start(f32[8,2,8,1024]{3,2,1,0:T(8,128)S(1)} %bitcast_add_fusion) | copy-start | bytes 1572868
  53.2 6.9 %collective-permute-start.15 = (bf16[2,8,1024]{2,1,0:T(8,128)(2,1)S(1)}, bf16[2,8,1024]{2,1,0:T(8,128)(2,1)S(1)}, u32[]{:S(2)}, u32[]{:S(2)}) collective-permute-start(bf16[2,8,1024]{2,1,0:T(8,128)(2,1)S(1)} %fusion.81), channel_id=1, source_target_pairs={{0,8},{8,16},{16,24},{24,32},{32,40},{40,48},{48,56},{56,0},{1,9},... | collective-permute-start | bytes 98312 | tf_op jit(solution)/shard_map/ppermute | solution.py:38
  55.4 39.2 %copy-start.6 = (f32[16,16,16,8]{3,2,1,0:T(8,128)S(1)}, f32[16,16,16,8]{3,2,1,0:T(8,128)}, u32[]{:S(2)}) copy-start(f32[16,16,16,8]{3,2,1,0:T(8,128)} %fusion.23) | copy-start | bytes 393220
  55.4 6.6 %collective-permute-start.5 = (bf16[4,2,8,1024]{3,2,1,0:T(8,128)(2,1)S(1)}, bf16[4,2,8,1024]{3,2,1,0:T(8,128)(2,1)S(1)}, u32[]{:S(2)}, u32[]{:S(2)}) collective-permute-start(bf16[4,2,8,1024]{3,2,1,0:T(8,128)(2,1)S(1)} %fusion.40), channel_id=1, source_target_pairs={{0,8},{8,16},{16,24},{24,32},{32,40},{40,48},{48,56},{56,0},{1,9},... | collective-permute-start | bytes 393224 | tf_op jit(solution)/shard_map/ppermute | solution.py:38
  60.1 5.2 %collective-permute-start.16 = (bf16[2,8,1024]{2,1,0:T(8,128)(2,1)S(1)}, bf16[2,8,1024]{2,1,0:T(8,128)(2,1)S(1)}, u32[]{:S(2)}, u32[]{:S(2)}) collective-permute-start(bf16[2,8,1024]{2,1,0:T(8,128)(2,1)S(1)} %fusion.70), channel_id=1, source_target_pairs={{0,8},{8,16},{16,24},{24,32},{32,40},{40,48},{48,56},{56,0},{1,9},... | collective-permute-start | bytes 98312 | tf_op jit(solution)/shard_map/ppermute | solution.py:38
  63.1 6.3 %collective-permute-start.6 = (bf16[4,2,8,1024]{3,2,1,0:T(8,128)(2,1)S(1)}, bf16[4,2,8,1024]{3,2,1,0:T(8,128)(2,1)S(1)}, u32[]{:S(2)}, u32[]{:S(2)}) collective-permute-start(bf16[4,2,8,1024]{3,2,1,0:T(8,128)(2,1)S(1)} %fusion.39), channel_id=1, source_target_pairs={{0,8},{8,16},{16,24},{24,32},{32,40},{40,48},{48,56},{56,0},{1,9},... | collective-permute-start | bytes 393224 | tf_op jit(solution)/shard_map/ppermute | solution.py:38
  65.3 6.2 %collective-permute-start.17 = (bf16[2,8,1024]{2,1,0:T(8,128)(2,1)S(1)}, bf16[2,8,1024]{2,1,0:T(8,128)(2,1)S(1)}, u32[]{:S(2)}, u32[]{:S(2)}) collective-permute-start(bf16[2,8,1024]{2,1,0:T(8,128)(2,1)S(1)} %fusion.69), channel_id=1, source_target_pairs={{0,8},{8,16},{16,24},{24,32},{32,40},{40,48},{48,56},{56,0},{1,9},... | collective-permute-start | bytes 98312 | tf_op jit(solution)/shard_map/ppermute | solution.py:38
  70.5 6.4 %collective-permute-start.7 = (bf16[4,2,8,1024]{3,2,1,0:T(8,128)(2,1)S(1)}, bf16[4,2,8,1024]{3,2,1,0:T(8,128)(2,1)S(1)}, u32[]{:S(2)}, u32[]{:S(2)}) collective-permute-start(bf16[4,2,8,1024]{3,2,1,0:T(8,128)(2,1)S(1)} %fusion.38), channel_id=1, source_target_pairs={{0,8},{8,16},{16,24},{24,32},{32,40},{40,48},{48,56},{56,0},{1,9},... | collective-permute-start | bytes 393224 | tf_op jit(solution)/shard_map/ppermute | solution.py:38
  71.5 5.8 %collective-permute-start.18 = (bf16[2,8,1024]{2,1,0:T(8,128)(2,1)S(1)}, bf16[2,8,1024]{2,1,0:T(8,128)(2,1)S(1)}, u32[]{:S(2)}, u32[]{:S(2)}) collective-permute-start(bf16[2,8,1024]{2,1,0:T(8,128)(2,1)S(1)} %fusion.68), channel_id=1, source_target_pairs={{0,8},{8,16},{16,24},{24,32},{32,40},{40,48},{48,56},{56,0},{1,9},... | collective-permute-start | bytes 98312 | tf_op jit(solution)/shard_map/ppermute | solution.py:38
  77.2 5.2 %collective-permute-start.8 = (bf16[2,8,1024]{2,1,0:T(8,128)(2,1)S(1)}, bf16[2,8,1024]{2,1,0:T(8,128)(2,1)S(1)}, u32[]{:S(2)}, u32[]{:S(2)}) collective-permute-start(bf16[2,8,1024]{2,1,0:T(8,128)(2,1)S(1)} %fusion.80), channel_id=1, source_target_pairs={{0,64},{64,128},{128,192},{192,0},{1,65},{65,129},{129,193},{193,1... | collective-permute-start | bytes 98312 | tf_op jit(solution)/shard_map/ppermute | solution.py:38
  77.3 5.4 %collective-permute-start.19 = (bf16[2,8,1024]{2,1,0:T(8,128)(2,1)S(1)}, bf16[2,8,1024]{2,1,0:T(8,128)(2,1)S(1)}, u32[]{:S(2)}, u32[]{:S(2)}) collective-permute-start(bf16[2,8,1024]{2,1,0:T(8,128)(2,1)S(1)} %fusion.67), channel_id=1, source_target_pairs={{0,8},{8,16},{16,24},{24,32},{32,40},{40,48},{48,56},{56,0},{1,9},... | collective-permute-start | bytes 98312 | tf_op jit(solution)/shard_map/ppermute | solution.py:38
  82.4 5.4 %collective-permute-start.9 = (bf16[2,8,1024]{2,1,0:T(8,128)(2,1)S(1)}, bf16[2,8,1024]{2,1,0:T(8,128)(2,1)S(1)}, u32[]{:S(2)}, u32[]{:S(2)}) collective-permute-start(bf16[2,8,1024]{2,1,0:T(8,128)(2,1)S(1)} %fusion.73), channel_id=1, source_target_pairs={{0,64},{64,128},{128,192},{192,0},{1,65},{65,129},{129,193},{193,1... | collective-permute-start | bytes 98312 | tf_op jit(solution)/shard_map/ppermute | solution.py:38
  82.7 5.2 %collective-permute-start.20 = (bf16[2,8,1024]{2,1,0:T(8,128)(2,1)S(1)}, bf16[2,8,1024]{2,1,0:T(8,128)(2,1)S(1)}, u32[]{:S(2)}, u32[]{:S(2)}) collective-permute-start(bf16[2,8,1024]{2,1,0:T(8,128)(2,1)S(1)} %fusion.66), channel_id=1, source_target_pairs={{0,8},{8,16},{16,24},{24,32},{32,40},{40,48},{48,56},{56,0},{1,9},... | collective-permute-start | bytes 98312 | tf_op jit(solution)/shard_map/ppermute | solution.py:38
  87.8 5.2 %collective-permute-start.10 = (bf16[2,8,1024]{2,1,0:T(8,128)(2,1)S(1)}, bf16[2,8,1024]{2,1,0:T(8,128)(2,1)S(1)}, u32[]{:S(2)}, u32[]{:S(2)}) collective-permute-start(bf16[2,8,1024]{2,1,0:T(8,128)(2,1)S(1)} %fusion.72), channel_id=1, source_target_pairs={{0,64},{64,128},{128,192},{192,0},{1,65},{65,129},{129,193},{193,1... | collective-permute-start | bytes 98312 | tf_op jit(solution)/shard_map/ppermute | solution.py:38
  88.0 5.3 %collective-permute-start.21 = (bf16[2,8,1024]{2,1,0:T(8,128)(2,1)S(1)}, bf16[2,8,1024]{2,1,0:T(8,128)(2,1)S(1)}, u32[]{:S(2)}, u32[]{:S(2)}) collective-permute-start(bf16[2,8,1024]{2,1,0:T(8,128)(2,1)S(1)} %fusion.65), channel_id=1, source_target_pairs={{0,8},{8,16},{16,24},{24,32},{32,40},{40,48},{48,56},{56,0},{1,9},... | collective-permute-start | bytes 98312 | tf_op jit(solution)/shard_map/ppermute | solution.py:38
  94.6 1.6 %copy-start.8 = (bf16[16,8,64,64]{3,2,1,0:T(8,128)(2,1)S(1)}, bf16[16,8,64,64]{3,2,1,0:T(8,128)(2,1)}, u32[]{:S(2)}) copy-start(bf16[16,8,64,64]{3,2,1,0:T(8,128)(2,1)} %get-tuple-element.15) | copy-start | bytes 3145732
  101.8 4.3 %collective-permute-start.22 = (bf16[1,16,16,128]{3,1,2,0:T(8,128)(2,1)S(1)}, bf16[1,16,16,128]{3,1,2,0:T(8,128)(2,1)S(1)}, u32[]{:S(2)}, u32[]{:S(2)}) collective-permute-start(bf16[1,16,16,128]{3,1,2,0:T(8,128)(2,1)S(1)} %bitcast.189), channel_id=1, source_target_pairs={{0,1},{1,2},{2,3},{3,0},{4,5},{5,6},{6,7},{7,4},{8,9},{9,10},{10,1... | collective-permute-start | bytes 196616 | tf_op jit(solution)/shard_map/ppermute | solution.py:119
  102.4 5.5 %collective-permute-start.24 = (bf16[1,16,16,128]{3,1,2,0:T(8,128)(2,1)S(1)}, bf16[1,16,16,128]{3,1,2,0:T(8,128)(2,1)S(1)}, u32[]{:S(2)}, u32[]{:S(2)}) collective-permute-start(bf16[1,16,16,128]{3,1,2,0:T(8,128)(2,1)S(1)} %bitcast.190), channel_id=1, source_target_pairs={{0,3},{1,0},{2,1},{3,2},{4,7},{5,4},{6,5},{7,6},{8,11},{9,8},{10,9... | collective-permute-start | bytes 196616 | tf_op jit(solution)/shard_map/ppermute | solution.py:119
  103.9 5.8 %collective-permute-start.23 = (bf16[1,16,16,128]{3,1,2,0:T(8,128)(2,1)S(1)}, bf16[1,16,16,128]{3,1,2,0:T(8,128)(2,1)S(1)}, u32[]{:S(2)}, u32[]{:S(2)}) collective-permute-start(bf16[1,16,16,128]{3,1,2,0:T(8,128)(2,1)S(1)} %bitcast.191), channel_id=1, source_target_pairs={{0,2},{1,3},{2,0},{3,1},{4,6},{5,7},{6,4},{7,5},{8,10},{9,11},{10,... | collective-permute-start | bytes 196616 | tf_op jit(solution)/shard_map/ppermute | solution.py:119

commit v3 on v2

--- a/solution.py
+++ b/solution.py
@@ -40,6 +40,16 @@
     return s
 
 
+def direct_reduce_scatter(x, axis, n):
+    i = lax.axis_index(axis)
+    s = lax.dynamic_index_in_dim(x, i, 0, keepdims=False)
+    for shift in range(1, n):
+        send = lax.dynamic_index_in_dim(x, (i + shift) % n, 0, keepdims=False)
+        got = lax.ppermute(send.astype(jnp.bfloat16), axis, [(j, (j + shift) % n) for j in range(n)])
+        s = s + got.astype(jnp.float32)
+    return s
+
+
 def dft_table(mode_values, time_index, sidereal_period, norm_factor):
     cosine, sine = phases(mode_values, time_index, sidereal_period)
     cosine = cosine * jnp.float32(norm_factor)
@@ -66,10 +76,10 @@
         y = out[half_rows:] + got.astype(jnp.float32)
         if z_major:
             y = y.reshape(nz, ny, *y.shape[1:])
-            y = ring_reduce_scatter(ring_reduce_scatter(y, "tz", nz), "ty", ny)
+            y = direct_reduce_scatter(ring_reduce_scatter(y, "tz", nz), "ty", ny)
         else:
             y = y.reshape(ny, nz, *y.shape[1:])
-            y = ring_reduce_scatter(ring_reduce_scatter(y, "ty", ny), "tz", nz)
+            y = ring_reduce_scatter(direct_reduce_scatter(y, "ty", ny), "tz", nz)
         halves.append(y)
     return jnp.concatenate(halves, axis=1)
 

time: 112 us -> 114 us (1.018)
  starting transfers between devices: 24.1 us -> 32.8 us
  waiting for transfers between devices: 45.4 us -> 41.3 us
  other arithmetic: 15.6 us -> 13.1 us
    ppermute x20 -> x14, waiting for transfers between devices: 42 us -> 26.1 us  [ring_reduce_scatter(): got = lax.ppermute(s.astype(jnp.bfloat16), axis, fwd)]
    ppermute x0 -> x6, starting transfers between devices: none -> 12.1 us  [direct_reduce_scatter(): lax.ppermute(send.astype(jnp.bfloat16), axis, [(j, (j + shift) % n) for j...]
    ppermute x0 -> x6, waiting for transfers between devices: none -> 11.7 us  [direct_reduce_scatter(): lax.ppermute(send.astype(jnp.bfloat16), axis, [(j, (j + shift) % n) for j...]
    ppermute x20 -> x14, starting transfers between devices: 20.1 us -> 16.7 us  [ring_reduce_scatter(): got = lax.ppermute(s.astype(jnp.bfloat16), axis, fwd)]
    convert_element_type x16 -> x12, other arithmetic: 3.58 us -> 1.04 us  [ring_reduce_scatter(): got = lax.ppermute(s.astype(jnp.bfloat16), axis, fwd)]
  transfers between devices with their start and end apart: 25 -> 25, of which waited for: 17 -> 19; matrix products, arithmetic and copies ran while one was open for 20% -> 18% of each run, Pallas kernels for 0% -> 0%
where the time goes in v3:
time: 114 us; the launch traced here: 113 us
  waiting for transfers between devices  41.3 us (36%)
  starting transfers between devices  32.8 us (29%)
  matrix products  14.7 us (13%)
  other arithmetic  13.1 us (11%)
  local copies, waits for them, and re-layouts  9.58 us (8%)
  between operations  1.16 us (1%)
    ppermute x14, waiting for transfers between devices, ring_reduce_scatter(): got = lax.ppermute(s.astype(jnp.bfloat16), axis, fwd)  26.1 us
    ppermute x14, starting transfers between devices, ring_reduce_scatter(): got = lax.ppermute(s.astype(jnp.bfloat16), axis, fwd)  16.7 us
    ppermute x6, starting transfers between devices, direct_reduce_scatter(): lax.ppermute(send.astype(jnp.bfloat16), axis, [(j, (j + shift) % n) for j...  12.1 us
    ppermute x6, waiting for transfers between devices, direct_reduce_scatter(): lax.ppermute(send.astype(jnp.bfloat16), axis, [(j, (j + shift) % n) for j...  11.7 us
    dot_general x2, matrix products, spectra_of(): jnp.einsum('rdct,fctb->rdfb', table, part, precision=lax.Precision.HIGH)  6.53 us
    dot_general x1, matrix products, local(): jnp.einsum('mflpi,lpij->mflj', combined, code_matrix, precision=lax.Preci...  5.59 us
    neg x1, other arithmetic, realify(): upper = jnp.concatenate([real_part, -imag_part], axis=-1)  3.54 us
    ppermute x3, starting transfers between devices, local(): lax.ppermute(weights_bf, 'freq', [(j, (j + s) % fr_count) for j in range(...  3.51 us
  transfers between devices with their start and end apart: 25, of which 19 were waited for; matrix products, arithmetic and copies ran while one was open for 18% of the time, Pallas kernels for 0%

profile of v3, /device:TPU:6, one launch (start us, length us, event | category | flops | bytes accessed | tf_op | source)
XLA Modules:
  0.0 112.6 jit_solution(12094254444955722220)
XLA Ops:
  0.5 0.4 sine_multiply_fusion.1
  0.9 4.4 %fusion.14 = f32[64,2,8,1024]{3,0,2,1:T(8,128)S(1)} fusion(f32[16,2,64,1024]{3,2,1,0:T(8,128)} %param.6, f32[64,1,2,64]{3,0,2,1:T(8,128)S(1)} %get-tuple-element.22, f32[64,1,2,64]{3,0,2,1:T(8,128)S(1)} %get-tuple-element.21), kind=kOutput, calls=%fused_computation.14 | convolution fusion | flops 805322752 | bytes 8454144 | tf_op jit(solution)/shard_map/rdct,fctb->rdfb/dot_general | solution.py:73
  5.3 1.3 %slice.58 = bf16[32,2,8,1024]{3,0,2,1:T(8,128)(2,1)} slice(f32[64,2,8,1024]{3,0,2,1:T(8,128)S(1)} %fusion.14), slice={[0:32], [0:2], [0:8], [0:1024]} | slice | bytes 2097152 | tf_op jit(solution)/shard_map/slice | solution.py:75
  6.6 2.2 %fusion.17 = f32[64,2,8,1024]{3,0,2,1:T(8,128)S(1)} fusion(f32[16,2,64,1024]{3,2,1,0:T(8,128)S(1)} %copy-done.4, f32[64,1,2,64]{3,0,2,1:T(8,128)S(1)} %get-tuple-element.24, f32[64,1,2,64]{3,0,2,1:T(8,128)S(1)} %get-tuple-element.23), kind=kOutput, calls=%fused_computation.15 | convolution fusion | flops 805322752 | bytes 8519680 | tf_op jit(solution)/shard_map/rdct,fctb->rdfb/dot_general | solution.py:73
  8.8 1.1 %slice.57 = bf16[32,2,8,1024]{3,0,2,1:T(8,128)(2,1)} slice(f32[64,2,8,1024]{3,0,2,1:T(8,128)S(1)} %fusion.17), slice={[0:32], [0:2], [0:8], [0:1024]} | slice | bytes 2097152 | tf_op jit(solution)/shard_map/slice | solution.py:75
  9.9 1.1 copy-done.3
  11.0 0.5 collective-permute-start.11
  12.3 2.7 %fusion.23 = f32[16,16,16,8]{3,2,1,0:T(8,128)} fusion(f32[16,16,16]{2,1,0:T(8,128)S(1)} %bitcast.190, s32[16,16,16]{2,1,0:T(8,128)S(1)} %bitcast.191), kind=kLoop, calls=%fused_computation.24 | loop fusion | flops 65536 | bytes 163840 | tf_op jit(solution)/shard_map/jit(_where)/select_n | solution.py:111
  15.0 0.2 constant_dynamic-slice_fusion
  15.2 3.5 %slice_negate_fusion = (bf16[16,8,64,64]{3,2,1,0:T(8,128)(2,1)}, bf16[16,8,64,64]{3,2,1,0:T(8,128)(2,1)}, bf16[16,8,64,64]{3,2,1,0:T(8,128)(2,1)}) fusion(bf16[16,8,64,128]{3,2,1,0:T(8,128)(2,1)S(1)} %copy-done.5), kind=kLoop, calls=%fused_computation.163 | loop fusion | flops 524288 | bytes 5242880 | tf_op jit(solution)/shard_map/neg | solution.py:18
  18.8 1.6 %slice_add_fusion.1 = f32[32,2,8,1024]{3,0,2,1:T(8,128)S(1)} fusion(f32[64,2,8,1024]{3,0,2,1:T(8,128)S(1)} %copy-done.2, bf16[32,2,8,1024]{3,0,2,1:T(8,128)(2,1)} %collective-permute-done), kind=kLoop, calls=%fused_computation.20 | loop fusion | flops 1048576 | bytes 5242880 | tf_op jit(solution)/shard_map/add | solution.py:76
  20.4 1.7 %reshape.502 = f32[8,4,2,8,1024]{4,1,0,3,2:T(4,128)} reshape(f32[32,2,8,1024]{3,0,2,1:T(8,128)S(1)} %slice_add_fusion.1) | data formatting | bytes 4194304 | tf_op jit(solution)/shard_map/reshape | solution.py:78
  22.1 1.0 constant_dynamic-slice_fusion.12
  23.1 2.0 %collective-permute-start.1 = (bf16[4,2,8,1024]{3,2,1,0:T(8,128)(2,1)S(1)}, bf16[4,2,8,1024]{3,2,1,0:T(8,128)(2,1)S(1)}, u32[]{:S(2)}, u32[]{:S(2)}) collective-permute-start(bf16[4,2,8,1024]{3,2,1,0:T(8,128)(2,1)S(1)} %bitcast.192), channel_id=1, source_target_pairs={{0,8},{8,16},{16,24},{24,32},{32,40},{40,48},{48,56},{56,0},{1,9},... | collective-permute-start | bytes 393224 | tf_op jit(solution)/shard_map/ppermute | solution.py:38
  25.1 2.2 %fusion.20 = f32[4,8,2,8,1024]{4,1,0,3,2:T(8,128)S(1)} fusion(f32[64,2,8,1024]{3,0,2,1:T(8,128)} %copy-done.3, bf16[32,2,8,1024]{3,0,2,1:T(8,128)(2,1)} %collective-permute-done.11), kind=kLoop, calls=%fused_computation.18 | loop fusion | flops 1048576 | bytes 5242880 | tf_op jit(solution)/shard_map/reshape | solution.py:81
  27.6 1.7 %collective-permute-start.12 = (bf16[8,2,8,1024]{3,2,1,0:T(8,128)(2,1)S(1)}, bf16[8,2,8,1024]{3,2,1,0:T(8,128)(2,1)S(1)}, u32[]{:S(2)}, u32[]{:S(2)}) collective-permute-start(bf16[8,2,8,1024]{3,2,1,0:T(8,128)(2,1)S(1)} %bitcast.187), channel_id=1, source_target_pairs={{0,64},{64,128},{128,192},{192,0},{1,65},{65,129},{129,193},{193,1... | collective-permute-start | bytes 786440 | tf_op jit(solution)/shard_map/ppermute | solution.py:48
  29.4 3.0 %collective-permute-start.13 = (bf16[8,2,8,1024]{3,2,1,0:T(8,128)(2,1)S(1)}, bf16[8,2,8,1024]{3,2,1,0:T(8,128)(2,1)S(1)}, u32[]{:S(2)}, u32[]{:S(2)}) collective-permute-start(bf16[8,2,8,1024]{3,2,1,0:T(8,128)(2,1)S(1)} %bitcast.188), channel_id=1, source_target_pairs={{0,128},{64,192},{128,0},{192,64},{1,129},{65,193},{129,1},{193,65... | collective-permute-start | bytes 786440 | tf_op jit(solution)/shard_map/ppermute | solution.py:48
  32.5 1.6 %collective-permute-start.14 = (bf16[8,2,8,1024]{3,2,1,0:T(8,128)(2,1)S(1)}, bf16[8,2,8,1024]{3,2,1,0:T(8,128)(2,1)S(1)}, u32[]{:S(2)}, u32[]{:S(2)}) collective-permute-start(bf16[8,2,8,1024]{3,2,1,0:T(8,128)(2,1)S(1)} %bitcast.189), channel_id=1, source_target_pairs={{0,192},{64,0},{128,64},{192,128},{1,193},{65,1},{129,65},{193,129... | collective-permute-start | bytes 786440 | tf_op jit(solution)/shard_map/ppermute | solution.py:48
  34.4 2.5 %collective-permute-done.12 = bf16[8,2,8,1024]{3,2,1,0:T(8,128)(2,1)S(1)} collective-permute-done((bf16[8,2,8,1024]{3,2,1,0:T(8,128)(2,1)S(1)}, bf16[8,2,8,1024]{3,2,1,0:T(8,128)(2,1)S(1)}, u32[]{:S(2)}, u32[]{:S(2)}) %collective-permute-start.12) | collective-permute-done | bytes 262176 | tf_op jit(solution)/shard_map/ppermute | solution.py:48
  36.9 6.8 %collective-permute-done.13 = bf16[8,2,8,1024]{3,2,1,0:T(8,128)(2,1)S(1)} collective-permute-done((bf16[8,2,8,1024]{3,2,1,0:T(8,128)(2,1)S(1)}, bf16[8,2,8,1024]{3,2,1,0:T(8,128)(2,1)S(1)}, u32[]{:S(2)}, u32[]{:S(2)}) %collective-permute-start.13) | collective-permute-done | bytes 262176 | tf_op jit(solution)/shard_map/ppermute | solution.py:48
  43.7 0.4 fusion.36
  44.1 2.0 %collective-permute-start.15 = (bf16[2,8,1024]{2,1,0:T(8,128)(2,1)S(1)}, bf16[2,8,1024]{2,1,0:T(8,128)(2,1)S(1)}, u32[]{:S(2)}, u32[]{:S(2)}) collective-permute-start(bf16[2,8,1024]{2,1,0:T(8,128)(2,1)S(1)} %fusion.85), channel_id=1, source_target_pairs={{0,8},{8,16},{16,24},{24,32},{32,40},{40,48},{48,56},{56,0},{1,9},... | collective-permute-start | bytes 98312 | tf_op jit(solution)/shard_map/ppermute | solution.py:38
  46.2 2.0 %collective-permute-start.2 = (bf16[4,2,8,1024]{3,2,1,0:T(8,128)(2,1)S(1)}, bf16[4,2,8,1024]{3,2,1,0:T(8,128)(2,1)S(1)}, u32[]{:S(2)}, u32[]{:S(2)}) collective-permute-start(bf16[4,2,8,1024]{3,2,1,0:T(8,128)(2,1)S(1)} %fusion.45), channel_id=1, source_target_pairs={{0,8},{8,16},{16,24},{24,32},{32,40},{40,48},{48,56},{56,0},{1,9},... | collective-permute-start | bytes 393224 | tf_op jit(solution)/shard_map/ppermute | solution.py:38
  48.2 2.3 %collective-permute-done.15 = bf16[2,8,1024]{2,1,0:T(8,128)(2,1)S(1)} collective-permute-done((bf16[2,8,1024]{2,1,0:T(8,128)(2,1)S(1)}, bf16[2,8,1024]{2,1,0:T(8,128)(2,1)S(1)}, u32[]{:S(2)}, u32[]{:S(2)}) %collective-permute-start.15) | collective-permute-done | bytes 32800 | tf_op jit(solution)/shard_map/ppermute | solution.py:38
  50.5 0.9 collective-permute-start.16
  51.5 1.0 collective-permute-done.2
  52.7 1.5 %collective-permute-start.3 = (bf16[4,2,8,1024]{3,2,1,0:T(8,128)(2,1)S(1)}, bf16[4,2,8,1024]{3,2,1,0:T(8,128)(2,1)S(1)}, u32[]{:S(2)}, u32[]{:S(2)}) collective-permute-start(bf16[4,2,8,1024]{3,2,1,0:T(8,128)(2,1)S(1)} %fusion.44), channel_id=1, source_target_pairs={{0,8},{8,16},{16,24},{24,32},{32,40},{40,48},{48,56},{56,0},{1,9},... | collective-permute-start | bytes 393224 | tf_op jit(solution)/shard_map/ppermute | solution.py:38
  54.1 2.0 %collective-permute-done.16 = bf16[2,8,1024]{2,1,0:T(8,128)(2,1)S(1)} collective-permute-done((bf16[2,8,1024]{2,1,0:T(8,128)(2,1)S(1)}, bf16[2,8,1024]{2,1,0:T(8,128)(2,1)S(1)}, u32[]{:S(2)}, u32[]{:S(2)}) %collective-permute-start.16) | collective-permute-done | bytes 32800 | tf_op jit(solution)/shard_map/ppermute | solution.py:38
  56.1 0.6 collective-permute-start.17
  56.7 2.2 %collective-permute-done.3 = bf16[4,2,8,1024]{3,2,1,0:T(8,128)(2,1)S(1)} collective-permute-done((bf16[4,2,8,1024]{3,2,1,0:T(8,128)(2,1)S(1)}, bf16[4,2,8,1024]{3,2,1,0:T(8,128)(2,1)S(1)}, u32[]{:S(2)}, u32[]{:S(2)}) %collective-permute-start.3) | collective-permute-done | bytes 131104 | tf_op jit(solution)/shard_map/ppermute | solution.py:38
  59.1 0.8 collective-permute-start.4
  59.9 1.7 %collective-permute-done.17 = bf16[2,8,1024]{2,1,0:T(8,128)(2,1)S(1)} collective-permute-done((bf16[2,8,1024]{2,1,0:T(8,128)(2,1)S(1)}, bf16[2,8,1024]{2,1,0:T(8,128)(2,1)S(1)}, u32[]{:S(2)}, u32[]{:S(2)}) %collective-permute-start.17) | collective-permute-done | bytes 32800 | tf_op jit(solution)/shard_map/ppermute | solution.py:38
  61.7 0.8 collective-permute-start.18
  62.5 2.9 %collective-permute-done.4 = bf16[4,2,8,1024]{3,2,1,0:T(8,128)(2,1)S(1)} collective-permute-done((bf16[4,2,8,1024]{3,2,1,0:T(8,128)(2,1)S(1)}, bf16[4,2,8,1024]{3,2,1,0:T(8,128)(2,1)S(1)}, u32[]{:S(2)}, u32[]{:S(2)}) %collective-permute-start.4) | collective-permute-done | bytes 131104 | tf_op jit(solution)/shard_map/ppermute | solution.py:38
  65.5 1.0 collective-permute-start.5
  66.5 0.7 collective-permute-done.18
  67.2 1.9 %collective-permute-start.19 = (bf16[2,8,1024]{2,1,0:T(8,128)(2,1)S(1)}, bf16[2,8,1024]{2,1,0:T(8,128)(2,1)S(1)}, u32[]{:S(2)}, u32[]{:S(2)}) collective-permute-start(bf16[2,8,1024]{2,1,0:T(8,128)(2,1)S(1)} %fusion.69), channel_id=1, source_target_pairs={{0,8},{8,16},{16,24},{24,32},{32,40},{40,48},{48,56},{56,0},{1,9},... | collective-permute-start | bytes 98312 | tf_op jit(solution)/shard_map/ppermute | solution.py:38
  69.1 2.9 %collective-permute-done.5 = bf16[4,2,8,1024]{3,2,1,0:T(8,128)(2,1)S(1)} collective-permute-done((bf16[4,2,8,1024]{3,2,1,0:T(8,128)(2,1)S(1)}, bf16[4,2,8,1024]{3,2,1,0:T(8,128)(2,1)S(1)}, u32[]{:S(2)}, u32[]{:S(2)}) %collective-permute-start.5) | collective-permute-done | bytes 131104 | tf_op jit(solution)/shard_map/ppermute | solution.py:38
  72.2 0.4 collective-permute-start.6
  72.8 2.4 %collective-permute-start.20 = (bf16[2,8,1024]{2,1,0:T(8,128)(2,1)S(1)}, bf16[2,8,1024]{2,1,0:T(8,128)(2,1)S(1)}, u32[]{:S(2)}, u32[]{:S(2)}) collective-permute-start(bf16[2,8,1024]{2,1,0:T(8,128)(2,1)S(1)} %fusion.68), channel_id=1, source_target_pairs={{0,8},{8,16},{16,24},{24,32},{32,40},{40,48},{48,56},{56,0},{1,9},... | collective-permute-start | bytes 98312 | tf_op jit(solution)/shard_map/ppermute | solution.py:38
  75.2 4.3 %collective-permute-done.6 = bf16[4,2,8,1024]{3,2,1,0:T(8,128)(2,1)S(1)} collective-permute-done((bf16[4,2,8,1024]{3,2,1,0:T(8,128)(2,1)S(1)}, bf16[4,2,8,1024]{3,2,1,0:T(8,128)(2,1)S(1)}, u32[]{:S(2)}, u32[]{:S(2)}) %collective-permute-start.6) | collective-permute-done | bytes 131104 | tf_op jit(solution)/shard_map/ppermute | solution.py:38
  79.8 0.4 collective-permute-done.20
  80.2 0.3 collective-permute-start.21
  80.5 5.4 %collective-permute-done.7 = bf16[4,2,8,1024]{3,2,1,0:T(8,128)(2,1)S(1)} collective-permute-done((bf16[4,2,8,1024]{3,2,1,0:T(8,128)(2,1)S(1)}, bf16[4,2,8,1024]{3,2,1,0:T(8,128)(2,1)S(1)}, u32[]{:S(2)}, u32[]{:S(2)}) %collective-permute-start.7) | collective-permute-done | bytes 131104 | tf_op jit(solution)/shard_map/ppermute | solution.py:38
  86.1 0.6 fusion.82
  86.8 2.7 %collective-permute-start.10 = (bf16[2,8,1024]{2,1,0:T(8,128)(2,1)}, bf16[2,8,1024]{2,1,0:T(8,128)(2,1)}, u32[]{:S(2)}, u32[]{:S(2)}) collective-permute-start(bf16[2,8,1024]{2,1,0:T(8,128)(2,1)} %get-tuple-element.19), channel_id=1, source_target_pairs={{0,192},{64,0},{128,64},{192,128},{1,193},{65,1},{129,65},{193,129... | collective-permute-start | bytes 98312 | tf_op jit(solution)/shard_map/ppermute | solution.py:48
  89.4 3.2 %collective-permute-start.9 = (bf16[2,8,1024]{2,1,0:T(8,128)(2,1)}, bf16[2,8,1024]{2,1,0:T(8,128)(2,1)}, u32[]{:S(2)}, u32[]{:S(2)}) collective-permute-start(bf16[2,8,1024]{2,1,0:T(8,128)(2,1)} %get-tuple-element.20), channel_id=1, source_target_pairs={{0,128},{64,192},{128,0},{192,64},{1,129},{65,193},{129,1},{193,65... | collective-permute-start | bytes 98312 | tf_op jit(solution)/shard_map/ppermute | solution.py:48
  92.8 2.1 %collective-permute-done.8 = bf16[2,8,1024]{2,1,0:T(8,128)(2,1)} collective-permute-done((bf16[2,8,1024]{2,1,0:T(8,128)(2,1)}, bf16[2,8,1024]{2,1,0:T(8,128)(2,1)}, u32[]{:S(2)}, u32[]{:S(2)}) %collective-permute-start.8) | collective-permute-done | bytes 32800 | tf_op jit(solution)/shard_map/ppermute | solution.py:48
  94.9 0.3 collective-permute-done.9
  95.2 0.8 fusion.75
  96.2 0.2 maximum_bitcast_fusion.4
  96.6 1.5 %fusion.21 = f32[16,16,8,128]{3,2,1,0:T(8,128)S(1)} fusion(f32[16,16,16,8]{3,2,1,0:T(8,128)S(1)} %copy-done.6, bf16[16,16,128,1]{2,1,0,3:T(8,128)(2,1)S(1)} %reshape.516), kind=kOutput, calls=%fused_computation.21 | convolution fusion | flops 25165824 | bytes 1245184 | tf_op jit(solution)/shard_map/mfblp,mfbi->mflpi/dot_general | solution.py:116
  98.2 5.6 %fusion.29 = bf16[16,128,16]{1,2,0:T(8,128)(2,1)S(1)} fusion(bf16[16,8,64,64]{3,2,1,0:T(8,128)(2,1)} %get-tuple-element.17, bf16[16,8,64,64]{3,2,1,0:T(8,128)(2,1)} %get-tuple-element.16, bf16[16,8,64,64]{3,2,1,0:T(8,128)(2,1)S(1)} %copy-done.8, f32[16,16,8,128]{3,2,1,0:T(8,128)S(1)} %fusion.21), kind=kOutput, calls=%fused_computation.30 | convolution fusion | flops 218136576 | bytes 4259840 | tf_op jit(solution)/shard_map/mflpi,lpij->mflj/dot_general | solution.py:119
  103.8 0.6 collective-permute-start.22
  104.3 1.5 %collective-permute-start.24 = (bf16[1,16,16,128]{3,1,2,0:T(8,128)(2,1)S(1)}, bf16[1,16,16,128]{3,1,2,0:T(8,128)(2,1)S(1)}, u32[]{:S(2)}, u32[]{:S(2)}) collective-permute-start(bf16[1,16,16,128]{3,1,2,0:T(8,128)(2,1)S(1)} %bitcast.194), channel_id=1, source_target_pairs={{0,3},{1,0},{2,1},{3,2},{4,7},{5,4},{6,5},{7,6},{8,11},{9,8},{10,9... | collective-permute-start | bytes 196616 | tf_op jit(solution)/shard_map/ppermute | solution.py:129
  105.9 1.4 %collective-permute-start.23 = (bf16[1,16,16,128]{3,1,2,0:T(8,128)(2,1)S(1)}, bf16[1,16,16,128]{3,1,2,0:T(8,128)(2,1)S(1)}, u32[]{:S(2)}, u32[]{:S(2)}) collective-permute-start(bf16[1,16,16,128]{3,1,2,0:T(8,128)(2,1)S(1)} %bitcast.195), channel_id=1, source_target_pairs={{0,2},{1,3},{2,0},{3,1},{4,6},{5,7},{6,4},{7,5},{8,10},{9,11},{10,... | collective-permute-start | bytes 196616 | tf_op jit(solution)/shard_map/ppermute | solution.py:129
  107.3 0.3 fusion.55
  107.6 0.5 collective-permute-done.22
  108.1 0.3 convolution_add_fusion.1
  108.4 1.4 %collective-permute-done.24 = bf16[1,16,16,128]{3,1,2,0:T(8,128)(2,1)S(1)} collective-permute-done((bf16[1,16,16,128]{3,1,2,0:T(8,128)(2,1)S(1)}, bf16[1,16,16,128]{3,1,2,0:T(8,128)(2,1)S(1)}, u32[]{:S(2)}, u32[]{:S(2)}) %collective-permute-start.24) | collective-permute-done | bytes 65568 | tf_op jit(solution)/shard_map/ppermute | solution.py:129
  109.8 0.3 fusion.51
  110.1 1.6 %collective-permute-done.23 = bf16[1,16,16,128]{3,1,2,0:T(8,128)(2,1)S(1)} collective-permute-done((bf16[1,16,16,128]{3,1,2,0:T(8,128)(2,1)S(1)}, bf16[1,16,16,128]{3,1,2,0:T(8,128)(2,1)S(1)}, u32[]{:S(2)}, u32[]{:S(2)}) %collective-permute-start.23) | collective-permute-done | bytes 65568 | tf_op jit(solution)/shard_map/ppermute | solution.py:129
  111.6 0.3 fusion.33
  111.9 0.7 copy.27
  (70 shorter events, 3.5 us)
Async XLA Ops:
  0.0 15.0 %copy-start = (f32[16,64,64]{2,1,0:T(8,128)S(1)}, f32[16,64,64]{2,1,0:T(8,128)}, u32[]{:S(2)}) copy-start(f32[16,64,64]{2,1,0:T(8,128)} %param.10) | copy-start | bytes 786436
  0.9 5.7 %copy-start.4 = (f32[16,2,64,1024]{3,2,1,0:T(8,128)S(1)}, f32[16,2,64,1024]{3,2,1,0:T(8,128)}, u32[]{:S(2)}) copy-start(f32[16,2,64,1024]{3,2,1,0:T(8,128)} %param.6) | copy-start | bytes 25165828
  5.3 3.5 %copy-start.1 = (f32[64,2,8,1024]{3,0,2,1:T(8,128)}, f32[64,2,8,1024]{3,0,2,1:T(8,128)S(1)}, u32[]{:S(2)}) copy-start(f32[64,2,8,1024]{3,0,2,1:T(8,128)S(1)} %fusion.14) | copy-start | bytes 12582916
  6.5 12.2 %collective-permute-start = (bf16[32,2,8,1024]{3,0,2,1:T(8,128)(2,1)}, bf16[32,2,8,1024]{3,0,2,1:T(8,128)(2,1)}, u32[]{:S(2)}, u32[]{:S(2)}) collective-permute-start(bf16[32,2,8,1024]{3,0,2,1:T(8,128)(2,1)} %slice.58), channel_id=1, source_target_pairs={{0,4},{4,0},{1,5},{5,1},{2,6},{6,2},{3,7},{7,3},{8,12},{12,8},{9,1... | collective-permute-start | bytes 3145736 | tf_op jit(solution)/shard_map/ppermute | solution.py:75
  8.8 2.3 %copy-start.3 = (f32[64,2,8,1024]{3,0,2,1:T(8,128)}, f32[64,2,8,1024]{3,0,2,1:T(8,128)S(1)}, u32[]{:S(2)}) copy-start(f32[64,2,8,1024]{3,0,2,1:T(8,128)S(1)} %fusion.17) | copy-start | bytes 12582916
  8.8 3.6 %copy-start.9 = (f32[1,16,16,16]{3,2,1,0:T(8,128)S(1)}, f32[1,16,16,16]{3,2,1,0:T(8,128)}, u32[]{:S(2)}) copy-start(f32[1,16,16,16]{3,2,1,0:T(8,128)} %param.9) | copy-start | bytes 49156
  8.8 3.6 %copy-start.10 = (s32[1,16,16,16]{3,2,1,0:T(8,128)S(1)}, s32[1,16,16,16]{3,2,1,0:T(8,128)}, u32[]{:S(2)}) copy-start(s32[1,16,16,16]{3,2,1,0:T(8,128)} %param.8) | copy-start | bytes 49156
  11.0 4.2 %copy-start.5 = (bf16[16,8,64,128]{3,2,1,0:T(8,128)(2,1)S(1)}, bf16[16,8,64,128]{3,2,1,0:T(8,128)(2,1)}, u32[]{:S(2)}) copy-start(bf16[16,8,64,128]{3,2,1,0:T(8,128)(2,1)} %param.7) | copy-start | bytes 6291460
  11.0 14.1 %collective-permute-start.11 = (bf16[32,2,8,1024]{3,0,2,1:T(8,128)(2,1)}, bf16[32,2,8,1024]{3,0,2,1:T(8,128)(2,1)}, u32[]{:S(2)}, u32[]{:S(2)}) collective-permute-start(bf16[32,2,8,1024]{3,0,2,1:T(8,128)(2,1)} %slice.57), channel_id=1, source_target_pairs={{0,4},{4,0},{1,5},{5,1},{2,6},{6,2},{3,7},{7,3},{8,12},{12,8},{9,1... | collective-permute-start | bytes 3145736 | tf_op jit(solution)/shard_map/ppermute | solution.py:75
  15.2 3.6 %copy-start.2 = (f32[64,2,8,1024]{3,0,2,1:T(8,128)S(1)}, f32[64,2,8,1024]{3,0,2,1:T(8,128)}, u32[]{:S(2)}) copy-start(f32[64,2,8,1024]{3,0,2,1:T(8,128)} %copy-done.1) | copy-start | bytes 12582916
  23.1 22.9 %collective-permute-start.1 = (bf16[4,2,8,1024]{3,2,1,0:T(8,128)(2,1)S(1)}, bf16[4,2,8,1024]{3,2,1,0:T(8,128)(2,1)S(1)}, u32[]{:S(2)}, u32[]{:S(2)}) collective-permute-start(bf16[4,2,8,1024]{3,2,1,0:T(8,128)(2,1)S(1)} %bitcast.192), channel_id=1, source_target_pairs={{0,8},{8,16},{16,24},{24,32},{32,40},{40,48},{48,56},{56,0},{1,9},... | collective-permute-start | bytes 393224 | tf_op jit(solution)/shard_map/ppermute | solution.py:38
  27.3 6.9 %copy-start.7 = (f32[8,4,2,8,1024]{4,1,0,3,2:T(4,128)S(1)}, f32[8,4,2,8,1024]{4,1,0,3,2:T(4,128)}, u32[]{:S(2)}) copy-start(f32[8,4,2,8,1024]{4,1,0,3,2:T(4,128)} %reshape.502) | copy-start | bytes 6291460
  27.6 9.4 %collective-permute-start.12 = (bf16[8,2,8,1024]{3,2,1,0:T(8,128)(2,1)S(1)}, bf16[8,2,8,1024]{3,2,1,0:T(8,128)(2,1)S(1)}, u32[]{:S(2)}, u32[]{:S(2)}) collective-permute-start(bf16[8,2,8,1024]{3,2,1,0:T(8,128)(2,1)S(1)} %bitcast.187), channel_id=1, source_target_pairs={{0,64},{64,128},{128,192},{192,0},{1,65},{65,129},{129,193},{193,1... | collective-permute-start | bytes 786440 | tf_op jit(solution)/shard_map/ppermute | solution.py:48
  29.4 14.3 %collective-permute-start.13 = (bf16[8,2,8,1024]{3,2,1,0:T(8,128)(2,1)S(1)}, bf16[8,2,8,1024]{3,2,1,0:T(8,128)(2,1)S(1)}, u32[]{:S(2)}, u32[]{:S(2)}) collective-permute-start(bf16[8,2,8,1024]{3,2,1,0:T(8,128)(2,1)S(1)} %bitcast.188), channel_id=1, source_target_pairs={{0,128},{64,192},{128,0},{192,64},{1,129},{65,193},{129,1},{193,65... | collective-permute-start | bytes 786440 | tf_op jit(solution)/shard_map/ppermute | solution.py:48
  32.5 11.2 %collective-permute-start.14 = (bf16[8,2,8,1024]{3,2,1,0:T(8,128)(2,1)S(1)}, bf16[8,2,8,1024]{3,2,1,0:T(8,128)(2,1)S(1)}, u32[]{:S(2)}, u32[]{:S(2)}) collective-permute-start(bf16[8,2,8,1024]{3,2,1,0:T(8,128)(2,1)S(1)} %bitcast.189), channel_id=1, source_target_pairs={{0,192},{64,0},{128,64},{192,128},{1,193},{65,1},{129,65},{193,129... | collective-permute-start | bytes 786440 | tf_op jit(solution)/shard_map/ppermute | solution.py:48
  44.1 6.4 %collective-permute-start.15 = (bf16[2,8,1024]{2,1,0:T(8,128)(2,1)S(1)}, bf16[2,8,1024]{2,1,0:T(8,128)(2,1)S(1)}, u32[]{:S(2)}, u32[]{:S(2)}) collective-permute-start(bf16[2,8,1024]{2,1,0:T(8,128)(2,1)S(1)} %fusion.85), channel_id=1, source_target_pairs={{0,8},{8,16},{16,24},{24,32},{32,40},{40,48},{48,56},{56,0},{1,9},... | collective-permute-start | bytes 98312 | tf_op jit(solution)/shard_map/ppermute | solution.py:38
  46.2 6.3 %collective-permute-start.2 = (bf16[4,2,8,1024]{3,2,1,0:T(8,128)(2,1)S(1)}, bf16[4,2,8,1024]{3,2,1,0:T(8,128)(2,1)S(1)}, u32[]{:S(2)}, u32[]{:S(2)}) collective-permute-start(bf16[4,2,8,1024]{3,2,1,0:T(8,128)(2,1)S(1)} %fusion.45), channel_id=1, source_target_pairs={{0,8},{8,16},{16,24},{24,32},{32,40},{40,48},{48,56},{56,0},{1,9},... | collective-permute-start | bytes 393224 | tf_op jit(solution)/shard_map/ppermute | solution.py:38
  50.5 5.5 %collective-permute-start.16 = (bf16[2,8,1024]{2,1,0:T(8,128)(2,1)S(1)}, bf16[2,8,1024]{2,1,0:T(8,128)(2,1)S(1)}, u32[]{:S(2)}, u32[]{:S(2)}) collective-permute-start(bf16[2,8,1024]{2,1,0:T(8,128)(2,1)S(1)} %fusion.72), channel_id=1, source_target_pairs={{0,8},{8,16},{16,24},{24,32},{32,40},{40,48},{48,56},{56,0},{1,9},... | collective-permute-start | bytes 98312 | tf_op jit(solution)/shard_map/ppermute | solution.py:38
  52.7 6.3 %collective-permute-start.3 = (bf16[4,2,8,1024]{3,2,1,0:T(8,128)(2,1)S(1)}, bf16[4,2,8,1024]{3,2,1,0:T(8,128)(2,1)S(1)}, u32[]{:S(2)}, u32[]{:S(2)}) collective-permute-start(bf16[4,2,8,1024]{3,2,1,0:T(8,128)(2,1)S(1)} %fusion.44), channel_id=1, source_target_pairs={{0,8},{8,16},{16,24},{24,32},{32,40},{40,48},{48,56},{56,0},{1,9},... | collective-permute-start | bytes 393224 | tf_op jit(solution)/shard_map/ppermute | solution.py:38
  56.1 5.6 %collective-permute-start.17 = (bf16[2,8,1024]{2,1,0:T(8,128)(2,1)S(1)}, bf16[2,8,1024]{2,1,0:T(8,128)(2,1)S(1)}, u32[]{:S(2)}, u32[]{:S(2)}) collective-permute-start(bf16[2,8,1024]{2,1,0:T(8,128)(2,1)S(1)} %fusion.71), channel_id=1, source_target_pairs={{0,8},{8,16},{16,24},{24,32},{32,40},{40,48},{48,56},{56,0},{1,9},... | collective-permute-start | bytes 98312 | tf_op jit(solution)/shard_map/ppermute | solution.py:38
  59.1 37.5 %copy-start.6 = (f32[16,16,16,8]{3,2,1,0:T(8,128)S(1)}, f32[16,16,16,8]{3,2,1,0:T(8,128)}, u32[]{:S(2)}) copy-start(f32[16,16,16,8]{3,2,1,0:T(8,128)} %fusion.23) | copy-start | bytes 393220
  59.1 6.3 %collective-permute-start.4 = (bf16[4,2,8,1024]{3,2,1,0:T(8,128)(2,1)S(1)}, bf16[4,2,8,1024]{3,2,1,0:T(8,128)(2,1)S(1)}, u32[]{:S(2)}, u32[]{:S(2)}) collective-permute-start(bf16[4,2,8,1024]{3,2,1,0:T(8,128)(2,1)S(1)} %fusion.43), channel_id=1, source_target_pairs={{0,8},{8,16},{16,24},{24,32},{32,40},{40,48},{48,56},{56,0},{1,9},... | collective-permute-start | bytes 393224 | tf_op jit(solution)/shard_map/ppermute | solution.py:38
  61.7 5.6 %collective-permute-start.18 = (bf16[2,8,1024]{2,1,0:T(8,128)(2,1)S(1)}, bf16[2,8,1024]{2,1,0:T(8,128)(2,1)S(1)}, u32[]{:S(2)}, u32[]{:S(2)}) collective-permute-start(bf16[2,8,1024]{2,1,0:T(8,128)(2,1)S(1)} %fusion.70), channel_id=1, source_target_pairs={{0,8},{8,16},{16,24},{24,32},{32,40},{40,48},{48,56},{56,0},{1,9},... | collective-permute-start | bytes 98312 | tf_op jit(solution)/shard_map/ppermute | solution.py:38
  65.5 6.5 %collective-permute-start.5 = (bf16[4,2,8,1024]{3,2,1,0:T(8,128)(2,1)S(1)}, bf16[4,2,8,1024]{3,2,1,0:T(8,128)(2,1)S(1)}, u32[]{:S(2)}, u32[]{:S(2)}) collective-permute-start(bf16[4,2,8,1024]{3,2,1,0:T(8,128)(2,1)S(1)} %fusion.42), channel_id=1, source_target_pairs={{0,8},{8,16},{16,24},{24,32},{32,40},{40,48},{48,56},{56,0},{1,9},... | collective-permute-start | bytes 393224 | tf_op jit(solution)/shard_map/ppermute | solution.py:38
  67.2 5.6 %collective-permute-start.19 = (bf16[2,8,1024]{2,1,0:T(8,128)(2,1)S(1)}, bf16[2,8,1024]{2,1,0:T(8,128)(2,1)S(1)}, u32[]{:S(2)}, u32[]{:S(2)}) collective-permute-start(bf16[2,8,1024]{2,1,0:T(8,128)(2,1)S(1)} %fusion.69), channel_id=1, source_target_pairs={{0,8},{8,16},{16,24},{24,32},{32,40},{40,48},{48,56},{56,0},{1,9},... | collective-permute-start | bytes 98312 | tf_op jit(solution)/shard_map/ppermute | solution.py:38
  72.2 7.3 %collective-permute-start.6 = (bf16[4,2,8,1024]{3,2,1,0:T(8,128)(2,1)S(1)}, bf16[4,2,8,1024]{3,2,1,0:T(8,128)(2,1)S(1)}, u32[]{:S(2)}, u32[]{:S(2)}) collective-permute-start(bf16[4,2,8,1024]{3,2,1,0:T(8,128)(2,1)S(1)} %fusion.41), channel_id=1, source_target_pairs={{0,8},{8,16},{16,24},{24,32},{32,40},{40,48},{48,56},{56,0},{1,9},... | collective-permute-start | bytes 393224 | tf_op jit(solution)/shard_map/ppermute | solution.py:38
  72.8 7.4 %collective-permute-start.20 = (bf16[2,8,1024]{2,1,0:T(8,128)(2,1)S(1)}, bf16[2,8,1024]{2,1,0:T(8,128)(2,1)S(1)}, u32[]{:S(2)}, u32[]{:S(2)}) collective-permute-start(bf16[2,8,1024]{2,1,0:T(8,128)(2,1)S(1)} %fusion.68), channel_id=1, source_target_pairs={{0,8},{8,16},{16,24},{24,32},{32,40},{40,48},{48,56},{56,0},{1,9},... | collective-permute-start | bytes 98312 | tf_op jit(solution)/shard_map/ppermute | solution.py:38
  79.7 6.3 %collective-permute-start.7 = (bf16[4,2,8,1024]{3,2,1,0:T(8,128)(2,1)S(1)}, bf16[4,2,8,1024]{3,2,1,0:T(8,128)(2,1)S(1)}, u32[]{:S(2)}, u32[]{:S(2)}) collective-permute-start(bf16[4,2,8,1024]{3,2,1,0:T(8,128)(2,1)S(1)} %fusion.40), channel_id=1, source_target_pairs={{0,8},{8,16},{16,24},{24,32},{32,40},{40,48},{48,56},{56,0},{1,9},... | collective-permute-start | bytes 393224 | tf_op jit(solution)/shard_map/ppermute | solution.py:38
  80.2 12.4 %collective-permute-start.21 = (bf16[2,8,1024]{2,1,0:T(8,128)(2,1)S(1)}, bf16[2,8,1024]{2,1,0:T(8,128)(2,1)S(1)}, u32[]{:S(2)}, u32[]{:S(2)}) collective-permute-start(bf16[2,8,1024]{2,1,0:T(8,128)(2,1)S(1)} %fusion.67), channel_id=1, source_target_pairs={{0,8},{8,16},{16,24},{24,32},{32,40},{40,48},{48,56},{56,0},{1,9},... | collective-permute-start | bytes 98312 | tf_op jit(solution)/shard_map/ppermute | solution.py:38
  86.8 6.1 %collective-permute-start.10 = (bf16[2,8,1024]{2,1,0:T(8,128)(2,1)}, bf16[2,8,1024]{2,1,0:T(8,128)(2,1)}, u32[]{:S(2)}, u32[]{:S(2)}) collective-permute-start(bf16[2,8,1024]{2,1,0:T(8,128)(2,1)} %get-tuple-element.19), channel_id=1, source_target_pairs={{0,192},{64,0},{128,64},{192,128},{1,193},{65,1},{129,65},{193,129... | collective-permute-start | bytes 98312 | tf_op jit(solution)/shard_map/ppermute | solution.py:48
  89.4 5.5 %collective-permute-start.8 = (bf16[2,8,1024]{2,1,0:T(8,128)(2,1)}, bf16[2,8,1024]{2,1,0:T(8,128)(2,1)}, u32[]{:S(2)}, u32[]{:S(2)}) collective-permute-start(bf16[2,8,1024]{2,1,0:T(8,128)(2,1)} %get-tuple-element.18), channel_id=1, source_target_pairs={{0,64},{64,128},{128,192},{192,0},{1,65},{65,129},{129,193},{193,1... | collective-permute-start | bytes 98312 | tf_op jit(solution)/shard_map/ppermute | solution.py:48
  89.4 5.8 %collective-permute-start.9 = (bf16[2,8,1024]{2,1,0:T(8,128)(2,1)}, bf16[2,8,1024]{2,1,0:T(8,128)(2,1)}, u32[]{:S(2)}, u32[]{:S(2)}) collective-permute-start(bf16[2,8,1024]{2,1,0:T(8,128)(2,1)} %get-tuple-element.20), channel_id=1, source_target_pairs={{0,128},{64,192},{128,0},{192,64},{1,129},{65,193},{129,1},{193,65... | collective-permute-start | bytes 98312 | tf_op jit(solution)/shard_map/ppermute | solution.py:48
  96.6 1.6 %copy-start.8 = (bf16[16,8,64,64]{3,2,1,0:T(8,128)(2,1)S(1)}, bf16[16,8,64,64]{3,2,1,0:T(8,128)(2,1)}, u32[]{:S(2)}) copy-start(bf16[16,8,64,64]{3,2,1,0:T(8,128)(2,1)} %get-tuple-element.15) | copy-start | bytes 3145732
  103.8 4.3 %collective-permute-start.22 = (bf16[1,16,16,128]{3,1,2,0:T(8,128)(2,1)S(1)}, bf16[1,16,16,128]{3,1,2,0:T(8,128)(2,1)S(1)}, u32[]{:S(2)}, u32[]{:S(2)}) collective-permute-start(bf16[1,16,16,128]{3,1,2,0:T(8,128)(2,1)S(1)} %bitcast.193), channel_id=1, source_target_pairs={{0,1},{1,2},{2,3},{3,0},{4,5},{5,6},{6,7},{7,4},{8,9},{9,10},{10,1... | collective-permute-start | bytes 196616 | tf_op jit(solution)/shard_map/ppermute | solution.py:129
  104.3 5.5 %collective-permute-start.24 = (bf16[1,16,16,128]{3,1,2,0:T(8,128)(2,1)S(1)}, bf16[1,16,16,128]{3,1,2,0:T(8,128)(2,1)S(1)}, u32[]{:S(2)}, u32[]{:S(2)}) collective-permute-start(bf16[1,16,16,128]{3,1,2,0:T(8,128)(2,1)S(1)} %bitcast.194), channel_id=1, source_target_pairs={{0,3},{1,0},{2,1},{3,2},{4,7},{5,4},{6,5},{7,6},{8,11},{9,8},{10,9... | collective-permute-start | bytes 196616 | tf_op jit(solution)/shard_map/ppermute | solution.py:129
  105.9 5.8 %collective-permute-start.23 = (bf16[1,16,16,128]{3,1,2,0:T(8,128)(2,1)S(1)}, bf16[1,16,16,128]{3,1,2,0:T(8,128)(2,1)S(1)}, u32[]{:S(2)}, u32[]{:S(2)}) collective-permute-start(bf16[1,16,16,128]{3,1,2,0:T(8,128)(2,1)S(1)} %bitcast.195), channel_id=1, source_target_pairs={{0,2},{1,3},{2,0},{3,1},{4,6},{5,7},{6,4},{7,5},{8,10},{9,11},{10,... | collective-permute-start | bytes 196616 | tf_op jit(solution)/shard_map/ppermute | solution.py:129

commit v4 on v2

--- a/solution.py
+++ b/solution.py
@@ -9,15 +9,6 @@
 
 ELLS = 1024
 TM_AXES = ("ty", "tz", "tc")
-
-
-def realify(codebook):
-    half = codebook.shape[-1] // 2
-    real_part = codebook[..., :half]
-    imag_part = codebook[..., half:]
-    upper = jnp.concatenate([real_part, -imag_part], axis=-1)
-    lower = jnp.concatenate([imag_part, real_part], axis=-1)
-    return jnp.concatenate([upper, lower], axis=-2)
 
 
 def phases(mode_values, time_index, sidereal_period):
@@ -97,7 +88,6 @@
         modes_dev, chans_dev, bblocks, 2 * block_len
     )
     vectors = vectors.astype(jnp.float32)
-    code_matrix = realify(codebook).astype(jnp.float32)
     block_selector = jnp.where(
         block_index[..., None] == jnp.arange(code_count, dtype=jnp.int32),
         block_scale[..., None],
@@ -106,7 +96,13 @@
     combined = jnp.einsum(
         "mfblp,mfbi->mflpi", block_selector, vectors, precision=lax.Precision.HIGH
     )
-    weights = jnp.einsum("mflpi,lpij->mflj", combined, code_matrix, precision=lax.Precision.HIGH)
+    half = block_len
+    codes = codebook.astype(jnp.float32)
+    from_re = jnp.einsum("mflpi,lpij->mflj", combined[..., :half], codes, precision=lax.Precision.HIGH)
+    from_im = jnp.einsum("mflpi,lpij->mflj", combined[..., half:], codes, precision=lax.Precision.HIGH)
+    weights = jnp.concatenate(
+        [from_re[..., :half] + from_im[..., half:], from_im[..., :half] - from_re[..., half:]], axis=-1
+    )
     weights_bf = weights.astype(jnp.bfloat16)
     fr_pos = lax.axis_index("freq")
     basis_cols = lax.dynamic_slice_in_dim(fg_basis, fr_pos * chans_dev, chans_dev, 2)

time: 112 us -> 108 us (0.964)
  the two profiles are of different devices: /device:TPU:6 before, /device:TPU:16 now
where the time goes in v4:
time: 108 us
  waiting for transfers between devices  38.4 us (36%)
  starting transfers between devices  30.1 us (28%)
  other arithmetic  13.8 us (13%)
  local copies, waits for them, and re-layouts  13.6 us (13%)
  matrix products  10.7 us (10%)
  between operations  1.08 us (1%)
    ppermute x20, waiting for transfers between devices, ring_reduce_scatter(): got = lax.ppermute(s.astype(jnp.bfloat16), axis, fwd)  35.3 us
    ppermute x20, starting transfers between devices, ring_reduce_scatter(): got = lax.ppermute(s.astype(jnp.bfloat16), axis, fwd)  24.5 us
    dot_general x2, matrix products, spectra_of(): jnp.einsum('rdct,fctb->rdfb', table, part, precision=lax.Precision.HIGH)  6.54 us
    ppermute x3, starting transfers between devices, local(): lax.ppermute(weights_bf, 'freq', [(j, (j + s) % fr_count) for j in range(...  5.12 us
    convert_element_type x16, other arithmetic, ring_reduce_scatter(): got = lax.ppermute(s.astype(jnp.bfloat16), axis, fwd)  5.01 us
    add x1, other arithmetic, spectra_of(): y = out[half_rows:] + got.astype(jnp.float32)  3.37 us
    ppermute x3, waiting for transfers between devices, local(): lax.ppermute(weights_bf, 'freq', [(j, (j + s) % fr_count) for j in range(...  3.03 us
    reshape x1, local copies, waits for them, and re-layouts, spectra_of(): y = y.reshape(nz, ny, *y.shape[1:])  2.91 us
  transfers between devices with their start and end apart: 25, of which 17 were waited for; matrix products, arithmetic and copies ran while one was open for 23% of the time, Pallas kernels for 0%

profile of v4, /device:TPU:16, one launch (start us, length us, event | category | flops | bytes accessed | tf_op | source)
XLA Modules:
  0.0 107.7 jit_solution(17106873134853994437)
XLA Ops:
  0.5 0.4 sine_multiply_fusion.1
  0.9 4.4 %fusion.6 = f32[64,2,8,1024]{3,0,2,1:T(8,128)S(1)} fusion(f32[16,2,64,1024]{3,2,1,0:T(8,128)} %param.6, f32[64,1,2,64]{3,0,2,1:T(8,128)S(1)} %get-tuple-element.20, f32[64,1,2,64]{3,0,2,1:T(8,128)S(1)} %get-tuple-element.19), kind=kOutput, calls=%fused_computation.6 | convolution fusion | flops 805322752 | bytes 8454144 | tf_op jit(solution)/shard_map/rdct,fctb->rdfb/dot_general | solution.py:54
  5.3 1.3 %slice.89 = bf16[32,2,8,1024]{3,0,2,1:T(8,128)(2,1)} slice(f32[64,2,8,1024]{3,0,2,1:T(8,128)S(1)} %fusion.6), slice={[0:32], [0:2], [0:8], [0:1024]} | slice | bytes 2097152 | tf_op jit(solution)/shard_map/slice | solution.py:56
  6.6 2.2 %fusion.9 = f32[64,2,8,1024]{3,0,2,1:T(8,128)S(1)} fusion(f32[16,2,64,1024]{3,2,1,0:T(8,128)S(1)} %copy-done.3, f32[64,1,2,64]{3,0,2,1:T(8,128)S(1)} %get-tuple-element.22, f32[64,1,2,64]{3,0,2,1:T(8,128)S(1)} %get-tuple-element.21), kind=kOutput, calls=%fused_computation.7 | convolution fusion | flops 805322752 | bytes 8519680 | tf_op jit(solution)/shard_map/rdct,fctb->rdfb/dot_general | solution.py:54
  8.8 1.3 %slice.88 = bf16[32,2,8,1024]{3,0,2,1:T(8,128)(2,1)} slice(f32[64,2,8,1024]{3,0,2,1:T(8,128)S(1)} %fusion.9), slice={[0:32], [0:2], [0:8], [0:1024]} | slice | bytes 2097152 | tf_op jit(solution)/shard_map/slice | solution.py:56
  10.1 0.9 copy-done.2
  11.1 0.5 collective-permute-start.11
  11.6 3.4 %slice_add_fusion.1 = f32[32,2,8,1024]{3,0,2,1:T(8,128)} fusion(f32[64,2,8,1024]{3,0,2,1:T(8,128)} %copy-done.1, bf16[32,2,8,1024]{3,0,2,1:T(8,128)(2,1)S(1)} %collective-permute-done), kind=kLoop, calls=%fused_computation.12 | loop fusion | flops 1048576 | bytes 5242880 | tf_op jit(solution)/shard_map/add | solution.py:57
  14.9 2.9 %reshape.534 = f32[8,4,2,8,1024]{4,1,0,3,2:T(4,128)} reshape(f32[32,2,8,1024]{3,0,2,1:T(8,128)} %slice_add_fusion.1) | data formatting | bytes 4194304 | tf_op jit(solution)/shard_map/reshape | solution.py:59
  17.9 1.0 constant_dynamic-slice_fusion.12
  18.9 2.0 %collective-permute-start.1 = (bf16[4,2,8,1024]{3,2,1,0:T(8,128)(2,1)S(1)}, bf16[4,2,8,1024]{3,2,1,0:T(8,128)(2,1)S(1)}, u32[]{:S(2)}, u32[]{:S(2)}) collective-permute-start(bf16[4,2,8,1024]{3,2,1,0:T(8,128)(2,1)S(1)} %bitcast.206), channel_id=1, source_target_pairs={{0,8},{8,16},{16,24},{24,32},{32,40},{40,48},{48,56},{56,0},{1,9},... | collective-permute-start | bytes 393224 | tf_op jit(solution)/shard_map/ppermute | solution.py:29
  20.9 2.2 %fusion.12 = f32[4,8,2,8,1024]{4,1,0,3,2:T(8,128)S(1)} fusion(f32[64,2,8,1024]{3,0,2,1:T(8,128)} %copy-done.2, bf16[32,2,8,1024]{3,0,2,1:T(8,128)(2,1)} %collective-permute-done.11), kind=kLoop, calls=%fused_computation.10 | loop fusion | flops 1048576 | bytes 5242880 | tf_op jit(solution)/shard_map/reshape | solution.py:62
  23.3 1.4 %collective-permute-start.12 = (bf16[8,2,8,1024]{3,2,1,0:T(8,128)(2,1)S(1)}, bf16[8,2,8,1024]{3,2,1,0:T(8,128)(2,1)S(1)}, u32[]{:S(2)}, u32[]{:S(2)}) collective-permute-start(bf16[8,2,8,1024]{3,2,1,0:T(8,128)(2,1)S(1)} %bitcast.203), channel_id=1, source_target_pairs={{0,64},{64,128},{128,192},{192,0},{1,65},{65,129},{129,193},{193,1... | collective-permute-start | bytes 786440 | tf_op jit(solution)/shard_map/ppermute | solution.py:29
  24.6 1.1 constant_dynamic-slice_fusion.11
  25.8 2.7 %collective-permute-done.1 = bf16[4,2,8,1024]{3,2,1,0:T(8,128)(2,1)S(1)} collective-permute-done((bf16[4,2,8,1024]{3,2,1,0:T(8,128)(2,1)S(1)}, bf16[4,2,8,1024]{3,2,1,0:T(8,128)(2,1)S(1)}, u32[]{:S(2)}, u32[]{:S(2)}) %collective-permute-start.1) | collective-permute-done | bytes 131104 | tf_op jit(solution)/shard_map/ppermute | solution.py:29
  28.8 2.5 %collective-permute-done.12 = bf16[8,2,8,1024]{3,2,1,0:T(8,128)(2,1)S(1)} collective-permute-done((bf16[8,2,8,1024]{3,2,1,0:T(8,128)(2,1)S(1)}, bf16[8,2,8,1024]{3,2,1,0:T(8,128)(2,1)S(1)}, u32[]{:S(2)}, u32[]{:S(2)}) %collective-permute-start.12) | collective-permute-done | bytes 262176 | tf_op jit(solution)/shard_map/ppermute | solution.py:29
  31.3 0.3 fusion.21
  31.6 1.4 %collective-permute-start.13 = (bf16[8,2,8,1024]{3,2,1,0:T(8,128)(2,1)S(1)}, bf16[8,2,8,1024]{3,2,1,0:T(8,128)(2,1)S(1)}, u32[]{:S(2)}, u32[]{:S(2)}) collective-permute-start(bf16[8,2,8,1024]{3,2,1,0:T(8,128)(2,1)S(1)} %fusion.21), channel_id=1, source_target_pairs={{0,64},{64,128},{128,192},{192,0},{1,65},{65,129},{129,193},{193,1... | collective-permute-start | bytes 786440 | tf_op jit(solution)/shard_map/ppermute | solution.py:29
  33.8 1.1 %collective-permute-done.2 = bf16[4,2,8,1024]{3,2,1,0:T(8,128)(2,1)S(1)} collective-permute-done((bf16[4,2,8,1024]{3,2,1,0:T(8,128)(2,1)S(1)}, bf16[4,2,8,1024]{3,2,1,0:T(8,128)(2,1)S(1)}, u32[]{:S(2)}, u32[]{:S(2)}) %collective-permute-start.2) | collective-permute-done | bytes 131104 | tf_op jit(solution)/shard_map/ppermute | solution.py:29
  34.9 0.8 fusion.30
  35.7 0.8 collective-permute-start.3
  36.6 2.2 %collective-permute-done.13 = bf16[8,2,8,1024]{3,2,1,0:T(8,128)(2,1)S(1)} collective-permute-done((bf16[8,2,8,1024]{3,2,1,0:T(8,128)(2,1)S(1)}, bf16[8,2,8,1024]{3,2,1,0:T(8,128)(2,1)S(1)}, u32[]{:S(2)}, u32[]{:S(2)}) %collective-permute-start.13) | collective-permute-done | bytes 262176 | tf_op jit(solution)/shard_map/ppermute | solution.py:29
  38.8 1.0 fusion.20
  39.8 1.3 %collective-permute-start.14 = (bf16[8,2,8,1024]{3,2,1,0:T(8,128)(2,1)}, bf16[8,2,8,1024]{3,2,1,0:T(8,128)(2,1)}, u32[]{:S(2)}, u32[]{:S(2)}) collective-permute-start(bf16[8,2,8,1024]{3,2,1,0:T(8,128)(2,1)} %fusion.20), channel_id=1, source_target_pairs={{0,64},{64,128},{128,192},{192,0},{1,65},{65,129},{129,193},{193,1... | collective-permute-start | bytes 786440 | tf_op jit(solution)/shard_map/ppermute | solution.py:29
  41.1 1.0 copy.14
  42.1 1.7 %copy.15 = f32[16,16,16]{1,2,0:T(8,128)} copy(f32[16,16,16]{2,1,0:T(8,128)} %bitcast.205) | data formatting | bytes 32768 | tf_op jit(solution)/shard_map/jit(_where)/broadcast_in_dim | solution.py:91
  43.7 1.2 %fusion.29 = bf16[4,2,8,1024]{3,2,1,0:T(8,128)(2,1)S(1)} fusion(f32[1,4,2,8,1024]{4,1,0,3,2:T(4,128)} %get-tuple-element.10, bf16[4,2,8,1024]{3,2,1,0:T(8,128)(2,1)} %collective-permute-done.3), kind=kLoop, calls=%fused_computation.47 | loop fusion | flops 196608 | bytes 524288 | tf_op jit(solution)/shard_map/convert_element_type | solution.py:29
  44.9 2.0 %collective-permute-start.4 = (bf16[4,2,8,1024]{3,2,1,0:T(8,128)(2,1)S(1)}, bf16[4,2,8,1024]{3,2,1,0:T(8,128)(2,1)S(1)}, u32[]{:S(2)}, u32[]{:S(2)}) collective-permute-start(bf16[4,2,8,1024]{3,2,1,0:T(8,128)(2,1)S(1)} %fusion.29), channel_id=1, source_target_pairs={{0,8},{8,16},{16,24},{24,32},{32,40},{40,48},{48,56},{56,0},{1,9},... | collective-permute-start | bytes 393224 | tf_op jit(solution)/shard_map/ppermute | solution.py:29
  47.0 1.3 %bitcast_add_fusion = f32[8,2,8,1024]{3,2,1,0:T(8,128)S(1)} fusion(f32[1,8,2,8,1024]{4,1,0,3,2:T(8,128)S(1)} %get-tuple-element.13, bf16[8,2,8,1024]{3,2,1,0:T(8,128)(2,1)} %collective-permute-done.14), kind=kLoop, calls=%fused_computation.29 | loop fusion | flops 262144 | bytes 1310720 | tf_op jit(solution)/shard_map/add | solution.py:30
  48.3 2.0 %collective-permute-start.15 = (bf16[2,8,1024]{2,1,0:T(8,128)(2,1)S(1)}, bf16[2,8,1024]{2,1,0:T(8,128)(2,1)S(1)}, u32[]{:S(2)}, u32[]{:S(2)}) collective-permute-start(bf16[2,8,1024]{2,1,0:T(8,128)(2,1)S(1)} %fusion.73), channel_id=1, source_target_pairs={{0,8},{8,16},{16,24},{24,32},{32,40},{40,48},{48,56},{56,0},{1,9},... | collective-permute-start | bytes 98312 | tf_op jit(solution)/shard_map/ppermute | solution.py:29
  50.2 2.4 %collective-permute-done.4 = bf16[4,2,8,1024]{3,2,1,0:T(8,128)(2,1)S(1)} collective-permute-done((bf16[4,2,8,1024]{3,2,1,0:T(8,128)(2,1)S(1)}, bf16[4,2,8,1024]{3,2,1,0:T(8,128)(2,1)S(1)}, u32[]{:S(2)}, u32[]{:S(2)}) %collective-permute-start.4) | collective-permute-done | bytes 131104 | tf_op jit(solution)/shard_map/ppermute | solution.py:29
  52.7 1.1 %fusion.28 = bf16[4,2,8,1024]{3,2,1,0:T(8,128)(2,1)S(1)} fusion(f32[1,4,2,8,1024]{4,1,0,3,2:T(4,128)} %get-tuple-element.9, bf16[4,2,8,1024]{3,2,1,0:T(8,128)(2,1)S(1)} %collective-permute-done.4), kind=kLoop, calls=%fused_computation.45 | loop fusion | flops 196608 | bytes 524288 | tf_op jit(solution)/shard_map/convert_element_type | solution.py:29
  53.8 0.8 collective-permute-start.5
  54.6 1.5 %collective-permute-start.16 = (bf16[2,8,1024]{2,1,0:T(8,128)(2,1)S(1)}, bf16[2,8,1024]{2,1,0:T(8,128)(2,1)S(1)}, u32[]{:S(2)}, u32[]{:S(2)}) collective-permute-start(bf16[2,8,1024]{2,1,0:T(8,128)(2,1)S(1)} %fusion.62), channel_id=1, source_target_pairs={{0,8},{8,16},{16,24},{24,32},{32,40},{40,48},{48,56},{56,0},{1,9},... | collective-permute-start | bytes 98312 | tf_op jit(solution)/shard_map/ppermute | solution.py:29
  56.1 4.0 %collective-permute-done.5 = bf16[4,2,8,1024]{3,2,1,0:T(8,128)(2,1)S(1)} collective-permute-done((bf16[4,2,8,1024]{3,2,1,0:T(8,128)(2,1)S(1)}, bf16[4,2,8,1024]{3,2,1,0:T(8,128)(2,1)S(1)}, u32[]{:S(2)}, u32[]{:S(2)}) %collective-permute-start.5) | collective-permute-done | bytes 131104 | tf_op jit(solution)/shard_map/ppermute | solution.py:29
  60.3 0.4 collective-permute-done.16
  60.8 1.9 %collective-permute-start.17 = (bf16[2,8,1024]{2,1,0:T(8,128)(2,1)S(1)}, bf16[2,8,1024]{2,1,0:T(8,128)(2,1)S(1)}, u32[]{:S(2)}, u32[]{:S(2)}) collective-permute-start(bf16[2,8,1024]{2,1,0:T(8,128)(2,1)S(1)} %fusion.61), channel_id=1, source_target_pairs={{0,8},{8,16},{16,24},{24,32},{32,40},{40,48},{48,56},{56,0},{1,9},... | collective-permute-start | bytes 98312 | tf_op jit(solution)/shard_map/ppermute | solution.py:29
  62.7 4.6 %collective-permute-done.6 = bf16[4,2,8,1024]{3,2,1,0:T(8,128)(2,1)S(1)} collective-permute-done((bf16[4,2,8,1024]{3,2,1,0:T(8,128)(2,1)S(1)}, bf16[4,2,8,1024]{3,2,1,0:T(8,128)(2,1)S(1)}, u32[]{:S(2)}, u32[]{:S(2)}) %collective-permute-start.6) | collective-permute-done | bytes 131104 | tf_op jit(solution)/shard_map/ppermute | solution.py:29
  67.6 0.4 collective-permute-done.17
  68.0 0.8 collective-permute-start.18
  68.9 4.9 %collective-permute-done.7 = bf16[4,2,8,1024]{3,2,1,0:T(8,128)(2,1)S(1)} collective-permute-done((bf16[4,2,8,1024]{3,2,1,0:T(8,128)(2,1)S(1)}, bf16[4,2,8,1024]{3,2,1,0:T(8,128)(2,1)S(1)}, u32[]{:S(2)}, u32[]{:S(2)}) %collective-permute-start.7) | collective-permute-done | bytes 131104 | tf_op jit(solution)/shard_map/ppermute | solution.py:29
  73.9 3.1 %collective-permute-start.8 = (bf16[2,8,1024]{2,1,0:T(8,128)(2,1)S(1)}, bf16[2,8,1024]{2,1,0:T(8,128)(2,1)S(1)}, u32[]{:S(2)}, u32[]{:S(2)}) collective-permute-start(bf16[2,8,1024]{2,1,0:T(8,128)(2,1)S(1)} %fusion.72), channel_id=1, source_target_pairs={{0,64},{64,128},{128,192},{192,0},{1,65},{65,129},{129,193},{193,1... | collective-permute-start | bytes 98312 | tf_op jit(solution)/shard_map/ppermute | solution.py:29
  77.2 1.5 %collective-permute-done.8 = bf16[2,8,1024]{2,1,0:T(8,128)(2,1)S(1)} collective-permute-done((bf16[2,8,1024]{2,1,0:T(8,128)(2,1)S(1)}, bf16[2,8,1024]{2,1,0:T(8,128)(2,1)S(1)}, u32[]{:S(2)}, u32[]{:S(2)}) %collective-permute-start.8) | collective-permute-done | bytes 32800 | tf_op jit(solution)/shard_map/ppermute | solution.py:29
  78.7 2.4 %collective-permute-start.9 = (bf16[2,8,1024]{2,1,0:T(8,128)(2,1)S(1)}, bf16[2,8,1024]{2,1,0:T(8,128)(2,1)S(1)}, u32[]{:S(2)}, u32[]{:S(2)}) collective-permute-start(bf16[2,8,1024]{2,1,0:T(8,128)(2,1)S(1)} %fusion.65), channel_id=1, source_target_pairs={{0,64},{64,128},{128,192},{192,0},{1,65},{65,129},{129,193},{193,1... | collective-permute-start | bytes 98312 | tf_op jit(solution)/shard_map/ppermute | solution.py:29
  81.1 1.2 %collective-permute-done.19 = bf16[2,8,1024]{2,1,0:T(8,128)(2,1)S(1)} collective-permute-done((bf16[2,8,1024]{2,1,0:T(8,128)(2,1)S(1)}, bf16[2,8,1024]{2,1,0:T(8,128)(2,1)S(1)}, u32[]{:S(2)}, u32[]{:S(2)}) %collective-permute-start.19) | collective-permute-done | bytes 32800 | tf_op jit(solution)/shard_map/ppermute | solution.py:29
  82.4 0.3 collective-permute-done.9
  82.7 2.6 %collective-permute-start.10 = (bf16[2,8,1024]{2,1,0:T(8,128)(2,1)S(1)}, bf16[2,8,1024]{2,1,0:T(8,128)(2,1)S(1)}, u32[]{:S(2)}, u32[]{:S(2)}) collective-permute-start(bf16[2,8,1024]{2,1,0:T(8,128)(2,1)S(1)} %fusion.64), channel_id=1, source_target_pairs={{0,64},{64,128},{128,192},{192,0},{1,65},{65,129},{129,193},{193,1... | collective-permute-start | bytes 98312 | tf_op jit(solution)/shard_map/ppermute | solution.py:29
  85.3 2.2 %collective-permute-done.20 = bf16[2,8,1024]{2,1,0:T(8,128)(2,1)S(1)} collective-permute-done((bf16[2,8,1024]{2,1,0:T(8,128)(2,1)S(1)}, bf16[2,8,1024]{2,1,0:T(8,128)(2,1)S(1)}, u32[]{:S(2)}, u32[]{:S(2)}) %collective-permute-start.20) | collective-permute-done | bytes 32800 | tf_op jit(solution)/shard_map/ppermute | solution.py:29
  87.8 4.9 %collective-permute-done.21 = bf16[2,8,1024]{2,1,0:T(8,128)(2,1)S(1)} collective-permute-done((bf16[2,8,1024]{2,1,0:T(8,128)(2,1)S(1)}, bf16[2,8,1024]{2,1,0:T(8,128)(2,1)S(1)}, u32[]{:S(2)}, u32[]{:S(2)}) %collective-permute-start.21) | collective-permute-done | bytes 32800 | tf_op jit(solution)/shard_map/ppermute | solution.py:29
  92.7 0.8 fusion.56
  93.7 0.2 maximum_bitcast_fusion.4
  94.1 0.5 convolution_bitcast_fusion
  94.6 0.4 slice_bitcast_fusion
  94.9 1.2 %convolution_bitcast_fusion.1 = f32[1,16,16,128]{3,1,2,0:T(8,128)S(1)} fusion(bf16[16,8,64,128]{3,2,1,0:T(8,128)(2,1)S(1)} %copy-done, f32[16,16,8,64]{3,2,1,0:T(8,128)S(1)} %get-tuple-element.15), kind=kOutput, calls=%fused_computation.16 | convolution fusion | flops 100663296 | bytes 2752512 | tf_op jit(solution)/shard_map/mflpi,lpij->mflj/dot_general | solution.py:102
  96.2 1.2 %convolution_bitcast_fusion.2 = f32[1,16,16,128]{3,1,2,0:T(8,128)S(1)} fusion(bf16[16,8,64,128]{3,2,1,0:T(8,128)(2,1)S(1)} %copy-done, f32[16,16,8,64]{3,2,1,0:T(8,128)S(1)} %get-tuple-element.16), kind=kOutput, calls=%fused_computation.17 | convolution fusion | flops 100663296 | bytes 2752512 | tf_op jit(solution)/shard_map/mflpi,lpij->mflj/dot_general | solution.py:101
  97.6 1.5 %collective-permute-start.22 = (bf16[1,16,16,128]{3,1,2,0:T(8,128)(2,1)S(1)}, bf16[1,16,16,128]{3,1,2,0:T(8,128)(2,1)S(1)}, u32[]{:S(2)}, u32[]{:S(2)}) collective-permute-start(bf16[1,16,16,128]{3,1,2,0:T(8,128)(2,1)S(1)} %pad_maximum_fusion), channel_id=1, source_target_pairs={{0,1},{1,2},{2,3},{3,0},{4,5},{5,6},{6,7},{7,4},{8,9},{9,10},{10,1... | collective-permute-start | bytes 196616 | tf_op jit(solution)/shard_map/ppermute | solution.py:115
  99.2 1.8 %collective-permute-start.24 = (bf16[1,16,16,128]{3,1,2,0:T(8,128)(2,1)S(1)}, bf16[1,16,16,128]{3,1,2,0:T(8,128)(2,1)S(1)}, u32[]{:S(2)}, u32[]{:S(2)}) collective-permute-start(bf16[1,16,16,128]{3,1,2,0:T(8,128)(2,1)S(1)} %pad_maximum_fusion), channel_id=1, source_target_pairs={{0,3},{1,0},{2,1},{3,2},{4,7},{5,4},{6,5},{7,6},{8,11},{9,8},{10,9... | collective-permute-start | bytes 196616 | tf_op jit(solution)/shard_map/ppermute | solution.py:115
  101.0 1.8 %collective-permute-start.23 = (bf16[1,16,16,128]{3,1,2,0:T(8,128)(2,1)S(1)}, bf16[1,16,16,128]{3,1,2,0:T(8,128)(2,1)S(1)}, u32[]{:S(2)}, u32[]{:S(2)}) collective-permute-start(bf16[1,16,16,128]{3,1,2,0:T(8,128)(2,1)S(1)} %pad_maximum_fusion), channel_id=1, source_target_pairs={{0,2},{1,3},{2,0},{3,1},{4,6},{5,7},{6,4},{7,5},{8,10},{9,11},{10,... | collective-permute-start | bytes 196616 | tf_op jit(solution)/shard_map/ppermute | solution.py:115
  102.8 0.3 fusion.43
  103.2 0.3 convolution_add_fusion.1
  103.5 0.3 fusion.39
  103.8 2.9 %collective-permute-done.23 = bf16[1,16,16,128]{3,1,2,0:T(8,128)(2,1)S(1)} collective-permute-done((bf16[1,16,16,128]{3,1,2,0:T(8,128)(2,1)S(1)}, bf16[1,16,16,128]{3,1,2,0:T(8,128)(2,1)S(1)}, u32[]{:S(2)}, u32[]{:S(2)}) %collective-permute-start.23) | collective-permute-done | bytes 65568 | tf_op jit(solution)/shard_map/ppermute | solution.py:115
  106.7 0.3 fusion.16
  107.0 0.7 copy.33
  (74 shorter events, 3.2 us)
Async XLA Ops:
  0.0 94.9 %copy-start = (bf16[16,8,64,128]{3,2,1,0:T(8,128)(2,1)S(1)}, bf16[16,8,64,128]{3,2,1,0:T(8,128)(2,1)}, u32[]{:S(2)}) copy-start(bf16[16,8,64,128]{3,2,1,0:T(8,128)(2,1)} %param.7) | copy-start | bytes 6291460
  0.9 5.7 %copy-start.3 = (f32[16,2,64,1024]{3,2,1,0:T(8,128)S(1)}, f32[16,2,64,1024]{3,2,1,0:T(8,128)}, u32[]{:S(2)}) copy-start(f32[16,2,64,1024]{3,2,1,0:T(8,128)} %param.6) | copy-start | bytes 25165828
  5.3 3.5 %copy-start.1 = (f32[64,2,8,1024]{3,0,2,1:T(8,128)}, f32[64,2,8,1024]{3,0,2,1:T(8,128)S(1)}, u32[]{:S(2)}) copy-start(f32[64,2,8,1024]{3,0,2,1:T(8,128)S(1)} %fusion.6) | copy-start | bytes 12582916
  6.6 5.0 %collective-permute-start = (bf16[32,2,8,1024]{3,0,2,1:T(8,128)(2,1)}, bf16[32,2,8,1024]{3,0,2,1:T(8,128)(2,1)S(1)}, u32[]{:S(2)}, u32[]{:S(2)}) collective-permute-start(bf16[32,2,8,1024]{3,0,2,1:T(8,128)(2,1)} %slice.89), channel_id=1, source_target_pairs={{0,4},{4,0},{1,5},{5,1},{2,6},{6,2},{3,7},{7,3},{8,12},{12,8},{9,1... | collective-permute-start | bytes 3145736 | tf_op jit(solution)/shard_map/ppermute | solution.py:56
  8.8 2.3 %copy-start.2 = (f32[64,2,8,1024]{3,0,2,1:T(8,128)}, f32[64,2,8,1024]{3,0,2,1:T(8,128)S(1)}, u32[]{:S(2)}) copy-start(f32[64,2,8,1024]{3,0,2,1:T(8,128)S(1)} %fusion.9) | copy-start | bytes 12582916
  11.1 9.8 %collective-permute-start.11 = (bf16[32,2,8,1024]{3,0,2,1:T(8,128)(2,1)}, bf16[32,2,8,1024]{3,0,2,1:T(8,128)(2,1)}, u32[]{:S(2)}, u32[]{:S(2)}) collective-permute-start(bf16[32,2,8,1024]{3,0,2,1:T(8,128)(2,1)} %slice.88), channel_id=1, source_target_pairs={{0,4},{4,0},{1,5},{5,1},{2,6},{6,2},{3,7},{7,3},{8,12},{12,8},{9,1... | collective-permute-start | bytes 3145736 | tf_op jit(solution)/shard_map/ppermute | solution.py:56
  18.9 5.7 %copy-start.4 = (f32[8,4,2,8,1024]{4,1,0,3,2:T(4,128)S(1)}, f32[8,4,2,8,1024]{4,1,0,3,2:T(4,128)}, u32[]{:S(2)}) copy-start(f32[8,4,2,8,1024]{4,1,0,3,2:T(4,128)} %reshape.534) | copy-start | bytes 6291460
  18.9 9.6 %collective-permute-start.1 = (bf16[4,2,8,1024]{3,2,1,0:T(8,128)(2,1)S(1)}, bf16[4,2,8,1024]{3,2,1,0:T(8,128)(2,1)S(1)}, u32[]{:S(2)}, u32[]{:S(2)}) collective-permute-start(bf16[4,2,8,1024]{3,2,1,0:T(8,128)(2,1)S(1)} %bitcast.206), channel_id=1, source_target_pairs={{0,8},{8,16},{16,24},{24,32},{32,40},{40,48},{48,56},{56,0},{1,9},... | collective-permute-start | bytes 393224 | tf_op jit(solution)/shard_map/ppermute | solution.py:29
  23.3 8.0 %collective-permute-start.12 = (bf16[8,2,8,1024]{3,2,1,0:T(8,128)(2,1)S(1)}, bf16[8,2,8,1024]{3,2,1,0:T(8,128)(2,1)S(1)}, u32[]{:S(2)}, u32[]{:S(2)}) collective-permute-start(bf16[8,2,8,1024]{3,2,1,0:T(8,128)(2,1)S(1)} %bitcast.203), channel_id=1, source_target_pairs={{0,64},{64,128},{128,192},{192,0},{1,65},{65,129},{129,193},{193,1... | collective-permute-start | bytes 786440 | tf_op jit(solution)/shard_map/ppermute | solution.py:29
  25.7 7.3 %copy-start.8 = (f32[16,64,64]{2,1,0:T(8,128)S(1)}, f32[16,64,64]{2,1,0:T(8,128)}, u32[]{:S(2)}) copy-start(f32[16,64,64]{2,1,0:T(8,128)} %param.10) | copy-start | bytes 786436
  28.7 6.3 %collective-permute-start.2 = (bf16[4,2,8,1024]{3,2,1,0:T(8,128)(2,1)S(1)}, bf16[4,2,8,1024]{3,2,1,0:T(8,128)(2,1)S(1)}, u32[]{:S(2)}, u32[]{:S(2)}) collective-permute-start(bf16[4,2,8,1024]{3,2,1,0:T(8,128)(2,1)S(1)} %fusion.31), channel_id=1, source_target_pairs={{0,8},{8,16},{16,24},{24,32},{32,40},{40,48},{48,56},{56,0},{1,9},... | collective-permute-start | bytes 393224 | tf_op jit(solution)/shard_map/ppermute | solution.py:29
  31.6 7.2 %collective-permute-start.13 = (bf16[8,2,8,1024]{3,2,1,0:T(8,128)(2,1)S(1)}, bf16[8,2,8,1024]{3,2,1,0:T(8,128)(2,1)S(1)}, u32[]{:S(2)}, u32[]{:S(2)}) collective-permute-start(bf16[8,2,8,1024]{3,2,1,0:T(8,128)(2,1)S(1)} %fusion.21), channel_id=1, source_target_pairs={{0,64},{64,128},{128,192},{192,0},{1,65},{65,129},{129,193},{193,1... | collective-permute-start | bytes 786440 | tf_op jit(solution)/shard_map/ppermute | solution.py:29
  35.7 8.0 %collective-permute-start.3 = (bf16[4,2,8,1024]{3,2,1,0:T(8,128)(2,1)}, bf16[4,2,8,1024]{3,2,1,0:T(8,128)(2,1)}, u32[]{:S(2)}, u32[]{:S(2)}) collective-permute-start(bf16[4,2,8,1024]{3,2,1,0:T(8,128)(2,1)} %fusion.30), channel_id=1, source_target_pairs={{0,8},{8,16},{16,24},{24,32},{32,40},{40,48},{48,56},{56,0},{1,9},... | collective-permute-start | bytes 393224 | tf_op jit(solution)/shard_map/ppermute | solution.py:29
  39.8 7.2 %collective-permute-start.14 = (bf16[8,2,8,1024]{3,2,1,0:T(8,128)(2,1)}, bf16[8,2,8,1024]{3,2,1,0:T(8,128)(2,1)}, u32[]{:S(2)}, u32[]{:S(2)}) collective-permute-start(bf16[8,2,8,1024]{3,2,1,0:T(8,128)(2,1)} %fusion.20), channel_id=1, source_target_pairs={{0,64},{64,128},{128,192},{192,0},{1,65},{65,129},{129,193},{193,1... | collective-permute-start | bytes 786440 | tf_op jit(solution)/shard_map/ppermute | solution.py:29
  43.7 16.3 %copy-start.7 = (f32[1,4,2,8,1024]{4,1,0,3,2:T(4,128)S(1)}, f32[1,4,2,8,1024]{4,1,0,3,2:T(4,128)}, u32[]{:S(2)}) copy-start(f32[1,4,2,8,1024]{4,1,0,3,2:T(4,128)} %get-tuple-element.8) | copy-start | bytes 786436
  43.7 23.6 %copy-start.6 = (f32[1,4,2,8,1024]{4,1,0,3,2:T(4,128)S(1)}, f32[1,4,2,8,1024]{4,1,0,3,2:T(4,128)}, u32[]{:S(2)}) copy-start(f32[1,4,2,8,1024]{4,1,0,3,2:T(4,128)} %get-tuple-element.7) | copy-start | bytes 786436
  44.9 7.7 %collective-permute-start.4 = (bf16[4,2,8,1024]{3,2,1,0:T(8,128)(2,1)S(1)}, bf16[4,2,8,1024]{3,2,1,0:T(8,128)(2,1)S(1)}, u32[]{:S(2)}, u32[]{:S(2)}) collective-permute-start(bf16[4,2,8,1024]{3,2,1,0:T(8,128)(2,1)S(1)} %fusion.29), channel_id=1, source_target_pairs={{0,8},{8,16},{16,24},{24,32},{32,40},{40,48},{48,56},{56,0},{1,9},... | collective-permute-start | bytes 393224 | tf_op jit(solution)/shard_map/ppermute | solution.py:29
  48.2 39.3 %copy-start.5 = (f32[8,2,8,1024]{3,2,1,0:T(8,128)}, f32[8,2,8,1024]{3,2,1,0:T(8,128)S(1)}, u32[]{:S(2)}) copy-start(f32[8,2,8,1024]{3,2,1,0:T(8,128)S(1)} %bitcast_add_fusion) | copy-start | bytes 1572868
  48.3 6.3 %collective-permute-start.15 = (bf16[2,8,1024]{2,1,0:T(8,128)(2,1)S(1)}, bf16[2,8,1024]{2,1,0:T(8,128)(2,1)S(1)}, u32[]{:S(2)}, u32[]{:S(2)}) collective-permute-start(bf16[2,8,1024]{2,1,0:T(8,128)(2,1)S(1)} %fusion.73), channel_id=1, source_target_pairs={{0,8},{8,16},{16,24},{24,32},{32,40},{40,48},{48,56},{56,0},{1,9},... | collective-permute-start | bytes 98312 | tf_op jit(solution)/shard_map/ppermute | solution.py:29
  53.8 40.3 %copy-start.9 = (f32[16,16,16]{1,2,0:T(8,128)S(1)}, f32[16,16,16]{1,2,0:T(8,128)}, u32[]{:S(2)}) copy-start(f32[16,16,16]{1,2,0:T(8,128)} %copy.15) | copy-start | bytes 49156
  53.8 6.3 %collective-permute-start.5 = (bf16[4,2,8,1024]{3,2,1,0:T(8,128)(2,1)S(1)}, bf16[4,2,8,1024]{3,2,1,0:T(8,128)(2,1)S(1)}, u32[]{:S(2)}, u32[]{:S(2)}) collective-permute-start(bf16[4,2,8,1024]{3,2,1,0:T(8,128)(2,1)S(1)} %fusion.28), channel_id=1, source_target_pairs={{0,8},{8,16},{16,24},{24,32},{32,40},{40,48},{48,56},{56,0},{1,9},... | collective-permute-start | bytes 393224 | tf_op jit(solution)/shard_map/ppermute | solution.py:29
  54.6 6.2 %collective-permute-start.16 = (bf16[2,8,1024]{2,1,0:T(8,128)(2,1)S(1)}, bf16[2,8,1024]{2,1,0:T(8,128)(2,1)S(1)}, u32[]{:S(2)}, u32[]{:S(2)}) collective-permute-start(bf16[2,8,1024]{2,1,0:T(8,128)(2,1)S(1)} %fusion.62), channel_id=1, source_target_pairs={{0,8},{8,16},{16,24},{24,32},{32,40},{40,48},{48,56},{56,0},{1,9},... | collective-permute-start | bytes 98312 | tf_op jit(solution)/shard_map/ppermute | solution.py:29
  60.2 7.1 %collective-permute-start.6 = (bf16[4,2,8,1024]{3,2,1,0:T(8,128)(2,1)S(1)}, bf16[4,2,8,1024]{3,2,1,0:T(8,128)(2,1)S(1)}, u32[]{:S(2)}, u32[]{:S(2)}) collective-permute-start(bf16[4,2,8,1024]{3,2,1,0:T(8,128)(2,1)S(1)} %fusion.27), channel_id=1, source_target_pairs={{0,8},{8,16},{16,24},{24,32},{32,40},{40,48},{48,56},{56,0},{1,9},... | collective-permute-start | bytes 393224 | tf_op jit(solution)/shard_map/ppermute | solution.py:29
  60.8 7.2 %collective-permute-start.17 = (bf16[2,8,1024]{2,1,0:T(8,128)(2,1)S(1)}, bf16[2,8,1024]{2,1,0:T(8,128)(2,1)S(1)}, u32[]{:S(2)}, u32[]{:S(2)}) collective-permute-start(bf16[2,8,1024]{2,1,0:T(8,128)(2,1)S(1)} %fusion.61), channel_id=1, source_target_pairs={{0,8},{8,16},{16,24},{24,32},{32,40},{40,48},{48,56},{56,0},{1,9},... | collective-permute-start | bytes 98312 | tf_op jit(solution)/shard_map/ppermute | solution.py:29
  67.5 6.3 %collective-permute-start.7 = (bf16[4,2,8,1024]{3,2,1,0:T(8,128)(2,1)S(1)}, bf16[4,2,8,1024]{3,2,1,0:T(8,128)(2,1)S(1)}, u32[]{:S(2)}, u32[]{:S(2)}) collective-permute-start(bf16[4,2,8,1024]{3,2,1,0:T(8,128)(2,1)S(1)} %fusion.26), channel_id=1, source_target_pairs={{0,8},{8,16},{16,24},{24,32},{32,40},{40,48},{48,56},{56,0},{1,9},... | collective-permute-start | bytes 393224 | tf_op jit(solution)/shard_map/ppermute | solution.py:29
  68.0 9.0 %collective-permute-start.18 = (bf16[2,8,1024]{2,1,0:T(8,128)(2,1)S(1)}, bf16[2,8,1024]{2,1,0:T(8,128)(2,1)S(1)}, u32[]{:S(2)}, u32[]{:S(2)}) collective-permute-start(bf16[2,8,1024]{2,1,0:T(8,128)(2,1)S(1)} %fusion.60), channel_id=1, source_target_pairs={{0,8},{8,16},{16,24},{24,32},{32,40},{40,48},{48,56},{56,0},{1,9},... | collective-permute-start | bytes 98312 | tf_op jit(solution)/shard_map/ppermute | solution.py:29
  73.9 4.7 %collective-permute-start.8 = (bf16[2,8,1024]{2,1,0:T(8,128)(2,1)S(1)}, bf16[2,8,1024]{2,1,0:T(8,128)(2,1)S(1)}, u32[]{:S(2)}, u32[]{:S(2)}) collective-permute-start(bf16[2,8,1024]{2,1,0:T(8,128)(2,1)S(1)} %fusion.72), channel_id=1, source_target_pairs={{0,64},{64,128},{128,192},{192,0},{1,65},{65,129},{129,193},{193,1... | collective-permute-start | bytes 98312 | tf_op jit(solution)/shard_map/ppermute | solution.py:29
  77.1 5.2 %collective-permute-start.19 = (bf16[2,8,1024]{2,1,0:T(8,128)(2,1)S(1)}, bf16[2,8,1024]{2,1,0:T(8,128)(2,1)S(1)}, u32[]{:S(2)}, u32[]{:S(2)}) collective-permute-start(bf16[2,8,1024]{2,1,0:T(8,128)(2,1)S(1)} %fusion.59), channel_id=1, source_target_pairs={{0,8},{8,16},{16,24},{24,32},{32,40},{40,48},{48,56},{56,0},{1,9},... | collective-permute-start | bytes 98312 | tf_op jit(solution)/shard_map/ppermute | solution.py:29
  78.7 4.0 %collective-permute-start.9 = (bf16[2,8,1024]{2,1,0:T(8,128)(2,1)S(1)}, bf16[2,8,1024]{2,1,0:T(8,128)(2,1)S(1)}, u32[]{:S(2)}, u32[]{:S(2)}) collective-permute-start(bf16[2,8,1024]{2,1,0:T(8,128)(2,1)S(1)} %fusion.65), channel_id=1, source_target_pairs={{0,64},{64,128},{128,192},{192,0},{1,65},{65,129},{129,193},{193,1... | collective-permute-start | bytes 98312 | tf_op jit(solution)/shard_map/ppermute | solution.py:29
  82.3 5.2 %collective-permute-start.20 = (bf16[2,8,1024]{2,1,0:T(8,128)(2,1)S(1)}, bf16[2,8,1024]{2,1,0:T(8,128)(2,1)S(1)}, u32[]{:S(2)}, u32[]{:S(2)}) collective-permute-start(bf16[2,8,1024]{2,1,0:T(8,128)(2,1)S(1)} %fusion.58), channel_id=1, source_target_pairs={{0,8},{8,16},{16,24},{24,32},{32,40},{40,48},{48,56},{56,0},{1,9},... | collective-permute-start | bytes 98312 | tf_op jit(solution)/shard_map/ppermute | solution.py:29
  82.7 4.9 %collective-permute-start.10 = (bf16[2,8,1024]{2,1,0:T(8,128)(2,1)S(1)}, bf16[2,8,1024]{2,1,0:T(8,128)(2,1)S(1)}, u32[]{:S(2)}, u32[]{:S(2)}) collective-permute-start(bf16[2,8,1024]{2,1,0:T(8,128)(2,1)S(1)} %fusion.64), channel_id=1, source_target_pairs={{0,64},{64,128},{128,192},{192,0},{1,65},{65,129},{129,193},{193,1... | collective-permute-start | bytes 98312 | tf_op jit(solution)/shard_map/ppermute | solution.py:29
  87.5 5.2 %collective-permute-start.21 = (bf16[2,8,1024]{2,1,0:T(8,128)(2,1)S(1)}, bf16[2,8,1024]{2,1,0:T(8,128)(2,1)S(1)}, u32[]{:S(2)}, u32[]{:S(2)}) collective-permute-start(bf16[2,8,1024]{2,1,0:T(8,128)(2,1)S(1)} %fusion.57), channel_id=1, source_target_pairs={{0,8},{8,16},{16,24},{24,32},{32,40},{40,48},{48,56},{56,0},{1,9},... | collective-permute-start | bytes 98312 | tf_op jit(solution)/shard_map/ppermute | solution.py:29
  97.6 5.6 %collective-permute-start.22 = (bf16[1,16,16,128]{3,1,2,0:T(8,128)(2,1)S(1)}, bf16[1,16,16,128]{3,1,2,0:T(8,128)(2,1)S(1)}, u32[]{:S(2)}, u32[]{:S(2)}) collective-permute-start(bf16[1,16,16,128]{3,1,2,0:T(8,128)(2,1)S(1)} %pad_maximum_fusion), channel_id=1, source_target_pairs={{0,1},{1,2},{2,3},{3,0},{4,5},{5,6},{6,7},{7,4},{8,9},{9,10},{10,1... | collective-permute-start | bytes 196616 | tf_op jit(solution)/shard_map/ppermute | solution.py:115
  99.2 4.3 %collective-permute-start.24 = (bf16[1,16,16,128]{3,1,2,0:T(8,128)(2,1)S(1)}, bf16[1,16,16,128]{3,1,2,0:T(8,128)(2,1)S(1)}, u32[]{:S(2)}, u32[]{:S(2)}) collective-permute-start(bf16[1,16,16,128]{3,1,2,0:T(8,128)(2,1)S(1)} %pad_maximum_fusion), channel_id=1, source_target_pairs={{0,3},{1,0},{2,1},{3,2},{4,7},{5,4},{6,5},{7,6},{8,11},{9,8},{10,9... | collective-permute-start | bytes 196616 | tf_op jit(solution)/shard_map/ppermute | solution.py:115
  101.0 5.8 %collective-permute-start.23 = (bf16[1,16,16,128]{3,1,2,0:T(8,128)(2,1)S(1)}, bf16[1,16,16,128]{3,1,2,0:T(8,128)(2,1)S(1)}, u32[]{:S(2)}, u32[]{:S(2)}) collective-permute-start(bf16[1,16,16,128]{3,1,2,0:T(8,128)(2,1)S(1)} %pad_maximum_fusion), channel_id=1, source_target_pairs={{0,2},{1,3},{2,0},{3,1},{4,6},{5,7},{6,4},{7,5},{8,10},{9,11},{10,... | collective-permute-start | bytes 196616 | tf_op jit(solution)/shard_map/ppermute | solution.py:115

commit v5 on v4

--- a/solution.py
+++ b/solution.py
@@ -46,20 +46,22 @@
     halves = []
     for part, z_major in ((visibility[:h], True), (visibility[h:], False)):
         if z_major:
-            pair = (jy[None, :] * nz + jz[:, None]).reshape(-1)
+            pair = jy[None, :] * nz + jz[:, None]
         else:
-            pair = (jy[:, None] * nz + jz[None, :]).reshape(-1)
-        rows = jnp.concatenate([pair * 2 + (1 - c), pair * 2 + c])
-        table = dft_table(mode_step * rows, time_index, sidereal_period, norm_factor)
-        out = jnp.einsum("rdct,fctb->rdfb", table, part, precision=lax.Precision.HIGH)
-        half_rows = ny * nz
-        got = lax.ppermute(out[:half_rows].astype(jnp.bfloat16), "tc", [(0, 1), (1, 0)])
-        y = out[half_rows:] + got.astype(jnp.float32)
+            pair = jy[:, None] * nz + jz[None, :]
+        n1, n2 = pair.shape
+
+        def block(tc_of):
+            rows = (pair * 2 + tc_of).reshape(-1)
+            table = dft_table(mode_step * rows, time_index, sidereal_period, norm_factor)
+            table = table.reshape(n1, n2, *table.shape[1:])
+            return jnp.einsum("uvdct,fctb->uvdfb", table, part, precision=lax.Precision.HIGH)
+
+        got = lax.ppermute(block(1 - c).astype(jnp.bfloat16), "tc", [(0, 1), (1, 0)])
+        y = block(c) + got.astype(jnp.float32)
         if z_major:
-            y = y.reshape(nz, ny, *y.shape[1:])
             y = ring_reduce_scatter(ring_reduce_scatter(y, "tz", nz), "ty", ny)
         else:
-            y = y.reshape(ny, nz, *y.shape[1:])
             y = ring_reduce_scatter(ring_reduce_scatter(y, "ty", ny), "tz", nz)
         halves.append(y)
     return jnp.concatenate(halves, axis=1)

time: 108 us -> 108 us (level)
  the two profiles are of different devices: /device:TPU:16 before, /device:TPU:6 now
where the time goes in v5:
time: 108 us; the launch traced here: 107 us
  waiting for transfers between devices  41.3 us (38%)
  starting transfers between devices  22.6 us (21%)
  matrix products  22 us (20%)
  other arithmetic  9.99 us (9%)
  local copies, waits for them, and re-layouts  9.9 us (9%)
  between operations  1.09 us (1%)
    ppermute x20, waiting for transfers between devices, ring_reduce_scatter(): got = lax.ppermute(s.astype(jnp.bfloat16), axis, fwd)  37.8 us
    ppermute x20, starting transfers between devices, ring_reduce_scatter(): got = lax.ppermute(s.astype(jnp.bfloat16), axis, fwd)  18.6 us
    dot_general x4, matrix products, block(): jnp.einsum('uvdct,fctb->uvdfb', table, part, precision=lax.Precision.HIGH)  17 us
    convert_element_type x16, other arithmetic, ring_reduce_scatter(): got = lax.ppermute(s.astype(jnp.bfloat16), axis, fwd)  7.71 us
    dynamic_slice x2, local copies, waits for them, and re-layouts, take(): return lax.dynamic_index_in_dim(a, k % n, 0, keepdims=False)  4.05 us
    ppermute x3, waiting for transfers between devices, local(): lax.ppermute(weights_bf, 'freq', [(j, (j + s) % fr_count) for j in range(...  3.52 us
    ppermute x3, starting transfers between devices, local(): lax.ppermute(weights_bf, 'freq', [(j, (j + s) % fr_count) for j in range(...  3.44 us
  transfers between devices with their start and end apart: 25, of which 21 were waited for; matrix products, arithmetic and copies ran while one was open for 29% of the time, Pallas kernels for 0%

profile of v5, /device:TPU:6, one launch (start us, length us, event | category | flops | bytes accessed | tf_op | source)
XLA Modules:
  0.0 106.9 jit_solution(1557378440692569276)
XLA Ops:
  0.1 0.2 sine_multiply_fusion.3
  0.3 4.7 %bitcast_convert_fusion.1 = bf16[8,4,2,8,1024]{4,0,3,2,1:T(8,128)(2,1)} fusion(f32[16,2,64,1024]{3,2,1,0:T(8,128)} %param.6, f32[8,4,1,1,64]{4,0,3,2,1:T(8,128)S(1)} %get-tuple-element.35, f32[8,4,1,1,64]{4,0,3,2,1:T(8,128)S(1)} %get-tuple-element.36, f32[8,4,1,1,64]{4,0,3,2,1:T(8,128)S(1)} %get-tuple-element.37), kind=kOutput, calls=%fused_computation.14 | convolution fusion | flops 403202048 | bytes 5267456 | tf_op jit(solution)/shard_map/uvdct,fctb->uvdfb/dot_general | solution.py:58
  5.1 0.2 sine_multiply_fusion.1
  5.3 4.5 %bitcast_convert_fusion = bf16[4,8,2,8,1024]{4,1,3,2,0:T(8,128)(2,1)} fusion(f32[16,2,64,1024]{3,2,1,0:T(8,128)} %param.6, f32[4,8,1,1,64]{4,1,3,2,0:T(8,128)S(1)} %get-tuple-element.40, f32[4,8,1,1,64]{4,1,3,2,0:T(8,128)S(1)} %get-tuple-element.41, f32[4,8,1,1,64]{4,1,3,2,0:T(8,128)S(1)} %get-tuple-element.42), kind=kOutput, calls=%fused_computation.12 | convolution fusion | flops 403202048 | bytes 5267456 | tf_op jit(solution)/shard_map/uvdct,fctb->uvdfb/dot_general | solution.py:58
  9.9 0.5 collective-permute-start.11
  10.4 3.7 %bitcast_add_fusion.1 = f32[8,4,2,8,1024]{4,0,3,2,1:T(8,128)S(1)} fusion(bf16[8,4,2,8,1024]{4,0,3,2,1:T(8,128)(2,1)S(1)} %collective-permute-done, f32[16,2,64,1024]{3,2,1,0:T(8,128)} %param.6, f32[8,4,1,1,64]{4,0,3,2,1:T(8,128)S(1)} %get-tuple-element.25, f32[8,4,1,1,64]{4,0,3,2,1:T(8,128)S(1)} %get-tuple-element.24, ...), kind=kOutput, calls=%fused_computation.15 | convolution fusion | flops 403726336 | bytes 7364608 | tf_op jit(solution)/shard_map/uvdct,fctb->uvdfb/dot_general | solution.py:58
  14.1 0.3 dynamic-slice_convert_fusion.1
  14.4 2.0 %collective-permute-start.1 = (bf16[4,2,8,1024]{3,2,1,0:T(8,128)(2,1)S(1)}, bf16[4,2,8,1024]{3,2,1,0:T(8,128)(2,1)S(1)}, u32[]{:S(2)}, u32[]{:S(2)}) collective-permute-start(bf16[4,2,8,1024]{3,2,1,0:T(8,128)(2,1)S(1)} %bitcast.217), channel_id=1, source_target_pairs={{0,8},{8,16},{16,24},{24,32},{32,40},{40,48},{48,56},{56,0},{1,9},... | collective-permute-start | bytes 393224 | tf_op jit(solution)/shard_map/ppermute | solution.py:29
  16.4 4.0 %bitcast_add_fusion = f32[4,8,2,8,1024]{4,1,3,2,0:T(8,128)S(1)} fusion(bf16[4,8,2,8,1024]{4,1,3,2,0:T(8,128)(2,1)} %collective-permute-done.11, f32[16,2,64,1024]{3,2,1,0:T(8,128)} %param.6, f32[4,8,1,1,64]{4,1,3,2,0:T(8,128)S(1)} %get-tuple-element.31, f32[4,8,1,1,64]{4,1,3,2,0:T(8,128)S(1)} %get-tuple-element.30, ...), kind=kOutput, calls=%fused_computation.13 | convolution fusion | flops 403726336 | bytes 7364608 | tf_op jit(solution)/shard_map/uvdct,fctb->uvdfb/dot_general | solution.py:58
  20.5 3.0 %constant_dynamic-slice_fusion.14 = (f32[1,4,2,8,1024]{4,0,3,2,1:T(1,128)S(1)}, f32[1,4,2,8,1024]{4,0,3,2,1:T(1,128)S(1)}, f32[1,4,2,8,1024]{4,0,3,2,1:T(1,128)S...) fusion(f32[8,4,2,8,1024]{4,0,3,2,1:T(8,128)S(1)} %bitcast_add_f, ...), kind=kLoop, calls=%fused_computation.189 | loop fusion | bytes 3670044 | tf_op jit(solution)/shard_map/jit(dynamic_index_in_dim)/dynamic_slice | solution.py:25
  23.4 0.6 collective-permute-done.1
  24.1 1.4 %collective-permute-start.2 = (bf16[4,2,8,1024]{3,2,1,0:T(8,128)(2,1)S(1)}, bf16[4,2,8,1024]{3,2,1,0:T(8,128)(2,1)}, u32[]{:S(2)}, u32[]{:S(2)}) collective-permute-start(bf16[4,2,8,1024]{3,2,1,0:T(8,128)(2,1)S(1)} %fusion.38), channel_id=1, source_target_pairs={{0,8},{8,16},{16,24},{24,32},{32,40},{40,48},{48,56},{56,0},{1,9},... | collective-permute-start | bytes 393224 | tf_op jit(solution)/shard_map/ppermute | solution.py:29
  25.5 1.7 %collective-permute-start.12 = (bf16[8,2,8,1024]{3,0,2,1:T(8,128)(2,1)S(1)}, bf16[8,2,8,1024]{3,0,2,1:T(8,128)(2,1)}, u32[]{:S(2)}, u32[]{:S(2)}) collective-permute-start(bf16[8,2,8,1024]{3,0,2,1:T(8,128)(2,1)S(1)} %fusion.32), channel_id=1, source_target_pairs={{0,64},{64,128},{128,192},{192,0},{1,65},{65,129},{129,193},{193,1... | collective-permute-start | bytes 786440 | tf_op jit(solution)/shard_map/ppermute | solution.py:29
  27.2 4.1 %collective-permute-done.2 = bf16[4,2,8,1024]{3,2,1,0:T(8,128)(2,1)} collective-permute-done((bf16[4,2,8,1024]{3,2,1,0:T(8,128)(2,1)S(1)}, bf16[4,2,8,1024]{3,2,1,0:T(8,128)(2,1)}, u32[]{:S(2)}, u32[]{:S(2)}) %collective-permute-start.2) | collective-permute-done | bytes 131104 | tf_op jit(solution)/shard_map/ppermute | solution.py:29
  31.3 1.0 fusion.37
  32.3 0.3 collective-permute-start.3
  32.5 2.1 %collective-permute-done.12 = bf16[8,2,8,1024]{3,0,2,1:T(8,128)(2,1)} collective-permute-done((bf16[8,2,8,1024]{3,0,2,1:T(8,128)(2,1)S(1)}, bf16[8,2,8,1024]{3,0,2,1:T(8,128)(2,1)}, u32[]{:S(2)}, u32[]{:S(2)}) %collective-permute-start.12) | collective-permute-done | bytes 262176 | tf_op jit(solution)/shard_map/ppermute | solution.py:29
  34.6 1.9 %fusion.28 = bf16[8,2,8,1024]{3,0,2,1:T(8,128)(2,1)} fusion(f32[4,8,2,8,1024]{4,1,3,2,0:T(8,128)} %copy-done.1, s32[]{:T(128)S(6)} %select_n.289, bf16[8,2,8,1024]{3,0,2,1:T(8,128)(2,1)} %collective-permute-done.12), kind=kLoop, calls=%fused_computation.35 | loop fusion | flops 393216 | bytes 1048580 | tf_op jit(solution)/shard_map/convert_element_type | solution.py:29
  36.5 0.3 collective-permute-start.13
  36.8 1.2 %constant_dynamic-slice_fusion = f32[16,64,16]{2,1,0:T(8,128)S(1)} fusion(f32[16,64,64]{2,1,0:T(8,128)} %param.10, s32[]{:T(128)S(6)} %select_n.296), kind=kLoop, calls=%fused_computation.175 | loop fusion | bytes 131076 | tf_op jit(solution)/shard_map/dynamic_slice | solution.py:110
  38.8 1.7 %fusion.36 = bf16[4,2,8,1024]{3,2,1,0:T(8,128)(2,1)} fusion(f32[1,4,2,8,1024]{4,0,3,2,1:T(1,128)} %get-tuple-element.10, bf16[4,2,8,1024]{3,2,1,0:T(8,128)(2,1)} %collective-permute-done.3), kind=kLoop, calls=%fused_computation.49 | loop fusion | flops 196608 | bytes 524288 | tf_op jit(solution)/shard_map/convert_element_type | solution.py:29
  40.5 1.8 %collective-permute-start.4 = (bf16[4,2,8,1024]{3,2,1,0:T(8,128)(2,1)}, bf16[4,2,8,1024]{3,2,1,0:T(8,128)(2,1)}, u32[]{:S(2)}, u32[]{:S(2)}) collective-permute-start(bf16[4,2,8,1024]{3,2,1,0:T(8,128)(2,1)} %fusion.36), channel_id=1, source_target_pairs={{0,8},{8,16},{16,24},{24,32},{32,40},{40,48},{48,56},{56,0},{1,9},... | collective-permute-start | bytes 393224 | tf_op jit(solution)/shard_map/ppermute | solution.py:29
  42.3 2.5 %collective-permute-done.13 = bf16[8,2,8,1024]{3,0,2,1:T(8,128)(2,1)} collective-permute-done((bf16[8,2,8,1024]{3,0,2,1:T(8,128)(2,1)}, bf16[8,2,8,1024]{3,0,2,1:T(8,128)(2,1)}, u32[]{:S(2)}, u32[]{:S(2)}) %collective-permute-start.13) | collective-permute-done | bytes 262176 | tf_op jit(solution)/shard_map/ppermute | solution.py:29
  44.9 1.9 %fusion.27 = bf16[8,2,8,1024]{3,0,2,1:T(8,128)(2,1)} fusion(f32[4,8,2,8,1024]{4,1,3,2,0:T(8,128)} %copy-done.1, s32[]{:T(128)S(6)} %select_n.291, bf16[8,2,8,1024]{3,0,2,1:T(8,128)(2,1)} %collective-permute-done.13), kind=kLoop, calls=%fused_computation.33 | loop fusion | flops 393216 | bytes 1048580 | tf_op jit(solution)/shard_map/convert_element_type | solution.py:29
  46.9 1.0 copy.13
  47.9 1.7 %copy.14 = f32[16,16,16]{1,2,0:T(8,128)} copy(f32[16,16,16]{2,1,0:T(8,128)} %bitcast.219) | data formatting | bytes 32768 | tf_op jit(solution)/shard_map/jit(_where)/broadcast_in_dim | solution.py:93
  49.5 1.0 fusion.35
  50.6 2.2 %collective-permute-start.5 = (bf16[4,2,8,1024]{3,2,1,0:T(8,128)(2,1)S(1)}, bf16[4,2,8,1024]{3,2,1,0:T(8,128)(2,1)S(1)}, u32[]{:S(2)}, u32[]{:S(2)}) collective-permute-start(bf16[4,2,8,1024]{3,2,1,0:T(8,128)(2,1)S(1)} %fusion.35), channel_id=1, source_target_pairs={{0,8},{8,16},{16,24},{24,32},{32,40},{40,48},{48,56},{56,0},{1,9},... | collective-permute-start | bytes 393224 | tf_op jit(solution)/shard_map/ppermute | solution.py:29
  52.7 1.9 %collective-permute-done.14 = bf16[8,2,8,1024]{3,0,2,1:T(8,128)(2,1)} collective-permute-done((bf16[8,2,8,1024]{3,0,2,1:T(8,128)(2,1)}, bf16[8,2,8,1024]{3,0,2,1:T(8,128)(2,1)}, u32[]{:S(2)}, u32[]{:S(2)}) %collective-permute-start.14) | collective-permute-done | bytes 262176 | tf_op jit(solution)/shard_map/ppermute | solution.py:29
  54.7 1.2 %bitcast_add_fusion.2 = f32[8,2,8,1024]{3,0,2,1:T(8,128)S(1)} fusion(f32[4,8,2,8,1024]{4,1,3,2,0:T(8,128)} %copy-done.1, s32[]{:T(128)S(6)} %select_n.293, bf16[8,2,8,1024]{3,0,2,1:T(8,128)(2,1)} %collective-permute-done.14), kind=kLoop, calls=%fused_computation.31 | loop fusion | flops 262144 | bytes 1310724 | tf_op jit(solution)/shard_map/add | solution.py:30
  55.9 2.0 %collective-permute-start.15 = (bf16[2,8,1024]{2,1,0:T(8,128)(2,1)S(1)}, bf16[2,8,1024]{2,1,0:T(8,128)(2,1)S(1)}, u32[]{:S(2)}, u32[]{:S(2)}) collective-permute-start(bf16[2,8,1024]{2,1,0:T(8,128)(2,1)S(1)} %bitcast.220), channel_id=1, source_target_pairs={{0,8},{8,16},{16,24},{24,32},{32,40},{40,48},{48,56},{56,0},{1,9},... | collective-permute-start | bytes 98312 | tf_op jit(solution)/shard_map/ppermute | solution.py:29
  57.9 1.1 %constant_dynamic-slice_fusion.7 = (f32[1,2,8,1024]{3,0,2,1:T(1,128)S(1)}, f32[1,2,8,1024]{3,0,2,1:T(1,128)}, f32[1,2,8,1024]{3,0,2,1:T(1,128)S(1)}, f32[1,2,8,1...) fusion(f32[8,2,8,1024]{3,0,2,1:T(8,128)S(1)} %bitcast_add_fusio, ...), kind=kLoop, calls=%fused_computation.182 | loop fusion | bytes 917532 | tf_op jit(solution)/shard_map/jit(dynamic_index_in_dim)/dynamic_slice | solution.py:25
  59.0 2.3 %collective-permute-done.15 = bf16[2,8,1024]{2,1,0:T(8,128)(2,1)S(1)} collective-permute-done((bf16[2,8,1024]{2,1,0:T(8,128)(2,1)S(1)}, bf16[2,8,1024]{2,1,0:T(8,128)(2,1)S(1)}, u32[]{:S(2)}, u32[]{:S(2)}) %collective-permute-start.15) | collective-permute-done | bytes 32800 | tf_op jit(solution)/shard_map/ppermute | solution.py:29
  61.3 1.7 %collective-permute-start.16 = (bf16[2,8,1024]{2,1,0:T(8,128)(2,1)S(1)}, bf16[2,8,1024]{2,1,0:T(8,128)(2,1)S(1)}, u32[]{:S(2)}, u32[]{:S(2)}) collective-permute-start(bf16[2,8,1024]{2,1,0:T(8,128)(2,1)S(1)} %fusion.84), channel_id=1, source_target_pairs={{0,8},{8,16},{16,24},{24,32},{32,40},{40,48},{48,56},{56,0},{1,9},... | collective-permute-start | bytes 98312 | tf_op jit(solution)/shard_map/ppermute | solution.py:29
  63.0 2.6 %collective-permute-start.6 = (bf16[4,2,8,1024]{3,2,1,0:T(8,128)(2,1)S(1)}, bf16[4,2,8,1024]{3,2,1,0:T(8,128)(2,1)S(1)}, u32[]{:S(2)}, u32[]{:S(2)}) collective-permute-start(bf16[4,2,8,1024]{3,2,1,0:T(8,128)(2,1)S(1)} %fusion.34), channel_id=1, source_target_pairs={{0,8},{8,16},{16,24},{24,32},{32,40},{40,48},{48,56},{56,0},{1,9},... | collective-permute-start | bytes 393224 | tf_op jit(solution)/shard_map/ppermute | solution.py:29
  65.6 1.0 collective-permute-done.16
  66.6 0.7 collective-permute-start.17
  67.3 3.2 %collective-permute-done.6 = bf16[4,2,8,1024]{3,2,1,0:T(8,128)(2,1)S(1)} collective-permute-done((bf16[4,2,8,1024]{3,2,1,0:T(8,128)(2,1)S(1)}, bf16[4,2,8,1024]{3,2,1,0:T(8,128)(2,1)S(1)}, u32[]{:S(2)}, u32[]{:S(2)}) %collective-permute-start.6) | collective-permute-done | bytes 131104 | tf_op jit(solution)/shard_map/ppermute | solution.py:29
  70.5 0.5 collective-permute-start.7
  71.0 0.8 collective-permute-done.17
  71.8 0.9 collective-permute-start.18
  72.7 4.1 %collective-permute-done.7 = bf16[4,2,8,1024]{3,2,1,0:T(8,128)(2,1)S(1)} collective-permute-done((bf16[4,2,8,1024]{3,2,1,0:T(8,128)(2,1)S(1)}, bf16[4,2,8,1024]{3,2,1,0:T(8,128)(2,1)S(1)}, u32[]{:S(2)}, u32[]{:S(2)}) %collective-permute-start.7) | collective-permute-done | bytes 131104 | tf_op jit(solution)/shard_map/ppermute | solution.py:29
  77.3 4.8 %collective-permute-done.8 = bf16[2,8,1024]{2,1,0:T(8,128)(2,1)S(1)} collective-permute-done((bf16[2,8,1024]{2,1,0:T(8,128)(2,1)S(1)}, bf16[2,8,1024]{2,1,0:T(8,128)(2,1)S(1)}, u32[]{:S(2)}, u32[]{:S(2)}) %collective-permute-start.8) | collective-permute-done | bytes 32800 | tf_op jit(solution)/shard_map/ppermute | solution.py:29
  82.4 0.3 collective-permute-start.20
  82.7 4.6 %collective-permute-done.9 = bf16[2,8,1024]{2,1,0:T(8,128)(2,1)S(1)} collective-permute-done((bf16[2,8,1024]{2,1,0:T(8,128)(2,1)S(1)}, bf16[2,8,1024]{2,1,0:T(8,128)(2,1)S(1)}, u32[]{:S(2)}, u32[]{:S(2)}) %collective-permute-start.9) | collective-permute-done | bytes 32800 | tf_op jit(solution)/shard_map/ppermute | solution.py:29
  87.4 0.4 collective-permute-done.20
  87.9 4.6 %collective-permute-done.10 = bf16[2,8,1024]{2,1,0:T(8,128)(2,1)S(1)} collective-permute-done((bf16[2,8,1024]{2,1,0:T(8,128)(2,1)S(1)}, bf16[2,8,1024]{2,1,0:T(8,128)(2,1)S(1)}, u32[]{:S(2)}, u32[]{:S(2)}) %collective-permute-start.10) | collective-permute-done | bytes 32800 | tf_op jit(solution)/shard_map/ppermute | solution.py:29
  92.7 0.3 collective-permute-done.21
  93.2 0.2 maximum_bitcast_fusion
  93.6 1.4 %convolution_bitcast_fusion = f32[1,16,16,8,128]{4,3,2,1,0:T(8,128)S(1)} fusion(f32[16,16,16]{1,2,0:T(8,128)} %copy.14, s32[16,16,16]{1,2,0:T(8,128)S(1)} %copy.13, bf16[16,16,128,1]{2,1,0,3:T(8,128)(2,1)S(1)} %reshape.761), kind=kOutput, calls=%fused_computation.16 | convolution fusion | flops 25231360 | bytes 1146880 | tf_op jit(solution)/shard_map/mfblp,mfbi->mflpi/dot_general | solution.py:98
  94.9 0.4 slice_bitcast_fusion
  95.3 1.2 %convolution_bitcast_fusion.1 = f32[1,16,16,128]{3,1,2,0:T(8,128)S(1)} fusion(bf16[16,8,64,128]{3,2,1,0:T(8,128)(2,1)S(1)} %copy-done, f32[16,16,8,64]{3,2,1,0:T(8,128)S(1)} %get-tuple-element.12), kind=kOutput, calls=%fused_computation.19 | convolution fusion | flops 100663296 | bytes 2752512 | tf_op jit(solution)/shard_map/mflpi,lpij->mflj/dot_general | solution.py:104
  96.5 1.2 %convolution_bitcast_fusion.2 = f32[1,16,16,128]{3,1,2,0:T(8,128)S(1)} fusion(bf16[16,8,64,128]{3,2,1,0:T(8,128)(2,1)S(1)} %copy-done, f32[16,16,8,64]{3,2,1,0:T(8,128)S(1)} %get-tuple-element.13), kind=kOutput, calls=%fused_computation.20 | convolution fusion | flops 100663296 | bytes 2752512 | tf_op jit(solution)/shard_map/mflpi,lpij->mflj/dot_general | solution.py:103
  98.0 0.5 collective-permute-start.22
  98.5 1.6 %collective-permute-start.24 = (bf16[1,16,16,128]{3,1,2,0:T(8,128)(2,1)S(1)}, bf16[1,16,16,128]{3,1,2,0:T(8,128)(2,1)S(1)}, u32[]{:S(2)}, u32[]{:S(2)}) collective-permute-start(bf16[1,16,16,128]{3,1,2,0:T(8,128)(2,1)S(1)} %pad_maximum_fusion), channel_id=1, source_target_pairs={{0,3},{1,0},{2,1},{3,2},{4,7},{5,4},{6,5},{7,6},{8,11},{9,8},{10,9... | collective-permute-start | bytes 196616 | tf_op jit(solution)/shard_map/ppermute | solution.py:117
  100.1 1.3 %collective-permute-start.23 = (bf16[1,16,16,128]{3,1,2,0:T(8,128)(2,1)S(1)}, bf16[1,16,16,128]{3,1,2,0:T(8,128)(2,1)S(1)}, u32[]{:S(2)}, u32[]{:S(2)}) collective-permute-start(bf16[1,16,16,128]{3,1,2,0:T(8,128)(2,1)S(1)} %pad_maximum_fusion), channel_id=1, source_target_pairs={{0,2},{1,3},{2,0},{3,1},{4,6},{5,7},{6,4},{7,5},{8,10},{9,11},{10,... | collective-permute-start | bytes 196616 | tf_op jit(solution)/shard_map/ppermute | solution.py:117
  101.5 0.3 fusion.45
  101.8 0.6 collective-permute-done.22
  102.4 0.3 convolution_add_fusion.1
  102.7 1.3 %collective-permute-done.24 = bf16[1,16,16,128]{3,1,2,0:T(8,128)(2,1)S(1)} collective-permute-done((bf16[1,16,16,128]{3,1,2,0:T(8,128)(2,1)S(1)}, bf16[1,16,16,128]{3,1,2,0:T(8,128)(2,1)S(1)}, u32[]{:S(2)}, u32[]{:S(2)}) %collective-permute-start.24) | collective-permute-done | bytes 65568 | tf_op jit(solution)/shard_map/ppermute | solution.py:117
  104.0 0.3 fusion.41
  104.3 1.6 %collective-permute-done.23 = bf16[1,16,16,128]{3,1,2,0:T(8,128)(2,1)S(1)} collective-permute-done((bf16[1,16,16,128]{3,1,2,0:T(8,128)(2,1)S(1)}, bf16[1,16,16,128]{3,1,2,0:T(8,128)(2,1)S(1)}, u32[]{:S(2)}, u32[]{:S(2)}) %collective-permute-start.23) | collective-permute-done | bytes 65568 | tf_op jit(solution)/shard_map/ppermute | solution.py:117
  105.9 0.3 fusion.23
  106.2 0.7 copy.20
  (51 shorter events, 2.3 us)
Async XLA Ops:
  0.0 95.3 %copy-start = (bf16[16,8,64,128]{3,2,1,0:T(8,128)(2,1)S(1)}, bf16[16,8,64,128]{3,2,1,0:T(8,128)(2,1)}, u32[]{:S(2)}) copy-start(bf16[16,8,64,128]{3,2,1,0:T(8,128)(2,1)} %param.7) | copy-start | bytes 6291460
  5.0 5.4 %collective-permute-start = (bf16[8,4,2,8,1024]{4,0,3,2,1:T(8,128)(2,1)}, bf16[8,4,2,8,1024]{4,0,3,2,1:T(8,128)(2,1)S(1)}, u32[]{:S(2)}, u32[]{:S(2)}) collective-permute-start(bf16[8,4,2,8,1024]{4,0,3,2,1:T(8,128)(2,1)} %bitcast_convert_fusion.1), channel_id=1, source_target_pairs={{0,4},{4,0},{1,5},{5,1},{2,6},{6,2},{3,7},{7,3},{8,12},{12,8},{9,1... | collective-permute-start | bytes 3145736 | tf_op jit(solution)/shard_map/ppermute | solution.py:60
  9.9 6.5 %collective-permute-start.11 = (bf16[4,8,2,8,1024]{4,1,3,2,0:T(8,128)(2,1)}, bf16[4,8,2,8,1024]{4,1,3,2,0:T(8,128)(2,1)}, u32[]{:S(2)}, u32[]{:S(2)}) collective-permute-start(bf16[4,8,2,8,1024]{4,1,3,2,0:T(8,128)(2,1)} %bitcast_convert_fusion), channel_id=1, source_target_pairs={{0,4},{4,0},{1,5},{5,1},{2,6},{6,2},{3,7},{7,3},{8,12},{12,8},{9,1... | collective-permute-start | bytes 3145736 | tf_op jit(solution)/shard_map/ppermute | solution.py:60
  14.4 9.6 %collective-permute-start.1 = (bf16[4,2,8,1024]{3,2,1,0:T(8,128)(2,1)S(1)}, bf16[4,2,8,1024]{3,2,1,0:T(8,128)(2,1)S(1)}, u32[]{:S(2)}, u32[]{:S(2)}) collective-permute-start(bf16[4,2,8,1024]{3,2,1,0:T(8,128)(2,1)S(1)} %bitcast.217), channel_id=1, source_target_pairs={{0,8},{8,16},{16,24},{24,32},{32,40},{40,48},{48,56},{56,0},{1,9},... | collective-permute-start | bytes 393224 | tf_op jit(solution)/shard_map/ppermute | solution.py:29
  20.5 5.0 %copy-start.1 = (f32[4,8,2,8,1024]{4,1,3,2,0:T(8,128)}, f32[4,8,2,8,1024]{4,1,3,2,0:T(8,128)S(1)}, u32[]{:S(2)}) copy-start(f32[4,8,2,8,1024]{4,1,3,2,0:T(8,128)S(1)} %bitcast_add_fusion) | copy-start | bytes 6291460
  24.1 7.2 %collective-permute-start.2 = (bf16[4,2,8,1024]{3,2,1,0:T(8,128)(2,1)S(1)}, bf16[4,2,8,1024]{3,2,1,0:T(8,128)(2,1)}, u32[]{:S(2)}, u32[]{:S(2)}) collective-permute-start(bf16[4,2,8,1024]{3,2,1,0:T(8,128)(2,1)S(1)} %fusion.38), channel_id=1, source_target_pairs={{0,8},{8,16},{16,24},{24,32},{32,40},{40,48},{48,56},{56,0},{1,9},... | collective-permute-start | bytes 393224 | tf_op jit(solution)/shard_map/ppermute | solution.py:29
  25.5 9.1 %collective-permute-start.12 = (bf16[8,2,8,1024]{3,0,2,1:T(8,128)(2,1)S(1)}, bf16[8,2,8,1024]{3,0,2,1:T(8,128)(2,1)}, u32[]{:S(2)}, u32[]{:S(2)}) collective-permute-start(bf16[8,2,8,1024]{3,0,2,1:T(8,128)(2,1)S(1)} %fusion.32), channel_id=1, source_target_pairs={{0,64},{64,128},{128,192},{192,0},{1,65},{65,129},{129,193},{193,1... | collective-permute-start | bytes 786440 | tf_op jit(solution)/shard_map/ppermute | solution.py:29
  32.3 6.5 %collective-permute-start.3 = (bf16[4,2,8,1024]{3,2,1,0:T(8,128)(2,1)S(1)}, bf16[4,2,8,1024]{3,2,1,0:T(8,128)(2,1)}, u32[]{:S(2)}, u32[]{:S(2)}) collective-permute-start(bf16[4,2,8,1024]{3,2,1,0:T(8,128)(2,1)S(1)} %fusion.37), channel_id=1, source_target_pairs={{0,8},{8,16},{16,24},{24,32},{32,40},{40,48},{48,56},{56,0},{1,9},... | collective-permute-start | bytes 393224 | tf_op jit(solution)/shard_map/ppermute | solution.py:29
  36.5 8.4 %collective-permute-start.13 = (bf16[8,2,8,1024]{3,0,2,1:T(8,128)(2,1)}, bf16[8,2,8,1024]{3,0,2,1:T(8,128)(2,1)}, u32[]{:S(2)}, u32[]{:S(2)}) collective-permute-start(bf16[8,2,8,1024]{3,0,2,1:T(8,128)(2,1)} %fusion.28), channel_id=1, source_target_pairs={{0,64},{64,128},{128,192},{192,0},{1,65},{65,129},{129,193},{193,1... | collective-permute-start | bytes 786440 | tf_op jit(solution)/shard_map/ppermute | solution.py:29
  40.5 9.0 %collective-permute-start.4 = (bf16[4,2,8,1024]{3,2,1,0:T(8,128)(2,1)}, bf16[4,2,8,1024]{3,2,1,0:T(8,128)(2,1)}, u32[]{:S(2)}, u32[]{:S(2)}) collective-permute-start(bf16[4,2,8,1024]{3,2,1,0:T(8,128)(2,1)} %fusion.36), channel_id=1, source_target_pairs={{0,8},{8,16},{16,24},{24,32},{32,40},{40,48},{48,56},{56,0},{1,9},... | collective-permute-start | bytes 393224 | tf_op jit(solution)/shard_map/ppermute | solution.py:29
  46.8 7.9 %collective-permute-start.14 = (bf16[8,2,8,1024]{3,0,2,1:T(8,128)(2,1)}, bf16[8,2,8,1024]{3,0,2,1:T(8,128)(2,1)}, u32[]{:S(2)}, u32[]{:S(2)}) collective-permute-start(bf16[8,2,8,1024]{3,0,2,1:T(8,128)(2,1)} %fusion.27), channel_id=1, source_target_pairs={{0,64},{64,128},{128,192},{192,0},{1,65},{65,129},{129,193},{193,1... | collective-permute-start | bytes 786440 | tf_op jit(solution)/shard_map/ppermute | solution.py:29
  50.6 12.4 %collective-permute-start.5 = (bf16[4,2,8,1024]{3,2,1,0:T(8,128)(2,1)S(1)}, bf16[4,2,8,1024]{3,2,1,0:T(8,128)(2,1)S(1)}, u32[]{:S(2)}, u32[]{:S(2)}) collective-permute-start(bf16[4,2,8,1024]{3,2,1,0:T(8,128)(2,1)S(1)} %fusion.35), channel_id=1, source_target_pairs={{0,8},{8,16},{16,24},{24,32},{32,40},{40,48},{48,56},{56,0},{1,9},... | collective-permute-start | bytes 393224 | tf_op jit(solution)/shard_map/ppermute | solution.py:29
  55.9 5.3 %collective-permute-start.15 = (bf16[2,8,1024]{2,1,0:T(8,128)(2,1)S(1)}, bf16[2,8,1024]{2,1,0:T(8,128)(2,1)S(1)}, u32[]{:S(2)}, u32[]{:S(2)}) collective-permute-start(bf16[2,8,1024]{2,1,0:T(8,128)(2,1)S(1)} %bitcast.220), channel_id=1, source_target_pairs={{0,8},{8,16},{16,24},{24,32},{32,40},{40,48},{48,56},{56,0},{1,9},... | collective-permute-start | bytes 98312 | tf_op jit(solution)/shard_map/ppermute | solution.py:29
  61.3 5.3 %collective-permute-start.16 = (bf16[2,8,1024]{2,1,0:T(8,128)(2,1)S(1)}, bf16[2,8,1024]{2,1,0:T(8,128)(2,1)S(1)}, u32[]{:S(2)}, u32[]{:S(2)}) collective-permute-start(bf16[2,8,1024]{2,1,0:T(8,128)(2,1)S(1)} %fusion.84), channel_id=1, source_target_pairs={{0,8},{8,16},{16,24},{24,32},{32,40},{40,48},{48,56},{56,0},{1,9},... | collective-permute-start | bytes 98312 | tf_op jit(solution)/shard_map/ppermute | solution.py:29
  63.0 30.0 %copy-start.2 = (f32[1,2,8,1024]{3,0,2,1:T(1,128)S(1)}, f32[1,2,8,1024]{3,0,2,1:T(1,128)}, u32[]{:S(2)}) copy-start(f32[1,2,8,1024]{3,0,2,1:T(1,128)} %get-tuple-element.15) | copy-start | bytes 196612
  63.0 7.5 %collective-permute-start.6 = (bf16[4,2,8,1024]{3,2,1,0:T(8,128)(2,1)S(1)}, bf16[4,2,8,1024]{3,2,1,0:T(8,128)(2,1)S(1)}, u32[]{:S(2)}, u32[]{:S(2)}) collective-permute-start(bf16[4,2,8,1024]{3,2,1,0:T(8,128)(2,1)S(1)} %fusion.34), channel_id=1, source_target_pairs={{0,8},{8,16},{16,24},{24,32},{32,40},{40,48},{48,56},{56,0},{1,9},... | collective-permute-start | bytes 393224 | tf_op jit(solution)/shard_map/ppermute | solution.py:29
  66.6 5.2 %collective-permute-start.17 = (bf16[2,8,1024]{2,1,0:T(8,128)(2,1)S(1)}, bf16[2,8,1024]{2,1,0:T(8,128)(2,1)S(1)}, u32[]{:S(2)}, u32[]{:S(2)}) collective-permute-start(bf16[2,8,1024]{2,1,0:T(8,128)(2,1)S(1)} %fusion.83), channel_id=1, source_target_pairs={{0,8},{8,16},{16,24},{24,32},{32,40},{40,48},{48,56},{56,0},{1,9},... | collective-permute-start | bytes 98312 | tf_op jit(solution)/shard_map/ppermute | solution.py:29
  70.5 6.3 %collective-permute-start.7 = (bf16[4,2,8,1024]{3,2,1,0:T(8,128)(2,1)S(1)}, bf16[4,2,8,1024]{3,2,1,0:T(8,128)(2,1)S(1)}, u32[]{:S(2)}, u32[]{:S(2)}) collective-permute-start(bf16[4,2,8,1024]{3,2,1,0:T(8,128)(2,1)S(1)} %fusion.33), channel_id=1, source_target_pairs={{0,8},{8,16},{16,24},{24,32},{32,40},{40,48},{48,56},{56,0},{1,9},... | collective-permute-start | bytes 393224 | tf_op jit(solution)/shard_map/ppermute | solution.py:29
  71.8 5.3 %collective-permute-start.18 = (bf16[2,8,1024]{2,1,0:T(8,128)(2,1)S(1)}, bf16[2,8,1024]{2,1,0:T(8,128)(2,1)S(1)}, u32[]{:S(2)}, u32[]{:S(2)}) collective-permute-start(bf16[2,8,1024]{2,1,0:T(8,128)(2,1)S(1)} %fusion.82), channel_id=1, source_target_pairs={{0,8},{8,16},{16,24},{24,32},{32,40},{40,48},{48,56},{56,0},{1,9},... | collective-permute-start | bytes 98312 | tf_op jit(solution)/shard_map/ppermute | solution.py:29
  76.9 5.2 %collective-permute-start.8 = (bf16[2,8,1024]{2,1,0:T(8,128)(2,1)S(1)}, bf16[2,8,1024]{2,1,0:T(8,128)(2,1)S(1)}, u32[]{:S(2)}, u32[]{:S(2)}) collective-permute-start(bf16[2,8,1024]{2,1,0:T(8,128)(2,1)S(1)} %fusion.92), channel_id=1, source_target_pairs={{0,64},{64,128},{128,192},{192,0},{1,65},{65,129},{129,193},{193,1... | collective-permute-start | bytes 98312 | tf_op jit(solution)/shard_map/ppermute | solution.py:29
  77.2 5.2 %collective-permute-start.19 = (bf16[2,8,1024]{2,1,0:T(8,128)(2,1)S(1)}, bf16[2,8,1024]{2,1,0:T(8,128)(2,1)S(1)}, u32[]{:S(2)}, u32[]{:S(2)}) collective-permute-start(bf16[2,8,1024]{2,1,0:T(8,128)(2,1)S(1)} %fusion.81), channel_id=1, source_target_pairs={{0,8},{8,16},{16,24},{24,32},{32,40},{40,48},{48,56},{56,0},{1,9},... | collective-permute-start | bytes 98312 | tf_op jit(solution)/shard_map/ppermute | solution.py:29
  82.1 5.2 %collective-permute-start.9 = (bf16[2,8,1024]{2,1,0:T(8,128)(2,1)S(1)}, bf16[2,8,1024]{2,1,0:T(8,128)(2,1)S(1)}, u32[]{:S(2)}, u32[]{:S(2)}) collective-permute-start(bf16[2,8,1024]{2,1,0:T(8,128)(2,1)S(1)} %fusion.91), channel_id=1, source_target_pairs={{0,64},{64,128},{128,192},{192,0},{1,65},{65,129},{129,193},{193,1... | collective-permute-start | bytes 98312 | tf_op jit(solution)/shard_map/ppermute | solution.py:29
  82.4 5.4 %collective-permute-start.20 = (bf16[2,8,1024]{2,1,0:T(8,128)(2,1)S(1)}, bf16[2,8,1024]{2,1,0:T(8,128)(2,1)S(1)}, u32[]{:S(2)}, u32[]{:S(2)}) collective-permute-start(bf16[2,8,1024]{2,1,0:T(8,128)(2,1)S(1)} %fusion.80), channel_id=1, source_target_pairs={{0,8},{8,16},{16,24},{24,32},{32,40},{40,48},{48,56},{56,0},{1,9},... | collective-permute-start | bytes 98312 | tf_op jit(solution)/shard_map/ppermute | solution.py:29
  87.3 5.2 %collective-permute-start.10 = (bf16[2,8,1024]{2,1,0:T(8,128)(2,1)S(1)}, bf16[2,8,1024]{2,1,0:T(8,128)(2,1)S(1)}, u32[]{:S(2)}, u32[]{:S(2)}) collective-permute-start(bf16[2,8,1024]{2,1,0:T(8,128)(2,1)S(1)} %fusion.90), channel_id=1, source_target_pairs={{0,64},{64,128},{128,192},{192,0},{1,65},{65,129},{129,193},{193,1... | collective-permute-start | bytes 98312 | tf_op jit(solution)/shard_map/ppermute | solution.py:29
  87.8 5.2 %collective-permute-start.21 = (bf16[2,8,1024]{2,1,0:T(8,128)(2,1)S(1)}, bf16[2,8,1024]{2,1,0:T(8,128)(2,1)S(1)}, u32[]{:S(2)}, u32[]{:S(2)}) collective-permute-start(bf16[2,8,1024]{2,1,0:T(8,128)(2,1)S(1)} %fusion.79), channel_id=1, source_target_pairs={{0,8},{8,16},{16,24},{24,32},{32,40},{40,48},{48,56},{56,0},{1,9},... | collective-permute-start | bytes 98312 | tf_op jit(solution)/shard_map/ppermute | solution.py:29
  98.0 4.3 %collective-permute-start.22 = (bf16[1,16,16,128]{3,1,2,0:T(8,128)(2,1)S(1)}, bf16[1,16,16,128]{3,1,2,0:T(8,128)(2,1)S(1)}, u32[]{:S(2)}, u32[]{:S(2)}) collective-permute-start(bf16[1,16,16,128]{3,1,2,0:T(8,128)(2,1)S(1)} %pad_maximum_fusion), channel_id=1, source_target_pairs={{0,1},{1,2},{2,3},{3,0},{4,5},{5,6},{6,7},{7,4},{8,9},{9,10},{10,1... | collective-permute-start | bytes 196616 | tf_op jit(solution)/shard_map/ppermute | solution.py:117
  98.5 5.5 %collective-permute-start.24 = (bf16[1,16,16,128]{3,1,2,0:T(8,128)(2,1)S(1)}, bf16[1,16,16,128]{3,1,2,0:T(8,128)(2,1)S(1)}, u32[]{:S(2)}, u32[]{:S(2)}) collective-permute-start(bf16[1,16,16,128]{3,1,2,0:T(8,128)(2,1)S(1)} %pad_maximum_fusion), channel_id=1, source_target_pairs={{0,3},{1,0},{2,1},{3,2},{4,7},{5,4},{6,5},{7,6},{8,11},{9,8},{10,9... | collective-permute-start | bytes 196616 | tf_op jit(solution)/shard_map/ppermute | solution.py:117
  100.1 5.8 %collective-permute-start.23 = (bf16[1,16,16,128]{3,1,2,0:T(8,128)(2,1)S(1)}, bf16[1,16,16,128]{3,1,2,0:T(8,128)(2,1)S(1)}, u32[]{:S(2)}, u32[]{:S(2)}) collective-permute-start(bf16[1,16,16,128]{3,1,2,0:T(8,128)(2,1)S(1)} %pad_maximum_fusion), channel_id=1, source_target_pairs={{0,2},{1,3},{2,0},{3,1},{4,6},{5,7},{6,4},{7,5},{8,10},{9,11},{10,... | collective-permute-start | bytes 196616 | tf_op jit(solution)/shard_map/ppermute | solution.py:117

commit v6 on v4

--- a/solution.py
+++ b/solution.py
@@ -17,14 +17,14 @@
     return (jnp.cos(angle), jnp.sin(angle))
 
 
-def ring_reduce_scatter(x, axis, n):
+def ring_reduce_scatter(x, axis, n, first=None):
     i = lax.axis_index(axis)
     fwd = [(j, (j + 1) % n) for j in range(n)]
 
     def take(a, k):
         return lax.dynamic_index_in_dim(a, k % n, 0, keepdims=False)
 
-    s = take(x, i - 1)
+    s = take(x, i - 1) if first is None else first
     for k in range(n - 1):
         got = lax.ppermute(s.astype(jnp.bfloat16), axis, fwd)
         s = got.astype(jnp.float32) + take(x, i - k - 2)
@@ -53,14 +53,16 @@
         table = dft_table(mode_step * rows, time_index, sidereal_period, norm_factor)
         out = jnp.einsum("rdct,fctb->rdfb", table, part, precision=lax.Precision.HIGH)
         half_rows = ny * nz
-        got = lax.ppermute(out[:half_rows].astype(jnp.bfloat16), "tc", [(0, 1), (1, 0)])
-        y = out[half_rows:] + got.astype(jnp.float32)
-        if z_major:
-            y = y.reshape(nz, ny, *y.shape[1:])
-            y = ring_reduce_scatter(ring_reduce_scatter(y, "tz", nz), "ty", ny)
-        else:
-            y = y.reshape(ny, nz, *y.shape[1:])
-            y = ring_reduce_scatter(ring_reduce_scatter(y, "ty", ny), "tz", nz)
+        ax1, n1, ax2, n2 = ("tz", nz, "ty", ny) if z_major else ("ty", ny, "tz", nz)
+        other = out[:half_rows].reshape(n1, n2, *out.shape[1:])
+        mine = out[half_rows:].reshape(n1, n2, *out.shape[1:])
+        lead = (lax.axis_index(ax1) - 1) % n1
+        pair_swap = [(0, 1), (1, 0)]
+        head = lax.ppermute(lax.dynamic_index_in_dim(other, lead, 0, keepdims=False).astype(jnp.bfloat16), "tc", pair_swap)
+        rest = lax.ppermute(other.astype(jnp.bfloat16), "tc", pair_swap)
+        first = lax.dynamic_index_in_dim(mine, lead, 0, keepdims=False) + head.astype(jnp.float32)
+        y = mine + rest.astype(jnp.float32)
+        y = ring_reduce_scatter(ring_reduce_scatter(y, ax1, n1, first=first), ax2, n2)
         halves.append(y)
     return jnp.concatenate(halves, axis=1)
 

time: 108 us -> 123 us (1.14)
  the two profiles are of different devices: /device:TPU:16 before, /device:TPU:6 now
where the time goes in v6:
time: 123 us; the launch traced here: 122 us
  waiting for transfers between devices  41.5 us (34%)
  starting transfers between devices  29.6 us (24%)
  local copies, waits for them, and re-layouts  23.5 us (19%)
  other arithmetic  13.7 us (11%)
  matrix products  12.6 us (10%)
  between operations  1.31 us (1%)
    ppermute x20, waiting for transfers between devices, ring_reduce_scatter(): got = lax.ppermute(s.astype(jnp.bfloat16), axis, fwd)  38 us
    ppermute x20, starting transfers between devices, ring_reduce_scatter(): got = lax.ppermute(s.astype(jnp.bfloat16), axis, fwd)  25 us
    dot_general x2, matrix products, spectra_of(): jnp.einsum('rdct,fctb->rdfb', table, part, precision=lax.Precision.HIGH)  8.47 us
    convert_element_type x18, other arithmetic, ring_reduce_scatter(): got = lax.ppermute(s.astype(jnp.bfloat16), axis, fwd)  7.37 us
    unnamed x22, local copies, waits for them, and re-layouts  5.73 us
    reshape x2, local copies, waits for them, and re-layouts, spectra_of(): mine = out[half_rows:].reshape(n1, n2, *out.shape[1:])  4.78 us
    add x2, other arithmetic, spectra_of(): y = mine + rest.astype(jnp.float32)  3.91 us
    ppermute x3, waiting for transfers between devices, local(): lax.ppermute(weights_bf, 'freq', [(j, (j + s) % fr_count) for j in range(...  3.49 us
  transfers between devices with their start and end apart: 27, of which 18 were waited for; matrix products, arithmetic and copies ran while one was open for 27% of the time, Pallas kernels for 0%

profile of v6, /device:TPU:6, one launch (start us, length us, event | category | flops | bytes accessed | tf_op | source)
XLA Modules:
  0.0 122.2 jit_solution(6793403903255562949)
XLA Ops:
  0.9 4.2 %fusion.6 = f32[64,2,8,1024]{3,0,2,1:T(8,128)S(1)} fusion(f32[16,2,64,1024]{3,2,1,0:T(8,128)} %param.6, f32[64,1,2,64]{3,0,2,1:T(8,128)S(1)} %get-tuple-element.22, f32[64,1,2,64]{3,0,2,1:T(8,128)S(1)} %get-tuple-element.21), kind=kOutput, calls=%fused_computation.6 | convolution fusion | flops 805322752 | bytes 8454144 | tf_op jit(solution)/shard_map/rdct,fctb->rdfb/dot_general | solution.py:54
  5.1 2.0 %copy-done.2 = f32[64,2,8,1024]{3,0,2,1:T(8,128)} copy-done((f32[64,2,8,1024]{3,0,2,1:T(8,128)}, f32[64,2,8,1024]{3,0,2,1:T(8,128)S(1)}, u32[]{:S(2)}) %copy-start.2) | copy-done | bytes 4194328
  7.3 1.2 reshape.541
  8.5 1.0 constant_dynamic-slice_fusion.13
  9.5 0.6 collective-permute-start
  10.1 4.2 %fusion.9 = f32[64,2,8,1024]{3,0,2,1:T(8,128)S(1)} fusion(f32[16,2,64,1024]{3,2,1,0:T(8,128)} %param.6, f32[64,1,2,64]{3,0,2,1:T(8,128)S(1)} %get-tuple-element.24, f32[64,1,2,64]{3,0,2,1:T(8,128)S(1)} %get-tuple-element.23), kind=kOutput, calls=%fused_computation.7 | convolution fusion | flops 805322752 | bytes 8454144 | tf_op jit(solution)/shard_map/rdct,fctb->rdfb/dot_general | solution.py:54
  14.4 1.9 %copy-done.1 = f32[64,2,8,1024]{3,0,2,1:T(8,128)} copy-done((f32[64,2,8,1024]{3,0,2,1:T(8,128)}, f32[64,2,8,1024]{3,0,2,1:T(8,128)S(1)}, u32[]{:S(2)}) %copy-start.1) | copy-done | bytes 4194328
  16.3 1.2 slice_bitcast_fusion
  17.5 1.0 constant_dynamic-slice_fusion.4
  18.5 0.9 copy.72
  19.4 0.5 collective-permute-start.12
  19.9 1.9 %slice_bitcast_fusion.1 = f32[4,8,2,8,1024]{4,1,0,3,2:T(8,128)S(1)} fusion(f32[64,2,8,1024]{3,0,2,1:T(8,128)} %copy-done.1), kind=kLoop, calls=%fused_computation.9 | loop fusion | bytes 4194304 | tf_op jit(solution)/shard_map/reshape | solution.py:58
  22.0 0.8 copy-done.3
  22.9 1.5 %slice.48 = f32[32,2,8,1024]{3,0,2,1:T(8,128)} slice(f32[64,2,8,1024]{3,0,2,1:T(8,128)S(1)} %copy-done.3), slice={[32:64], [0:2], [0:8], [0:1024]} | slice | bytes 4194304 | tf_op jit(solution)/shard_map/slice | solution.py:58
  24.4 2.9 %reshape.540 = f32[8,4,2,8,1024]{4,1,0,3,2:T(4,128)} reshape(f32[32,2,8,1024]{3,0,2,1:T(8,128)} %slice.48) | data formatting | bytes 4194304 | tf_op jit(solution)/shard_map/reshape | solution.py:58
  27.3 1.0 constant_dynamic-slice_fusion.14
  29.1 1.1 fusion.32
  30.2 2.0 %collective-permute-start.1 = (bf16[4,2,8,1024]{3,2,1,0:T(8,128)(2,1)S(1)}, bf16[4,2,8,1024]{3,2,1,0:T(8,128)(2,1)S(1)}, u32[]{:S(2)}, u32[]{:S(2)}) collective-permute-start(bf16[4,2,8,1024]{3,2,1,0:T(8,128)(2,1)S(1)} %fusion.32), channel_id=1, source_target_pairs={{0,8},{8,16},{16,24},{24,32},{32,40},{40,48},{48,56},{56,0},{1,9},... | collective-permute-start | bytes 393224 | tf_op jit(solution)/shard_map/ppermute | solution.py:29
  32.2 1.2 %fusion.21 = bf16[8,2,8,1024]{3,2,1,0:T(8,128)(2,1)S(1)} fusion(f32[1,8,2,8,1024]{4,1,0,3,2:T(8,128)S(1)} %constant_dynamic-slice_fusion.5, bf16[8,2,8,1024]{3,2,1,0:T(8,128)(2,1)} %collective-permute-done.12), kind=kLoop, calls=%fused_computation.34 | loop fusion | flops 393216 | bytes 1048576 | tf_op jit(solution)/shard_map/convert_element_type | solution.py:29
  33.4 1.7 %collective-permute-start.13 = (bf16[8,2,8,1024]{3,2,1,0:T(8,128)(2,1)S(1)}, bf16[8,2,8,1024]{3,2,1,0:T(8,128)(2,1)S(1)}, u32[]{:S(2)}, u32[]{:S(2)}) collective-permute-start(bf16[8,2,8,1024]{3,2,1,0:T(8,128)(2,1)S(1)} %fusion.21), channel_id=1, source_target_pairs={{0,64},{64,128},{128,192},{192,0},{1,65},{65,129},{129,193},{193,1... | collective-permute-start | bytes 786440 | tf_op jit(solution)/shard_map/ppermute | solution.py:29
  35.1 2.2 %convert_add_fusion = f32[4,8,2,8,1024]{4,1,0,3,2:T(8,128)S(1)} fusion(bf16[4,8,2,8,1024]{4,1,0,3,2:T(8,128)(2,1)} %collective-permute-done.14, f32[64,2,8,1024]{3,0,2,1:T(8,128)} %copy-done.1), kind=kLoop, calls=%fused_computation.10 | loop fusion | flops 1048576 | bytes 5242880 | tf_op jit(solution)/shard_map/add | solution.py:64
  37.4 5.3 %collective-permute-done.13 = bf16[8,2,8,1024]{3,2,1,0:T(8,128)(2,1)S(1)} collective-permute-done((bf16[8,2,8,1024]{3,2,1,0:T(8,128)(2,1)S(1)}, bf16[8,2,8,1024]{3,2,1,0:T(8,128)(2,1)S(1)}, u32[]{:S(2)}, u32[]{:S(2)}) %collective-permute-start.13) | collective-permute-done | bytes 262176 | tf_op jit(solution)/shard_map/ppermute | solution.py:29
  43.0 0.6 collective-permute-start.15
  43.6 1.7 %convert_add_fusion.1 = f32[4,8,2,8,1024]{4,1,0,3,2:T(8,128)S(1)} fusion(f32[4,8,2,8,1024]{4,1,0,3,2:T(8,128)S(1)} %bitcast.218, bf16[4,8,2,8,1024]{4,1,0,3,2:T(8,128)(2,1)} %bitcast.215), kind=kLoop, calls=%fused_computation.11 | loop fusion | flops 1048576 | bytes 5242880 | tf_op jit(solution)/shard_map/add | solution.py:64
  45.3 1.1 constant_dynamic-slice_fusion.12
  46.4 0.8 fusion.31
  47.3 1.9 %collective-permute-start.3 = (bf16[4,2,8,1024]{3,2,1,0:T(8,128)(2,1)}, bf16[4,2,8,1024]{3,2,1,0:T(8,128)(2,1)}, u32[]{:S(2)}, u32[]{:S(2)}) collective-permute-start(bf16[4,2,8,1024]{3,2,1,0:T(8,128)(2,1)} %fusion.31), channel_id=1, source_target_pairs={{0,8},{8,16},{16,24},{24,32},{32,40},{40,48},{48,56},{56,0},{1,9},... | collective-permute-start | bytes 393224 | tf_op jit(solution)/shard_map/ppermute | solution.py:29
  49.2 2.5 %collective-permute-done.15 = bf16[8,2,8,1024]{3,2,1,0:T(8,128)(2,1)S(1)} collective-permute-done((bf16[8,2,8,1024]{3,2,1,0:T(8,128)(2,1)S(1)}, bf16[8,2,8,1024]{3,2,1,0:T(8,128)(2,1)S(1)}, u32[]{:S(2)}, u32[]{:S(2)}) %collective-permute-start.15) | collective-permute-done | bytes 262176 | tf_op jit(solution)/shard_map/ppermute | solution.py:29
  51.7 1.0 fusion.19
  52.8 1.0 copy.14
  53.8 1.7 %copy.15 = f32[16,16,16]{1,2,0:T(8,128)} copy(f32[16,16,16]{2,1,0:T(8,128)} %bitcast.227) | data formatting | bytes 32768 | tf_op jit(solution)/shard_map/jit(_where)/broadcast_in_dim | solution.py:93
  55.4 1.2 fusion.30
  56.6 2.0 %collective-permute-start.4 = (bf16[4,2,8,1024]{3,2,1,0:T(8,128)(2,1)S(1)}, bf16[4,2,8,1024]{3,2,1,0:T(8,128)(2,1)S(1)}, u32[]{:S(2)}, u32[]{:S(2)}) collective-permute-start(bf16[4,2,8,1024]{3,2,1,0:T(8,128)(2,1)S(1)} %fusion.30), channel_id=1, source_target_pairs={{0,8},{8,16},{16,24},{24,32},{32,40},{40,48},{48,56},{56,0},{1,9},... | collective-permute-start | bytes 393224 | tf_op jit(solution)/shard_map/ppermute | solution.py:29
  58.6 1.9 %collective-permute-done.16 = bf16[8,2,8,1024]{3,2,1,0:T(8,128)(2,1)} collective-permute-done((bf16[8,2,8,1024]{3,2,1,0:T(8,128)(2,1)}, bf16[8,2,8,1024]{3,2,1,0:T(8,128)(2,1)}, u32[]{:S(2)}, u32[]{:S(2)}) %collective-permute-start.16) | collective-permute-done | bytes 262176 | tf_op jit(solution)/shard_map/ppermute | solution.py:29
  60.6 1.3 %bitcast_add_fusion = f32[8,2,8,1024]{3,2,1,0:T(8,128)S(1)} fusion(f32[1,8,2,8,1024]{4,1,0,3,2:T(8,128)S(1)} %get-tuple-element.15, bf16[8,2,8,1024]{3,2,1,0:T(8,128)(2,1)} %collective-permute-done.16), kind=kLoop, calls=%fused_computation.28 | loop fusion | flops 262144 | bytes 1310720 | tf_op jit(solution)/shard_map/add | solution.py:30
  61.9 2.0 %collective-permute-start.17 = (bf16[2,8,1024]{2,1,0:T(8,128)(2,1)S(1)}, bf16[2,8,1024]{2,1,0:T(8,128)(2,1)S(1)}, u32[]{:S(2)}, u32[]{:S(2)}) collective-permute-start(bf16[2,8,1024]{2,1,0:T(8,128)(2,1)S(1)} %fusion.74), channel_id=1, source_target_pairs={{0,8},{8,16},{16,24},{24,32},{32,40},{40,48},{48,56},{56,0},{1,9},... | collective-permute-start | bytes 98312 | tf_op jit(solution)/shard_map/ppermute | solution.py:29
  64.2 1.1 fusion.29
  65.3 1.7 %collective-permute-start.5 = (bf16[4,2,8,1024]{3,2,1,0:T(8,128)(2,1)S(1)}, bf16[4,2,8,1024]{3,2,1,0:T(8,128)(2,1)S(1)}, u32[]{:S(2)}, u32[]{:S(2)}) collective-permute-start(bf16[4,2,8,1024]{3,2,1,0:T(8,128)(2,1)S(1)} %fusion.29), channel_id=1, source_target_pairs={{0,8},{8,16},{16,24},{24,32},{32,40},{40,48},{48,56},{56,0},{1,9},... | collective-permute-start | bytes 393224 | tf_op jit(solution)/shard_map/ppermute | solution.py:29
  67.0 1.6 %collective-permute-done.17 = bf16[2,8,1024]{2,1,0:T(8,128)(2,1)S(1)} collective-permute-done((bf16[2,8,1024]{2,1,0:T(8,128)(2,1)S(1)}, bf16[2,8,1024]{2,1,0:T(8,128)(2,1)S(1)}, u32[]{:S(2)}, u32[]{:S(2)}) %collective-permute-start.17) | collective-permute-done | bytes 32800 | tf_op jit(solution)/shard_map/ppermute | solution.py:29
  68.6 1.6 %collective-permute-start.18 = (bf16[2,8,1024]{2,1,0:T(8,128)(2,1)S(1)}, bf16[2,8,1024]{2,1,0:T(8,128)(2,1)S(1)}, u32[]{:S(2)}, u32[]{:S(2)}) collective-permute-start(bf16[2,8,1024]{2,1,0:T(8,128)(2,1)S(1)} %fusion.63), channel_id=1, source_target_pairs={{0,8},{8,16},{16,24},{24,32},{32,40},{40,48},{48,56},{56,0},{1,9},... | collective-permute-start | bytes 98312 | tf_op jit(solution)/shard_map/ppermute | solution.py:29
  70.2 1.4 %collective-permute-done.5 = bf16[4,2,8,1024]{3,2,1,0:T(8,128)(2,1)S(1)} collective-permute-done((bf16[4,2,8,1024]{3,2,1,0:T(8,128)(2,1)S(1)}, bf16[4,2,8,1024]{3,2,1,0:T(8,128)(2,1)S(1)}, u32[]{:S(2)}, u32[]{:S(2)}) %collective-permute-start.5) | collective-permute-done | bytes 131104 | tf_op jit(solution)/shard_map/ppermute | solution.py:29
  71.8 2.4 %collective-permute-start.6 = (bf16[4,2,8,1024]{3,2,1,0:T(8,128)(2,1)S(1)}, bf16[4,2,8,1024]{3,2,1,0:T(8,128)(2,1)S(1)}, u32[]{:S(2)}, u32[]{:S(2)}) collective-permute-start(bf16[4,2,8,1024]{3,2,1,0:T(8,128)(2,1)S(1)} %fusion.28), channel_id=1, source_target_pairs={{0,8},{8,16},{16,24},{24,32},{32,40},{40,48},{48,56},{56,0},{1,9},... | collective-permute-start | bytes 393224 | tf_op jit(solution)/shard_map/ppermute | solution.py:29
  74.1 2.6 %collective-permute-start.19 = (bf16[2,8,1024]{2,1,0:T(8,128)(2,1)S(1)}, bf16[2,8,1024]{2,1,0:T(8,128)(2,1)S(1)}, u32[]{:S(2)}, u32[]{:S(2)}) collective-permute-start(bf16[2,8,1024]{2,1,0:T(8,128)(2,1)S(1)} %fusion.62), channel_id=1, source_target_pairs={{0,8},{8,16},{16,24},{24,32},{32,40},{40,48},{48,56},{56,0},{1,9},... | collective-permute-start | bytes 98312 | tf_op jit(solution)/shard_map/ppermute | solution.py:29
  76.7 2.1 %collective-permute-done.6 = bf16[4,2,8,1024]{3,2,1,0:T(8,128)(2,1)S(1)} collective-permute-done((bf16[4,2,8,1024]{3,2,1,0:T(8,128)(2,1)S(1)}, bf16[4,2,8,1024]{3,2,1,0:T(8,128)(2,1)S(1)}, u32[]{:S(2)}, u32[]{:S(2)}) %collective-permute-start.6) | collective-permute-done | bytes 131104 | tf_op jit(solution)/shard_map/ppermute | solution.py:29
  78.9 1.5 %collective-permute-start.7 = (bf16[4,2,8,1024]{3,2,1,0:T(8,128)(2,1)S(1)}, bf16[4,2,8,1024]{3,2,1,0:T(8,128)(2,1)S(1)}, u32[]{:S(2)}, u32[]{:S(2)}) collective-permute-start(bf16[4,2,8,1024]{3,2,1,0:T(8,128)(2,1)S(1)} %fusion.27), channel_id=1, source_target_pairs={{0,8},{8,16},{16,24},{24,32},{32,40},{40,48},{48,56},{56,0},{1,9},... | collective-permute-start | bytes 393224 | tf_op jit(solution)/shard_map/ppermute | solution.py:29
  80.5 2.6 %collective-permute-start.20 = (bf16[2,8,1024]{2,1,0:T(8,128)(2,1)S(1)}, bf16[2,8,1024]{2,1,0:T(8,128)(2,1)S(1)}, u32[]{:S(2)}, u32[]{:S(2)}) collective-permute-start(bf16[2,8,1024]{2,1,0:T(8,128)(2,1)S(1)} %fusion.61), channel_id=1, source_target_pairs={{0,8},{8,16},{16,24},{24,32},{32,40},{40,48},{48,56},{56,0},{1,9},... | collective-permute-start | bytes 98312 | tf_op jit(solution)/shard_map/ppermute | solution.py:29
  83.0 3.5 %collective-permute-done.7 = bf16[4,2,8,1024]{3,2,1,0:T(8,128)(2,1)S(1)} collective-permute-done((bf16[4,2,8,1024]{3,2,1,0:T(8,128)(2,1)S(1)}, bf16[4,2,8,1024]{3,2,1,0:T(8,128)(2,1)S(1)}, u32[]{:S(2)}, u32[]{:S(2)}) %collective-permute-start.7) | collective-permute-done | bytes 131104 | tf_op jit(solution)/shard_map/ppermute | solution.py:29
  87.2 1.0 collective-permute-start.21
  88.2 5.0 %collective-permute-done.8 = bf16[4,2,8,1024]{3,2,1,0:T(8,128)(2,1)S(1)} collective-permute-done((bf16[4,2,8,1024]{3,2,1,0:T(8,128)(2,1)S(1)}, bf16[4,2,8,1024]{3,2,1,0:T(8,128)(2,1)S(1)}, u32[]{:S(2)}, u32[]{:S(2)}) %collective-permute-start.8) | collective-permute-done | bytes 131104 | tf_op jit(solution)/shard_map/ppermute | solution.py:29
  93.4 1.2 collective-permute-start.9
  94.7 4.1 %collective-permute-done.9 = bf16[2,8,1024]{2,1,0:T(8,128)(2,1)S(1)} collective-permute-done((bf16[2,8,1024]{2,1,0:T(8,128)(2,1)S(1)}, bf16[2,8,1024]{2,1,0:T(8,128)(2,1)S(1)}, u32[]{:S(2)}, u32[]{:S(2)}) %collective-permute-start.9) | collective-permute-done | bytes 32800 | tf_op jit(solution)/shard_map/ppermute | solution.py:29
  98.9 0.9 collective-permute-done.22
  99.9 4.1 %collective-permute-done.10 = bf16[2,8,1024]{2,1,0:T(8,128)(2,1)S(1)} collective-permute-done((bf16[2,8,1024]{2,1,0:T(8,128)(2,1)S(1)}, bf16[2,8,1024]{2,1,0:T(8,128)(2,1)S(1)}, u32[]{:S(2)}, u32[]{:S(2)}) %collective-permute-start.10) | collective-permute-done | bytes 32800 | tf_op jit(solution)/shard_map/ppermute | solution.py:29
  104.1 0.9 collective-permute-done.23
  105.2 4.0 %collective-permute-done.11 = bf16[2,8,1024]{2,1,0:T(8,128)(2,1)S(1)} collective-permute-done((bf16[2,8,1024]{2,1,0:T(8,128)(2,1)S(1)}, bf16[2,8,1024]{2,1,0:T(8,128)(2,1)S(1)}, u32[]{:S(2)}, u32[]{:S(2)}) %collective-permute-start.11) | collective-permute-done | bytes 32800 | tf_op jit(solution)/shard_map/ppermute | solution.py:29
  110.6 1.2 %convolution_bitcast_fusion.1 = f32[1,16,16,128]{3,1,2,0:T(8,128)S(1)} fusion(bf16[16,8,64,128]{3,2,1,0:T(8,128)(2,1)S(1)} %copy-done, f32[16,16,8,64]{3,2,1,0:T(8,128)S(1)} %get-tuple-element.17), kind=kOutput, calls=%fused_computation.15 | convolution fusion | flops 100663296 | bytes 2752512 | tf_op jit(solution)/shard_map/mflpi,lpij->mflj/dot_general | solution.py:104
  111.9 1.2 %convolution_bitcast_fusion.2 = f32[1,16,16,128]{3,1,2,0:T(8,128)S(1)} fusion(bf16[16,8,64,128]{3,2,1,0:T(8,128)(2,1)S(1)} %copy-done, f32[16,16,8,64]{3,2,1,0:T(8,128)S(1)} %get-tuple-element.18), kind=kOutput, calls=%fused_computation.16 | convolution fusion | flops 100663296 | bytes 2752512 | tf_op jit(solution)/shard_map/mflpi,lpij->mflj/dot_general | solution.py:103
  113.3 0.5 collective-permute-start.24
  113.9 1.6 %collective-permute-start.26 = (bf16[1,16,16,128]{3,1,2,0:T(8,128)(2,1)S(1)}, bf16[1,16,16,128]{3,1,2,0:T(8,128)(2,1)S(1)}, u32[]{:S(2)}, u32[]{:S(2)}) collective-permute-start(bf16[1,16,16,128]{3,1,2,0:T(8,128)(2,1)S(1)} %pad_maximum_fusion), channel_id=1, source_target_pairs={{0,3},{1,0},{2,1},{3,2},{4,7},{5,4},{6,5},{7,6},{8,11},{9,8},{10,9... | collective-permute-start | bytes 196616 | tf_op jit(solution)/shard_map/ppermute | solution.py:117
  115.4 1.4 %collective-permute-start.25 = (bf16[1,16,16,128]{3,1,2,0:T(8,128)(2,1)S(1)}, bf16[1,16,16,128]{3,1,2,0:T(8,128)(2,1)S(1)}, u32[]{:S(2)}, u32[]{:S(2)}) collective-permute-start(bf16[1,16,16,128]{3,1,2,0:T(8,128)(2,1)S(1)} %pad_maximum_fusion), channel_id=1, source_target_pairs={{0,2},{1,3},{2,0},{3,1},{4,6},{5,7},{6,4},{7,5},{8,10},{9,11},{10,... | collective-permute-start | bytes 196616 | tf_op jit(solution)/shard_map/ppermute | solution.py:117
  117.1 0.5 collective-permute-done.24
  118.0 1.4 %collective-permute-done.26 = bf16[1,16,16,128]{3,1,2,0:T(8,128)(2,1)S(1)} collective-permute-done((bf16[1,16,16,128]{3,1,2,0:T(8,128)(2,1)S(1)}, bf16[1,16,16,128]{3,1,2,0:T(8,128)(2,1)S(1)}, u32[]{:S(2)}, u32[]{:S(2)}) %collective-permute-start.26) | collective-permute-done | bytes 65568 | tf_op jit(solution)/shard_map/ppermute | solution.py:117
  119.6 1.6 %collective-permute-done.25 = bf16[1,16,16,128]{3,1,2,0:T(8,128)(2,1)S(1)} collective-permute-done((bf16[1,16,16,128]{3,1,2,0:T(8,128)(2,1)S(1)}, bf16[1,16,16,128]{3,1,2,0:T(8,128)(2,1)S(1)}, u32[]{:S(2)}, u32[]{:S(2)}) %collective-permute-start.25) | collective-permute-done | bytes 65568 | tf_op jit(solution)/shard_map/ppermute | solution.py:117
  121.5 0.7 copy.35
  (85 shorter events, 6.8 us)
Async XLA Ops:
  0.0 110.6 %copy-start = (bf16[16,8,64,128]{3,2,1,0:T(8,128)(2,1)S(1)}, bf16[16,8,64,128]{3,2,1,0:T(8,128)(2,1)}, u32[]{:S(2)}) copy-start(bf16[16,8,64,128]{3,2,1,0:T(8,128)(2,1)} %param.7) | copy-start | bytes 6291460
  5.1 2.0 %copy-start.2 = (f32[64,2,8,1024]{3,0,2,1:T(8,128)}, f32[64,2,8,1024]{3,0,2,1:T(8,128)S(1)}, u32[]{:S(2)}) copy-start(f32[64,2,8,1024]{3,0,2,1:T(8,128)S(1)} %fusion.6) | copy-start | bytes 12582916
  8.5 35.1 %collective-permute-start.2 = (bf16[8,4,2,8,1024]{4,1,0,3,2:T(4,128)(2,1)}, bf16[8,4,2,8,1024]{4,1,0,3,2:T(4,128)(2,1)}, u32[]{:S(2)}, u32[]{:S(2)}) collective-permute-start(bf16[8,4,2,8,1024]{4,1,0,3,2:T(4,128)(2,1)} %reshape.541), channel_id=1, source_target_pairs={{0,4},{4,0},{1,5},{5,1},{2,6},{6,2},{3,7},{7,3},{8,12},{12,8},{9,1... | collective-permute-start | bytes 3145736 | tf_op jit(solution)/shard_map/ppermute | solution.py:62
  9.5 19.6 %collective-permute-start = (bf16[4,2,8,1024]{3,2,1,0:T(8,128)(2,1)S(1)}, bf16[4,2,8,1024]{3,2,1,0:T(8,128)(2,1)}, u32[]{:S(2)}, u32[]{:S(2)}) collective-permute-start(bf16[4,2,8,1024]{3,2,1,0:T(8,128)(2,1)S(1)} %bitcast.228), channel_id=1, source_target_pairs={{0,4},{4,0},{1,5},{5,1},{2,6},{6,2},{3,7},{7,3},{8,12},{12,8},{9,1... | collective-permute-start | bytes 393224 | tf_op jit(solution)/shard_map/ppermute | solution.py:61
  14.4 2.0 %copy-start.1 = (f32[64,2,8,1024]{3,0,2,1:T(8,128)}, f32[64,2,8,1024]{3,0,2,1:T(8,128)S(1)}, u32[]{:S(2)}) copy-start(f32[64,2,8,1024]{3,0,2,1:T(8,128)S(1)} %fusion.9) | copy-start | bytes 12582916
  17.5 17.5 %collective-permute-start.14 = (bf16[4,8,2,8,1024]{4,1,0,3,2:T(8,128)(2,1)}, bf16[4,8,2,8,1024]{4,1,0,3,2:T(8,128)(2,1)}, u32[]{:S(2)}, u32[]{:S(2)}) collective-permute-start(bf16[4,8,2,8,1024]{4,1,0,3,2:T(8,128)(2,1)} %slice_bitcast_fusion), channel_id=1, source_target_pairs={{0,4},{4,0},{1,5},{5,1},{2,6},{6,2},{3,7},{7,3},{8,12},{12,8},{9,1... | collective-permute-start | bytes 3145736 | tf_op jit(solution)/shard_map/ppermute | solution.py:62
  19.4 12.8 %collective-permute-start.12 = (bf16[8,2,8,1024]{3,2,1,0:T(8,128)(2,1)}, bf16[8,2,8,1024]{3,2,1,0:T(8,128)(2,1)}, u32[]{:S(2)}, u32[]{:S(2)}) collective-permute-start(bf16[8,2,8,1024]{3,2,1,0:T(8,128)(2,1)} %bitcast.212), channel_id=1, source_target_pairs={{0,4},{4,0},{1,5},{5,1},{2,6},{6,2},{3,7},{7,3},{8,12},{12,8},{9,1... | collective-permute-start | bytes 786440 | tf_op jit(solution)/shard_map/ppermute | solution.py:61
  19.9 1.9 %copy-start.8 = (f32[16,64,64]{2,1,0:T(8,128)S(1)}, f32[16,64,64]{2,1,0:T(8,128)}, u32[]{:S(2)}) copy-start(f32[16,64,64]{2,1,0:T(8,128)} %param.10) | copy-start | bytes 786436
  19.9 3.0 %copy-start.3 = (f32[64,2,8,1024]{3,0,2,1:T(8,128)S(1)}, f32[64,2,8,1024]{3,0,2,1:T(8,128)}, u32[]{:S(2)}) copy-start(f32[64,2,8,1024]{3,0,2,1:T(8,128)} %copy-done.2) | copy-start | bytes 12582916
  30.2 16.3 %collective-permute-start.1 = (bf16[4,2,8,1024]{3,2,1,0:T(8,128)(2,1)S(1)}, bf16[4,2,8,1024]{3,2,1,0:T(8,128)(2,1)S(1)}, u32[]{:S(2)}, u32[]{:S(2)}) collective-permute-start(bf16[4,2,8,1024]{3,2,1,0:T(8,128)(2,1)S(1)} %fusion.32), channel_id=1, source_target_pairs={{0,8},{8,16},{16,24},{24,32},{32,40},{40,48},{48,56},{56,0},{1,9},... | collective-permute-start | bytes 393224 | tf_op jit(solution)/shard_map/ppermute | solution.py:29
  33.4 9.3 %collective-permute-start.13 = (bf16[8,2,8,1024]{3,2,1,0:T(8,128)(2,1)S(1)}, bf16[8,2,8,1024]{3,2,1,0:T(8,128)(2,1)S(1)}, u32[]{:S(2)}, u32[]{:S(2)}) collective-permute-start(bf16[8,2,8,1024]{3,2,1,0:T(8,128)(2,1)S(1)} %fusion.21), channel_id=1, source_target_pairs={{0,64},{64,128},{128,192},{192,0},{1,65},{65,129},{129,193},{193,1... | collective-permute-start | bytes 786440 | tf_op jit(solution)/shard_map/ppermute | solution.py:29
  37.3 6.3 %copy-start.4 = (f32[8,4,2,8,1024]{4,1,0,3,2:T(4,128)S(1)}, f32[8,4,2,8,1024]{4,1,0,3,2:T(4,128)}, u32[]{:S(2)}) copy-start(f32[8,4,2,8,1024]{4,1,0,3,2:T(4,128)} %reshape.540) | copy-start | bytes 6291460
  43.0 8.6 %collective-permute-start.15 = (bf16[8,2,8,1024]{3,2,1,0:T(8,128)(2,1)S(1)}, bf16[8,2,8,1024]{3,2,1,0:T(8,128)(2,1)S(1)}, u32[]{:S(2)}, u32[]{:S(2)}) collective-permute-start(bf16[8,2,8,1024]{3,2,1,0:T(8,128)(2,1)S(1)} %fusion.20), channel_id=1, source_target_pairs={{0,64},{64,128},{128,192},{192,0},{1,65},{65,129},{129,193},{193,1... | collective-permute-start | bytes 786440 | tf_op jit(solution)/shard_map/ppermute | solution.py:29
  47.3 8.2 %collective-permute-start.3 = (bf16[4,2,8,1024]{3,2,1,0:T(8,128)(2,1)}, bf16[4,2,8,1024]{3,2,1,0:T(8,128)(2,1)}, u32[]{:S(2)}, u32[]{:S(2)}) collective-permute-start(bf16[4,2,8,1024]{3,2,1,0:T(8,128)(2,1)} %fusion.31), channel_id=1, source_target_pairs={{0,8},{8,16},{16,24},{24,32},{32,40},{40,48},{48,56},{56,0},{1,9},... | collective-permute-start | bytes 393224 | tf_op jit(solution)/shard_map/ppermute | solution.py:29
  52.7 7.9 %collective-permute-start.16 = (bf16[8,2,8,1024]{3,2,1,0:T(8,128)(2,1)}, bf16[8,2,8,1024]{3,2,1,0:T(8,128)(2,1)}, u32[]{:S(2)}, u32[]{:S(2)}) collective-permute-start(bf16[8,2,8,1024]{3,2,1,0:T(8,128)(2,1)} %fusion.19), channel_id=1, source_target_pairs={{0,64},{64,128},{128,192},{192,0},{1,65},{65,129},{129,193},{193,1... | collective-permute-start | bytes 786440 | tf_op jit(solution)/shard_map/ppermute | solution.py:29
  55.4 16.2 %copy-start.7 = (f32[1,4,2,8,1024]{4,1,0,3,2:T(4,128)S(1)}, f32[1,4,2,8,1024]{4,1,0,3,2:T(4,128)}, u32[]{:S(2)}) copy-start(f32[1,4,2,8,1024]{4,1,0,3,2:T(4,128)} %get-tuple-element.11) | copy-start | bytes 786436
  55.4 23.3 %copy-start.6 = (f32[1,4,2,8,1024]{4,1,0,3,2:T(4,128)S(1)}, f32[1,4,2,8,1024]{4,1,0,3,2:T(4,128)}, u32[]{:S(2)}) copy-start(f32[1,4,2,8,1024]{4,1,0,3,2:T(4,128)} %get-tuple-element.10) | copy-start | bytes 786436
  55.4 31.1 %copy-start.5 = (f32[1,4,2,8,1024]{4,1,0,3,2:T(4,128)S(1)}, f32[1,4,2,8,1024]{4,1,0,3,2:T(4,128)}, u32[]{:S(2)}) copy-start(f32[1,4,2,8,1024]{4,1,0,3,2:T(4,128)} %get-tuple-element.9) | copy-start | bytes 786436
  56.6 7.6 %collective-permute-start.4 = (bf16[4,2,8,1024]{3,2,1,0:T(8,128)(2,1)S(1)}, bf16[4,2,8,1024]{3,2,1,0:T(8,128)(2,1)S(1)}, u32[]{:S(2)}, u32[]{:S(2)}) collective-permute-start(bf16[4,2,8,1024]{3,2,1,0:T(8,128)(2,1)S(1)} %fusion.30), channel_id=1, source_target_pairs={{0,8},{8,16},{16,24},{24,32},{32,40},{40,48},{48,56},{56,0},{1,9},... | collective-permute-start | bytes 393224 | tf_op jit(solution)/shard_map/ppermute | solution.py:29
  61.9 6.7 %collective-permute-start.17 = (bf16[2,8,1024]{2,1,0:T(8,128)(2,1)S(1)}, bf16[2,8,1024]{2,1,0:T(8,128)(2,1)S(1)}, u32[]{:S(2)}, u32[]{:S(2)}) collective-permute-start(bf16[2,8,1024]{2,1,0:T(8,128)(2,1)S(1)} %fusion.74), channel_id=1, source_target_pairs={{0,8},{8,16},{16,24},{24,32},{32,40},{40,48},{48,56},{56,0},{1,9},... | collective-permute-start | bytes 98312 | tf_op jit(solution)/shard_map/ppermute | solution.py:29
  65.3 6.3 %collective-permute-start.5 = (bf16[4,2,8,1024]{3,2,1,0:T(8,128)(2,1)S(1)}, bf16[4,2,8,1024]{3,2,1,0:T(8,128)(2,1)S(1)}, u32[]{:S(2)}, u32[]{:S(2)}) collective-permute-start(bf16[4,2,8,1024]{3,2,1,0:T(8,128)(2,1)S(1)} %fusion.29), channel_id=1, source_target_pairs={{0,8},{8,16},{16,24},{24,32},{32,40},{40,48},{48,56},{56,0},{1,9},... | collective-permute-start | bytes 393224 | tf_op jit(solution)/shard_map/ppermute | solution.py:29
  68.6 5.5 %collective-permute-start.18 = (bf16[2,8,1024]{2,1,0:T(8,128)(2,1)S(1)}, bf16[2,8,1024]{2,1,0:T(8,128)(2,1)S(1)}, u32[]{:S(2)}, u32[]{:S(2)}) collective-permute-start(bf16[2,8,1024]{2,1,0:T(8,128)(2,1)S(1)} %fusion.63), channel_id=1, source_target_pairs={{0,8},{8,16},{16,24},{24,32},{32,40},{40,48},{48,56},{56,0},{1,9},... | collective-permute-start | bytes 98312 | tf_op jit(solution)/shard_map/ppermute | solution.py:29
  71.6 38.2 %copy-start.9 = (f32[16,16,16]{1,2,0:T(8,128)S(1)}, f32[16,16,16]{1,2,0:T(8,128)}, u32[]{:S(2)}) copy-start(f32[16,16,16]{1,2,0:T(8,128)} %copy.15) | copy-start | bytes 49156
  71.8 7.0 %collective-permute-start.6 = (bf16[4,2,8,1024]{3,2,1,0:T(8,128)(2,1)S(1)}, bf16[4,2,8,1024]{3,2,1,0:T(8,128)(2,1)S(1)}, u32[]{:S(2)}, u32[]{:S(2)}) collective-permute-start(bf16[4,2,8,1024]{3,2,1,0:T(8,128)(2,1)S(1)} %fusion.28), channel_id=1, source_target_pairs={{0,8},{8,16},{16,24},{24,32},{32,40},{40,48},{48,56},{56,0},{1,9},... | collective-permute-start | bytes 393224 | tf_op jit(solution)/shard_map/ppermute | solution.py:29
  74.1 6.3 %collective-permute-start.19 = (bf16[2,8,1024]{2,1,0:T(8,128)(2,1)S(1)}, bf16[2,8,1024]{2,1,0:T(8,128)(2,1)S(1)}, u32[]{:S(2)}, u32[]{:S(2)}) collective-permute-start(bf16[2,8,1024]{2,1,0:T(8,128)(2,1)S(1)} %fusion.62), channel_id=1, source_target_pairs={{0,8},{8,16},{16,24},{24,32},{32,40},{40,48},{48,56},{56,0},{1,9},... | collective-permute-start | bytes 98312 | tf_op jit(solution)/shard_map/ppermute | solution.py:29
  78.9 7.6 %collective-permute-start.7 = (bf16[4,2,8,1024]{3,2,1,0:T(8,128)(2,1)S(1)}, bf16[4,2,8,1024]{3,2,1,0:T(8,128)(2,1)S(1)}, u32[]{:S(2)}, u32[]{:S(2)}) collective-permute-start(bf16[4,2,8,1024]{3,2,1,0:T(8,128)(2,1)S(1)} %fusion.27), channel_id=1, source_target_pairs={{0,8},{8,16},{16,24},{24,32},{32,40},{40,48},{48,56},{56,0},{1,9},... | collective-permute-start | bytes 393224 | tf_op jit(solution)/shard_map/ppermute | solution.py:29
  80.5 6.7 %collective-permute-start.20 = (bf16[2,8,1024]{2,1,0:T(8,128)(2,1)S(1)}, bf16[2,8,1024]{2,1,0:T(8,128)(2,1)S(1)}, u32[]{:S(2)}, u32[]{:S(2)}) collective-permute-start(bf16[2,8,1024]{2,1,0:T(8,128)(2,1)S(1)} %fusion.61), channel_id=1, source_target_pairs={{0,8},{8,16},{16,24},{24,32},{32,40},{40,48},{48,56},{56,0},{1,9},... | collective-permute-start | bytes 98312 | tf_op jit(solution)/shard_map/ppermute | solution.py:29
  86.7 6.5 %collective-permute-start.8 = (bf16[4,2,8,1024]{3,2,1,0:T(8,128)(2,1)S(1)}, bf16[4,2,8,1024]{3,2,1,0:T(8,128)(2,1)S(1)}, u32[]{:S(2)}, u32[]{:S(2)}) collective-permute-start(bf16[4,2,8,1024]{3,2,1,0:T(8,128)(2,1)S(1)} %fusion.26), channel_id=1, source_target_pairs={{0,8},{8,16},{16,24},{24,32},{32,40},{40,48},{48,56},{56,0},{1,9},... | collective-permute-start | bytes 393224 | tf_op jit(solution)/shard_map/ppermute | solution.py:29
  87.2 7.4 %collective-permute-start.21 = (bf16[2,8,1024]{2,1,0:T(8,128)(2,1)S(1)}, bf16[2,8,1024]{2,1,0:T(8,128)(2,1)S(1)}, u32[]{:S(2)}, u32[]{:S(2)}) collective-permute-start(bf16[2,8,1024]{2,1,0:T(8,128)(2,1)S(1)} %fusion.60), channel_id=1, source_target_pairs={{0,8},{8,16},{16,24},{24,32},{32,40},{40,48},{48,56},{56,0},{1,9},... | collective-permute-start | bytes 98312 | tf_op jit(solution)/shard_map/ppermute | solution.py:29
  93.4 5.4 %collective-permute-start.9 = (bf16[2,8,1024]{2,1,0:T(8,128)(2,1)S(1)}, bf16[2,8,1024]{2,1,0:T(8,128)(2,1)S(1)}, u32[]{:S(2)}, u32[]{:S(2)}) collective-permute-start(bf16[2,8,1024]{2,1,0:T(8,128)(2,1)S(1)} %fusion.73), channel_id=1, source_target_pairs={{0,64},{64,128},{128,192},{192,0},{1,65},{65,129},{129,193},{193,1... | collective-permute-start | bytes 98312 | tf_op jit(solution)/shard_map/ppermute | solution.py:29
  94.6 5.2 %collective-permute-start.22 = (bf16[2,8,1024]{2,1,0:T(8,128)(2,1)S(1)}, bf16[2,8,1024]{2,1,0:T(8,128)(2,1)S(1)}, u32[]{:S(2)}, u32[]{:S(2)}) collective-permute-start(bf16[2,8,1024]{2,1,0:T(8,128)(2,1)S(1)} %fusion.59), channel_id=1, source_target_pairs={{0,8},{8,16},{16,24},{24,32},{32,40},{40,48},{48,56},{56,0},{1,9},... | collective-permute-start | bytes 98312 | tf_op jit(solution)/shard_map/ppermute | solution.py:29
  98.8 5.2 %collective-permute-start.10 = (bf16[2,8,1024]{2,1,0:T(8,128)(2,1)S(1)}, bf16[2,8,1024]{2,1,0:T(8,128)(2,1)S(1)}, u32[]{:S(2)}, u32[]{:S(2)}) collective-permute-start(bf16[2,8,1024]{2,1,0:T(8,128)(2,1)S(1)} %fusion.66), channel_id=1, source_target_pairs={{0,64},{64,128},{128,192},{192,0},{1,65},{65,129},{129,193},{193,1... | collective-permute-start | bytes 98312 | tf_op jit(solution)/shard_map/ppermute | solution.py:29
  99.8 5.2 %collective-permute-start.23 = (bf16[2,8,1024]{2,1,0:T(8,128)(2,1)S(1)}, bf16[2,8,1024]{2,1,0:T(8,128)(2,1)S(1)}, u32[]{:S(2)}, u32[]{:S(2)}) collective-permute-start(bf16[2,8,1024]{2,1,0:T(8,128)(2,1)S(1)} %fusion.58), channel_id=1, source_target_pairs={{0,8},{8,16},{16,24},{24,32},{32,40},{40,48},{48,56},{56,0},{1,9},... | collective-permute-start | bytes 98312 | tf_op jit(solution)/shard_map/ppermute | solution.py:29
  104.0 5.2 %collective-permute-start.11 = (bf16[2,8,1024]{2,1,0:T(8,128)(2,1)S(1)}, bf16[2,8,1024]{2,1,0:T(8,128)(2,1)S(1)}, u32[]{:S(2)}, u32[]{:S(2)}) collective-permute-start(bf16[2,8,1024]{2,1,0:T(8,128)(2,1)S(1)} %fusion.65), channel_id=1, source_target_pairs={{0,64},{64,128},{128,192},{192,0},{1,65},{65,129},{129,193},{193,1... | collective-permute-start | bytes 98312 | tf_op jit(solution)/shard_map/ppermute | solution.py:29
  113.3 4.3 %collective-permute-start.24 = (bf16[1,16,16,128]{3,1,2,0:T(8,128)(2,1)S(1)}, bf16[1,16,16,128]{3,1,2,0:T(8,128)(2,1)S(1)}, u32[]{:S(2)}, u32[]{:S(2)}) collective-permute-start(bf16[1,16,16,128]{3,1,2,0:T(8,128)(2,1)S(1)} %pad_maximum_fusion), channel_id=1, source_target_pairs={{0,1},{1,2},{2,3},{3,0},{4,5},{5,6},{6,7},{7,4},{8,9},{9,10},{10,1... | collective-permute-start | bytes 196616 | tf_op jit(solution)/shard_map/ppermute | solution.py:117
  113.9 5.5 %collective-permute-start.26 = (bf16[1,16,16,128]{3,1,2,0:T(8,128)(2,1)S(1)}, bf16[1,16,16,128]{3,1,2,0:T(8,128)(2,1)S(1)}, u32[]{:S(2)}, u32[]{:S(2)}) collective-permute-start(bf16[1,16,16,128]{3,1,2,0:T(8,128)(2,1)S(1)} %pad_maximum_fusion), channel_id=1, source_target_pairs={{0,3},{1,0},{2,1},{3,2},{4,7},{5,4},{6,5},{7,6},{8,11},{9,8},{10,9... | collective-permute-start | bytes 196616 | tf_op jit(solution)/shard_map/ppermute | solution.py:117
  115.4 5.8 %collective-permute-start.25 = (bf16[1,16,16,128]{3,1,2,0:T(8,128)(2,1)S(1)}, bf16[1,16,16,128]{3,1,2,0:T(8,128)(2,1)S(1)}, u32[]{:S(2)}, u32[]{:S(2)}) collective-permute-start(bf16[1,16,16,128]{3,1,2,0:T(8,128)(2,1)S(1)} %pad_maximum_fusion), channel_id=1, source_target_pairs={{0,2},{1,3},{2,0},{3,1},{4,6},{5,7},{6,4},{7,5},{8,10},{9,11},{10,... | collective-permute-start | bytes 196616 | tf_op jit(solution)/shard_map/ppermute | solution.py:117

commit v7 on v4

--- a/solution.py
+++ b/solution.py
@@ -44,6 +44,8 @@
     jy = jnp.arange(ny, dtype=jnp.int32)
     jz = jnp.arange(nz, dtype=jnp.int32)
     halves = []
+    outs = []
+    half_rows = ny * nz
     for part, z_major in ((visibility[:h], True), (visibility[h:], False)):
         if z_major:
             pair = (jy[None, :] * nz + jz[:, None]).reshape(-1)
@@ -51,10 +53,12 @@
             pair = (jy[:, None] * nz + jz[None, :]).reshape(-1)
         rows = jnp.concatenate([pair * 2 + (1 - c), pair * 2 + c])
         table = dft_table(mode_step * rows, time_index, sidereal_period, norm_factor)
-        out = jnp.einsum("rdct,fctb->rdfb", table, part, precision=lax.Precision.HIGH)
-        half_rows = ny * nz
-        got = lax.ppermute(out[:half_rows].astype(jnp.bfloat16), "tc", [(0, 1), (1, 0)])
-        y = out[half_rows:] + got.astype(jnp.float32)
+        outs.append(jnp.einsum("rdct,fctb->rdfb", table, part, precision=lax.Precision.HIGH))
+    swapped = lax.ppermute(
+        jnp.stack([out[:half_rows] for out in outs]).astype(jnp.bfloat16), "tc", [(0, 1), (1, 0)]
+    )
+    for q, z_major in ((0, True), (1, False)):
+        y = outs[q][half_rows:] + swapped[q].astype(jnp.float32)
         if z_major:
             y = y.reshape(nz, ny, *y.shape[1:])
             y = ring_reduce_scatter(ring_reduce_scatter(y, "tz", nz), "ty", ny)

time: 108 us -> 116 us (1.074)
  the two profiles are of different devices: /device:TPU:16 before, /device:TPU:6 now
where the time goes in v7:
time: 116 us; the launch traced here: 115 us
  waiting for transfers between devices  56.8 us (49%)
  starting transfers between devices  17.8 us (15%)
  other arithmetic  15 us (13%)
  local copies, waits for them, and re-layouts  13.7 us (12%)
  matrix products  10.6 us (9%)
  between operations  1.18 us (1%)
    ppermute x20, waiting for transfers between devices, ring_reduce_scatter(): got = lax.ppermute(s.astype(jnp.bfloat16), axis, fwd)  49.7 us
    ppermute x20, starting transfers between devices, ring_reduce_scatter(): got = lax.ppermute(s.astype(jnp.bfloat16), axis, fwd)  14.3 us
    dot_general x2, matrix products, spectra_of(): jnp.einsum('rdct,fctb->rdfb', table, part, precision=lax.Precision.HIGH)  6.53 us
    add x1, other arithmetic, spectra_of(): y = outs[q][half_rows:] + swapped[q].astype(jnp.float32)  5.97 us
    convert_element_type x16, other arithmetic, ring_reduce_scatter(): got = lax.ppermute(s.astype(jnp.bfloat16), axis, fwd)  5.06 us
    dynamic_slice x4, local copies, waits for them, and re-layouts, take(): return lax.dynamic_index_in_dim(a, k % n, 0, keepdims=False)  4.65 us
    ppermute x1, waiting for transfers between devices, spectra_of(): lax.ppermute(jnp.stack([out[:half_rows] for out in outs]).astype(jnp.bflo...  3.6 us
    ppermute x3, starting transfers between devices, local(): lax.ppermute(weights_bf, 'freq', [(j, (j + s) % fr_count) for j in range(...  3.51 us
  transfers between devices with their start and end apart: 24, of which 22 were waited for; matrix products, arithmetic and copies ran while one was open for 12% of the time, Pallas kernels for 0%

profile of v7, /device:TPU:6, one launch (start us, length us, event | category | flops | bytes accessed | tf_op | source)
XLA Modules:
  0.0 115.2 jit_solution(13936337728264136777)
XLA Ops:
  0.5 0.4 sine_multiply_fusion.1
  0.9 4.4 %fusion.9 = f32[64,2,8,1024]{3,0,2,1:T(8,128)S(1)} fusion(f32[16,2,64,1024]{3,2,1,0:T(8,128)} %param.6, f32[64,1,2,64]{3,0,2,1:T(8,128)S(1)} %get-tuple-element.24, f32[64,1,2,64]{3,0,2,1:T(8,128)S(1)} %get-tuple-element.23), kind=kOutput, calls=%fused_computation.7 | convolution fusion | flops 805322752 | bytes 8454144 | tf_op jit(solution)/shard_map/rdct,fctb->rdfb/dot_general | solution.py:56
  5.5 2.2 %fusion.6 = f32[64,2,8,1024]{3,0,2,1:T(8,128)S(1)} fusion(f32[16,2,64,1024]{3,2,1,0:T(8,128)S(1)} %copy-done.3, f32[64,1,2,64]{3,0,2,1:T(8,128)S(1)} %get-tuple-element.22, f32[64,1,2,64]{3,0,2,1:T(8,128)S(1)} %get-tuple-element.21), kind=kOutput, calls=%fused_computation.6 | convolution fusion | flops 805322752 | bytes 8519680 | tf_op jit(solution)/shard_map/rdct,fctb->rdfb/dot_general | solution.py:56
  7.9 1.6 %pad_maximum_fusion = bf16[2,32,2,8,1024]{4,1,3,2,0:T(8,128)(2,1)} fusion(bf16[1,32,2,8,1024]{4,1,3,2,0:T(8,128)(2,1)S(1)} %fusion.18, bf16[1,32,2,8,1024]{4,1,3,2,0:T(8,128)(2,1)S(1)} %fusion.17), kind=kLoop, calls=%fused_computation.13 | loop fusion | flops 1048576 | bytes 4194304 | tf_op jit(solution)/shard_map/stack | solution.py:58
  9.4 0.9 copy-done.2
  11.2 3.6 %collective-permute-done = bf16[2,32,2,8,1024]{4,1,3,2,0:T(8,128)(2,1)} collective-permute-done((bf16[2,32,2,8,1024]{4,1,3,2,0:T(8,128)(2,1)}, bf16[2,32,2,8,1024]{4,1,3,2,0:T(8,128)(2,1)}, u32[]{:S(2)}, u32[]{:S(2)}) %collective-permute-start) | collective-permute-done | bytes 2097184 | tf_op jit(solution)/shard_map/ppermute | solution.py:57
  14.8 6.0 %slice_add_fusion.1 = (f32[32,2,8,1024]{3,0,2,1:T(8,128)}, f32[4,8,2,8,1024]{4,1,0,3,2:T(8,128)}) fusion(f32[64,2,8,1024]{3,0,2,1:T(8,128)} %copy-done.2, bf16[2,32,2,8,1024]{4,1,3,2,0:T(8,128)(2,1)} %collective-permute-done, f32[64,2,8,1024]{3,0,2,1:T(8,128)} %copy-done.1), kind=kLoop, calls=%fused_computation.12 | loop fusion | flops 2097152 | bytes 10485760 | tf_op jit(solution)/shard_map/add | solution.py:61
  20.8 2.9 %reshape.538 = f32[8,4,2,8,1024]{4,1,0,3,2:T(4,128)} reshape(f32[32,2,8,1024]{3,0,2,1:T(8,128)} %get-tuple-element.12) | data formatting | bytes 4194304 | tf_op jit(solution)/shard_map/reshape | solution.py:63
  23.7 1.1 constant_dynamic-slice_fusion.4
  24.9 1.6 %collective-permute-start.11 = (bf16[8,2,8,1024]{3,2,1,0:T(8,128)(2,1)S(1)}, bf16[8,2,8,1024]{3,2,1,0:T(8,128)(2,1)S(1)}, u32[]{:S(2)}, u32[]{:S(2)}) collective-permute-start(bf16[8,2,8,1024]{3,2,1,0:T(8,128)(2,1)S(1)} %bitcast.217), channel_id=1, source_target_pairs={{0,64},{64,128},{128,192},{192,0},{1,65},{65,129},{129,193},{193,1... | collective-permute-start | bytes 786440 | tf_op jit(solution)/shard_map/ppermute | solution.py:29
  26.5 1.0 constant_dynamic-slice_fusion.12
  27.6 2.0 %collective-permute-start.1 = (bf16[4,2,8,1024]{3,2,1,0:T(8,128)(2,1)S(1)}, bf16[4,2,8,1024]{3,2,1,0:T(8,128)(2,1)S(1)}, u32[]{:S(2)}, u32[]{:S(2)}) collective-permute-start(bf16[4,2,8,1024]{3,2,1,0:T(8,128)(2,1)S(1)} %bitcast.220), channel_id=1, source_target_pairs={{0,8},{8,16},{16,24},{24,32},{32,40},{40,48},{48,56},{56,0},{1,9},... | collective-permute-start | bytes 393224 | tf_op jit(solution)/shard_map/ppermute | solution.py:29
  29.6 1.5 %constant_dynamic-slice_fusion.3 = (f32[1,8,2,8,1024]{4,1,0,3,2:T(8,128)S(1)}, f32[1,8,2,8,1024]{4,1,0,3,2:T(8,128)S(1)}, f32[1,8,2,8,1024]{4,1,0,3,2:T(8,128)S(1)}) fusion(f32[4,8,2,8,1024]{4,1,0,3,2:T(8,128)} %get-tuple-element.13, s32[]{:T(128)S(6)} %select_n.235, s32[]{:T(128)S(6)} %select_n.239, s32[]{:T(128)S(6)} %select_n.237), kind=kLoop, calls=%fused_computation.144 | loop fusion | bytes 3145740 | tf_op jit(solution)/shard_map/jit(dynamic_index_in_dim)/dynamic_slice | solution.py:25
  31.1 3.5 %collective-permute-done.11 = bf16[8,2,8,1024]{3,2,1,0:T(8,128)(2,1)S(1)} collective-permute-done((bf16[8,2,8,1024]{3,2,1,0:T(8,128)(2,1)S(1)}, bf16[8,2,8,1024]{3,2,1,0:T(8,128)(2,1)S(1)}, u32[]{:S(2)}, u32[]{:S(2)}) %collective-permute-start.11) | collective-permute-done | bytes 262176 | tf_op jit(solution)/shard_map/ppermute | solution.py:29
  34.6 0.3 fusion.23
  34.9 0.4 collective-permute-start.12
  35.3 1.1 constant_dynamic-slice_fusion.11
  36.4 0.7 collective-permute-done.1
  37.1 0.8 fusion.33
  37.9 1.3 %collective-permute-start.2 = (bf16[4,2,8,1024]{3,2,1,0:T(8,128)(2,1)}, bf16[4,2,8,1024]{3,2,1,0:T(8,128)(2,1)}, u32[]{:S(2)}, u32[]{:S(2)}) collective-permute-start(bf16[4,2,8,1024]{3,2,1,0:T(8,128)(2,1)} %fusion.33), channel_id=1, source_target_pairs={{0,8},{8,16},{16,24},{24,32},{32,40},{40,48},{48,56},{56,0},{1,9},... | collective-permute-start | bytes 393224 | tf_op jit(solution)/shard_map/ppermute | solution.py:29
  39.1 4.6 %collective-permute-done.12 = bf16[8,2,8,1024]{3,2,1,0:T(8,128)(2,1)S(1)} collective-permute-done((bf16[8,2,8,1024]{3,2,1,0:T(8,128)(2,1)S(1)}, bf16[8,2,8,1024]{3,2,1,0:T(8,128)(2,1)S(1)}, u32[]{:S(2)}, u32[]{:S(2)}) %collective-permute-start.12) | collective-permute-done | bytes 262176 | tf_op jit(solution)/shard_map/ppermute | solution.py:29
  43.7 1.0 fusion.22
  44.9 1.0 copy.14
  45.9 1.7 %copy.15 = f32[16,16,16]{1,2,0:T(8,128)} copy(f32[16,16,16]{2,1,0:T(8,128)} %bitcast.219) | data formatting | bytes 32768 | tf_op jit(solution)/shard_map/jit(_where)/broadcast_in_dim | solution.py:95
  47.5 1.2 %fusion.32 = bf16[4,2,8,1024]{3,2,1,0:T(8,128)(2,1)S(1)} fusion(f32[1,4,2,8,1024]{4,1,0,3,2:T(4,128)} %get-tuple-element.11, bf16[4,2,8,1024]{3,2,1,0:T(8,128)(2,1)} %collective-permute-done.2), kind=kLoop, calls=%fused_computation.54 | loop fusion | flops 196608 | bytes 524288 | tf_op jit(solution)/shard_map/convert_element_type | solution.py:29
  48.8 2.0 %collective-permute-start.3 = (bf16[4,2,8,1024]{3,2,1,0:T(8,128)(2,1)S(1)}, bf16[4,2,8,1024]{3,2,1,0:T(8,128)(2,1)S(1)}, u32[]{:S(2)}, u32[]{:S(2)}) collective-permute-start(bf16[4,2,8,1024]{3,2,1,0:T(8,128)(2,1)S(1)} %fusion.32), channel_id=1, source_target_pairs={{0,8},{8,16},{16,24},{24,32},{32,40},{40,48},{48,56},{56,0},{1,9},... | collective-permute-start | bytes 393224 | tf_op jit(solution)/shard_map/ppermute | solution.py:29
  50.8 2.3 %collective-permute-done.13 = bf16[8,2,8,1024]{3,2,1,0:T(8,128)(2,1)} collective-permute-done((bf16[8,2,8,1024]{3,2,1,0:T(8,128)(2,1)}, bf16[8,2,8,1024]{3,2,1,0:T(8,128)(2,1)}, u32[]{:S(2)}, u32[]{:S(2)}) %collective-permute-start.13) | collective-permute-done | bytes 262176 | tf_op jit(solution)/shard_map/ppermute | solution.py:29
  53.0 1.3 %bitcast_add_fusion = f32[8,2,8,1024]{3,2,1,0:T(8,128)S(1)} fusion(f32[1,8,2,8,1024]{4,1,0,3,2:T(8,128)S(1)} %get-tuple-element.15, bf16[8,2,8,1024]{3,2,1,0:T(8,128)(2,1)} %collective-permute-done.13), kind=kLoop, calls=%fused_computation.34 | loop fusion | flops 262144 | bytes 1310720 | tf_op jit(solution)/shard_map/add | solution.py:30
  54.3 2.0 %collective-permute-start.14 = (bf16[2,8,1024]{2,1,0:T(8,128)(2,1)S(1)}, bf16[2,8,1024]{2,1,0:T(8,128)(2,1)S(1)}, u32[]{:S(2)}, u32[]{:S(2)}) collective-permute-start(bf16[2,8,1024]{2,1,0:T(8,128)(2,1)S(1)} %fusion.75), channel_id=1, source_target_pairs={{0,8},{8,16},{16,24},{24,32},{32,40},{40,48},{48,56},{56,0},{1,9},... | collective-permute-start | bytes 98312 | tf_op jit(solution)/shard_map/ppermute | solution.py:29
  56.3 1.4 %collective-permute-done.3 = bf16[4,2,8,1024]{3,2,1,0:T(8,128)(2,1)S(1)} collective-permute-done((bf16[4,2,8,1024]{3,2,1,0:T(8,128)(2,1)S(1)}, bf16[4,2,8,1024]{3,2,1,0:T(8,128)(2,1)S(1)}, u32[]{:S(2)}, u32[]{:S(2)}) %collective-permute-start.3) | collective-permute-done | bytes 131104 | tf_op jit(solution)/shard_map/ppermute | solution.py:29
  57.6 1.1 fusion.31
  58.7 0.6 collective-permute-start.4
  59.4 2.7 %collective-permute-done.14 = bf16[2,8,1024]{2,1,0:T(8,128)(2,1)S(1)} collective-permute-done((bf16[2,8,1024]{2,1,0:T(8,128)(2,1)S(1)}, bf16[2,8,1024]{2,1,0:T(8,128)(2,1)S(1)}, u32[]{:S(2)}, u32[]{:S(2)}) %collective-permute-start.14) | collective-permute-done | bytes 32800 | tf_op jit(solution)/shard_map/ppermute | solution.py:29
  62.2 2.8 %collective-permute-done.4 = bf16[4,2,8,1024]{3,2,1,0:T(8,128)(2,1)S(1)} collective-permute-done((bf16[4,2,8,1024]{3,2,1,0:T(8,128)(2,1)S(1)}, bf16[4,2,8,1024]{3,2,1,0:T(8,128)(2,1)S(1)}, u32[]{:S(2)}, u32[]{:S(2)}) %collective-permute-start.4) | collective-permute-done | bytes 131104 | tf_op jit(solution)/shard_map/ppermute | solution.py:29
  65.3 2.4 %collective-permute-done.15 = bf16[2,8,1024]{2,1,0:T(8,128)(2,1)S(1)} collective-permute-done((bf16[2,8,1024]{2,1,0:T(8,128)(2,1)S(1)}, bf16[2,8,1024]{2,1,0:T(8,128)(2,1)S(1)}, u32[]{:S(2)}, u32[]{:S(2)}) %collective-permute-start.15) | collective-permute-done | bytes 32800 | tf_op jit(solution)/shard_map/ppermute | solution.py:29
  67.6 0.6 collective-permute-start.16
  68.2 3.8 %collective-permute-done.5 = bf16[4,2,8,1024]{3,2,1,0:T(8,128)(2,1)S(1)} collective-permute-done((bf16[4,2,8,1024]{3,2,1,0:T(8,128)(2,1)S(1)}, bf16[4,2,8,1024]{3,2,1,0:T(8,128)(2,1)S(1)}, u32[]{:S(2)}, u32[]{:S(2)}) %collective-permute-start.5) | collective-permute-done | bytes 131104 | tf_op jit(solution)/shard_map/ppermute | solution.py:29
  72.3 0.9 collective-permute-done.16
  73.2 1.6 %collective-permute-start.17 = (bf16[2,8,1024]{2,1,0:T(8,128)(2,1)S(1)}, bf16[2,8,1024]{2,1,0:T(8,128)(2,1)S(1)}, u32[]{:S(2)}, u32[]{:S(2)}) collective-permute-start(bf16[2,8,1024]{2,1,0:T(8,128)(2,1)S(1)} %fusion.62), channel_id=1, source_target_pairs={{0,8},{8,16},{16,24},{24,32},{32,40},{40,48},{48,56},{56,0},{1,9},... | collective-permute-start | bytes 98312 | tf_op jit(solution)/shard_map/ppermute | solution.py:29
  74.8 4.8 %collective-permute-done.6 = bf16[4,2,8,1024]{3,2,1,0:T(8,128)(2,1)S(1)} collective-permute-done((bf16[4,2,8,1024]{3,2,1,0:T(8,128)(2,1)S(1)}, bf16[4,2,8,1024]{3,2,1,0:T(8,128)(2,1)S(1)}, u32[]{:S(2)}, u32[]{:S(2)}) %collective-permute-start.6) | collective-permute-done | bytes 131104 | tf_op jit(solution)/shard_map/ppermute | solution.py:29
  79.9 0.4 collective-permute-done.17
  80.3 0.7 collective-permute-start.18
  81.0 5.3 %collective-permute-done.7 = bf16[4,2,8,1024]{3,2,1,0:T(8,128)(2,1)S(1)} collective-permute-done((bf16[4,2,8,1024]{3,2,1,0:T(8,128)(2,1)S(1)}, bf16[4,2,8,1024]{3,2,1,0:T(8,128)(2,1)S(1)}, u32[]{:S(2)}, u32[]{:S(2)}) %collective-permute-start.7) | collective-permute-done | bytes 131104 | tf_op jit(solution)/shard_map/ppermute | solution.py:29
  86.5 0.6 collective-permute-start.8
  87.2 4.6 %collective-permute-done.8 = bf16[2,8,1024]{2,1,0:T(8,128)(2,1)S(1)} collective-permute-done((bf16[2,8,1024]{2,1,0:T(8,128)(2,1)S(1)}, bf16[2,8,1024]{2,1,0:T(8,128)(2,1)S(1)}, u32[]{:S(2)}, u32[]{:S(2)}) %collective-permute-start.8) | collective-permute-done | bytes 32800 | tf_op jit(solution)/shard_map/ppermute | solution.py:29
  91.9 0.4 collective-permute-done.19
  92.3 0.3 collective-permute-start.20
  92.6 4.4 %collective-permute-done.9 = bf16[2,8,1024]{2,1,0:T(8,128)(2,1)S(1)} collective-permute-done((bf16[2,8,1024]{2,1,0:T(8,128)(2,1)S(1)}, bf16[2,8,1024]{2,1,0:T(8,128)(2,1)S(1)}, u32[]{:S(2)}, u32[]{:S(2)}) %collective-permute-start.9) | collective-permute-done | bytes 32800 | tf_op jit(solution)/shard_map/ppermute | solution.py:29
  97.1 0.6 collective-permute-done.20
  97.9 4.3 %collective-permute-done.10 = bf16[2,8,1024]{2,1,0:T(8,128)(2,1)S(1)} collective-permute-done((bf16[2,8,1024]{2,1,0:T(8,128)(2,1)S(1)}, bf16[2,8,1024]{2,1,0:T(8,128)(2,1)S(1)}, u32[]{:S(2)}, u32[]{:S(2)}) %collective-permute-start.10) | collective-permute-done | bytes 32800 | tf_op jit(solution)/shard_map/ppermute | solution.py:29
  102.8 0.5 convolution_bitcast_fusion
  103.3 0.4 slice_bitcast_fusion
  103.6 1.2 %convolution_bitcast_fusion.1 = f32[1,16,16,128]{3,1,2,0:T(8,128)S(1)} fusion(bf16[16,8,64,128]{3,2,1,0:T(8,128)(2,1)S(1)} %copy-done, f32[16,16,8,64]{3,2,1,0:T(8,128)S(1)} %get-tuple-element.17), kind=kOutput, calls=%fused_computation.17 | convolution fusion | flops 100663296 | bytes 2752512 | tf_op jit(solution)/shard_map/mflpi,lpij->mflj/dot_general | solution.py:106
  104.9 1.2 %convolution_bitcast_fusion.2 = f32[1,16,16,128]{3,1,2,0:T(8,128)S(1)} fusion(bf16[16,8,64,128]{3,2,1,0:T(8,128)(2,1)S(1)} %copy-done, f32[16,16,8,64]{3,2,1,0:T(8,128)S(1)} %get-tuple-element.18), kind=kOutput, calls=%fused_computation.18 | convolution fusion | flops 100663296 | bytes 2752512 | tf_op jit(solution)/shard_map/mflpi,lpij->mflj/dot_general | solution.py:105
  106.3 0.6 collective-permute-start.21
  106.9 1.5 %collective-permute-start.23 = (bf16[1,16,16,128]{3,1,2,0:T(8,128)(2,1)S(1)}, bf16[1,16,16,128]{3,1,2,0:T(8,128)(2,1)S(1)}, u32[]{:S(2)}, u32[]{:S(2)}) collective-permute-start(bf16[1,16,16,128]{3,1,2,0:T(8,128)(2,1)S(1)} %pad_maximum_fusion.1), channel_id=1, source_target_pairs={{0,3},{1,0},{2,1},{3,2},{4,7},{5,4},{6,5},{7,6},{8,11},{9,8},{10,9... | collective-permute-start | bytes 196616 | tf_op jit(solution)/shard_map/ppermute | solution.py:119
  108.4 1.4 %collective-permute-start.22 = (bf16[1,16,16,128]{3,1,2,0:T(8,128)(2,1)S(1)}, bf16[1,16,16,128]{3,1,2,0:T(8,128)(2,1)S(1)}, u32[]{:S(2)}, u32[]{:S(2)}) collective-permute-start(bf16[1,16,16,128]{3,1,2,0:T(8,128)(2,1)S(1)} %pad_maximum_fusion.1), channel_id=1, source_target_pairs={{0,2},{1,3},{2,0},{3,1},{4,6},{5,7},{6,4},{7,5},{8,10},{9,11},{10,... | collective-permute-start | bytes 196616 | tf_op jit(solution)/shard_map/ppermute | solution.py:119
  109.8 0.3 fusion.45
  110.2 0.5 collective-permute-done.21
  110.7 0.3 convolution_add_fusion.1
  111.0 1.4 %collective-permute-done.23 = bf16[1,16,16,128]{3,1,2,0:T(8,128)(2,1)S(1)} collective-permute-done((bf16[1,16,16,128]{3,1,2,0:T(8,128)(2,1)S(1)}, bf16[1,16,16,128]{3,1,2,0:T(8,128)(2,1)S(1)}, u32[]{:S(2)}, u32[]{:S(2)}) %collective-permute-start.23) | collective-permute-done | bytes 65568 | tf_op jit(solution)/shard_map/ppermute | solution.py:119
  112.7 1.6 %collective-permute-done.22 = bf16[1,16,16,128]{3,1,2,0:T(8,128)(2,1)S(1)} collective-permute-done((bf16[1,16,16,128]{3,1,2,0:T(8,128)(2,1)S(1)}, bf16[1,16,16,128]{3,1,2,0:T(8,128)(2,1)S(1)}, u32[]{:S(2)}, u32[]{:S(2)}) %collective-permute-start.22) | collective-permute-done | bytes 65568 | tf_op jit(solution)/shard_map/ppermute | solution.py:119
  114.2 0.3 fusion.16
  114.5 0.7 copy.33
  (72 shorter events, 3.9 us)
Async XLA Ops:
  0.0 103.6 %copy-start = (bf16[16,8,64,128]{3,2,1,0:T(8,128)(2,1)S(1)}, bf16[16,8,64,128]{3,2,1,0:T(8,128)(2,1)}, u32[]{:S(2)}) copy-start(bf16[16,8,64,128]{3,2,1,0:T(8,128)(2,1)} %param.7) | copy-start | bytes 6291460
  0.9 4.6 %copy-start.3 = (f32[16,2,64,1024]{3,2,1,0:T(8,128)S(1)}, f32[16,2,64,1024]{3,2,1,0:T(8,128)}, u32[]{:S(2)}) copy-start(f32[16,2,64,1024]{3,2,1,0:T(8,128)} %param.6) | copy-start | bytes 25165828
  5.3 2.4 %copy-start.1 = (f32[64,2,8,1024]{3,0,2,1:T(8,128)}, f32[64,2,8,1024]{3,0,2,1:T(8,128)S(1)}, u32[]{:S(2)}) copy-start(f32[64,2,8,1024]{3,0,2,1:T(8,128)S(1)} %fusion.9) | copy-start | bytes 12582916
  7.7 2.6 %copy-start.2 = (f32[64,2,8,1024]{3,0,2,1:T(8,128)}, f32[64,2,8,1024]{3,0,2,1:T(8,128)S(1)}, u32[]{:S(2)}) copy-start(f32[64,2,8,1024]{3,0,2,1:T(8,128)S(1)} %fusion.6) | copy-start | bytes 12582916
  7.9 3.1 %copy-start.8 = (f32[16,64,64]{2,1,0:T(8,128)S(1)}, f32[16,64,64]{2,1,0:T(8,128)}, u32[]{:S(2)}) copy-start(f32[16,64,64]{2,1,0:T(8,128)} %param.10) | copy-start | bytes 786436
  10.3 4.5 %collective-permute-start = (bf16[2,32,2,8,1024]{4,1,3,2,0:T(8,128)(2,1)}, bf16[2,32,2,8,1024]{4,1,3,2,0:T(8,128)(2,1)}, u32[]{:S(2)}, u32[]{:S(2)}) collective-permute-start(bf16[2,32,2,8,1024]{4,1,3,2,0:T(8,128)(2,1)} %pad_maximum_fusion), channel_id=1, source_target_pairs={{0,4},{4,0},{1,5},{5,1},{2,6},{6,2},{3,7},{7,3},{8,12},{12,8},{9,1... | collective-permute-start | bytes 6291464 | tf_op jit(solution)/shard_map/ppermute | solution.py:57
  24.9 9.7 %collective-permute-start.11 = (bf16[8,2,8,1024]{3,2,1,0:T(8,128)(2,1)S(1)}, bf16[8,2,8,1024]{3,2,1,0:T(8,128)(2,1)S(1)}, u32[]{:S(2)}, u32[]{:S(2)}) collective-permute-start(bf16[8,2,8,1024]{3,2,1,0:T(8,128)(2,1)S(1)} %bitcast.217), channel_id=1, source_target_pairs={{0,64},{64,128},{128,192},{192,0},{1,65},{65,129},{129,193},{193,1... | collective-permute-start | bytes 786440 | tf_op jit(solution)/shard_map/ppermute | solution.py:29
  27.6 7.7 %copy-start.4 = (f32[8,4,2,8,1024]{4,1,0,3,2:T(4,128)S(1)}, f32[8,4,2,8,1024]{4,1,0,3,2:T(4,128)}, u32[]{:S(2)}) copy-start(f32[8,4,2,8,1024]{4,1,0,3,2:T(4,128)} %reshape.538) | copy-start | bytes 6291460
  27.6 9.5 %collective-permute-start.1 = (bf16[4,2,8,1024]{3,2,1,0:T(8,128)(2,1)S(1)}, bf16[4,2,8,1024]{3,2,1,0:T(8,128)(2,1)S(1)}, u32[]{:S(2)}, u32[]{:S(2)}) collective-permute-start(bf16[4,2,8,1024]{3,2,1,0:T(8,128)(2,1)S(1)} %bitcast.220), channel_id=1, source_target_pairs={{0,8},{8,16},{16,24},{24,32},{32,40},{40,48},{48,56},{56,0},{1,9},... | collective-permute-start | bytes 393224 | tf_op jit(solution)/shard_map/ppermute | solution.py:29
  34.9 8.8 %collective-permute-start.12 = (bf16[8,2,8,1024]{3,2,1,0:T(8,128)(2,1)S(1)}, bf16[8,2,8,1024]{3,2,1,0:T(8,128)(2,1)S(1)}, u32[]{:S(2)}, u32[]{:S(2)}) collective-permute-start(bf16[8,2,8,1024]{3,2,1,0:T(8,128)(2,1)S(1)} %fusion.23), channel_id=1, source_target_pairs={{0,64},{64,128},{128,192},{192,0},{1,65},{65,129},{129,193},{193,1... | collective-permute-start | bytes 786440 | tf_op jit(solution)/shard_map/ppermute | solution.py:29
  37.9 9.7 %collective-permute-start.2 = (bf16[4,2,8,1024]{3,2,1,0:T(8,128)(2,1)}, bf16[4,2,8,1024]{3,2,1,0:T(8,128)(2,1)}, u32[]{:S(2)}, u32[]{:S(2)}) collective-permute-start(bf16[4,2,8,1024]{3,2,1,0:T(8,128)(2,1)} %fusion.33), channel_id=1, source_target_pairs={{0,8},{8,16},{16,24},{24,32},{32,40},{40,48},{48,56},{56,0},{1,9},... | collective-permute-start | bytes 393224 | tf_op jit(solution)/shard_map/ppermute | solution.py:29
  44.8 8.2 %collective-permute-start.13 = (bf16[8,2,8,1024]{3,2,1,0:T(8,128)(2,1)}, bf16[8,2,8,1024]{3,2,1,0:T(8,128)(2,1)}, u32[]{:S(2)}, u32[]{:S(2)}) collective-permute-start(bf16[8,2,8,1024]{3,2,1,0:T(8,128)(2,1)} %fusion.22), channel_id=1, source_target_pairs={{0,64},{64,128},{128,192},{192,0},{1,65},{65,129},{129,193},{193,1... | collective-permute-start | bytes 786440 | tf_op jit(solution)/shard_map/ppermute | solution.py:29
  47.5 17.5 %copy-start.7 = (f32[1,4,2,8,1024]{4,1,0,3,2:T(4,128)S(1)}, f32[1,4,2,8,1024]{4,1,0,3,2:T(4,128)}, u32[]{:S(2)}) copy-start(f32[1,4,2,8,1024]{4,1,0,3,2:T(4,128)} %get-tuple-element.9) | copy-start | bytes 786436
  47.5 24.5 %copy-start.6 = (f32[1,4,2,8,1024]{4,1,0,3,2:T(4,128)S(1)}, f32[1,4,2,8,1024]{4,1,0,3,2:T(4,128)}, u32[]{:S(2)}) copy-start(f32[1,4,2,8,1024]{4,1,0,3,2:T(4,128)} %get-tuple-element.8) | copy-start | bytes 786436
  47.5 32.1 %copy-start.5 = (f32[1,4,2,8,1024]{4,1,0,3,2:T(4,128)S(1)}, f32[1,4,2,8,1024]{4,1,0,3,2:T(4,128)}, u32[]{:S(2)}) copy-start(f32[1,4,2,8,1024]{4,1,0,3,2:T(4,128)} %get-tuple-element.7) | copy-start | bytes 786436
  48.8 8.9 %collective-permute-start.3 = (bf16[4,2,8,1024]{3,2,1,0:T(8,128)(2,1)S(1)}, bf16[4,2,8,1024]{3,2,1,0:T(8,128)(2,1)S(1)}, u32[]{:S(2)}, u32[]{:S(2)}) collective-permute-start(bf16[4,2,8,1024]{3,2,1,0:T(8,128)(2,1)S(1)} %fusion.32), channel_id=1, source_target_pairs={{0,8},{8,16},{16,24},{24,32},{32,40},{40,48},{48,56},{56,0},{1,9},... | collective-permute-start | bytes 393224 | tf_op jit(solution)/shard_map/ppermute | solution.py:29
  54.3 7.8 %collective-permute-start.14 = (bf16[2,8,1024]{2,1,0:T(8,128)(2,1)S(1)}, bf16[2,8,1024]{2,1,0:T(8,128)(2,1)S(1)}, u32[]{:S(2)}, u32[]{:S(2)}) collective-permute-start(bf16[2,8,1024]{2,1,0:T(8,128)(2,1)S(1)} %fusion.75), channel_id=1, source_target_pairs={{0,8},{8,16},{16,24},{24,32},{32,40},{40,48},{48,56},{56,0},{1,9},... | collective-permute-start | bytes 98312 | tf_op jit(solution)/shard_map/ppermute | solution.py:29
  58.7 6.3 %collective-permute-start.4 = (bf16[4,2,8,1024]{3,2,1,0:T(8,128)(2,1)S(1)}, bf16[4,2,8,1024]{3,2,1,0:T(8,128)(2,1)S(1)}, u32[]{:S(2)}, u32[]{:S(2)}) collective-permute-start(bf16[4,2,8,1024]{3,2,1,0:T(8,128)(2,1)S(1)} %fusion.31), channel_id=1, source_target_pairs={{0,8},{8,16},{16,24},{24,32},{32,40},{40,48},{48,56},{56,0},{1,9},... | collective-permute-start | bytes 393224 | tf_op jit(solution)/shard_map/ppermute | solution.py:29
  62.1 5.5 %collective-permute-start.15 = (bf16[2,8,1024]{2,1,0:T(8,128)(2,1)S(1)}, bf16[2,8,1024]{2,1,0:T(8,128)(2,1)S(1)}, u32[]{:S(2)}, u32[]{:S(2)}) collective-permute-start(bf16[2,8,1024]{2,1,0:T(8,128)(2,1)S(1)} %fusion.64), channel_id=1, source_target_pairs={{0,8},{8,16},{16,24},{24,32},{32,40},{40,48},{48,56},{56,0},{1,9},... | collective-permute-start | bytes 98312 | tf_op jit(solution)/shard_map/ppermute | solution.py:29
  65.0 37.8 %copy-start.9 = (f32[16,16,16]{1,2,0:T(8,128)S(1)}, f32[16,16,16]{1,2,0:T(8,128)}, u32[]{:S(2)}) copy-start(f32[16,16,16]{1,2,0:T(8,128)} %copy.15) | copy-start | bytes 49156
  65.2 6.9 %collective-permute-start.5 = (bf16[4,2,8,1024]{3,2,1,0:T(8,128)(2,1)S(1)}, bf16[4,2,8,1024]{3,2,1,0:T(8,128)(2,1)S(1)}, u32[]{:S(2)}, u32[]{:S(2)}) collective-permute-start(bf16[4,2,8,1024]{3,2,1,0:T(8,128)(2,1)S(1)} %fusion.30), channel_id=1, source_target_pairs={{0,8},{8,16},{16,24},{24,32},{32,40},{40,48},{48,56},{56,0},{1,9},... | collective-permute-start | bytes 393224 | tf_op jit(solution)/shard_map/ppermute | solution.py:29
  67.6 5.5 %collective-permute-start.16 = (bf16[2,8,1024]{2,1,0:T(8,128)(2,1)S(1)}, bf16[2,8,1024]{2,1,0:T(8,128)(2,1)S(1)}, u32[]{:S(2)}, u32[]{:S(2)}) collective-permute-start(bf16[2,8,1024]{2,1,0:T(8,128)(2,1)S(1)} %fusion.63), channel_id=1, source_target_pairs={{0,8},{8,16},{16,24},{24,32},{32,40},{40,48},{48,56},{56,0},{1,9},... | collective-permute-start | bytes 98312 | tf_op jit(solution)/shard_map/ppermute | solution.py:29
  72.2 7.4 %collective-permute-start.6 = (bf16[4,2,8,1024]{3,2,1,0:T(8,128)(2,1)S(1)}, bf16[4,2,8,1024]{3,2,1,0:T(8,128)(2,1)S(1)}, u32[]{:S(2)}, u32[]{:S(2)}) collective-permute-start(bf16[4,2,8,1024]{3,2,1,0:T(8,128)(2,1)S(1)} %fusion.29), channel_id=1, source_target_pairs={{0,8},{8,16},{16,24},{24,32},{32,40},{40,48},{48,56},{56,0},{1,9},... | collective-permute-start | bytes 393224 | tf_op jit(solution)/shard_map/ppermute | solution.py:29
  73.2 7.1 %collective-permute-start.17 = (bf16[2,8,1024]{2,1,0:T(8,128)(2,1)S(1)}, bf16[2,8,1024]{2,1,0:T(8,128)(2,1)S(1)}, u32[]{:S(2)}, u32[]{:S(2)}) collective-permute-start(bf16[2,8,1024]{2,1,0:T(8,128)(2,1)S(1)} %fusion.62), channel_id=1, source_target_pairs={{0,8},{8,16},{16,24},{24,32},{32,40},{40,48},{48,56},{56,0},{1,9},... | collective-permute-start | bytes 98312 | tf_op jit(solution)/shard_map/ppermute | solution.py:29
  79.8 6.5 %collective-permute-start.7 = (bf16[4,2,8,1024]{3,2,1,0:T(8,128)(2,1)S(1)}, bf16[4,2,8,1024]{3,2,1,0:T(8,128)(2,1)S(1)}, u32[]{:S(2)}, u32[]{:S(2)}) collective-permute-start(bf16[4,2,8,1024]{3,2,1,0:T(8,128)(2,1)S(1)} %fusion.28), channel_id=1, source_target_pairs={{0,8},{8,16},{16,24},{24,32},{32,40},{40,48},{48,56},{56,0},{1,9},... | collective-permute-start | bytes 393224 | tf_op jit(solution)/shard_map/ppermute | solution.py:29
  80.3 6.7 %collective-permute-start.18 = (bf16[2,8,1024]{2,1,0:T(8,128)(2,1)S(1)}, bf16[2,8,1024]{2,1,0:T(8,128)(2,1)S(1)}, u32[]{:S(2)}, u32[]{:S(2)}) collective-permute-start(bf16[2,8,1024]{2,1,0:T(8,128)(2,1)S(1)} %fusion.61), channel_id=1, source_target_pairs={{0,8},{8,16},{16,24},{24,32},{32,40},{40,48},{48,56},{56,0},{1,9},... | collective-permute-start | bytes 98312 | tf_op jit(solution)/shard_map/ppermute | solution.py:29
  86.5 5.4 %collective-permute-start.8 = (bf16[2,8,1024]{2,1,0:T(8,128)(2,1)S(1)}, bf16[2,8,1024]{2,1,0:T(8,128)(2,1)S(1)}, u32[]{:S(2)}, u32[]{:S(2)}) collective-permute-start(bf16[2,8,1024]{2,1,0:T(8,128)(2,1)S(1)} %fusion.74), channel_id=1, source_target_pairs={{0,64},{64,128},{128,192},{192,0},{1,65},{65,129},{129,193},{193,1... | collective-permute-start | bytes 98312 | tf_op jit(solution)/shard_map/ppermute | solution.py:29
  87.1 5.2 %collective-permute-start.19 = (bf16[2,8,1024]{2,1,0:T(8,128)(2,1)S(1)}, bf16[2,8,1024]{2,1,0:T(8,128)(2,1)S(1)}, u32[]{:S(2)}, u32[]{:S(2)}) collective-permute-start(bf16[2,8,1024]{2,1,0:T(8,128)(2,1)S(1)} %fusion.60), channel_id=1, source_target_pairs={{0,8},{8,16},{16,24},{24,32},{32,40},{40,48},{48,56},{56,0},{1,9},... | collective-permute-start | bytes 98312 | tf_op jit(solution)/shard_map/ppermute | solution.py:29
  91.8 5.2 %collective-permute-start.9 = (bf16[2,8,1024]{2,1,0:T(8,128)(2,1)S(1)}, bf16[2,8,1024]{2,1,0:T(8,128)(2,1)S(1)}, u32[]{:S(2)}, u32[]{:S(2)}) collective-permute-start(bf16[2,8,1024]{2,1,0:T(8,128)(2,1)S(1)} %fusion.67), channel_id=1, source_target_pairs={{0,64},{64,128},{128,192},{192,0},{1,65},{65,129},{129,193},{193,1... | collective-permute-start | bytes 98312 | tf_op jit(solution)/shard_map/ppermute | solution.py:29
  92.3 5.4 %collective-permute-start.20 = (bf16[2,8,1024]{2,1,0:T(8,128)(2,1)S(1)}, bf16[2,8,1024]{2,1,0:T(8,128)(2,1)S(1)}, u32[]{:S(2)}, u32[]{:S(2)}) collective-permute-start(bf16[2,8,1024]{2,1,0:T(8,128)(2,1)S(1)} %fusion.59), channel_id=1, source_target_pairs={{0,8},{8,16},{16,24},{24,32},{32,40},{40,48},{48,56},{56,0},{1,9},... | collective-permute-start | bytes 98312 | tf_op jit(solution)/shard_map/ppermute | solution.py:29
  97.0 5.2 %collective-permute-start.10 = (bf16[2,8,1024]{2,1,0:T(8,128)(2,1)S(1)}, bf16[2,8,1024]{2,1,0:T(8,128)(2,1)S(1)}, u32[]{:S(2)}, u32[]{:S(2)}) collective-permute-start(bf16[2,8,1024]{2,1,0:T(8,128)(2,1)S(1)} %fusion.66), channel_id=1, source_target_pairs={{0,64},{64,128},{128,192},{192,0},{1,65},{65,129},{129,193},{193,1... | collective-permute-start | bytes 98312 | tf_op jit(solution)/shard_map/ppermute | solution.py:29
  106.3 4.3 %collective-permute-start.21 = (bf16[1,16,16,128]{3,1,2,0:T(8,128)(2,1)S(1)}, bf16[1,16,16,128]{3,1,2,0:T(8,128)(2,1)S(1)}, u32[]{:S(2)}, u32[]{:S(2)}) collective-permute-start(bf16[1,16,16,128]{3,1,2,0:T(8,128)(2,1)S(1)} %pad_maximum_fusion.1), channel_id=1, source_target_pairs={{0,1},{1,2},{2,3},{3,0},{4,5},{5,6},{6,7},{7,4},{8,9},{9,10},{10,1... | collective-permute-start | bytes 196616 | tf_op jit(solution)/shard_map/ppermute | solution.py:119
  106.9 5.5 %collective-permute-start.23 = (bf16[1,16,16,128]{3,1,2,0:T(8,128)(2,1)S(1)}, bf16[1,16,16,128]{3,1,2,0:T(8,128)(2,1)S(1)}, u32[]{:S(2)}, u32[]{:S(2)}) collective-permute-start(bf16[1,16,16,128]{3,1,2,0:T(8,128)(2,1)S(1)} %pad_maximum_fusion.1), channel_id=1, source_target_pairs={{0,3},{1,0},{2,1},{3,2},{4,7},{5,4},{6,5},{7,6},{8,11},{9,8},{10,9... | collective-permute-start | bytes 196616 | tf_op jit(solution)/shard_map/ppermute | solution.py:119
  108.4 5.8 %collective-permute-start.22 = (bf16[1,16,16,128]{3,1,2,0:T(8,128)(2,1)S(1)}, bf16[1,16,16,128]{3,1,2,0:T(8,128)(2,1)S(1)}, u32[]{:S(2)}, u32[]{:S(2)}) collective-permute-start(bf16[1,16,16,128]{3,1,2,0:T(8,128)(2,1)S(1)} %pad_maximum_fusion.1), channel_id=1, source_target_pairs={{0,2},{1,3},{2,0},{3,1},{4,6},{5,7},{6,4},{7,5},{8,10},{9,11},{10,... | collective-permute-start | bytes 196616 | tf_op jit(solution)/shard_map/ppermute | solution.py:119

commit v8 on v4

--- a/solution.py
+++ b/solution.py
@@ -21,8 +21,12 @@
     i = lax.axis_index(axis)
     fwd = [(j, (j + 1) % n) for j in range(n)]
 
+    m = x.shape[0] // n
+
     def take(a, k):
-        return lax.dynamic_index_in_dim(a, k % n, 0, keepdims=False)
+        if m == 1:
+            return lax.dynamic_index_in_dim(a, k % n, 0, keepdims=False)
+        return lax.dynamic_slice_in_dim(a, (k % n) * m, m, 0)
 
     s = take(x, i - 1)
     for k in range(n - 1):
@@ -56,10 +60,8 @@
         got = lax.ppermute(out[:half_rows].astype(jnp.bfloat16), "tc", [(0, 1), (1, 0)])
         y = out[half_rows:] + got.astype(jnp.float32)
         if z_major:
-            y = y.reshape(nz, ny, *y.shape[1:])
             y = ring_reduce_scatter(ring_reduce_scatter(y, "tz", nz), "ty", ny)
         else:
-            y = y.reshape(ny, nz, *y.shape[1:])
             y = ring_reduce_scatter(ring_reduce_scatter(y, "ty", ny), "tz", nz)
         halves.append(y)
     return jnp.concatenate(halves, axis=1)

time: 108 us -> 105 us (0.972)
  the two profiles are of different devices: /device:TPU:16 before, /device:TPU:6 now
where the time goes in v8:
time: 105 us; the launch traced here: 103 us
  waiting for transfers between devices  53.2 us (51%)
  other arithmetic  15.2 us (14%)
  starting transfers between devices  14 us (13%)
  matrix products  10.6 us (10%)
  local copies, waits for them, and re-layouts  8.59 us (8%)
  between operations  1.58 us (2%)
    ppermute x20, waiting for transfers between devices, ring_reduce_scatter(): got = lax.ppermute(s.astype(jnp.bfloat16), axis, fwd)  49.7 us
    ppermute x20, starting transfers between devices, ring_reduce_scatter(): got = lax.ppermute(s.astype(jnp.bfloat16), axis, fwd)  10 us
    convert_element_type x16, other arithmetic, ring_reduce_scatter(): got = lax.ppermute(s.astype(jnp.bfloat16), axis, fwd)  8.21 us
    dot_general x2, matrix products, spectra_of(): jnp.einsum('rdct,fctb->rdfb', table, part, precision=lax.Precision.HIGH)  6.54 us
    add x2, other arithmetic, spectra_of(): y = out[half_rows:] + got.astype(jnp.float32)  3.73 us
    ppermute x3, starting transfers between devices, local(): lax.ppermute(weights_bf, 'freq', [(j, (j + s) % fr_count) for j in range(...  3.48 us
    ppermute x3, waiting for transfers between devices, local(): lax.ppermute(weights_bf, 'freq', [(j, (j + s) % fr_count) for j in range(...  3.47 us
    slice x2, local copies, waits for them, and re-layouts, spectra_of(): out[:half_rows].astype(jnp.bfloat16)  2.6 us
  transfers between devices with their start and end apart: 25, of which 20 were waited for; matrix products, arithmetic and copies ran while one was open for 21% of the time, Pallas kernels for 0%

profile of v8, /device:TPU:6, one launch (start us, length us, event | category | flops | bytes accessed | tf_op | source)
XLA Modules:
  0.0 103.2 jit_solution(15143696885271446080)
XLA Ops:
  0.5 0.4 sine_multiply_fusion.1
  0.9 4.4 %fusion.6 = f32[64,2,8,1024]{3,0,2,1:T(8,128)S(1)} fusion(f32[16,2,64,1024]{3,2,1,0:T(8,128)} %param.6, f32[64,1,2,64]{3,0,2,1:T(8,128)S(1)} %get-tuple-element.20, f32[64,1,2,64]{3,0,2,1:T(8,128)S(1)} %get-tuple-element.19), kind=kOutput, calls=%fused_computation.6 | convolution fusion | flops 805322752 | bytes 8454144 | tf_op jit(solution)/shard_map/rdct,fctb->rdfb/dot_general | solution.py:58
  5.3 1.3 %slice.87 = bf16[32,2,8,1024]{3,0,2,1:T(8,128)(2,1)} slice(f32[64,2,8,1024]{3,0,2,1:T(8,128)S(1)} %fusion.6), slice={[0:32], [0:2], [0:8], [0:1024]} | slice | bytes 2097152 | tf_op jit(solution)/shard_map/slice | solution.py:60
  6.6 2.2 %fusion.9 = f32[64,2,8,1024]{3,0,2,1:T(8,128)S(1)} fusion(f32[16,2,64,1024]{3,2,1,0:T(8,128)S(1)} %copy-done.4, f32[64,1,2,64]{3,0,2,1:T(8,128)S(1)} %get-tuple-element.22, f32[64,1,2,64]{3,0,2,1:T(8,128)S(1)} %get-tuple-element.21), kind=kOutput, calls=%fused_computation.7 | convolution fusion | flops 805322752 | bytes 8519680 | tf_op jit(solution)/shard_map/rdct,fctb->rdfb/dot_general | solution.py:58
  8.8 1.3 %slice.86 = bf16[32,2,8,1024]{3,0,2,1:T(8,128)(2,1)} slice(f32[64,2,8,1024]{3,0,2,1:T(8,128)S(1)} %fusion.9), slice={[0:32], [0:2], [0:8], [0:1024]} | slice | bytes 2097152 | tf_op jit(solution)/shard_map/slice | solution.py:60
  10.1 1.0 copy-done.2
  11.1 0.5 collective-permute-start.11
  11.6 2.1 %slice_add_fusion.1 = f32[32,2,8,1024]{3,0,2,1:T(8,128)S(1)} fusion(f32[64,2,8,1024]{3,0,2,1:T(8,128)} %copy-done.1, bf16[32,2,8,1024]{3,0,2,1:T(8,128)(2,1)S(1)} %collective-permute-done), kind=kLoop, calls=%fused_computation.11 | loop fusion | flops 1048576 | bytes 5242880 | tf_op jit(solution)/shard_map/add | solution.py:61
  13.7 2.0 %collective-permute-start.1 = (bf16[4,2,8,1024]{3,0,2,1:T(4,128)(2,1)S(1)}, bf16[4,2,8,1024]{3,0,2,1:T(4,128)(2,1)S(1)}, u32[]{:S(2)}, u32[]{:S(2)}) collective-permute-start(bf16[4,2,8,1024]{3,0,2,1:T(4,128)(2,1)S(1)} %dynamic-slice_convert_fusion.1), channel_id=1, source_target_pairs={{0,8},{8,16},{16,24},{24,32},{32,40},{40,48},{48,56},{56,0},{1,9},... | collective-permute-start | bytes 393224 | tf_op jit(solution)/shard_map/ppermute | solution.py:33
  15.7 1.7 %slice_add_fusion = f32[32,2,8,1024]{3,0,2,1:T(8,128)S(1)} fusion(f32[64,2,8,1024]{3,0,2,1:T(8,128)S(1)} %copy-done.3, bf16[32,2,8,1024]{3,0,2,1:T(8,128)(2,1)} %collective-permute-done.11), kind=kLoop, calls=%fused_computation.9 | loop fusion | flops 1048576 | bytes 5242880 | tf_op jit(solution)/shard_map/add | solution.py:61
  17.4 5.9 %collective-permute-done.1 = bf16[4,2,8,1024]{3,0,2,1:T(4,128)(2,1)S(1)} collective-permute-done((bf16[4,2,8,1024]{3,0,2,1:T(4,128)(2,1)S(1)}, bf16[4,2,8,1024]{3,0,2,1:T(4,128)(2,1)S(1)}, u32[]{:S(2)}, u32[]{:S(2)}) %collective-permute-start.1) | collective-permute-done | bytes 131104 | tf_op jit(solution)/shard_map/ppermute | solution.py:33
  23.6 1.7 %collective-permute-start.12 = (bf16[8,2,8,1024]{3,0,2,1:T(8,128)(2,1)S(1)}, bf16[8,2,8,1024]{3,0,2,1:T(8,128)(2,1)S(1)}, u32[]{:S(2)}, u32[]{:S(2)}) collective-permute-start(bf16[8,2,8,1024]{3,0,2,1:T(8,128)(2,1)S(1)} %dynamic-slice_convert_fusion), channel_id=1, source_target_pairs={{0,64},{64,128},{128,192},{192,0},{1,65},{65,129},{129,193},{193,1... | collective-permute-start | bytes 786440 | tf_op jit(solution)/shard_map/ppermute | solution.py:33
  25.3 4.4 %collective-permute-done.2 = bf16[4,2,8,1024]{3,0,2,1:T(4,128)(2,1)S(1)} collective-permute-done((bf16[4,2,8,1024]{3,0,2,1:T(4,128)(2,1)S(1)}, bf16[4,2,8,1024]{3,0,2,1:T(4,128)(2,1)S(1)}, u32[]{:S(2)}, u32[]{:S(2)}) %collective-permute-start.2) | collective-permute-done | bytes 131104 | tf_op jit(solution)/shard_map/ppermute | solution.py:33
  29.7 1.1 %add_convert_fusion.6 = bf16[4,2,8,1024]{3,0,2,1:T(4,128)(2,1)S(1)} fusion(f32[32,2,8,1024]{3,0,2,1:T(8,128)} %copy-done.5, s32[]{:T(128)S(6)} %select_n.242, bf16[4,2,8,1024]{3,0,2,1:T(4,128)(2,1)S(1)} %collective-permute-done.2), kind=kLoop, calls=%fused_computation.39 | loop fusion | flops 196608 | bytes 524292 | tf_op jit(solution)/shard_map/convert_element_type | solution.py:33
  30.9 1.7 %collective-permute-done.12 = bf16[8,2,8,1024]{3,0,2,1:T(8,128)(2,1)S(1)} collective-permute-done((bf16[8,2,8,1024]{3,0,2,1:T(8,128)(2,1)S(1)}, bf16[8,2,8,1024]{3,0,2,1:T(8,128)(2,1)S(1)}, u32[]{:S(2)}, u32[]{:S(2)}) %collective-permute-start.12) | collective-permute-done | bytes 262176 | tf_op jit(solution)/shard_map/ppermute | solution.py:33
  32.6 1.1 %add_convert_fusion.1 = bf16[8,2,8,1024]{3,0,2,1:T(8,128)(2,1)S(1)} fusion(f32[32,2,8,1024]{3,0,2,1:T(8,128)} %copy-done.6, s32[]{:T(128)S(6)} %select_n.263, bf16[8,2,8,1024]{3,0,2,1:T(8,128)(2,1)S(1)} %collective-permute-done.12), kind=kLoop, calls=%fused_computation.29 | loop fusion | flops 393216 | bytes 1048580 | tf_op jit(solution)/shard_map/convert_element_type | solution.py:33
  33.7 0.4 collective-permute-start.13
  34.1 0.2 constant_dynamic-slice_fusion
  35.0 2.2 %collective-permute-done.3 = bf16[4,2,8,1024]{3,0,2,1:T(4,128)(2,1)} collective-permute-done((bf16[4,2,8,1024]{3,0,2,1:T(4,128)(2,1)S(1)}, bf16[4,2,8,1024]{3,0,2,1:T(4,128)(2,1)}, u32[]{:S(2)}, u32[]{:S(2)}) %collective-permute-start.3) | collective-permute-done | bytes 131104 | tf_op jit(solution)/shard_map/ppermute | solution.py:33
  37.2 1.2 %add_convert_fusion.5 = bf16[4,2,8,1024]{3,0,2,1:T(4,128)(2,1)S(1)} fusion(f32[32,2,8,1024]{3,0,2,1:T(8,128)} %copy-done.5, s32[]{:T(128)S(6)} %select_n.244, bf16[4,2,8,1024]{3,0,2,1:T(4,128)(2,1)} %collective-permute-done.3), kind=kLoop, calls=%fused_computation.38 | loop fusion | flops 196608 | bytes 524292 | tf_op jit(solution)/shard_map/convert_element_type | solution.py:33
  38.4 3.5 %collective-permute-done.13 = bf16[8,2,8,1024]{3,0,2,1:T(8,128)(2,1)} collective-permute-done((bf16[8,2,8,1024]{3,0,2,1:T(8,128)(2,1)S(1)}, bf16[8,2,8,1024]{3,0,2,1:T(8,128)(2,1)}, u32[]{:S(2)}, u32[]{:S(2)}) %collective-permute-start.13) | collective-permute-done | bytes 262176 | tf_op jit(solution)/shard_map/ppermute | solution.py:33
  42.0 1.2 %add_convert_fusion = bf16[8,2,8,1024]{3,0,2,1:T(8,128)(2,1)S(1)} fusion(f32[32,2,8,1024]{3,0,2,1:T(8,128)} %copy-done.6, s32[]{:T(128)S(6)} %select_n.264, bf16[8,2,8,1024]{3,0,2,1:T(8,128)(2,1)} %collective-permute-done.13), kind=kLoop, calls=%fused_computation.28 | loop fusion | flops 393216 | bytes 1048580 | tf_op jit(solution)/shard_map/convert_element_type | solution.py:33
  43.1 0.3 collective-permute-start.14
  43.6 1.0 copy.13
  44.6 1.0 copy.14
  45.8 1.2 %add_convert_fusion.4 = bf16[4,2,8,1024]{3,0,2,1:T(4,128)(2,1)S(1)} fusion(f32[32,2,8,1024]{3,0,2,1:T(8,128)} %copy-done.5, s32[]{:T(128)S(6)} %select_n.246, bf16[4,2,8,1024]{3,0,2,1:T(4,128)(2,1)} %collective-permute-done.4), kind=kLoop, calls=%fused_computation.37 | loop fusion | flops 196608 | bytes 524292 | tf_op jit(solution)/shard_map/convert_element_type | solution.py:33
  47.0 3.9 %collective-permute-done.14 = bf16[8,2,8,1024]{3,0,2,1:T(8,128)(2,1)S(1)} collective-permute-done((bf16[8,2,8,1024]{3,0,2,1:T(8,128)(2,1)S(1)}, bf16[8,2,8,1024]{3,0,2,1:T(8,128)(2,1)S(1)}, u32[]{:S(2)}, u32[]{:S(2)}) %collective-permute-start.14) | collective-permute-done | bytes 262176 | tf_op jit(solution)/shard_map/ppermute | solution.py:33
  51.0 1.1 %dynamic-slice_add_fusion = f32[8,2,8,1024]{3,0,2,1:T(8,128)S(1)} fusion(f32[32,2,8,1024]{3,0,2,1:T(8,128)} %copy-done.6, s32[]{:T(128)S(6)} %select_n.265, bf16[8,2,8,1024]{3,0,2,1:T(8,128)(2,1)S(1)} %collective-permute-done.14), kind=kLoop, calls=%fused_computation.27 | loop fusion | flops 262144 | bytes 1310724 | tf_op jit(solution)/shard_map/add | solution.py:34
  52.2 0.5 constant_dynamic-slice_fusion.7
  52.7 4.6 %collective-permute-done.15 = bf16[2,8,1024]{2,1,0:T(8,128)(2,1)S(1)} collective-permute-done((bf16[2,8,1024]{2,1,0:T(8,128)(2,1)S(1)}, bf16[2,8,1024]{2,1,0:T(8,128)(2,1)S(1)}, u32[]{:S(2)}, u32[]{:S(2)}) %collective-permute-start.15) | collective-permute-done | bytes 32800 | tf_op jit(solution)/shard_map/ppermute | solution.py:33
  57.5 1.2 %add_convert_fusion.3 = bf16[4,2,8,1024]{3,0,2,1:T(4,128)(2,1)S(1)} fusion(f32[32,2,8,1024]{3,0,2,1:T(8,128)} %copy-done.5, s32[]{:T(128)S(6)} %select_n.248, bf16[4,2,8,1024]{3,0,2,1:T(4,128)(2,1)S(1)} %collective-permute-done.5), kind=kLoop, calls=%fused_computation.36 | loop fusion | flops 196608 | bytes 524292 | tf_op jit(solution)/shard_map/convert_element_type | solution.py:33
  58.6 1.4 %collective-permute-start.6 = (bf16[4,2,8,1024]{3,0,2,1:T(4,128)(2,1)S(1)}, bf16[4,2,8,1024]{3,0,2,1:T(4,128)(2,1)S(1)}, u32[]{:S(2)}, u32[]{:S(2)}) collective-permute-start(bf16[4,2,8,1024]{3,0,2,1:T(4,128)(2,1)S(1)} %add_convert_fusion.3), channel_id=1, source_target_pairs={{0,8},{8,16},{16,24},{24,32},{32,40},{40,48},{48,56},{56,0},{1,9},... | collective-permute-start | bytes 393224 | tf_op jit(solution)/shard_map/ppermute | solution.py:33
  60.0 2.5 %collective-permute-done.16 = bf16[2,8,1024]{2,1,0:T(8,128)(2,1)S(1)} collective-permute-done((bf16[2,8,1024]{2,1,0:T(8,128)(2,1)S(1)}, bf16[2,8,1024]{2,1,0:T(8,128)(2,1)S(1)}, u32[]{:S(2)}, u32[]{:S(2)}) %collective-permute-start.16) | collective-permute-done | bytes 32800 | tf_op jit(solution)/shard_map/ppermute | solution.py:33
  62.7 2.2 %collective-permute-done.6 = bf16[4,2,8,1024]{3,0,2,1:T(4,128)(2,1)S(1)} collective-permute-done((bf16[4,2,8,1024]{3,0,2,1:T(4,128)(2,1)S(1)}, bf16[4,2,8,1024]{3,0,2,1:T(4,128)(2,1)S(1)}, u32[]{:S(2)}, u32[]{:S(2)}) %collective-permute-start.6) | collective-permute-done | bytes 131104 | tf_op jit(solution)/shard_map/ppermute | solution.py:33
  64.9 1.1 %add_convert_fusion.2 = bf16[4,2,8,1024]{3,0,2,1:T(4,128)(2,1)S(1)} fusion(f32[32,2,8,1024]{3,0,2,1:T(8,128)} %copy-done.5, s32[]{:T(128)S(6)} %select_n.250, bf16[4,2,8,1024]{3,0,2,1:T(4,128)(2,1)S(1)} %collective-permute-done.6), kind=kLoop, calls=%fused_computation.35 | loop fusion | flops 196608 | bytes 524292 | tf_op jit(solution)/shard_map/convert_element_type | solution.py:33
  66.0 1.2 %collective-permute-start.7 = (bf16[4,2,8,1024]{3,0,2,1:T(4,128)(2,1)S(1)}, bf16[4,2,8,1024]{3,0,2,1:T(4,128)(2,1)S(1)}, u32[]{:S(2)}, u32[]{:S(2)}) collective-permute-start(bf16[4,2,8,1024]{3,0,2,1:T(4,128)(2,1)S(1)} %add_convert_fusion.2), channel_id=1, source_target_pairs={{0,8},{8,16},{16,24},{24,32},{32,40},{40,48},{48,56},{56,0},{1,9},... | collective-permute-start | bytes 393224 | tf_op jit(solution)/shard_map/ppermute | solution.py:33
  67.3 0.5 collective-permute-done.17
  67.8 1.8 %collective-permute-start.18 = (bf16[2,8,1024]{2,1,0:T(8,128)(2,1)S(1)}, bf16[2,8,1024]{2,1,0:T(8,128)(2,1)S(1)}, u32[]{:S(2)}, u32[]{:S(2)}) collective-permute-start(bf16[2,8,1024]{2,1,0:T(8,128)(2,1)S(1)} %fusion.45), channel_id=1, source_target_pairs={{0,8},{8,16},{16,24},{24,32},{32,40},{40,48},{48,56},{56,0},{1,9},... | collective-permute-start | bytes 98312 | tf_op jit(solution)/shard_map/ppermute | solution.py:33
  69.6 3.2 %collective-permute-done.7 = bf16[4,2,8,1024]{3,0,2,1:T(4,128)(2,1)S(1)} collective-permute-done((bf16[4,2,8,1024]{3,0,2,1:T(4,128)(2,1)S(1)}, bf16[4,2,8,1024]{3,0,2,1:T(4,128)(2,1)S(1)}, u32[]{:S(2)}, u32[]{:S(2)}) %collective-permute-start.7) | collective-permute-done | bytes 131104 | tf_op jit(solution)/shard_map/ppermute | solution.py:33
  72.8 1.1 %dynamic-slice_add_fusion.1 = f32[4,2,8,1024]{3,0,2,1:T(4,128)S(1)} fusion(f32[32,2,8,1024]{3,0,2,1:T(8,128)} %copy-done.5, s32[]{:T(128)S(6)} %select_n.252, bf16[4,2,8,1024]{3,0,2,1:T(4,128)(2,1)S(1)} %collective-permute-done.7), kind=kLoop, calls=%fused_computation.34 | loop fusion | flops 131072 | bytes 655364 | tf_op jit(solution)/shard_map/add | solution.py:34
  74.1 0.2 constant_dynamic-slice_fusion.10
  74.5 4.8 %collective-permute-done.8 = bf16[2,8,1024]{2,1,0:T(8,128)(2,1)S(1)} collective-permute-done((bf16[2,8,1024]{2,1,0:T(8,128)(2,1)S(1)}, bf16[2,8,1024]{2,1,0:T(8,128)(2,1)S(1)}, u32[]{:S(2)}, u32[]{:S(2)}) %collective-permute-start.8) | collective-permute-done | bytes 32800 | tf_op jit(solution)/shard_map/ppermute | solution.py:33
  79.4 0.2 collective-permute-done.19
  79.7 4.8 %collective-permute-done.9 = bf16[2,8,1024]{2,1,0:T(8,128)(2,1)S(1)} collective-permute-done((bf16[2,8,1024]{2,1,0:T(8,128)(2,1)S(1)}, bf16[2,8,1024]{2,1,0:T(8,128)(2,1)S(1)}, u32[]{:S(2)}, u32[]{:S(2)}) %collective-permute-start.9) | collective-permute-done | bytes 32800 | tf_op jit(solution)/shard_map/ppermute | solution.py:33
  84.6 0.2 collective-permute-done.20
  84.8 0.3 collective-permute-start.21
  85.1 4.6 %collective-permute-done.10 = bf16[2,8,1024]{2,1,0:T(8,128)(2,1)S(1)} collective-permute-done((bf16[2,8,1024]{2,1,0:T(8,128)(2,1)S(1)}, bf16[2,8,1024]{2,1,0:T(8,128)(2,1)S(1)}, u32[]{:S(2)}, u32[]{:S(2)}) %collective-permute-start.10) | collective-permute-done | bytes 32800 | tf_op jit(solution)/shard_map/ppermute | solution.py:33
  89.9 0.3 collective-permute-done.21
  90.5 0.2 maximum_bitcast_fusion.4
  90.8 0.5 convolution_bitcast_fusion
  91.3 0.4 slice_bitcast_fusion
  91.6 1.2 %convolution_bitcast_fusion.1 = f32[1,16,16,128]{3,1,2,0:T(8,128)S(1)} fusion(bf16[16,8,64,128]{3,2,1,0:T(8,128)(2,1)S(1)} %copy-done, f32[16,16,8,64]{3,2,1,0:T(8,128)S(1)} %get-tuple-element.5), kind=kOutput, calls=%fused_computation.15 | convolution fusion | flops 100663296 | bytes 2752512 | tf_op jit(solution)/shard_map/mflpi,lpij->mflj/dot_general | solution.py:104
  92.9 1.2 %convolution_bitcast_fusion.2 = f32[1,16,16,128]{3,1,2,0:T(8,128)S(1)} fusion(bf16[16,8,64,128]{3,2,1,0:T(8,128)(2,1)S(1)} %copy-done, f32[16,16,8,64]{3,2,1,0:T(8,128)S(1)} %get-tuple-element.6), kind=kOutput, calls=%fused_computation.16 | convolution fusion | flops 100663296 | bytes 2752512 | tf_op jit(solution)/shard_map/mflpi,lpij->mflj/dot_general | solution.py:103
  94.3 0.5 collective-permute-start.22
  94.9 1.6 %collective-permute-start.24 = (bf16[1,16,16,128]{3,1,2,0:T(8,128)(2,1)S(1)}, bf16[1,16,16,128]{3,1,2,0:T(8,128)(2,1)S(1)}, u32[]{:S(2)}, u32[]{:S(2)}) collective-permute-start(bf16[1,16,16,128]{3,1,2,0:T(8,128)(2,1)S(1)} %pad_maximum_fusion), channel_id=1, source_target_pairs={{0,3},{1,0},{2,1},{3,2},{4,7},{5,4},{6,5},{7,6},{8,11},{9,8},{10,9... | collective-permute-start | bytes 196616 | tf_op jit(solution)/shard_map/ppermute | solution.py:117
  96.4 1.4 %collective-permute-start.23 = (bf16[1,16,16,128]{3,1,2,0:T(8,128)(2,1)S(1)}, bf16[1,16,16,128]{3,1,2,0:T(8,128)(2,1)S(1)}, u32[]{:S(2)}, u32[]{:S(2)}) collective-permute-start(bf16[1,16,16,128]{3,1,2,0:T(8,128)(2,1)S(1)} %pad_maximum_fusion), channel_id=1, source_target_pairs={{0,2},{1,3},{2,0},{3,1},{4,6},{5,7},{6,4},{7,5},{8,10},{9,11},{10,... | collective-permute-start | bytes 196616 | tf_op jit(solution)/shard_map/ppermute | solution.py:117
  97.8 0.3 fusion.32
  98.2 0.5 collective-permute-done.22
  98.7 0.3 convolution_add_fusion.1
  99.0 1.4 %collective-permute-done.24 = bf16[1,16,16,128]{3,1,2,0:T(8,128)(2,1)S(1)} collective-permute-done((bf16[1,16,16,128]{3,1,2,0:T(8,128)(2,1)S(1)}, bf16[1,16,16,128]{3,1,2,0:T(8,128)(2,1)S(1)}, u32[]{:S(2)}, u32[]{:S(2)}) %collective-permute-start.24) | collective-permute-done | bytes 65568 | tf_op jit(solution)/shard_map/ppermute | solution.py:117
  100.4 0.3 fusion.28
  100.7 1.6 %collective-permute-done.23 = bf16[1,16,16,128]{3,1,2,0:T(8,128)(2,1)S(1)} collective-permute-done((bf16[1,16,16,128]{3,1,2,0:T(8,128)(2,1)S(1)}, bf16[1,16,16,128]{3,1,2,0:T(8,128)(2,1)S(1)}, u32[]{:S(2)}, u32[]{:S(2)}) %collective-permute-start.23) | collective-permute-done | bytes 65568 | tf_op jit(solution)/shard_map/ppermute | solution.py:117
  102.2 0.3 fusion.15
  102.5 0.7 copy.20
  (69 shorter events, 2.8 us)
Async XLA Ops:
  0.0 91.6 %copy-start = (bf16[16,8,64,128]{3,2,1,0:T(8,128)(2,1)S(1)}, bf16[16,8,64,128]{3,2,1,0:T(8,128)(2,1)}, u32[]{:S(2)}) copy-start(bf16[16,8,64,128]{3,2,1,0:T(8,128)(2,1)} %param.7) | copy-start | bytes 6291460
  0.9 5.7 %copy-start.4 = (f32[16,2,64,1024]{3,2,1,0:T(8,128)S(1)}, f32[16,2,64,1024]{3,2,1,0:T(8,128)}, u32[]{:S(2)}) copy-start(f32[16,2,64,1024]{3,2,1,0:T(8,128)} %param.6) | copy-start | bytes 25165828
  5.3 3.5 %copy-start.1 = (f32[64,2,8,1024]{3,0,2,1:T(8,128)}, f32[64,2,8,1024]{3,0,2,1:T(8,128)S(1)}, u32[]{:S(2)}) copy-start(f32[64,2,8,1024]{3,0,2,1:T(8,128)S(1)} %fusion.6) | copy-start | bytes 12582916
  6.6 5.0 %collective-permute-start = (bf16[32,2,8,1024]{3,0,2,1:T(8,128)(2,1)}, bf16[32,2,8,1024]{3,0,2,1:T(8,128)(2,1)S(1)}, u32[]{:S(2)}, u32[]{:S(2)}) collective-permute-start(bf16[32,2,8,1024]{3,0,2,1:T(8,128)(2,1)} %slice.87), channel_id=1, source_target_pairs={{0,4},{4,0},{1,5},{5,1},{2,6},{6,2},{3,7},{7,3},{8,12},{12,8},{9,1... | collective-permute-start | bytes 3145736 | tf_op jit(solution)/shard_map/ppermute | solution.py:60
  8.8 2.3 %copy-start.2 = (f32[64,2,8,1024]{3,0,2,1:T(8,128)}, f32[64,2,8,1024]{3,0,2,1:T(8,128)S(1)}, u32[]{:S(2)}) copy-start(f32[64,2,8,1024]{3,0,2,1:T(8,128)S(1)} %fusion.9) | copy-start | bytes 12582916
  11.1 4.6 %collective-permute-start.11 = (bf16[32,2,8,1024]{3,0,2,1:T(8,128)(2,1)}, bf16[32,2,8,1024]{3,0,2,1:T(8,128)(2,1)}, u32[]{:S(2)}, u32[]{:S(2)}) collective-permute-start(bf16[32,2,8,1024]{3,0,2,1:T(8,128)(2,1)} %slice.86), channel_id=1, source_target_pairs={{0,4},{4,0},{1,5},{5,1},{2,6},{6,2},{3,7},{7,3},{8,12},{12,8},{9,1... | collective-permute-start | bytes 3145736 | tf_op jit(solution)/shard_map/ppermute | solution.py:60
  11.6 4.1 %copy-start.3 = (f32[64,2,8,1024]{3,0,2,1:T(8,128)S(1)}, f32[64,2,8,1024]{3,0,2,1:T(8,128)}, u32[]{:S(2)}) copy-start(f32[64,2,8,1024]{3,0,2,1:T(8,128)} %copy-done.2) | copy-start | bytes 12582916
  13.7 9.7 %copy-start.5 = (f32[32,2,8,1024]{3,0,2,1:T(8,128)}, f32[32,2,8,1024]{3,0,2,1:T(8,128)S(1)}, u32[]{:S(2)}) copy-start(f32[32,2,8,1024]{3,0,2,1:T(8,128)S(1)} %slice_add_fusion.1) | copy-start | bytes 6291460
  13.7 9.6 %collective-permute-start.1 = (bf16[4,2,8,1024]{3,0,2,1:T(4,128)(2,1)S(1)}, bf16[4,2,8,1024]{3,0,2,1:T(4,128)(2,1)S(1)}, u32[]{:S(2)}, u32[]{:S(2)}) collective-permute-start(bf16[4,2,8,1024]{3,0,2,1:T(4,128)(2,1)S(1)} %dynamic-slice_convert_fusion.1), channel_id=1, source_target_pairs={{0,8},{8,16},{16,24},{24,32},{32,40},{40,48},{48,56},{56,0},{1,9},... | collective-permute-start | bytes 393224 | tf_op jit(solution)/shard_map/ppermute | solution.py:33
  17.4 6.1 %copy-start.6 = (f32[32,2,8,1024]{3,0,2,1:T(8,128)}, f32[32,2,8,1024]{3,0,2,1:T(8,128)S(1)}, u32[]{:S(2)}) copy-start(f32[32,2,8,1024]{3,0,2,1:T(8,128)S(1)} %slice_add_fusion) | copy-start | bytes 6291460
  17.4 16.6 %copy-start.7 = (f32[16,64,64]{2,1,0:T(8,128)S(1)}, f32[16,64,64]{2,1,0:T(8,128)}, u32[]{:S(2)}) copy-start(f32[16,64,64]{2,1,0:T(8,128)} %param.10) | copy-start | bytes 786436
  23.4 6.3 %collective-permute-start.2 = (bf16[4,2,8,1024]{3,0,2,1:T(4,128)(2,1)S(1)}, bf16[4,2,8,1024]{3,0,2,1:T(4,128)(2,1)S(1)}, u32[]{:S(2)}, u32[]{:S(2)}) collective-permute-start(bf16[4,2,8,1024]{3,0,2,1:T(4,128)(2,1)S(1)} %add_convert_fusion.7), channel_id=1, source_target_pairs={{0,8},{8,16},{16,24},{24,32},{32,40},{40,48},{48,56},{56,0},{1,9},... | collective-permute-start | bytes 393224 | tf_op jit(solution)/shard_map/ppermute | solution.py:33
  23.6 9.0 %collective-permute-start.12 = (bf16[8,2,8,1024]{3,0,2,1:T(8,128)(2,1)S(1)}, bf16[8,2,8,1024]{3,0,2,1:T(8,128)(2,1)S(1)}, u32[]{:S(2)}, u32[]{:S(2)}) collective-permute-start(bf16[8,2,8,1024]{3,0,2,1:T(8,128)(2,1)S(1)} %dynamic-slice_convert_fusion), channel_id=1, source_target_pairs={{0,64},{64,128},{128,192},{192,0},{1,65},{65,129},{129,193},{193,1... | collective-permute-start | bytes 786440 | tf_op jit(solution)/shard_map/ppermute | solution.py:33
  30.8 6.4 %collective-permute-start.3 = (bf16[4,2,8,1024]{3,0,2,1:T(4,128)(2,1)S(1)}, bf16[4,2,8,1024]{3,0,2,1:T(4,128)(2,1)}, u32[]{:S(2)}, u32[]{:S(2)}) collective-permute-start(bf16[4,2,8,1024]{3,0,2,1:T(4,128)(2,1)S(1)} %add_convert_fusion.6), channel_id=1, source_target_pairs={{0,8},{8,16},{16,24},{24,32},{32,40},{40,48},{48,56},{56,0},{1,9},... | collective-permute-start | bytes 393224 | tf_op jit(solution)/shard_map/ppermute | solution.py:33
  33.7 8.3 %collective-permute-start.13 = (bf16[8,2,8,1024]{3,0,2,1:T(8,128)(2,1)S(1)}, bf16[8,2,8,1024]{3,0,2,1:T(8,128)(2,1)}, u32[]{:S(2)}, u32[]{:S(2)}) collective-permute-start(bf16[8,2,8,1024]{3,0,2,1:T(8,128)(2,1)S(1)} %add_convert_fusion.1), channel_id=1, source_target_pairs={{0,64},{64,128},{128,192},{192,0},{1,65},{65,129},{129,193},{193,1... | collective-permute-start | bytes 786440 | tf_op jit(solution)/shard_map/ppermute | solution.py:33
  38.4 7.4 %collective-permute-start.4 = (bf16[4,2,8,1024]{3,0,2,1:T(4,128)(2,1)S(1)}, bf16[4,2,8,1024]{3,0,2,1:T(4,128)(2,1)}, u32[]{:S(2)}, u32[]{:S(2)}) collective-permute-start(bf16[4,2,8,1024]{3,0,2,1:T(4,128)(2,1)S(1)} %add_convert_fusion.5), channel_id=1, source_target_pairs={{0,8},{8,16},{16,24},{24,32},{32,40},{40,48},{48,56},{56,0},{1,9},... | collective-permute-start | bytes 393224 | tf_op jit(solution)/shard_map/ppermute | solution.py:33
  43.1 7.8 %collective-permute-start.14 = (bf16[8,2,8,1024]{3,0,2,1:T(8,128)(2,1)S(1)}, bf16[8,2,8,1024]{3,0,2,1:T(8,128)(2,1)S(1)}, u32[]{:S(2)}, u32[]{:S(2)}) collective-permute-start(bf16[8,2,8,1024]{3,0,2,1:T(8,128)(2,1)S(1)} %add_convert_fusion), channel_id=1, source_target_pairs={{0,64},{64,128},{128,192},{192,0},{1,65},{65,129},{129,193},{193,1... | collective-permute-start | bytes 786440 | tf_op jit(solution)/shard_map/ppermute | solution.py:33
  46.9 10.5 %collective-permute-start.5 = (bf16[4,2,8,1024]{3,0,2,1:T(4,128)(2,1)S(1)}, bf16[4,2,8,1024]{3,0,2,1:T(4,128)(2,1)S(1)}, u32[]{:S(2)}, u32[]{:S(2)}) collective-permute-start(bf16[4,2,8,1024]{3,0,2,1:T(4,128)(2,1)S(1)} %add_convert_fusion.4), channel_id=1, source_target_pairs={{0,8},{8,16},{16,24},{24,32},{32,40},{40,48},{48,56},{56,0},{1,9},... | collective-permute-start | bytes 393224 | tf_op jit(solution)/shard_map/ppermute | solution.py:33
  52.2 5.2 %collective-permute-start.15 = (bf16[2,8,1024]{2,1,0:T(8,128)(2,1)S(1)}, bf16[2,8,1024]{2,1,0:T(8,128)(2,1)S(1)}, u32[]{:S(2)}, u32[]{:S(2)}) collective-permute-start(bf16[2,8,1024]{2,1,0:T(8,128)(2,1)S(1)} %bitcast.160), channel_id=1, source_target_pairs={{0,8},{8,16},{16,24},{24,32},{32,40},{40,48},{48,56},{56,0},{1,9},... | collective-permute-start | bytes 98312 | tf_op jit(solution)/shard_map/ppermute | solution.py:33
  57.4 5.2 %collective-permute-start.16 = (bf16[2,8,1024]{2,1,0:T(8,128)(2,1)S(1)}, bf16[2,8,1024]{2,1,0:T(8,128)(2,1)S(1)}, u32[]{:S(2)}, u32[]{:S(2)}) collective-permute-start(bf16[2,8,1024]{2,1,0:T(8,128)(2,1)S(1)} %fusion.47), channel_id=1, source_target_pairs={{0,8},{8,16},{16,24},{24,32},{32,40},{40,48},{48,56},{56,0},{1,9},... | collective-permute-start | bytes 98312 | tf_op jit(solution)/shard_map/ppermute | solution.py:33
  58.6 6.3 %collective-permute-start.6 = (bf16[4,2,8,1024]{3,0,2,1:T(4,128)(2,1)S(1)}, bf16[4,2,8,1024]{3,0,2,1:T(4,128)(2,1)S(1)}, u32[]{:S(2)}, u32[]{:S(2)}) collective-permute-start(bf16[4,2,8,1024]{3,0,2,1:T(4,128)(2,1)S(1)} %add_convert_fusion.3), channel_id=1, source_target_pairs={{0,8},{8,16},{16,24},{24,32},{32,40},{40,48},{48,56},{56,0},{1,9},... | collective-permute-start | bytes 393224 | tf_op jit(solution)/shard_map/ppermute | solution.py:33
  62.6 5.2 %collective-permute-start.17 = (bf16[2,8,1024]{2,1,0:T(8,128)(2,1)S(1)}, bf16[2,8,1024]{2,1,0:T(8,128)(2,1)S(1)}, u32[]{:S(2)}, u32[]{:S(2)}) collective-permute-start(bf16[2,8,1024]{2,1,0:T(8,128)(2,1)S(1)} %fusion.46), channel_id=1, source_target_pairs={{0,8},{8,16},{16,24},{24,32},{32,40},{40,48},{48,56},{56,0},{1,9},... | collective-permute-start | bytes 98312 | tf_op jit(solution)/shard_map/ppermute | solution.py:33
  66.0 6.8 %collective-permute-start.7 = (bf16[4,2,8,1024]{3,0,2,1:T(4,128)(2,1)S(1)}, bf16[4,2,8,1024]{3,0,2,1:T(4,128)(2,1)S(1)}, u32[]{:S(2)}, u32[]{:S(2)}) collective-permute-start(bf16[4,2,8,1024]{3,0,2,1:T(4,128)(2,1)S(1)} %add_convert_fusion.2), channel_id=1, source_target_pairs={{0,8},{8,16},{16,24},{24,32},{32,40},{40,48},{48,56},{56,0},{1,9},... | collective-permute-start | bytes 393224 | tf_op jit(solution)/shard_map/ppermute | solution.py:33
  67.8 6.5 %collective-permute-start.18 = (bf16[2,8,1024]{2,1,0:T(8,128)(2,1)S(1)}, bf16[2,8,1024]{2,1,0:T(8,128)(2,1)S(1)}, u32[]{:S(2)}, u32[]{:S(2)}) collective-permute-start(bf16[2,8,1024]{2,1,0:T(8,128)(2,1)S(1)} %fusion.45), channel_id=1, source_target_pairs={{0,8},{8,16},{16,24},{24,32},{32,40},{40,48},{48,56},{56,0},{1,9},... | collective-permute-start | bytes 98312 | tf_op jit(solution)/shard_map/ppermute | solution.py:33
  74.0 5.2 %collective-permute-start.8 = (bf16[2,8,1024]{2,1,0:T(8,128)(2,1)S(1)}, bf16[2,8,1024]{2,1,0:T(8,128)(2,1)S(1)}, u32[]{:S(2)}, u32[]{:S(2)}) collective-permute-start(bf16[2,8,1024]{2,1,0:T(8,128)(2,1)S(1)} %bitcast.159), channel_id=1, source_target_pairs={{0,64},{64,128},{128,192},{192,0},{1,65},{65,129},{129,193},{193,1... | collective-permute-start | bytes 98312 | tf_op jit(solution)/shard_map/ppermute | solution.py:33
  74.4 5.2 %collective-permute-start.19 = (bf16[2,8,1024]{2,1,0:T(8,128)(2,1)S(1)}, bf16[2,8,1024]{2,1,0:T(8,128)(2,1)S(1)}, u32[]{:S(2)}, u32[]{:S(2)}) collective-permute-start(bf16[2,8,1024]{2,1,0:T(8,128)(2,1)S(1)} %fusion.44), channel_id=1, source_target_pairs={{0,8},{8,16},{16,24},{24,32},{32,40},{40,48},{48,56},{56,0},{1,9},... | collective-permute-start | bytes 98312 | tf_op jit(solution)/shard_map/ppermute | solution.py:33
  79.3 5.2 %collective-permute-start.9 = (bf16[2,8,1024]{2,1,0:T(8,128)(2,1)S(1)}, bf16[2,8,1024]{2,1,0:T(8,128)(2,1)S(1)}, u32[]{:S(2)}, u32[]{:S(2)}) collective-permute-start(bf16[2,8,1024]{2,1,0:T(8,128)(2,1)S(1)} %fusion.50), channel_id=1, source_target_pairs={{0,64},{64,128},{128,192},{192,0},{1,65},{65,129},{129,193},{193,1... | collective-permute-start | bytes 98312 | tf_op jit(solution)/shard_map/ppermute | solution.py:33
  79.6 5.2 %collective-permute-start.20 = (bf16[2,8,1024]{2,1,0:T(8,128)(2,1)S(1)}, bf16[2,8,1024]{2,1,0:T(8,128)(2,1)S(1)}, u32[]{:S(2)}, u32[]{:S(2)}) collective-permute-start(bf16[2,8,1024]{2,1,0:T(8,128)(2,1)S(1)} %fusion.43), channel_id=1, source_target_pairs={{0,8},{8,16},{16,24},{24,32},{32,40},{40,48},{48,56},{56,0},{1,9},... | collective-permute-start | bytes 98312 | tf_op jit(solution)/shard_map/ppermute | solution.py:33
  84.5 5.2 %collective-permute-start.10 = (bf16[2,8,1024]{2,1,0:T(8,128)(2,1)S(1)}, bf16[2,8,1024]{2,1,0:T(8,128)(2,1)S(1)}, u32[]{:S(2)}, u32[]{:S(2)}) collective-permute-start(bf16[2,8,1024]{2,1,0:T(8,128)(2,1)S(1)} %fusion.49), channel_id=1, source_target_pairs={{0,64},{64,128},{128,192},{192,0},{1,65},{65,129},{129,193},{193,1... | collective-permute-start | bytes 98312 | tf_op jit(solution)/shard_map/ppermute | solution.py:33
  84.8 5.4 %collective-permute-start.21 = (bf16[2,8,1024]{2,1,0:T(8,128)(2,1)S(1)}, bf16[2,8,1024]{2,1,0:T(8,128)(2,1)S(1)}, u32[]{:S(2)}, u32[]{:S(2)}) collective-permute-start(bf16[2,8,1024]{2,1,0:T(8,128)(2,1)S(1)} %fusion.42), channel_id=1, source_target_pairs={{0,8},{8,16},{16,24},{24,32},{32,40},{40,48},{48,56},{56,0},{1,9},... | collective-permute-start | bytes 98312 | tf_op jit(solution)/shard_map/ppermute | solution.py:33
  94.3 4.3 %collective-permute-start.22 = (bf16[1,16,16,128]{3,1,2,0:T(8,128)(2,1)S(1)}, bf16[1,16,16,128]{3,1,2,0:T(8,128)(2,1)S(1)}, u32[]{:S(2)}, u32[]{:S(2)}) collective-permute-start(bf16[1,16,16,128]{3,1,2,0:T(8,128)(2,1)S(1)} %pad_maximum_fusion), channel_id=1, source_target_pairs={{0,1},{1,2},{2,3},{3,0},{4,5},{5,6},{6,7},{7,4},{8,9},{9,10},{10,1... | collective-permute-start | bytes 196616 | tf_op jit(solution)/shard_map/ppermute | solution.py:117
  94.9 5.5 %collective-permute-start.24 = (bf16[1,16,16,128]{3,1,2,0:T(8,128)(2,1)S(1)}, bf16[1,16,16,128]{3,1,2,0:T(8,128)(2,1)S(1)}, u32[]{:S(2)}, u32[]{:S(2)}) collective-permute-start(bf16[1,16,16,128]{3,1,2,0:T(8,128)(2,1)S(1)} %pad_maximum_fusion), channel_id=1, source_target_pairs={{0,3},{1,0},{2,1},{3,2},{4,7},{5,4},{6,5},{7,6},{8,11},{9,8},{10,9... | collective-permute-start | bytes 196616 | tf_op jit(solution)/shard_map/ppermute | solution.py:117
  96.4 5.8 %collective-permute-start.23 = (bf16[1,16,16,128]{3,1,2,0:T(8,128)(2,1)S(1)}, bf16[1,16,16,128]{3,1,2,0:T(8,128)(2,1)S(1)}, u32[]{:S(2)}, u32[]{:S(2)}) collective-permute-start(bf16[1,16,16,128]{3,1,2,0:T(8,128)(2,1)S(1)} %pad_maximum_fusion), channel_id=1, source_target_pairs={{0,2},{1,3},{2,0},{3,1},{4,6},{5,7},{6,4},{7,5},{8,10},{9,11},{10,... | collective-permute-start | bytes 196616 | tf_op jit(solution)/shard_map/ppermute | solution.py:117
